TPU v7x, 32 devices: a whole 2x2x4 slice. The times are simulated.
32 devices in a mesh: dp: 8 (over z, core), ctx: 4 (over y, x).
Axes of the slice: x: 2, y: 2, z: 4, core: 2. Of those that a mesh axis runs over, the one named last changes fastest.
Arguments:
- hidden: bfloat16 [8, 512, 3072], P('dp', 'ctx'), may hold values from -6 to 6
- gating: bfloat16 [8, 512, 3072], P('dp', 'ctx'), may hold values from -6 to 6
- dt_raw: bfloat16 [8, 512, 48], P('dp', 'ctx'), may hold values from -4 to 4
- b_input: bfloat16 [8, 512, 128], P('dp', 'ctx'), may hold values from -0.5 to 0.5
- c_input: bfloat16 [8, 512, 128], P('dp', 'ctx'), may hold values from -0.5 to 0.5
- resets: int32 [8, 2], P('dp'), may hold values 0 or 1
- cotangent: bfloat16 [8, 512, 3072], P('dp', 'ctx'), may hold values from -18 to 18
- parameters: float32 [3216], replicated, may hold values from -10 to 2
- adam_mean: float32 [8, 804], P('dp'), may hold values from -6 to 6
- adam_square: float32 [8, 804], P('dp'), may hold values from 0.1 to 2
- bucket_size: int32 [8], replicated, may hold values from 1 to 804, 3216 in all
- bucket_owner: int32 [8], replicated, may hold values from 0 to 7, each once
Outputs:
- normed: bfloat16 [8, 512, 3072], P('dp', 'ctx')
- grad_hidden: bfloat16 [8, 512, 3072], P('dp', 'ctx')
- grad_gating: bfloat16 [8, 512, 3072], P('dp', 'ctx')
- grad_dt: bfloat16 [8, 512, 48], P('dp', 'ctx')
- grad_b: bfloat16 [8, 512, 128], P('dp', 'ctx')
- grad_c: bfloat16 [8, 512, 128], P('dp', 'ctx')
- new_params: float32 [3216], replicated
- new_mean: float32 [8, 804], P('dp')
- new_square: float32 [8, 804], P('dp')
Inputs may be any that keep to these rules, and one draw needn't show every extreme that they name: `bucket_size`: the sizes sum to 3216; the largest is exactly 804. `bucket_owner`: each dp index owns exactly one bucket.
All inputs are finite; a program needn't handle non-finite values. No bound on the sum of `resets` on one device may be relied on, other than what follows from the above.
Results may differ from a plain program's by a relative error of at most 0.0076.
Values may be sent and summed in bfloat16 or wider, within the bound.
No kernel may reach another device: no remote copies, remote signals or barrier semaphores. Data moves between devices by JAX's collectives and lax.ppermute only.
A program may use at most 128 MiB of HBM per device.

v0:
```python
import jax
import jax.numpy as jnp
from jax import lax
from jax.sharding import PartitionSpec as P

SPAN = 256
CH = 3072


eps_norm = 1e-05
clip_norm = 64.0
beta_one = 0.9
beta_two = 0.95
adam_eps = 1e-08
learn_rate = 0.02
step_count = 100.0
highest = lax.Precision.HIGHEST


def from_root(value, axis, source):
    kept = jnp.where(lax.axis_index(axis) == source, value, 0).astype(value.dtype)
    return lax.psum(kept, axis)


def rounded(value):
    return lax.optimization_barrier(value.astype(jnp.bfloat16)).astype(jnp.float32)


def ssd_group(hidden, dt_raw, b_input, c_input, resets, a_log, dt_bias, skip):
    length = hidden.shape[0]
    heads = a_log.shape[0]
    width = hidden.shape[1] // heads
    blocks = length // SPAN
    step_sizes = jax.nn.softplus(dt_raw.astype(jnp.float32) + dt_bias)
    log_decay = (step_sizes * -jnp.exp(a_log)).reshape(blocks, SPAN, heads).transpose(0, 2, 1)
    cumul = jnp.cumsum(log_decay, axis=2)
    inputs = hidden.astype(jnp.float32).reshape(blocks, SPAN, heads, width)
    scaled = rounded(inputs * step_sizes.reshape(blocks, SPAN, heads, 1))
    b_rows = b_input.astype(jnp.float32).reshape(blocks, SPAN, -1)
    c_rows = c_input.astype(jnp.float32).reshape(blocks, SPAN, -1)
    scores = jnp.einsum("ctn,csn->cts", c_rows, b_rows, precision=highest)
    causal = jnp.arange(SPAN)[:, None] >= jnp.arange(SPAN)[None, :]
    spread = cumul[:, :, :, None] - cumul[:, :, None, :]
    decay = jnp.where(causal, jnp.exp(jnp.where(causal, spread, 0.0)), 0.0)
    weights = rounded(scores[:, None] * decay)
    intra = jnp.einsum("chts,cshp->cthp", weights, scaled, precision=highest)
    tail = cumul[:, :, -1:] - cumul
    b_decayed = rounded(b_rows[:, None] * jnp.exp(tail)[..., None])
    block_state = jnp.einsum("chsn,cshp->chnp", b_decayed, scaled, precision=highest)
    keep = 1.0 - resets.astype(jnp.float32)

    def advance(state, items):
        keep_one, total, added = items
        entering = state * keep_one
        return (jnp.exp(total)[:, None, None] * entering + added, entering)

    start_state = jnp.zeros(block_state.shape[1:], jnp.float32)
    last_state, entering = lax.scan(advance, start_state, (keep, cumul[:, :, -1], block_state))
    c_decayed = rounded(c_rows[:, None] * jnp.exp(cumul)[..., None])
    inter = jnp.einsum("chtn,chnp->cthp", c_decayed, rounded(entering), precision=highest)
    output = intra + inter + skip[:, None] * inputs
    return output.reshape(length, heads * width).astype(jnp.bfloat16)


def gate_values(y_values, gating):
    gated = y_values.astype(jnp.float32) * jax.nn.silu(gating.astype(jnp.float32))
    return (gated, jnp.sum(gated * gated, axis=-1))


def normalize(gated, total, gain):
    factor = lax.rsqrt(total / CH + eps_norm)
    return (factor, (gated * factor[..., None] * gain).astype(jnp.bfloat16))


def norm_backward(cotangent, gain, gated, factor, dot_total, y_values, gating):
    upstream = cotangent.astype(jnp.float32) * gain
    d_gated = (
        upstream * factor[..., None]
        - gated * (factor * factor * factor * dot_total / CH)[..., None]
    )
    gate_f = gating.astype(jnp.float32)
    sigma = jax.nn.sigmoid(gate_f)
    d_y = (d_gated * (gate_f * sigma)).astype(jnp.bfloat16)
    d_gate = (
        d_gated * y_values.astype(jnp.float32) * sigma * (1.0 + gate_f * (1.0 - sigma))
    ).astype(jnp.bfloat16)
    d_gain = jnp.sum(
        cotangent.astype(jnp.float32) * gated * factor[..., None], axis=tuple(range(gated.ndim - 1))
    )
    return (d_y, d_gate, d_gain)


def on_device(
    hidden,
    gating,
    dt_raw,
    b_input,
    c_input,
    resets,
    cotangent,
    parameters,
    adam_mean,
    adam_square,
    bucket_size,
    bucket_owner,
):
    heads_all = dt_raw.shape[2]
    groups = lax.axis_size("ctx")
    group = heads_all // groups
    state_size = b_input.shape[2]
    tokens = hidden.shape[1]
    first = lax.axis_index("ctx") * group
    head_params = parameters[: 3 * heads_all].reshape(3, heads_all)
    gain = parameters[3 * heads_all :]
    local_params = lax.dynamic_slice_in_dim(head_params, first, group, 1)
    b_all, c_all = (
        lax.all_gather(b_input, "ctx", axis=1, tiled=True),
        lax.all_gather(c_input, "ctx", axis=1, tiled=True),
    )
    seq_resets = resets[0]

    def local_fn(x_arg, dt_arg, b_arg, c_arg, a_arg, bias_arg, skip_arg):
        return ssd_group(x_arg, dt_arg, b_arg, c_arg, seq_resets, a_arg, bias_arg, skip_arg)

    x_heads, dt_heads = (
        lax.all_to_all(hidden, "ctx", split_axis=2, concat_axis=1, tiled=True),
        lax.all_to_all(dt_raw, "ctx", split_axis=2, concat_axis=1, tiled=True),
    )
    y_heads, pullback = jax.vjp(
        local_fn,
        x_heads[0],
        dt_heads[0],
        b_all[0],
        c_all[0],
        local_params[0],
        local_params[1],
        local_params[2],
    )
    y_seq = lax.all_to_all(y_heads[None], "ctx", split_axis=1, concat_axis=2, tiled=True)
    gated, total = gate_values(y_seq, gating)
    factor, normed = normalize(gated, total, gain)
    dot_total = jnp.sum(cotangent.astype(jnp.float32) * gain * gated, axis=-1)
    d_y, grad_gating, d_gain = norm_backward(
        cotangent, gain, gated, factor, dot_total, y_seq, gating
    )
    d_y_heads = lax.all_to_all(d_y, "ctx", split_axis=2, concat_axis=1, tiled=True)
    d_x, d_dt, d_b, d_c, d_alog, d_bias, d_skip = pullback(d_y_heads[0])
    d_pair = jnp.concatenate([d_b, d_c], axis=-1)
    grad_hidden, grad_dt, pair_parts = (
        lax.all_to_all(d_x[None], "ctx", split_axis=1, concat_axis=2, tiled=True),
        lax.all_to_all(d_dt[None], "ctx", split_axis=1, concat_axis=2, tiled=True),
        lax.all_to_all(d_pair[None], "ctx", split_axis=1, concat_axis=2, tiled=True),
    )
    pair_sum = jnp.sum(
        pair_parts.reshape(1, tokens, groups, 2 * state_size).astype(jnp.float32), axis=2
    ).astype(jnp.bfloat16)
    grad_b = pair_sum[..., :state_size]
    grad_c = pair_sum[..., state_size:]
    head_grads = jnp.stack([d_alog, d_bias, d_skip])
    full_heads = lax.dynamic_update_slice(
        jnp.zeros((3, heads_all), jnp.float32), head_grads, (0, first)
    )
    grad_part = jnp.concatenate([full_heads.reshape(-1), d_gain])
    gradient = lax.psum(grad_part, ("dp", "ctx"))
    grad_norm = jnp.sqrt(jnp.sum(gradient * gradient))
    shrink = jnp.minimum(1.0, clip_norm / (grad_norm + 1e-06))
    owners = lax.axis_size("dp")
    slot_cap = adam_mean.shape[1]
    total_len = parameters.shape[0]
    ends = jnp.cumsum(bucket_size)
    begins = ends - bucket_size
    order = jnp.arange(owners, dtype=jnp.int32)
    mine = lax.axis_index("dp")
    my_bucket = jnp.sum(jnp.where(bucket_owner == mine, order, 0))
    row_begin = jnp.sum(jnp.where(order == my_bucket, begins, 0))
    row_size = jnp.sum(jnp.where(order == my_bucket, bucket_size, 0))
    slots = jnp.arange(slot_cap, dtype=jnp.int32)
    valid = slots < row_size
    padding = jnp.zeros((slot_cap,), jnp.float32)
    grad_row = (
        jnp.where(
            valid,
            lax.dynamic_slice_in_dim(jnp.concatenate([gradient, padding]), row_begin, slot_cap),
            0.0,
        )
        * shrink
    )
    param_row = jnp.where(
        valid,
        lax.dynamic_slice_in_dim(jnp.concatenate([parameters, padding]), row_begin, slot_cap),
        0.0,
    )
    new_mean = beta_one * adam_mean[0] + (1.0 - beta_one) * grad_row
    new_square = beta_two * adam_square[0] + (1.0 - beta_two) * grad_row * grad_row
    direction = (
        new_mean
        / (1.0 - beta_one**step_count)
        / (jnp.sqrt(new_square / (1.0 - beta_two**step_count)) + adam_eps)
    )
    new_row = param_row - learn_rate * direction
    flat = jnp.arange(total_len, dtype=jnp.int32)
    bucket_of = jnp.sum((ends[None, :] <= flat[:, None]).astype(jnp.int32), axis=1)
    match = order[None, :] == bucket_of[:, None]
    owner_of = jnp.sum(jnp.where(match, bucket_owner[None, :], 0), axis=1)
    offset = flat - jnp.sum(jnp.where(match, begins[None, :], 0), axis=1)

    def place(owner, current):
        received = from_root(new_row, "dp", owner)
        picked = received[jnp.clip(offset, 0, slot_cap - 1)]
        return jnp.where(owner_of == owner, picked, current)

    new_params = lax.fori_loop(0, owners, place, jnp.zeros((total_len,), jnp.float32))
    return (
        normed,
        grad_hidden,
        grad_gating,
        grad_dt,
        grad_b,
        grad_c,
        new_params,
        new_mean[None],
        new_square[None],
    )


def solution(mesh):
    return jax.shard_map(
        on_device,
        mesh=mesh,
        in_specs=(
            P("dp", "ctx", None),
            P("dp", "ctx", None),
            P("dp", "ctx", None),
            P("dp", "ctx", None),
            P("dp", "ctx", None),
            P("dp", None),
            P("dp", "ctx", None),
            P(),
            P("dp", None),
            P("dp", None),
            P(),
            P(),
        ),
        out_specs=(
            P("dp", "ctx", None),
            P("dp", "ctx", None),
            P("dp", "ctx", None),
            P("dp", "ctx", None),
            P("dp", "ctx", None),
            P("dp", "ctx", None),
            P(),
            P("dp", None),
            P("dp", None),
        ),
        check_vma=False,
    )
```

profile of v0, /device:TPU:0, one launch (start us, length us, event | category | flops | bytes accessed | tf_op | source)
XLA Modules:
  0.0 522.5 jit_solution(12223929352879686177)
XLA Ops:
  3.1 5.2 all-to-all-start.1
  10.4 9.1 %all_gather.7 = bf16[1,512,128]{2,1,0:T(8,128)(2,1)S(1)} all-gather(bf16[1,128,128]{2,1,0:T(8,128)(2,1)} %param.21), channel_id=1, replica_groups=mesh['dp'=8,'ctx'=4] {'ctx'}, dimensions={1}, use_global_device_ids=true | all-gather | bytes 163840 | tf_op jit(solution)/shard_map/all_gather | solution.py:117
  19.5 8.2 %all_gather.6 = bf16[1,512,128]{2,1,0:T(8,128)(2,1)S(1)} all-gather(bf16[1,128,128]{2,1,0:T(8,128)(2,1)} %param.22), channel_id=1, replica_groups=mesh['dp'=8,'ctx'=4] {'ctx'}, dimensions={1}, use_global_device_ids=true | all-gather | bytes 163840 | tf_op jit(solution)/shard_map/all_gather | solution.py:118
  28.5 3.8 copy.220
  32.3 17.7 %reduce.25 = bf16[3072,128]{1,0:T(8,128)(2,1)} reduce(bf16[3072,1,128]{2,1,0:T(2,128)(2,1)S(1)} %bitcast.189, bf16[]{:T(256)} %broadcast.319), dimensions={1}, to_apply=%bitcast.118.reduce_sub_computation | reduce | bytes 1572866
  50.1 2.0 reshape.586
  52.0 4.4 all-to-all-start
  59.5 1.9 multiply_convert_fusion.2
  61.5 1.8 multiply_convert_fusion.1
  63.4 2.8 multiply_convert_fusion
  66.2 2.4 reshape.587
  71.4 2.2 copy.221
  73.6 2.6 reshape.555
  78.3 1.8 fusion.81
  80.2 7.1 %while.52 = (s32[]{:T(128)}, f32[12,128,64]{2,1,0:T(8,128)S(1)}, f32[2,12,128,64]{3,2,1,0:T(8,128)S(1)}, f32[2,12]{1,0:T(2,128)S(1)}, f32[2,12,1,1]{1,3,2,0:T(1,...) while((s32[]{:T(128)}, f32[12,128,64]{2,1,0:T(8,128)S(1)}, ...), condition=%wide.region_3.4_spmd.clone, body=%wide.region_2.3_spmd.clone.sunk | while | flops 589827 | bytes 5899176 | solution.py:58
  87.5 2.5 fusion.82
  93.9 4.1 copy.238
  98.0 6.2 %reduce.26 = bf16[512,768]{1,0:T(8,128)(2,1)} reduce(bf16[512,1,768]{2,1,0:T(2,128)(2,1)S(1)} %bitcast.183, bf16[]{:T(256)} %broadcast.319), dimensions={1}, to_apply=%bitcast.120.reduce_sub_computation | reduce | bytes 1572866
  104.2 2.0 reshape.588
  106.3 4.3 all-to-all-start.2
  113.8 4.9 all-to-all-done.2
  118.7 2.4 reshape.589
  122.6 1.9 copy.240
  127.8 2.5 fusion.31
  130.3 12.5 %copy.372 = bf16[1,128,3072]{1,0,2:T(2,128)(2,1)S(1)} copy(bf16[1,128,3072]{1,2,0:T(8,128)(2,1)S(1)} %get-tuple-element.653) | data formatting | bytes 1572864 | tf_op jit(solution)/shard_map/convert_element_type | solution.py:83
  142.8 17.7 %reduce.27 = bf16[3072,128]{1,0:T(8,128)(2,1)} reduce(bf16[3072,1,128]{2,1,0:T(2,128)(2,1)S(1)} %bitcast.185, bf16[]{:T(256)} %broadcast.319), dimensions={1}, to_apply=%bitcast.156.reduce_sub_computation | reduce | bytes 1572866
  160.5 2.1 reshape.590
  162.6 3.7 all-to-all-start.3
  171.6 2.3 copy.272
  173.9 2.3 copy.274
  176.2 2.1 reshape.591
  182.2 2.3 squeeze.55
  184.5 2.1 convolution_convert_fusion.3
  186.6 2.7 convolution_convert_fusion
  194.1 13.9 %while.53 = (s32[]{:T(128)}, f32[12,128,64]{2,1,0:T(8,128)S(1)}, f32[2,12]{1,0:T(2,128)}, f32[2,12,128,64]{3,2,1,0:T(8,128)}, f32[2,12,128,64]{2,3,1,0:T(8,128)}...) while((s32[]{:T(128)}, f32[12,128,64]{2,1,0:T(8,128)S(1)}, ...), condition=%wide.region_8.9_spmd.clone, body=%wide.region_6.8_spmd.clone.sunk | while | flops 688132 | bytes 4327636 | solution.py:58
  207.9 3.8 fusion.83
  211.8 2.8 convolution_convert_fusion.1
  219.4 5.7 %fusion.12 = (f32[2,12,256]{2,1,0:T(8,128)S(1)}, f32[2,12,256]{2,1,0:T(8,128)S(1)}, f32[2,256,256]{2,1,0:T(8,128)}) fusion(bf16[2,12,256,256]{3,2,1,0:T(8,128)(2,1)S(1)} %copy-done.16, f32[2,12,256]{2,1,0:T(8,128)S(1)} %copy-done.37, f32[2,256,256]{2,1,0:T(8,128)} %copy-done.26, pred[256,256]{1,0:T(8,128)(4,1)S(1)} %copy-done.41), kind=kLoop, calls=%fused_computation.33 | loop fusion | flops 18731008 | bytes 4333568 | tf_op jit(solution)/shard_map/transpose(jvp())/reduce_sum | solution.py:43
  225.2 3.8 fusion.14
  229.6 5.0 reduce-window.30
  237.7 4.2 all-to-all-start.5
  244.2 41.3 %psum.21 = f32[3216]{0:T(1024)S(1)} all-reduce(f32[3216]{0:T(1024)S(1)} %pad_maximum_fusion), channel_id=1, replica_groups=mesh['dp'=8,'ctx'=4] {'dp','ctx'}, use_global_device_ids=true, to_apply=%region_30.31 | all-reduce | flops 3216 | bytes 25728 | tf_op jit(solution)/shard_map/psum | solution.py:164
  289.0 5.3 %reduce.28 = bf16[512,768]{1,0:T(8,128)(2,1)S(1)} reduce(bf16[512,1,768]{2,1,0:T(2,128)(2,1)S(1)} %bitcast.187, bf16[]{:T(256)} %broadcast.319), dimensions={1}, to_apply=%bitcast.124.reduce_sub_computation | reduce | bytes 1572866
  295.8 2.1 reduce.30
  299.4 3.7 all-to-all-start.6
  303.8 4.6 all-to-all-done.6
  308.4 3.5 all-to-all-start.4
  312.0 204.6 %while.54 = (s32[]{:T(128)}, f32[3216]{0:T(1024)S(1)}, s32[3216]{0:T(1024)S(1)}, f32[804]{0:T(1024)S(1)}, s32[3216]{0:T(1024)S(1)}, /*index=5*/s32[]{:T(128)}, u32[]{:T(128)}, u32[]{:T(128)}, s32[]{:T(128)}) while((s32[]{:T(128)}, f32[3216]{0:T(1024)S(1)}, s32[3216]{0:T(1024)S(1)}, f32[804]{0:T(1024)S(1)}, s32[3216]{0:T(1024)S(1)}, ...), condition=%wide.region_37.38_spmd.clone, body=%wide.region_35.37_spmd.clone.sunk | while | flops 28223 | bytes 183773 | solution.py:212
  312.0 13.6 %psum.24 = f32[804]{0:T(1024)S(1)} all-reduce(f32[804]{0:T(1024)S(1)} %broadcast_select_fusion.2), channel_id=1, replica_groups=mesh['dp'=8,'ctx'=4] {'dp'}, use_global_device_ids=true, to_apply=%region_36.36 | all-reduce | flops 804 | bytes 6432 | tf_op jit(solution)/shard_map/while/body/eval_jaxpr/psum | solution.py:22
  325.7 11.8 %gather_fusion = f32[3216]{0:T(1024)S(1)} fusion(f32[804]{0:T(1024)S(1)} %psum.24, s32[4096]{0:T(1024)S(1)} %pad_clamp_fusion.2), kind=kCustom, calls=%fused_computation.clone.clone.1 | custom fusion | bytes 38592 | tf_op jit(solution)/shard_map/while/body/eval_jaxpr/gather | solution.py:209
  337.6 13.6 %psum.24 = f32[804]{0:T(1024)S(1)} all-reduce(f32[804]{0:T(1024)S(1)} %broadcast_select_fusion.2), channel_id=1, replica_groups=mesh['dp'=8,'ctx'=4] {'dp'}, use_global_device_ids=true, to_apply=%region_36.36 | all-reduce | flops 804 | bytes 6432 | tf_op jit(solution)/shard_map/while/body/eval_jaxpr/psum | solution.py:22
  351.2 11.8 %gather_fusion = f32[3216]{0:T(1024)S(1)} fusion(f32[804]{0:T(1024)S(1)} %psum.24, s32[4096]{0:T(1024)S(1)} %pad_clamp_fusion.2), kind=kCustom, calls=%fused_computation.clone.clone.1 | custom fusion | bytes 38592 | tf_op jit(solution)/shard_map/while/body/eval_jaxpr/gather | solution.py:209
  363.1 13.6 %psum.24 = f32[804]{0:T(1024)S(1)} all-reduce(f32[804]{0:T(1024)S(1)} %broadcast_select_fusion.2), channel_id=1, replica_groups=mesh['dp'=8,'ctx'=4] {'dp'}, use_global_device_ids=true, to_apply=%region_36.36 | all-reduce | flops 804 | bytes 6432 | tf_op jit(solution)/shard_map/while/body/eval_jaxpr/psum | solution.py:22
  376.8 11.8 %gather_fusion = f32[3216]{0:T(1024)S(1)} fusion(f32[804]{0:T(1024)S(1)} %psum.24, s32[4096]{0:T(1024)S(1)} %pad_clamp_fusion.2), kind=kCustom, calls=%fused_computation.clone.clone.1 | custom fusion | bytes 38592 | tf_op jit(solution)/shard_map/while/body/eval_jaxpr/gather | solution.py:209
  388.7 13.6 %psum.24 = f32[804]{0:T(1024)S(1)} all-reduce(f32[804]{0:T(1024)S(1)} %broadcast_select_fusion.2), channel_id=1, replica_groups=mesh['dp'=8,'ctx'=4] {'dp'}, use_global_device_ids=true, to_apply=%region_36.36 | all-reduce | flops 804 | bytes 6432 | tf_op jit(solution)/shard_map/while/body/eval_jaxpr/psum | solution.py:22
  402.4 11.8 %gather_fusion = f32[3216]{0:T(1024)S(1)} fusion(f32[804]{0:T(1024)S(1)} %psum.24, s32[4096]{0:T(1024)S(1)} %pad_clamp_fusion.2), kind=kCustom, calls=%fused_computation.clone.clone.1 | custom fusion | bytes 38592 | tf_op jit(solution)/shard_map/while/body/eval_jaxpr/gather | solution.py:209
  414.3 13.6 %psum.24 = f32[804]{0:T(1024)S(1)} all-reduce(f32[804]{0:T(1024)S(1)} %broadcast_select_fusion.2), channel_id=1, replica_groups=mesh['dp'=8,'ctx'=4] {'dp'}, use_global_device_ids=true, to_apply=%region_36.36 | all-reduce | flops 804 | bytes 6432 | tf_op jit(solution)/shard_map/while/body/eval_jaxpr/psum | solution.py:22
  428.0 11.8 %gather_fusion = f32[3216]{0:T(1024)S(1)} fusion(f32[804]{0:T(1024)S(1)} %psum.24, s32[4096]{0:T(1024)S(1)} %pad_clamp_fusion.2), kind=kCustom, calls=%fused_computation.clone.clone.1 | custom fusion | bytes 38592 | tf_op jit(solution)/shard_map/while/body/eval_jaxpr/gather | solution.py:209
  439.9 13.6 %psum.24 = f32[804]{0:T(1024)S(1)} all-reduce(f32[804]{0:T(1024)S(1)} %broadcast_select_fusion.2), channel_id=1, replica_groups=mesh['dp'=8,'ctx'=4] {'dp'}, use_global_device_ids=true, to_apply=%region_36.36 | all-reduce | flops 804 | bytes 6432 | tf_op jit(solution)/shard_map/while/body/eval_jaxpr/psum | solution.py:22
  453.5 11.8 %gather_fusion = f32[3216]{0:T(1024)S(1)} fusion(f32[804]{0:T(1024)S(1)} %psum.24, s32[4096]{0:T(1024)S(1)} %pad_clamp_fusion.2), kind=kCustom, calls=%fused_computation.clone.clone.1 | custom fusion | bytes 38592 | tf_op jit(solution)/shard_map/while/body/eval_jaxpr/gather | solution.py:209
  465.4 13.6 %psum.24 = f32[804]{0:T(1024)S(1)} all-reduce(f32[804]{0:T(1024)S(1)} %broadcast_select_fusion.2), channel_id=1, replica_groups=mesh['dp'=8,'ctx'=4] {'dp'}, use_global_device_ids=true, to_apply=%region_36.36 | all-reduce | flops 804 | bytes 6432 | tf_op jit(solution)/shard_map/while/body/eval_jaxpr/psum | solution.py:22
  479.1 11.8 %gather_fusion = f32[3216]{0:T(1024)S(1)} fusion(f32[804]{0:T(1024)S(1)} %psum.24, s32[4096]{0:T(1024)S(1)} %pad_clamp_fusion.2), kind=kCustom, calls=%fused_computation.clone.clone.1 | custom fusion | bytes 38592 | tf_op jit(solution)/shard_map/while/body/eval_jaxpr/gather | solution.py:209
  491.0 13.6 %psum.24 = f32[804]{0:T(1024)S(1)} all-reduce(f32[804]{0:T(1024)S(1)} %broadcast_select_fusion.2), channel_id=1, replica_groups=mesh['dp'=8,'ctx'=4] {'dp'}, use_global_device_ids=true, to_apply=%region_36.36 | all-reduce | flops 804 | bytes 6432 | tf_op jit(solution)/shard_map/while/body/eval_jaxpr/psum | solution.py:22
  504.7 11.8 %gather_fusion = f32[3216]{0:T(1024)S(1)} fusion(f32[804]{0:T(1024)S(1)} %psum.24, s32[4096]{0:T(1024)S(1)} %pad_clamp_fusion.2), kind=kCustom, calls=%fused_computation.clone.clone.1 | custom fusion | bytes 38592 | tf_op jit(solution)/shard_map/while/body/eval_jaxpr/gather | solution.py:209
  (373 shorter events, 81.0 us)
Async XLA Ops:
  3.1 49.0 %all-to-all-start.1 = ((bf16[4,2,768]{2,1,0:T(2,128)(2,1)}), bf16[4,2,768]{2,1,0:T(2,128)(2,1)S(1)}, u32[]{:S(2)}, u32[]{:S(2)}) async-start(bf16[4,2,768]{2,1,0:T(2,128)(2,1)} %reshape.584), calls=%async_computation.1 | async-start | bytes 24576 | tf_op jit(solution)/shard_map/all_to_all | solution.py:127
  9.1 23.2 %copy-start.76 = (f32[3,12]{1,0:T(4,128)}, f32[3,12]{1,0:T(4,128)S(1)}, u32[]{:S(2)}) copy-start(f32[3,12]{1,0:T(4,128)S(1)} %constant_dynamic-slice_fusion.4) | copy-start | bytes 436
  9.1 47.4 %copy-start.68 = (f32[12]{0:T(128)}, f32[12]{0:T(128)S(1)}, u32[]{:S(2)}) copy-start(f32[12]{0:T(128)S(1)} %get-tuple-element.665) | copy-start | bytes 148
  9.1 47.4 %copy-start.70 = (f32[12]{0:T(128)}, f32[12]{0:T(128)S(1)}, u32[]{:S(2)}) copy-start(f32[12]{0:T(128)S(1)} %get-tuple-element.666) | copy-start | bytes 148
  9.2 80.8 %copy-start.72 = (f32[12]{0:T(128)}, f32[12]{0:T(128)S(1)}, u32[]{:S(2)}) copy-start(f32[12]{0:T(128)S(1)} %get-tuple-element.664) | copy-start | bytes 148
  19.5 8.6 %copy-start.34 = (bf16[1,512,128]{2,1,0:T(8,128)(2,1)}, bf16[1,512,128]{2,1,0:T(8,128)(2,1)S(1)}, u32[]{:S(2)}) copy-start(bf16[1,512,128]{2,1,0:T(8,128)(2,1)S(1)} %all_gather.7) | copy-start | bytes 393220
  28.0 35.3 %copy-start.26 = (f32[2,256,256]{2,1,0:T(8,128)}, f32[2,256,256]{2,1,0:T(8,128)S(1)}, u32[]{:S(2)}) copy-start(f32[2,256,256]{2,1,0:T(8,128)S(1)} %fusion.80) | copy-start | bytes 1572868
  28.1 35.3 %copy-start.40 = (pred[256,256]{1,0:T(8,128)(4,1)}, pred[256,256]{1,0:T(8,128)(4,1)S(1)}, u32[]{:S(2)}) copy-start(pred[256,256]{1,0:T(8,128)(4,1)S(1)} %iota_compare_fusion) | copy-start | bytes 196612
  28.4 31.1 %copy-start.28 = (f32[2,256,128]{2,1,0:T(8,128)}, f32[2,256,128]{2,1,0:T(8,128)S(1)}, u32[]{:S(2)}) copy-start(f32[2,256,128]{2,1,0:T(8,128)S(1)} %convert_element_type.240) | copy-start | bytes 786436
  28.5 33.0 %copy-start.30 = (f32[2,256,128]{2,1,0:T(8,128)}, f32[2,256,128]{2,1,0:T(8,128)S(1)}, u32[]{:S(2)}) copy-start(f32[2,256,128]{2,1,0:T(8,128)S(1)} %convert_element_type.243) | copy-start | bytes 786436
  52.0 14.1 %all-to-all-start = ((bf16[4,2,49152]{2,1,0:T(2,128)(2,1)}), bf16[4,2,49152]{2,1,0:T(2,128)(2,1)}, u32[]{:S(2)}, u32[]{:S(2)}) async-start(bf16[4,2,49152]{2,1,0:T(2,128)(2,1)} %reshape.586), calls=%async_computation | async-start | bytes 1572864 | tf_op jit(solution)/shard_map/all_to_all | solution.py:126
  56.7 19.6 %copy-start.49 = (f32[2,256,12]{1,2,0:T(8,128)}, f32[2,256,12]{1,2,0:T(8,128)S(1)}, u32[]{:S(2)}) copy-start(f32[2,256,12]{1,2,0:T(8,128)S(1)} %get-tuple-element.659) | copy-start | bytes 73732
  58.3 5.0 copy-start.43
  59.2 4.1 copy-start.47
  59.5 3.8 copy-start.51
  59.5 3.8 copy-start.53
  59.5 3.8 copy-start.36
  87.5 3.0 copy-start.2
  87.5 3.1 copy-start.8
  104.2 6.4 %copy-start.58 = (f32[3216]{0:T(1024)S(1)}, f32[3216]{0:T(1024)}, u32[]{:S(2)}) copy-start(f32[3216]{0:T(1024)} %param.25) | copy-start | bytes 38596
  104.2 6.5 %copy-start.38 = (bf16[1,128,3072]{2,1,0:T(8,128)(2,1)S(1)}, bf16[1,128,3072]{2,1,0:T(8,128)(2,1)}, u32[]{:S(2)}) copy-start(bf16[1,128,3072]{2,1,0:T(8,128)(2,1)} %param.19) | copy-start | bytes 2359300
  106.3 5.6 %copy-start.39 = (bf16[1,128,3072]{2,1,0:T(8,128)(2,1)S(1)}, bf16[1,128,3072]{2,1,0:T(8,128)(2,1)}, u32[]{:S(2)}) copy-start(bf16[1,128,3072]{2,1,0:T(8,128)(2,1)} %param.24) | copy-start | bytes 2359300
  106.3 12.4 %all-to-all-start.2 = ((bf16[4,2,49152]{2,1,0:T(2,128)(2,1)}), bf16[4,2,49152]{2,1,0:T(2,128)(2,1)}, u32[]{:S(2)}, u32[]{:S(2)}) async-start(bf16[4,2,49152]{2,1,0:T(2,128)(2,1)} %reshape.588), calls=%async_computation.2 | async-start | bytes 1572864 | tf_op jit(solution)/shard_map/all_to_all | solution.py:139
  160.5 9.0 %copy-start.77 = (f32[1,804]{1,0:T(1,128)S(1)}, f32[1,804]{1,0:T(1,128)}, u32[]{:S(2)}) copy-start(f32[1,804]{1,0:T(1,128)} %param.27) | copy-start | bytes 9652
  160.5 9.0 %copy-start.78 = (f32[1,804]{1,0:T(1,128)S(1)}, f32[1,804]{1,0:T(1,128)}, u32[]{:S(2)}) copy-start(f32[1,804]{1,0:T(1,128)} %param.26) | copy-start | bytes 9652
  162.6 13.6 %all-to-all-start.3 = ((bf16[4,2,49152]{2,1,0:T(2,128)(2,1)}), bf16[4,2,49152]{2,1,0:T(2,128)(2,1)S(1)}, u32[]{:S(2)}, u32[]{:S(2)}) async-start(bf16[4,2,49152]{2,1,0:T(2,128)(2,1)} %reshape.590), calls=%async_computation.3 | async-start | bytes 1572864 | tf_op jit(solution)/shard_map/all_to_all | solution.py:146
  184.5 4.9 copy-start
  194.1 3.4 copy-start.74
  200.9 3.5 copy-start.74
  207.9 3.8 copy-start.10
  207.9 3.8 copy-start.15
  207.9 6.6 %copy-start.13 = (f32[1,128,3072]{1,0,2:T(1,128)S(1)}, f32[1,128,3072]{1,0,2:T(1,128)}, u32[]{:S(2)}) copy-start(f32[1,128,3072]{1,0,2:T(1,128)} %copy-done.12) | copy-start | bytes 4718596
  211.7 2.8 copy-start.18
  211.8 3.6 copy-start.3
  219.3 5.8 %copy-start.23 = (bf16[2,12,256,128]{3,2,1,0:T(8,128)(2,1)S(1)}, bf16[2,12,256,128]{3,2,1,0:T(8,128)(2,1)}, u32[]{:S(2)}) copy-start(bf16[2,12,256,128]{3,2,1,0:T(8,128)(2,1)} %convolution_convert_fusion.2) | copy-start | bytes 4718596
  219.3 5.8 %copy-start.24 = (bf16[2,12,256,128]{3,2,1,0:T(8,128)(2,1)S(1)}, bf16[2,12,256,128]{3,2,1,0:T(8,128)(2,1)}, u32[]{:S(2)}) copy-start(bf16[2,12,256,128]{3,2,1,0:T(8,128)(2,1)} %convolution_convert_fusion.1) | copy-start | bytes 4718596
  219.3 5.8 %copy-start.29 = (f32[2,256,128]{2,1,0:T(8,128)S(1)}, f32[2,256,128]{2,1,0:T(8,128)}, u32[]{:S(2)}) copy-start(f32[2,256,128]{2,1,0:T(8,128)} %copy-done.28) | copy-start | bytes 786436
  219.3 5.8 %copy-start.31 = (f32[2,256,128]{2,1,0:T(8,128)S(1)}, f32[2,256,128]{2,1,0:T(8,128)}, u32[]{:S(2)}) copy-start(f32[2,256,128]{2,1,0:T(8,128)} %copy-done.30) | copy-start | bytes 786436
  219.3 5.8 %copy-start.52 = (f32[2,12,256]{2,1,0:T(8,128)S(1)}, f32[2,12,256]{2,1,0:T(8,128)}, u32[]{:S(2)}) copy-start(f32[2,12,256]{2,1,0:T(8,128)} %copy-done.51) | copy-start | bytes 73732
  219.3 5.8 %copy-start.54 = (f32[2,12,256]{2,1,0:T(8,128)S(1)}, f32[2,12,256]{2,1,0:T(8,128)}, u32[]{:S(2)}) copy-start(f32[2,12,256]{2,1,0:T(8,128)} %copy-done.53) | copy-start | bytes 73732
  225.1 3.9 copy-start.44
  225.1 3.9 copy-start.62
  225.1 3.9 copy-start.64
  225.1 4.2 copy-start.81
  225.2 4.3 copy-start.48
  225.2 9.7 %copy-start.56 = (f32[2,256,12]{1,0,2:T(2,128)S(1)}, f32[2,256,12]{1,0,2:T(2,128)}, u32[]{:S(2)}) copy-start(f32[2,256,12]{1,0,2:T(2,128)} %copy-done.55) | copy-start | bytes 73732
  225.2 9.7 %copy-start.69 = (f32[12]{0:T(128)S(1)}, f32[12]{0:T(128)}, u32[]{:S(2)}) copy-start(f32[12]{0:T(128)} %copy-done.68) | copy-start | bytes 148
  225.2 9.7 %copy-start.71 = (f32[12]{0:T(128)S(1)}, f32[12]{0:T(128)}, u32[]{:S(2)}) copy-start(f32[12]{0:T(128)} %copy-done.70) | copy-start | bytes 148
  225.2 10.0 %copy-start.57 = (f32[1,4,128,12]{2,1,0,3:T(4,128)S(1)}, f32[1,4,128,12]{2,1,0,3:T(4,128)}, u32[]{:S(2)}) copy-start(f32[1,4,128,12]{2,1,0,3:T(4,128)} %copy.265) | copy-start | bytes 73732
  229.0 12.9 %copy-start.25 = (f32[2,256,256]{2,1,0:T(8,128)S(1)}, f32[2,256,256]{2,1,0:T(8,128)}, u32[]{:S(2)}) copy-start(f32[2,256,256]{2,1,0:T(8,128)} %get-tuple-element.586) | copy-start | bytes 1572868
  229.0 12.9 %copy-start.35 = (bf16[1,512,128]{2,1,0:T(8,128)(2,1)S(1)}, bf16[1,512,128]{2,1,0:T(8,128)(2,1)}, u32[]{:S(2)}) copy-start(bf16[1,512,128]{2,1,0:T(8,128)(2,1)} %copy-done.34) | copy-start | bytes 393220
  229.0 13.3 %copy-start.33 = (bf16[1,512,128]{2,1,0:T(8,128)(2,1)S(1)}, bf16[1,512,128]{2,1,0:T(8,128)(2,1)}, u32[]{:S(2)}) copy-start(bf16[1,512,128]{2,1,0:T(8,128)(2,1)} %copy-done.32) | copy-start | bytes 393220
  235.1 7.9 %copy-start.65 = (f32[768]{0:T(1024)S(1)}, f32[768]{0:T(1024)}, u32[]{:S(2)}) copy-start(f32[768]{0:T(1024)} %multiply_reduce_fusion) | copy-start | bytes 9220
  235.1 9.0 %copy-start.60 = (f32[3072]{0:T(1024)S(1)}, f32[3072]{0:T(1024)}, u32[]{:S(2)}) copy-start(f32[3072]{0:T(1024)} %get-tuple-element.587) | copy-start | bytes 36868
  235.5 50.6 %copy-start.27 = (bf16[2,256,12,64]{1,3,2,0:T(8,128)(2,1)S(1)}, bf16[2,256,12,64]{1,3,2,0:T(8,128)(2,1)}, u32[]{:S(2)}) copy-start(bf16[2,256,12,64]{1,3,2,0:T(8,128)(2,1)} %get-tuple-element.656) | copy-start | bytes 2359300
  237.7 61.7 %all-to-all-start.5 = ((bf16[4,2,768]{2,1,0:T(2,128)(2,1)}), bf16[4,2,768]{2,1,0:T(2,128)(2,1)S(1)}, u32[]{:S(2)}, u32[]{:S(2)}) async-start(bf16[4,2,768]{2,1,0:T(2,128)(2,1)} %reshape.594), calls=%async_computation.5 | async-start | bytes 24576 | tf_op jit(solution)/shard_map/all_to_all | solution.py:151
  295.3 7.7 %copy-start.59 = (f32[3216]{0:T(1024)S(1)}, f32[3216]{0:T(1024)}, u32[]{:S(2)}) copy-start(f32[3216]{0:T(1024)} %param.25) | copy-start | bytes 38596
  295.3 7.7 %copy-start.66 = (f32[804]{0:T(1024)S(1)}, f32[804]{0:T(1024)}, u32[]{:S(2)}) copy-start(f32[804]{0:T(1024)} %get-tuple-element.670) | copy-start | bytes 9652
  295.3 7.7 %copy-start.67 = (f32[804]{0:T(1024)S(1)}, f32[804]{0:T(1024)}, u32[]{:S(2)}) copy-start(f32[804]{0:T(1024)} %get-tuple-element.671) | copy-start | bytes 9652
  295.7 16.2 %copy-start.42 = (s32[3216]{0:T(1024)S(1)}, s32[3216]{0:T(1024)}, u32[]{:S(2)}) copy-start(s32[3216]{0:T(1024)} %get-tuple-element.880) | copy-start | bytes 38596
  295.8 16.2 %copy-start.45 = (f32[3216]{0:T(1024)S(1)}, f32[3216]{0:T(1024)}, u32[]{:S(2)}) copy-start(f32[3216]{0:T(1024)} %custom-call.2) | copy-start | bytes 38596
  299.4 9.0 %all-to-all-start.6 = ((bf16[4,2,16384]{2,1,0:T(2,128)(2,1)}), bf16[4,2,16384]{2,1,0:T(2,128)(2,1)S(1)}, u32[]{:S(2)}, u32[]{:S(2)}) async-start(bf16[4,2,16384]{2,1,0:T(2,128)(2,1)} %reshape.596), calls=%async_computation.6 | async-start | bytes 524288 | tf_op jit(solution)/shard_map/all_to_all | solution.py:152
  308.4 211.4 %all-to-all-start.4 = ((bf16[4,2,49152]{2,1,0:T(2,128)(2,1)}), bf16[4,2,49152]{2,1,0:T(2,128)(2,1)S(1)}, u32[]{:S(2)}, u32[]{:S(2)}) async-start(bf16[4,2,49152]{2,1,0:T(2,128)(2,1)} %reshape.592), calls=%async_computation.4 | async-start | bytes 1572864 | tf_op jit(solution)/shard_map/all_to_all | solution.py:150
  516.6 4.0 copy-start.46
  (32 other events, 51.9 us)
where the time goes:
time: 529 us; the launch traced here: 523 us
  local copies, waits for them, and re-layouts  188 us (36%)
  blocking collectives  167 us (32%)
  other arithmetic  103 us (19%)
  starting transfers between devices  28.9 us (5%)
  matrix products  20.4 us (4%)
  waiting for transfers between devices  9.52 us (2%)
    psum x8, blocking collectives, from_root(): return lax.psum(kept, axis)  109 us
    gather x8, local copies, waits for them, and re-layouts, place(): picked = received[jnp.clip(offset, 0, slot_cap - 1)]  94.7 us
    unnamed x10, other arithmetic  51.2 us
    psum x1, blocking collectives, on_device(): gradient = lax.psum(grad_part, ('dp', 'ctx'))  41.3 us
    unnamed x183, local copies, waits for them, and re-layouts  40.1 us
    convert_element_type x1, local copies, waits for them, and re-layouts, norm_backward(): d_y = (d_gated * (gate_f * sigma)).astype(jnp.bfloat16)  12.5 us
  transfers between devices with their start and end apart: 7, of which 2 were waited for; matrix products, arithmetic and copies ran while one was open for 31% of the time, Pallas kernels for 0%

commit v1 on v0

--- a/solution.py
+++ b/solution.py
@@ -15,11 +15,6 @@
 learn_rate = 0.02
 step_count = 100.0
 highest = lax.Precision.HIGHEST
-
-
-def from_root(value, axis, source):
-    kept = jnp.where(lax.axis_index(axis) == source, value, 0).astype(value.dtype)
-    return lax.psum(kept, axis)
 
 
 def rounded(value):
@@ -118,6 +113,16 @@
         lax.all_gather(c_input, "ctx", axis=1, tiled=True),
     )
     seq_resets = resets[0]
+    owners_n = lax.axis_size("dp")
+    cap_n = adam_mean.shape[1]
+    len_n = parameters.shape[0]
+    state_all = lax.all_gather(jnp.stack([adam_mean[0], adam_square[0]]), "dp", axis=0)
+    starts = jnp.cumsum(bucket_size) - bucket_size
+    laid = jnp.zeros((2, len_n + cap_n), jnp.float32)
+    for k in range(owners_n):
+        laid = lax.dynamic_update_slice(laid, state_all[bucket_owner[k]], (0, starts[k]))
+    mean_flat = laid[0, :len_n]
+    square_flat = laid[1, :len_n]
 
     def local_fn(x_arg, dt_arg, b_arg, c_arg, a_arg, bias_arg, skip_arg):
         return ssd_group(x_arg, dt_arg, b_arg, c_arg, seq_resets, a_arg, bias_arg, skip_arg)
@@ -185,31 +190,17 @@
         )
         * shrink
     )
-    param_row = jnp.where(
-        valid,
-        lax.dynamic_slice_in_dim(jnp.concatenate([parameters, padding]), row_begin, slot_cap),
-        0.0,
-    )
     new_mean = beta_one * adam_mean[0] + (1.0 - beta_one) * grad_row
     new_square = beta_two * adam_square[0] + (1.0 - beta_two) * grad_row * grad_row
+    grad_flat = gradient * shrink
+    mean_all = beta_one * mean_flat + (1.0 - beta_one) * grad_flat
+    square_all = beta_two * square_flat + (1.0 - beta_two) * grad_flat * grad_flat
     direction = (
-        new_mean
+        mean_all
         / (1.0 - beta_one**step_count)
-        / (jnp.sqrt(new_square / (1.0 - beta_two**step_count)) + adam_eps)
-    )
-    new_row = param_row - learn_rate * direction
-    flat = jnp.arange(total_len, dtype=jnp.int32)
-    bucket_of = jnp.sum((ends[None, :] <= flat[:, None]).astype(jnp.int32), axis=1)
-    match = order[None, :] == bucket_of[:, None]
-    owner_of = jnp.sum(jnp.where(match, bucket_owner[None, :], 0), axis=1)
-    offset = flat - jnp.sum(jnp.where(match, begins[None, :], 0), axis=1)
-
-    def place(owner, current):
-        received = from_root(new_row, "dp", owner)
-        picked = received[jnp.clip(offset, 0, slot_cap - 1)]
-        return jnp.where(owner_of == owner, picked, current)
-
-    new_params = lax.fori_loop(0, owners, place, jnp.zeros((total_len,), jnp.float32))
+        / (jnp.sqrt(square_all / (1.0 - beta_two**step_count)) + adam_eps)
+    )
+    new_params = parameters - learn_rate * direction
     return (
         normed,
         grad_hidden,

time: 529 us -> 374 us (0.71)
  blocking collectives: 167 us -> 72.3 us
  local copies, waits for them, and re-layouts: 188 us -> 99.3 us
  between operations: 4.84 us -> 34.9 us
    psum x8 -> x0, blocking collectives: 109 us -> none  [from_root(): return lax.psum(kept, axis)]
    gather x8 -> x0, local copies, waits for them, and re-layouts: 94.7 us -> none  [place(): picked = received[jnp.clip(offset, 0, slot_cap - 1)]]
    all_gather x0 -> x1, blocking collectives: none -> 14.3 us  [on_device(): lax.all_gather(jnp.stack([adam_mean[0], adam_square[0]]), 'dp', axis=0)]
    all_to_all x1, waiting for transfers between devices: 0.01 us -> 5.56 us  [on_device(): lax.all_to_all(d_x[None], 'ctx', split_axis=1, concat_axis=2, tiled=True)]
    unnamed x183 -> x171, local copies, waits for them, and re-layouts: 40.1 us -> 40.3 us
  transfers between devices with their start and end apart: 7 -> 7, of which waited for: 2 -> 1; matrix products, arithmetic and copies ran while one was open for 31% -> 19% of each run, Pallas kernels for 0% -> 0%
where the time goes in v1:
time: 374 us; the launch traced here: 367 us
  other arithmetic  105 us (28%)
  local copies, waits for them, and re-layouts  99.3 us (27%)
  blocking collectives  72.3 us (19%)
  between operations  34.9 us (9%)
  starting transfers between devices  29.3 us (8%)
  matrix products  20.4 us (5%)
  waiting for transfers between devices  5.57 us (1%)
    unnamed x10, other arithmetic  52.7 us
    psum x1, blocking collectives, on_device(): gradient = lax.psum(grad_part, ('dp', 'ctx'))  40.7 us
    unnamed x171, local copies, waits for them, and re-layouts  40.3 us
    all_gather x1, blocking collectives, on_device(): lax.all_gather(jnp.stack([adam_mean[0], adam_square[0]]), 'dp', axis=0)  14.3 us
    convert_element_type x1, local copies, waits for them, and re-layouts, norm_backward(): d_y = (d_gated * (gate_f * sigma)).astype(jnp.bfloat16)  13 us
    all_gather x1, blocking collectives, on_device(): lax.all_gather(b_input, 'ctx', axis=1, tiled=True)  9.13 us
    dot_general x3, matrix products, ssd_group(): jnp.einsum('chsn,cshp->chnp', b_decayed, scaled, precision=highest)  8.29 us
    all_gather x1, blocking collectives, on_device(): lax.all_gather(c_input, 'ctx', axis=1, tiled=True)  8.23 us
  transfers between devices with their start and end apart: 7, of which 1 were waited for; matrix products, arithmetic and copies ran while one was open for 19% of the time, Pallas kernels for 0%

profile of v1, /device:TPU:0, one launch (start us, length us, event | category | flops | bytes accessed | tf_op | source)
XLA Modules:
  0.0 367.2 jit_solution(14272552152918870720)
XLA Ops:
  3.3 5.2 %all-to-all-start.1 = ((bf16[4,2,768]{2,1,0:T(2,128)(2,1)}), bf16[4,2,768]{2,1,0:T(2,128)(2,1)S(1)}, u32[]{:S(2)}, u32[]{:S(2)}) async-start(bf16[4,2,768]{2,1,0:T(2,128)(2,1)} %reshape.560), calls=%async_computation.1 | async-start | bytes 24576 | tf_op jit(solution)/shard_map/all_to_all | solution.py:132
  10.6 9.1 %all_gather.13 = bf16[1,512,128]{2,1,0:T(8,128)(2,1)S(1)} all-gather(bf16[1,128,128]{2,1,0:T(8,128)(2,1)} %param.19), channel_id=1, replica_groups=mesh['dp'=8,'ctx'=4] {'ctx'}, dimensions={1}, use_global_device_ids=true | all-gather | bytes 163840 | tf_op jit(solution)/shard_map/all_gather | solution.py:112
  19.7 8.2 %all_gather.12 = bf16[1,512,128]{2,1,0:T(8,128)(2,1)S(1)} all-gather(bf16[1,128,128]{2,1,0:T(8,128)(2,1)} %param.20), channel_id=1, replica_groups=mesh['dp'=8,'ctx'=4] {'ctx'}, dimensions={1}, use_global_device_ids=true | all-gather | bytes 163840 | tf_op jit(solution)/shard_map/all_gather | solution.py:113
  28.7 3.8 %copy.220 = bf16[1,128,3072]{1,0,2:T(2,128)(2,1)S(1)} copy(bf16[1,128,3072]{2,1,0:T(8,128)(2,1)} %param.16) | data formatting | bytes 1572864 | tf_op args[0]
  32.5 17.9 %reduce.27 = bf16[3072,128]{1,0:T(8,128)(2,1)} reduce(bf16[3072,1,128]{2,1,0:T(2,128)(2,1)S(1)} %bitcast.223, bf16[]{:T(256)} %broadcast.249), dimensions={1}, to_apply=%bitcast.152.reduce_sub_computation | reduce | bytes 1572866
  50.4 2.0 reshape.562
  52.4 3.7 %all-to-all-start = ((bf16[4,2,49152]{2,1,0:T(2,128)(2,1)}), bf16[4,2,49152]{2,1,0:T(2,128)(2,1)S(1)}, u32[]{:S(2)}, u32[]{:S(2)}) async-start(bf16[4,2,49152]{2,1,0:T(2,128)(2,1)} %reshape.562), calls=%async_computation | async-start | bytes 1572864 | tf_op jit(solution)/shard_map/all_to_all | solution.py:131
  59.2 1.8 multiply_convert_fusion.2
  61.0 1.8 multiply_convert_fusion.1
  62.9 2.8 multiply_convert_fusion
  65.7 2.1 reshape.563
  67.7 3.2 bitcast_convert_fusion
  72.1 2.2 copy.221
  74.3 2.6 reshape.535
  78.9 1.8 fusion.88
  80.9 7.0 %while.36 = (s32[]{:T(128)}, f32[12,128,64]{2,1,0:T(8,128)S(1)}, f32[2,12,128,64]{3,2,1,0:T(8,128)S(1)}, f32[2,12]{1,0:T(2,128)S(1)}, f32[2,12,1,1]{1,3,2,0:T(1,...) while((s32[]{:T(128)}, f32[12,128,64]{2,1,0:T(8,128)S(1)}, ...), condition=%wide.region_3.4_spmd.clone, body=%wide.region_2.3_spmd.clone.sunk | while | flops 589827 | bytes 5899176 | solution.py:53
  88.1 2.5 fusion.89
  93.6 3.2 copy.238
  96.8 6.4 %reduce.28 = bf16[512,768]{1,0:T(8,128)(2,1)S(1)} reduce(bf16[512,1,768]{2,1,0:T(2,128)(2,1)} %bitcast.217, bf16[]{:T(256)} %broadcast.249), dimensions={1}, to_apply=%bitcast.154.reduce_sub_computation | reduce | bytes 1572866
  104.3 4.2 %all-to-all-start.2 = ((bf16[4,2,49152]{2,1,0:T(2,128)(2,1)}), bf16[4,2,49152]{2,1,0:T(2,128)(2,1)}, u32[]{:S(2)}, u32[]{:S(2)}) async-start(bf16[4,2,49152]{2,1,0:T(2,128)(2,1)} %reshape.564), calls=%async_computation.2 | async-start | bytes 1572864 | tf_op jit(solution)/shard_map/all_to_all | solution.py:144
  119.3 1.5 copy.241
  120.8 2.3 copy.242
  123.9 1.3 fusion.79
  125.3 3.7 %reshape.565 = bf16[512,1,768]{2,1,0:T(2,128)(2,1)} reshape(bf16[4,2,49152]{2,1,0:T(2,128)(2,1)} %all-to-all-done.2) | data formatting | bytes 1572864
  129.0 1.5 copy.239
  130.5 1.3 convert_bitcast_fusion
  131.8 3.0 copy.240
  134.9 2.0 multiply_reduce_fusion.1
  136.9 1.5 fusion.21
  138.4 2.5 fusion.30
  140.9 13.0 %copy.372 = bf16[1,128,3072]{1,0,2:T(2,128)(2,1)} copy(bf16[1,128,3072]{1,2,0:T(8,128)(2,1)S(1)} %get-tuple-element.489) | data formatting | bytes 1572864 | tf_op jit(solution)/shard_map/convert_element_type | solution.py:78
  153.9 18.5 %reduce.29 = bf16[3072,128]{1,0:T(8,128)(2,1)S(1)} reduce(bf16[3072,1,128]{2,1,0:T(2,128)(2,1)} %bitcast.219, bf16[]{:T(256)} %broadcast.249), dimensions={1}, to_apply=%bitcast.190.reduce_sub_computation | reduce | bytes 1572866
  173.4 4.1 %all-to-all-start.3 = ((bf16[4,2,49152]{2,1,0:T(2,128)(2,1)}), bf16[4,2,49152]{2,1,0:T(2,128)(2,1)S(1)}, u32[]{:S(2)}, u32[]{:S(2)}) async-start(bf16[4,2,49152]{2,1,0:T(2,128)(2,1)} %reshape.566), calls=%async_computation.3 | async-start | bytes 1572864 | tf_op jit(solution)/shard_map/all_to_all | solution.py:151
  200.0 14.3 %all-gather.1 = f32[8,2,804]{2,1,0:T(2,128)S(1)} all-gather(f32[1,2,804]{2,1,0:T(2,128)S(1)} %maximum_bitcast_fusion.1), channel_id=2, replica_groups=mesh['dp'=8,'ctx'=4] {'dp'}, dimensions={0}, use_global_device_ids=true | all-gather | bytes 57888 | tf_op jit(solution)/shard_map/all_gather | solution.py:119
  219.7 2.3 copy.272
  222.0 2.3 copy.274
  224.3 2.1 reshape.567
  226.3 1.5 copy.290
  228.7 1.5 copy.244
  230.2 2.3 squeeze.129
  232.5 2.1 convolution_convert_fusion.3
  234.7 2.7 convolution_convert_fusion
  237.4 1.8 convolution_convert_fusion.2
  240.7 1.4 broadcast.210
  242.1 13.7 %while.37 = (s32[]{:T(128)}, f32[12,128,64]{2,1,0:T(8,128)S(1)}, f32[2,12]{1,0:T(2,128)}, f32[2,12,128,64]{3,2,1,0:T(8,128)}, f32[2,12,128,64]{2,3,1,0:T(8,128)}...) while((s32[]{:T(128)}, f32[12,128,64]{2,1,0:T(8,128)S(1)}, ...), condition=%wide.region_8.9_spmd.clone, body=%wide.region_6.8_spmd.clone.sunk | while | flops 688132 | bytes 4327636 | solution.py:53
  243.1 1.3 dynamic_slice.149
  246.8 1.5 fusion.115
  249.9 1.3 dynamic_slice.149
  253.7 1.5 fusion.115
  255.8 3.8 %fusion.90 = f32[2,12,64,256]{3,2,1,0:T(8,128)S(1)} fusion(f32[2,12,128,64]{3,2,1,0:T(8,128)} %get-tuple-element.236, bf16[2,12,256,128]{3,2,1,0:T(8,128)(2,1)} %multiply_convert_fusion.2), kind=kOutput, calls=%fused_computation.192 | convolution fusion | flops 603979776 | bytes 3932160 | tf_op jit(solution)/shard_map/transpose(jvp(chsn,cshp->chnp))/dot_general | solution.py:44
  259.7 2.7 convolution_convert_fusion.1
  264.9 1.4 fusion.24
  266.5 5.7 %fusion.11 = (f32[2,12,256]{2,1,0:T(8,128)S(1)}, f32[2,12,256]{2,1,0:T(8,128)S(1)}, f32[2,256,256]{2,1,0:T(8,128)S(1)}) fusion(bf16[2,12,256,256]{3,2,1,0:T(8,128)(2,1)} %convolution_convert_fusion, f32[2,12,256]{2,1,0:T(8,128)S(1)} %copy-done.36, f32[2,256,256]{2,1,0:T(8,128)S(1)} %copy-done.25, pred[256,256]{1,0:T(8,128)(4,1)S(1)} %copy-done.38), kind=kLoop, calls=%fused_computation.26 | loop fusion | flops 18731008 | bytes 4333568 | tf_op jit(solution)/shard_map/transpose(jvp())/reduce_sum | solution.py:38
  272.4 3.8 %fusion.13 = (f32[2,256,128]{2,1,0:T(8,128)S(1)}, f32[2,12,256]{2,1,0:T(8,128)S(1)}, f32[2,12,256]{2,1,0:T(8,128)S(1)}, f32[2,256,128]{2,1,0:T(8,128)S(1)}) fusion(bf16[2,12,256,128]{3,2,1,0:T(8,128)(2,1)S(1)} %copy-done.22, f32[2,12,256]{2,1,0:T(8,128)S(1)} %copy-done.48, f32[2,256,128]{2,1,0:T(8,128)S(1)} %copy-done.30, f32[2,256,128]{2,1,0:T(8,128)S(1)} %copy-done.28, ...), kind=kLoop, calls=%fused_computation.32 | loop fusion | flops 7720960 | bytes 4292608 | tf_op jit(solution)/shard_map/transpose(jvp())/reduce_sum | solution.py:54
  276.8 5.0 %reduce-window.31 = f32[2,12,2,128]{3,1,2,0:T(8,128)S(1)} reduce-window(f32[2,12,2,128]{3,1,2,0:T(8,128)S(1)} %copy.261, f32[]{:T(128)} %constant.128.clone.1), window={size=1x1x1x128 pad=0_0x0_0x0_0x0_127}, to_apply=%region_15.16 | reduce-window | flops 780288 | bytes 49156 | tf_op jit(solution)/shard_map/reduce-window.2
  282.7 1.5 reduce.31
  285.0 4.2 %all-to-all-start.5 = ((bf16[4,2,768]{2,1,0:T(2,128)(2,1)}), bf16[4,2,768]{2,1,0:T(2,128)(2,1)S(1)}, u32[]{:S(2)}, u32[]{:S(2)}) async-start(bf16[4,2,768]{2,1,0:T(2,128)(2,1)} %reshape.570), calls=%async_computation.5 | async-start | bytes 24576 | tf_op jit(solution)/shard_map/all_to_all | solution.py:156
  292.5 1.6 copy.250
  294.1 5.5 %reduce.30 = bf16[512,768]{1,0:T(8,128)(2,1)S(1)} reduce(bf16[512,1,768]{2,1,0:T(2,128)(2,1)S(1)} %bitcast.221, bf16[]{:T(256)} %broadcast.249), dimensions={1}, to_apply=%bitcast.158.reduce_sub_computation | reduce | bytes 1572866
  301.0 2.2 reduce.32
  304.2 4.3 %all-to-all-start.6 = ((bf16[4,2,16384]{2,1,0:T(2,128)(2,1)}), bf16[4,2,16384]{2,1,0:T(2,128)(2,1)S(1)}, u32[]{:S(2)}, u32[]{:S(2)}) async-start(bf16[4,2,16384]{2,1,0:T(2,128)(2,1)} %reshape.572), calls=%async_computation.6 | async-start | bytes 524288 | tf_op jit(solution)/shard_map/all_to_all | solution.py:157
  308.6 40.7 %psum.7 = f32[3216]{0:T(1024)S(1)} all-reduce(f32[3216]{0:T(1024)S(1)} %pad_maximum_fusion), channel_id=1, replica_groups=mesh['dp'=8,'ctx'=4] {'dp','ctx'}, use_global_device_ids=true, to_apply=%region_27.28 | all-reduce | flops 3216 | bytes 25728 | tf_op jit(solution)/shard_map/psum | solution.py:169
  350.6 3.6 all-to-all-start.4
  358.8 5.6 %all-to-all-done.4 = bf16[4,2,49152]{2,1,0:T(2,128)(2,1)S(1)} async-done(((bf16[4,2,49152]{2,1,0:T(2,128)(2,1)}), bf16[4,2,49152]{2,1,0:T(2,128)(2,1)S(1)}, u32[]{:S(2)}, u32[]{:S(2)}) %all-to-all-start.4) | async-done | bytes 786464 | tf_op jit(solution)/shard_map/all_to_all | solution.py:155
  (316 shorter events, 59.9 us)
Async XLA Ops:
  3.3 49.1 %all-to-all-start.1 = ((bf16[4,2,768]{2,1,0:T(2,128)(2,1)}), bf16[4,2,768]{2,1,0:T(2,128)(2,1)S(1)}, u32[]{:S(2)}, u32[]{:S(2)}) async-start(bf16[4,2,768]{2,1,0:T(2,128)(2,1)} %reshape.560), calls=%async_computation.1 | async-start | bytes 24576 | tf_op jit(solution)/shard_map/all_to_all | solution.py:132
  9.3 23.2 %copy-start.73 = (f32[3,12]{1,0:T(4,128)}, f32[3,12]{1,0:T(4,128)S(1)}, u32[]{:S(2)}) copy-start(f32[3,12]{1,0:T(4,128)S(1)} %constant_dynamic-slice_fusion.4) | copy-start | bytes 436
  9.3 46.8 %copy-start.65 = (f32[12]{0:T(128)}, f32[12]{0:T(128)S(1)}, u32[]{:S(2)}) copy-start(f32[12]{0:T(128)S(1)} %get-tuple-element.511) | copy-start | bytes 148
  9.4 46.9 %copy-start.67 = (f32[12]{0:T(128)}, f32[12]{0:T(128)S(1)}, u32[]{:S(2)}) copy-start(f32[12]{0:T(128)S(1)} %get-tuple-element.512) | copy-start | bytes 148
  9.4 81.3 %copy-start.69 = (f32[12]{0:T(128)}, f32[12]{0:T(128)S(1)}, u32[]{:S(2)}) copy-start(f32[12]{0:T(128)S(1)} %get-tuple-element.510) | copy-start | bytes 148
  19.7 8.6 %copy-start.33 = (bf16[1,512,128]{2,1,0:T(8,128)(2,1)}, bf16[1,512,128]{2,1,0:T(8,128)(2,1)S(1)}, u32[]{:S(2)}) copy-start(bf16[1,512,128]{2,1,0:T(8,128)(2,1)S(1)} %all_gather.13) | copy-start | bytes 393220
  28.2 34.7 %copy-start.24 = (f32[2,256,256]{2,1,0:T(8,128)}, f32[2,256,256]{2,1,0:T(8,128)S(1)}, u32[]{:S(2)}) copy-start(f32[2,256,256]{2,1,0:T(8,128)S(1)} %fusion.87) | copy-start | bytes 1572868
  28.2 34.6 %copy-start.37 = (pred[256,256]{1,0:T(8,128)(4,1)}, pred[256,256]{1,0:T(8,128)(4,1)S(1)}, u32[]{:S(2)}) copy-start(pred[256,256]{1,0:T(8,128)(4,1)S(1)} %iota_compare_fusion) | copy-start | bytes 196612
  28.6 30.5 %copy-start.27 = (f32[2,256,128]{2,1,0:T(8,128)}, f32[2,256,128]{2,1,0:T(8,128)S(1)}, u32[]{:S(2)}) copy-start(f32[2,256,128]{2,1,0:T(8,128)S(1)} %convert_element_type.229) | copy-start | bytes 786436
  28.7 32.4 %copy-start.29 = (f32[2,256,128]{2,1,0:T(8,128)}, f32[2,256,128]{2,1,0:T(8,128)S(1)}, u32[]{:S(2)}) copy-start(f32[2,256,128]{2,1,0:T(8,128)S(1)} %convert_element_type.232) | copy-start | bytes 786436
  52.4 13.3 %all-to-all-start = ((bf16[4,2,49152]{2,1,0:T(2,128)(2,1)}), bf16[4,2,49152]{2,1,0:T(2,128)(2,1)S(1)}, u32[]{:S(2)}, u32[]{:S(2)}) async-start(bf16[4,2,49152]{2,1,0:T(2,128)(2,1)} %reshape.562), calls=%async_computation | async-start | bytes 1572864 | tf_op jit(solution)/shard_map/all_to_all | solution.py:131
  56.3 20.6 %copy-start.43 = (f32[2,256,12]{1,2,0:T(8,128)}, f32[2,256,12]{1,2,0:T(8,128)S(1)}, u32[]{:S(2)}) copy-start(f32[2,256,12]{1,2,0:T(8,128)S(1)} %get-tuple-element.503) | copy-start | bytes 73732
  58.9 4.0 %copy-start.41 = (f32[2,12,256]{2,0,1:T(2,128)}, f32[2,12,256]{2,0,1:T(2,128)S(1)}, u32[]{:S(2)}) copy-start(f32[2,12,256]{2,0,1:T(2,128)S(1)} %reduce_window_sum.56) | copy-start | bytes 73732
  59.1 3.7 %copy-start.45 = (f32[2,12,256]{2,1,0:T(8,128)}, f32[2,12,256]{2,1,0:T(8,128)S(1)}, u32[]{:S(2)}) copy-start(f32[2,12,256]{2,1,0:T(8,128)S(1)} %get-tuple-element.506) | copy-start | bytes 73732
  59.2 3.7 %copy-start.47 = (f32[2,12,256]{2,1,0:T(8,128)}, f32[2,12,256]{2,1,0:T(8,128)S(1)}, u32[]{:S(2)}) copy-start(f32[2,12,256]{2,1,0:T(8,128)S(1)} %get-tuple-element.507) | copy-start | bytes 73732
  59.2 3.7 %copy-start.35 = (f32[2,12,256]{2,1,0:T(8,128)}, f32[2,12,256]{2,1,0:T(8,128)S(1)}, u32[]{:S(2)}) copy-start(f32[2,12,256]{2,1,0:T(8,128)S(1)} %get-tuple-element.505) | copy-start | bytes 73732
  87.9 2.7 copy-start.56
  87.9 2.7 copy-start.5
  88.1 2.5 copy-start.19
  88.1 3.0 copy-start.2
  88.1 3.1 copy-start.8
  103.3 5.2 %copy-start.53 = (f32[3216]{0:T(1024)S(1)}, f32[3216]{0:T(1024)}, u32[]{:S(2)}) copy-start(f32[3216]{0:T(1024)} %param.23) | copy-start | bytes 38596
  103.3 5.3 %copy-start.58 = (s32[8]{0:T(128)S(1)}, s32[8]{0:T(128)}, u32[]{:S(2)}) copy-start(s32[8]{0:T(128)} %param.27) | copy-start | bytes 100
  104.3 21.0 %all-to-all-start.2 = ((bf16[4,2,49152]{2,1,0:T(2,128)(2,1)}), bf16[4,2,49152]{2,1,0:T(2,128)(2,1)}, u32[]{:S(2)}, u32[]{:S(2)}) async-start(bf16[4,2,49152]{2,1,0:T(2,128)(2,1)} %reshape.564), calls=%async_computation.2 | async-start | bytes 1572864 | tf_op jit(solution)/shard_map/all_to_all | solution.py:144
  119.3 3.8 %copy-start.77 = (s32[8]{0:T(128)S(1)}, s32[8]{0:T(128)}, u32[]{:S(2)}) copy-start(s32[8]{0:T(128)} %param.26) | copy-start | bytes 100
  172.4 27.6 %copy-start.63 = (f32[1,804]{1,0:T(1,128)S(1)}, f32[1,804]{1,0:T(1,128)}, u32[]{:S(2)}) copy-start(f32[1,804]{1,0:T(1,128)} %param.25) | copy-start | bytes 9652
  172.4 27.6 %copy-start.64 = (f32[1,804]{1,0:T(1,128)S(1)}, f32[1,804]{1,0:T(1,128)}, u32[]{:S(2)}) copy-start(f32[1,804]{1,0:T(1,128)} %param.24) | copy-start | bytes 9652
  173.4 50.9 %all-to-all-start.3 = ((bf16[4,2,49152]{2,1,0:T(2,128)(2,1)}), bf16[4,2,49152]{2,1,0:T(2,128)(2,1)S(1)}, u32[]{:S(2)}, u32[]{:S(2)}) async-start(bf16[4,2,49152]{2,1,0:T(2,128)(2,1)} %reshape.566), calls=%async_computation.3 | async-start | bytes 1572864 | tf_op jit(solution)/shard_map/all_to_all | solution.py:151
  232.5 4.9 %copy-start = (bf16[2,256,12,64]{1,0,3,2:T(2,128)(2,1)}, bf16[2,256,12,64]{1,0,3,2:T(2,128)(2,1)S(1)}, u32[]{:S(2)}) copy-start(bf16[2,256,12,64]{1,0,3,2:T(2,128)(2,1)S(1)} %squeeze.129) | copy-start | bytes 2359300
  232.5 2.1 copy-start.9
  234.7 2.8 copy-start.20
  242.1 3.3 copy-start.71
  248.9 3.4 copy-start.71
  255.8 3.8 %copy-start.10 = (bf16[2,256,12,64]{1,3,2,0:T(8,128)(2,1)S(1)}, bf16[2,256,12,64]{1,3,2,0:T(8,128)(2,1)}, u32[]{:S(2)}) copy-start(bf16[2,256,12,64]{1,3,2,0:T(8,128)(2,1)} %copy-done.7) | copy-start | bytes 2359300
  255.8 3.8 %copy-start.16 = (f32[2,12,128,64]{3,2,1,0:T(8,128)S(1)}, f32[2,12,128,64]{3,2,1,0:T(8,128)}, u32[]{:S(2)}) copy-start(f32[2,12,128,64]{3,2,1,0:T(8,128)} %get-tuple-element.236) | copy-start | bytes 2359300
  255.8 6.5 %copy-start.13 = (f32[1,128,3072]{1,0,2:T(1,128)S(1)}, f32[1,128,3072]{1,0,2:T(1,128)}, u32[]{:S(2)}) copy-start(f32[1,128,3072]{1,0,2:T(1,128)} %copy-done.12) | copy-start | bytes 4718596
  259.6 2.7 copy-start.18
  259.7 3.0 copy-start.3
  266.5 5.8 %copy-start.22 = (bf16[2,12,256,128]{3,2,1,0:T(8,128)(2,1)S(1)}, bf16[2,12,256,128]{3,2,1,0:T(8,128)(2,1)}, u32[]{:S(2)}) copy-start(bf16[2,12,256,128]{3,2,1,0:T(8,128)(2,1)} %convolution_convert_fusion.2) | copy-start | bytes 4718596
  266.5 5.8 %copy-start.23 = (bf16[2,12,256,128]{3,2,1,0:T(8,128)(2,1)S(1)}, bf16[2,12,256,128]{3,2,1,0:T(8,128)(2,1)}, u32[]{:S(2)}) copy-start(bf16[2,12,256,128]{3,2,1,0:T(8,128)(2,1)} %convolution_convert_fusion.1) | copy-start | bytes 4718596
  266.5 5.8 %copy-start.28 = (f32[2,256,128]{2,1,0:T(8,128)S(1)}, f32[2,256,128]{2,1,0:T(8,128)}, u32[]{:S(2)}) copy-start(f32[2,256,128]{2,1,0:T(8,128)} %copy-done.27) | copy-start | bytes 786436
  266.5 5.8 %copy-start.30 = (f32[2,256,128]{2,1,0:T(8,128)S(1)}, f32[2,256,128]{2,1,0:T(8,128)}, u32[]{:S(2)}) copy-start(f32[2,256,128]{2,1,0:T(8,128)} %copy-done.29) | copy-start | bytes 786436
  266.5 5.8 %copy-start.46 = (f32[2,12,256]{2,1,0:T(8,128)S(1)}, f32[2,12,256]{2,1,0:T(8,128)}, u32[]{:S(2)}) copy-start(f32[2,12,256]{2,1,0:T(8,128)} %copy-done.45) | copy-start | bytes 73732
  266.5 5.8 %copy-start.48 = (f32[2,12,256]{2,1,0:T(8,128)S(1)}, f32[2,12,256]{2,1,0:T(8,128)}, u32[]{:S(2)}) copy-start(f32[2,12,256]{2,1,0:T(8,128)} %copy-done.47) | copy-start | bytes 73732
  272.3 3.9 %copy-start.40 = (f32[2,12,2,128]{3,1,2,0:T(8,128)S(1)}, f32[2,12,2,128]{3,1,2,0:T(8,128)}, u32[]{:S(2)}) copy-start(f32[2,12,2,128]{3,1,2,0:T(8,128)} %copy-done.39) | copy-start | bytes 73732
  272.3 3.9 %copy-start.57 = (f32[2,12]{1,0:T(2,128)S(1)}, f32[2,12]{1,0:T(2,128)}, u32[]{:S(2)}) copy-start(f32[2,12]{1,0:T(2,128)} %copy-done.56) | copy-start | bytes 292
  272.3 3.9 %copy-start.60 = (f32[2,12,2]{1,2,0:T(2,128)S(1)}, f32[2,12,2]{1,2,0:T(2,128)}, u32[]{:S(2)}) copy-start(f32[2,12,2]{1,2,0:T(2,128)} %copy-done.59) | copy-start | bytes 580
  272.3 4.2 %copy-start.76 = (f32[2,12]{1,0:T(2,128)S(1)}, f32[2,12]{1,0:T(2,128)}, u32[]{:S(2)}) copy-start(f32[2,12]{1,0:T(2,128)} %get-tuple-element.237) | copy-start | bytes 292
  272.4 4.3 %copy-start.42 = (f32[2,12,256]{2,0,1:T(2,128)S(1)}, f32[2,12,256]{2,0,1:T(2,128)}, u32[]{:S(2)}) copy-start(f32[2,12,256]{2,0,1:T(2,128)} %copy-done.41) | copy-start | bytes 73732
  272.4 9.7 %copy-start.50 = (f32[2,256,12]{1,0,2:T(2,128)S(1)}, f32[2,256,12]{1,0,2:T(2,128)}, u32[]{:S(2)}) copy-start(f32[2,256,12]{1,0,2:T(2,128)} %copy-done.49) | copy-start | bytes 73732
  272.4 9.7 %copy-start.66 = (f32[12]{0:T(128)S(1)}, f32[12]{0:T(128)}, u32[]{:S(2)}) copy-start(f32[12]{0:T(128)} %copy-done.65) | copy-start | bytes 148
  272.4 9.7 %copy-start.68 = (f32[12]{0:T(128)S(1)}, f32[12]{0:T(128)}, u32[]{:S(2)}) copy-start(f32[12]{0:T(128)} %copy-done.67) | copy-start | bytes 148
  272.4 9.9 %copy-start.51 = (f32[1,4,128,12]{2,1,0,3:T(4,128)S(1)}, f32[1,4,128,12]{2,1,0,3:T(4,128)}, u32[]{:S(2)}) copy-start(f32[1,4,128,12]{2,1,0,3:T(4,128)} %copy.265) | copy-start | bytes 73732
  276.2 13.0 %copy-start.34 = (bf16[1,512,128]{2,1,0:T(8,128)(2,1)S(1)}, bf16[1,512,128]{2,1,0:T(8,128)(2,1)}, u32[]{:S(2)}) copy-start(bf16[1,512,128]{2,1,0:T(8,128)(2,1)} %copy-done.33) | copy-start | bytes 393220
  276.2 13.4 %copy-start.32 = (bf16[1,512,128]{2,1,0:T(8,128)(2,1)S(1)}, bf16[1,512,128]{2,1,0:T(8,128)(2,1)}, u32[]{:S(2)}) copy-start(bf16[1,512,128]{2,1,0:T(8,128)(2,1)} %copy-done.31) | copy-start | bytes 393220
  282.7 8.5 %copy-start.26 = (bf16[2,256,12,64]{1,3,2,0:T(8,128)(2,1)S(1)}, bf16[2,256,12,64]{1,3,2,0:T(8,128)(2,1)}, u32[]{:S(2)}) copy-start(bf16[2,256,12,64]{1,3,2,0:T(8,128)(2,1)} %get-tuple-element.492) | copy-start | bytes 2359300
  285.0 19.2 %all-to-all-start.5 = ((bf16[4,2,768]{2,1,0:T(2,128)(2,1)}), bf16[4,2,768]{2,1,0:T(2,128)(2,1)S(1)}, u32[]{:S(2)}, u32[]{:S(2)}) async-start(bf16[4,2,768]{2,1,0:T(2,128)(2,1)} %reshape.570), calls=%async_computation.5 | async-start | bytes 24576 | tf_op jit(solution)/shard_map/all_to_all | solution.py:156
  300.6 7.9 %copy-start.55 = (f32[3072]{0:T(1024)S(1)}, f32[3072]{0:T(1024)}, u32[]{:S(2)}) copy-start(f32[3072]{0:T(1024)} %get-tuple-element.436) | copy-start | bytes 36868
  301.0 53.2 %copy-start.61 = (f32[804]{0:T(1024)S(1)}, f32[804]{0:T(1024)}, u32[]{:S(2)}) copy-start(f32[804]{0:T(1024)} %get-tuple-element.532) | copy-start | bytes 9652
  301.0 53.2 %copy-start.62 = (f32[804]{0:T(1024)S(1)}, f32[804]{0:T(1024)}, u32[]{:S(2)}) copy-start(f32[804]{0:T(1024)} %get-tuple-element.533) | copy-start | bytes 9652
  303.3 52.8 %copy-start.52 = (f32[3216]{0:T(1024)S(1)}, f32[3216]{0:T(1024)}, u32[]{:S(2)}) copy-start(f32[3216]{0:T(1024)} %get-tuple-element.445) | copy-start | bytes 38596
  303.3 52.8 %copy-start.54 = (f32[3216]{0:T(1024)S(1)}, f32[3216]{0:T(1024)}, u32[]{:S(2)}) copy-start(f32[3216]{0:T(1024)} %param.23) | copy-start | bytes 38596
  304.2 46.4 %all-to-all-start.6 = ((bf16[4,2,16384]{2,1,0:T(2,128)(2,1)}), bf16[4,2,16384]{2,1,0:T(2,128)(2,1)S(1)}, u32[]{:S(2)}, u32[]{:S(2)}) async-start(bf16[4,2,16384]{2,1,0:T(2,128)(2,1)} %reshape.572), calls=%async_computation.6 | async-start | bytes 524288 | tf_op jit(solution)/shard_map/all_to_all | solution.py:157
  350.6 13.8 %all-to-all-start.4 = ((bf16[4,2,49152]{2,1,0:T(2,128)(2,1)}), bf16[4,2,49152]{2,1,0:T(2,128)(2,1)S(1)}, u32[]{:S(2)}, u32[]{:S(2)}) async-start(bf16[4,2,49152]{2,1,0:T(2,128)(2,1)} %reshape.568), calls=%async_computation.4 | async-start | bytes 1572864 | tf_op jit(solution)/shard_map/all_to_all | solution.py:155
  (26 other events, 33.6 us)

commit v2 on v1

--- a/solution.py
+++ b/solution.py
@@ -15,6 +15,25 @@
 learn_rate = 0.02
 step_count = 100.0
 highest = lax.Precision.HIGHEST
+
+
+def to_heads(x, groups):
+    _, t, c = x.shape
+    x = x.reshape(t, groups, c // groups).transpose(1, 0, 2)
+    x = lax.all_to_all(x, "ctx", 0, 0, tiled=True)
+    return x.reshape(groups * t, c // groups)
+
+
+def from_heads(x, groups):
+    tw, w = x.shape
+    x = x.reshape(groups, tw // groups, w)
+    return lax.all_to_all(x, "ctx", 0, 0, tiled=True)
+
+
+def to_positions(x, groups):
+    parts = from_heads(x, groups)
+    _, t, w = parts.shape
+    return parts.transpose(1, 0, 2).reshape(1, t, groups * w)
 
 
 def rounded(value):
@@ -108,10 +127,9 @@
     head_params = parameters[: 3 * heads_all].reshape(3, heads_all)
     gain = parameters[3 * heads_all :]
     local_params = lax.dynamic_slice_in_dim(head_params, first, group, 1)
-    b_all, c_all = (
-        lax.all_gather(b_input, "ctx", axis=1, tiled=True),
-        lax.all_gather(c_input, "ctx", axis=1, tiled=True),
-    )
+    bc_all = lax.all_gather(jnp.concatenate([b_input, c_input], axis=2), "ctx", axis=1, tiled=True)
+    b_all = bc_all[..., :state_size]
+    c_all = bc_all[..., state_size:]
     seq_resets = resets[0]
     owners_n = lax.axis_size("dp")
     cap_n = adam_mean.shape[1]
@@ -128,8 +146,8 @@
         return ssd_group(x_arg, dt_arg, b_arg, c_arg, seq_resets, a_arg, bias_arg, skip_arg)
 
     x_heads, dt_heads = (
-        lax.all_to_all(hidden, "ctx", split_axis=2, concat_axis=1, tiled=True),
-        lax.all_to_all(dt_raw, "ctx", split_axis=2, concat_axis=1, tiled=True),
+        to_heads(hidden, groups)[None],
+        to_heads(dt_raw, groups)[None],
     )
     y_heads, pullback = jax.vjp(
         local_fn,
@@ -141,24 +159,22 @@
         local_params[1],
         local_params[2],
     )
-    y_seq = lax.all_to_all(y_heads[None], "ctx", split_axis=1, concat_axis=2, tiled=True)
+    y_seq = to_positions(y_heads, groups)
     gated, total = gate_values(y_seq, gating)
     factor, normed = normalize(gated, total, gain)
     dot_total = jnp.sum(cotangent.astype(jnp.float32) * gain * gated, axis=-1)
     d_y, grad_gating, d_gain = norm_backward(
         cotangent, gain, gated, factor, dot_total, y_seq, gating
     )
-    d_y_heads = lax.all_to_all(d_y, "ctx", split_axis=2, concat_axis=1, tiled=True)
+    d_y_heads = to_heads(d_y, groups)[None]
     d_x, d_dt, d_b, d_c, d_alog, d_bias, d_skip = pullback(d_y_heads[0])
     d_pair = jnp.concatenate([d_b, d_c], axis=-1)
     grad_hidden, grad_dt, pair_parts = (
-        lax.all_to_all(d_x[None], "ctx", split_axis=1, concat_axis=2, tiled=True),
-        lax.all_to_all(d_dt[None], "ctx", split_axis=1, concat_axis=2, tiled=True),
-        lax.all_to_all(d_pair[None], "ctx", split_axis=1, concat_axis=2, tiled=True),
-    )
-    pair_sum = jnp.sum(
-        pair_parts.reshape(1, tokens, groups, 2 * state_size).astype(jnp.float32), axis=2
-    ).astype(jnp.bfloat16)
+        to_positions(d_x, groups),
+        to_positions(d_dt, groups),
+        from_heads(d_pair, groups),
+    )
+    pair_sum = jnp.sum(pair_parts.astype(jnp.float32), axis=0)[None].astype(jnp.bfloat16)
     grad_b = pair_sum[..., :state_size]
     grad_c = pair_sum[..., state_size:]
     head_grads = jnp.stack([d_alog, d_bias, d_skip])

time: 374 us -> 269 us (0.72); the launches traced: 367 us -> 266 us
  other arithmetic: 105 us -> 55.5 us
  local copies, waits for them, and re-layouts: 99.3 us -> 56 us
  blocking collectives: 72.3 us -> 64.4 us
    unnamed x10 -> x3, other arithmetic: 52.7 us -> 0.01 us
    unnamed x171 -> x140, local copies, waits for them, and re-layouts: 40.3 us -> 18.8 us
    convert_element_type x2 -> x0, local copies, waits for them, and re-layouts: 16 us -> none  [the longest x1 13 us: norm_backward(): d_y = (d_gated * (gate_f * sigma)).astype(jnp.bfloat16)]
    all_gather x2 -> x1, blocking collectives: 17.4 us -> 9.49 us  [on_device(): lax.all_gather(jnp.concatenate([b_input, c_input], axis=2), 'ctx', axis=1...]
  transfers between devices with their start and end apart: 7 -> 7, of which waited for: 1 -> 1; matrix products, arithmetic and copies ran while one was open for 19% -> 15% of each run, Pallas kernels for 0% -> 0%
where the time goes in v2:
time: 269 us; the launch traced here: 266 us
  blocking collectives  64.4 us (24%)
  local copies, waits for them, and re-layouts  56 us (21%)
  other arithmetic  55.5 us (21%)
  between operations  33.8 us (13%)
  starting transfers between devices  29.5 us (11%)
  matrix products  20.5 us (8%)
  waiting for transfers between devices  6.4 us (2%)
    psum x1, blocking collectives, on_device(): gradient = lax.psum(grad_part, ('dp', 'ctx'))  40.7 us
    unnamed x140, local copies, waits for them, and re-layouts  18.8 us
    all_to_all x4, starting transfers between devices, from_heads(): return lax.all_to_all(x, 'ctx', 0, 0, tiled=True)  16.5 us
    all_gather x1, blocking collectives, on_device(): lax.all_gather(jnp.stack([adam_mean[0], adam_square[0]]), 'dp', axis=0)  14.3 us
    all_to_all x3, starting transfers between devices, to_heads(): x = lax.all_to_all(x, 'ctx', 0, 0, tiled=True)  13 us
    all_gather x1, blocking collectives, on_device(): lax.all_gather(jnp.concatenate([b_input, c_input], axis=2), 'ctx', axis=1...  9.49 us
    convert_element_type x6, other arithmetic, rounded(): value.astype(jnp.bfloat16)  7.75 us
    dot_general x3, matrix products, ssd_group(): jnp.einsum('chsn,cshp->chnp', b_decayed, scaled, precision=highest)  7.27 us
  transfers between devices with their start and end apart: 7, of which 1 were waited for; matrix products, arithmetic and copies ran while one was open for 15% of the time, Pallas kernels for 0%

profile of v2, /device:TPU:0, one launch (start us, length us, event | category | flops | bytes accessed | tf_op | source)
XLA Modules:
  0.0 266.2 jit_solution(17527639215730785852)
XLA Ops:
  0.7 1.4 reshape.401
  2.0 5.2 %all-to-all-start.1 = ((bf16[4,128,12]{1,2,0:T(8,128)(2,1)}), bf16[4,128,12]{1,2,0:T(8,128)(2,1)S(1)}, u32[]{:S(2)}, u32[]{:S(2)}) async-start(bf16[4,128,12]{1,2,0:T(8,128)(2,1)} %bitcast.2), calls=%async_computation.1 | async-start | bytes 32768 | tf_op jit(solution)/shard_map/all_to_all | solution.py:23
  8.1 1.2 subtract_bitcast_fusion
  10.1 9.5 %all_gather.9 = bf16[1,512,256]{2,1,0:T(8,128)(2,1)S(1)} all-gather(bf16[1,128,256]{2,1,0:T(8,128)(2,1)S(1)} %pad_maximum_fusion.1), channel_id=1, replica_groups=mesh['dp'=8,'ctx'=4] {'ctx'}, dimensions={1}, use_global_device_ids=true | all-gather | bytes 327680 | tf_op jit(solution)/shard_map/all_gather | solution.py:130
  20.0 1.2 copy.197
  21.2 3.5 %all-to-all-start = ((bf16[4,128,768]{1,2,0:T(8,128)(2,1)}), bf16[4,128,768]{1,2,0:T(8,128)(2,1)S(1)}, u32[]{:S(2)}, u32[]{:S(2)}) async-start(bf16[4,128,768]{1,2,0:T(8,128)(2,1)} %bitcast.1), calls=%async_computation | async-start | bytes 1572864 | tf_op jit(solution)/shard_map/all_to_all | solution.py:23
  25.3 1.1 reduce-window.24
  27.6 1.9 multiply_convert_fusion.2
  29.5 1.8 multiply_convert_fusion.1
  31.4 2.7 %multiply_convert_fusion = bf16[2,12,256,256]{3,2,1,0:T(8,128)(2,1)} fusion(f32[2,12,256]{2,1,0:T(8,128)S(1)} %get-tuple-element.507, f32[2,256,256]{2,1,0:T(8,128)S(1)} %fusion.82, pred[256,256]{1,0:T(8,128)(4,1)S(1)} %iota_compare_fusion), kind=kLoop, calls=%fused_computation.22 | loop fusion | flops 7864320 | bytes 3760128 | tf_op jit(solution)/shard_map/jvp()/convert_element_type | solution.py:40
  34.1 0.9 copy-done.16
  35.1 1.8 copy.198
  36.8 2.6 reshape.419
  39.7 1.0 copy-done.4
  41.5 1.8 fusion.83
  43.9 5.7 %while.36 = (s32[]{:T(128)}, f32[12,128,64]{2,1,0:T(8,128)S(1)}, f32[2,12,128,64]{3,2,1,0:T(8,128)S(1)}, f32[2,12]{1,0:T(2,128)S(1)}, f32[2,12,1,1]{1,3,2,0:T(1,...) while((s32[]{:T(128)}, f32[12,128,64]{2,1,0:T(8,128)S(1)}, ...), condition=%wide.region_3.4_spmd.clone, body=%wide.region_2.3_spmd.clone.sunk | while | flops 589827 | bytes 5899176 | solution.py:72
  49.8 2.5 fusion.84
  52.9 1.1 fusion.32
  55.3 1.0 copy.214
  56.3 4.4 %all-to-all-start.2 = ((bf16[4,128,768]{1,2,0:T(8,128)(2,1)}), bf16[4,128,768]{1,2,0:T(8,128)(2,1)}, u32[]{:S(2)}, u32[]{:S(2)}) async-start(bf16[4,128,768]{1,2,0:T(8,128)(2,1)} %copy.214), calls=%async_computation.2 | async-start | bytes 1572864 | tf_op jit(solution)/shard_map/all_to_all | solution.py:30
  71.1 1.5 copy.215
  72.7 2.3 copy.216
  75.8 1.3 fusion.73
  77.1 1.2 convert_element_type.233
  79.5 1.5 fusion.21
  81.0 2.7 fusion.30
  83.7 4.3 %all-to-all-start.3 = ((bf16[4,128,768]{1,2,0:T(8,128)(2,1)}), bf16[4,128,768]{1,2,0:T(8,128)(2,1)S(1)}, u32[]{:S(2)}, u32[]{:S(2)}) async-start(bf16[4,128,768]{1,2,0:T(8,128)(2,1)} %bitcast.186), calls=%async_computation.3 | async-start | bytes 1572864 | tf_op jit(solution)/shard_map/all_to_all | solution.py:23
  110.3 14.3 %all-gather.1 = f32[8,2,804]{2,1,0:T(2,128)S(1)} all-gather(f32[1,2,804]{2,1,0:T(2,128)S(1)} %maximum_bitcast_fusion), channel_id=2, replica_groups=mesh['dp'=8,'ctx'=4] {'dp'}, dimensions={0}, use_global_device_ids=true | all-gather | bytes 57888 | tf_op jit(solution)/shard_map/all_gather | solution.py:137
  129.1 2.3 copy.240
  131.4 2.3 copy.242
  134.6 1.5 copy.217
  136.1 2.3 squeeze_broadcast_in_dim_reshape.2
  138.4 2.1 convolution_convert_fusion.3
  140.5 2.7 %convolution_convert_fusion = bf16[2,12,256,256]{3,2,1,0:T(8,128)(2,1)} fusion(bf16[2,256,12,64]{1,3,2,0:T(8,128)(2,1)S(1)} %copy-done.9, bf16[2,256,12,64]{1,0,3,2:T(2,128)(2,1)S(1)} %squeeze_broadcast_in_dim_reshape.2), kind=kOutput, calls=%fused_computation.40 | convolution fusion | flops 202899456 | bytes 4718592 | tf_op jit(solution)/shard_map/transpose(jvp(chts,cshp->cthp))/dot_general | solution.py:60
  143.3 1.8 convolution_convert_fusion.2
  145.1 1.0 convert_element_type.208
  146.6 1.4 broadcast.150
  148.0 12.7 %while.37 = (s32[]{:T(128)}, f32[12,128,64]{2,1,0:T(8,128)S(1)}, f32[2,12]{1,0:T(2,128)}, f32[2,12,128,64]{3,2,1,0:T(8,128)}, f32[2,12,128,64]{2,3,1,0:T(8,128)}...) while((s32[]{:T(128)}, f32[12,128,64]{2,1,0:T(8,128)S(1)}, ...), condition=%wide.region_8.9_spmd.clone, body=%wide.region_6.8_spmd.clone.sunk | while | flops 688132 | bytes 4327756 | solution.py:72
  148.0 1.0 bitcast_dynamic-update-slice_fusion.5
  149.5 1.2 fusion.109
  150.7 1.0 constant_dynamic-slice_fusion.6
  152.1 1.6 fusion.110
  154.3 1.0 bitcast_dynamic-update-slice_fusion.5
  155.9 1.2 fusion.109
  157.1 1.0 constant_dynamic-slice_fusion.6
  158.4 1.6 fusion.110
  160.6 3.8 %fusion.85 = f32[2,12,64,256]{3,2,1,0:T(8,128)S(1)} fusion(f32[2,12,128,64]{3,2,1,0:T(8,128)} %get-tuple-element.236, bf16[2,12,256,128]{3,2,1,0:T(8,128)(2,1)} %multiply_convert_fusion.2), kind=kOutput, calls=%fused_computation.183 | convolution fusion | flops 603979776 | bytes 3932160 | tf_op jit(solution)/shard_map/transpose(jvp(chsn,cshp->chnp))/dot_general | solution.py:63
  164.5 1.7 convolution_convert_fusion.1
  168.0 1.4 fusion.24
  170.7 6.7 %fusion.11 = (f32[2,12,256]{2,1,0:T(8,128)}, f32[2,12,256]{2,1,0:T(8,128)}, f32[2,256,256]{2,1,0:T(8,128)}) fusion(bf16[2,12,256,256]{3,2,1,0:T(8,128)(2,1)} %convolution_convert_fusion, f32[2,12,256]{2,1,0:T(8,128)S(1)} %copy-done.34, f32[2,256,256]{2,1,0:T(8,128)} %copy-done.23, pred[256,256]{1,0:T(8,128)(4,1)S(1)} %copy-done.37), kind=kLoop, calls=%fused_computation.26 | loop fusion | flops 18731008 | bytes 4333568 | tf_op jit(solution)/shard_map/transpose(jvp())/reduce_sum | solution.py:57
  177.4 4.5 %fusion.13 = (f32[2,256,128]{2,1,0:T(8,128)}, f32[2,12,256]{2,1,0:T(8,128)}, f32[2,12,256]{2,1,0:T(8,128)}, f32[2,256,128]{2,1,0:T(8,128)S(1)}) fusion(bf16[2,12,256,128]{3,2,1,0:T(8,128)(2,1)S(1)} %copy-done.21, f32[2,12,256]{2,1,0:T(8,128)S(1)} %copy-done.45, f32[2,256,128]{2,1,0:T(8,128)S(1)} %copy-done.28, f32[2,256,128]{2,1,0:T(8,128)S(1)} %copy-done.26, ...), kind=kLoop, calls=%fused_computation.32 | loop fusion | flops 7720960 | bytes 4292608 | tf_op jit(solution)/shard_map/transpose(jvp())/reduce_sum | solution.py:73
  182.8 1.0 fusion.52
  184.7 0.9 add_add_fusion
  185.7 5.0 %reduce-window.31 = f32[2,12,2,128]{3,1,2,0:T(8,128)S(1)} reduce-window(f32[2,12,2,128]{3,1,2,0:T(8,128)S(1)} %copy.233, f32[]{:T(128)} %constant.128.clone.1), window={size=1x1x1x128 pad=0_0x0_0x0_0x0_127}, to_apply=%region_15.16 | reduce-window | flops 780288 | bytes 49156 | tf_op jit(solution)/shard_map/reduce-window.2
  190.9 1.5 multiply_reduce_fusion.2
  192.5 1.5 fusion.47
  194.0 4.2 %all-to-all-start.5 = ((bf16[4,128,12]{1,2,0:T(8,128)(2,1)}), bf16[4,128,12]{1,2,0:T(8,128)(2,1)S(1)}, u32[]{:S(2)}, u32[]{:S(2)}) async-start(bf16[4,128,12]{1,2,0:T(8,128)(2,1)} %fusion.47), calls=%async_computation.5 | async-start | bytes 32768 | tf_op jit(solution)/shard_map/all_to_all | solution.py:30
  198.2 1.5 fusion.35
  203.7 1.0 copy.223
  204.9 4.3 %all-to-all-start.6 = ((bf16[4,128,256]{2,1,0:T(8,128)(2,1)}), bf16[4,128,256]{2,1,0:T(8,128)(2,1)S(1)}, u32[]{:S(2)}, u32[]{:S(2)}) async-start(bf16[4,128,256]{2,1,0:T(8,128)(2,1)} %pad_maximum_fusion), calls=%async_computation.6 | async-start | bytes 524288 | tf_op jit(solution)/shard_map/all_to_all | solution.py:30
  209.3 40.7 %psum.7 = f32[3216]{0:T(1024)S(1)} all-reduce(f32[3216]{0:T(1024)S(1)} %pad_maximum_fusion.2), channel_id=1, replica_groups=mesh['dp'=8,'ctx'=4] {'dp','ctx'}, use_global_device_ids=true, to_apply=%region_27.28 | all-reduce | flops 3216 | bytes 25728 | tf_op jit(solution)/shard_map/psum | solution.py:185
  251.3 3.6 %all-to-all-start.4 = ((bf16[4,128,768]{1,2,0:T(8,128)(2,1)}), bf16[4,128,768]{1,2,0:T(8,128)(2,1)S(1)}, u32[]{:S(2)}, u32[]{:S(2)}) async-start(bf16[4,128,768]{1,2,0:T(8,128)(2,1)} %copy.223), calls=%async_computation.4 | async-start | bytes 1572864 | tf_op jit(solution)/shard_map/all_to_all | solution.py:30
  258.7 6.4 %all-to-all-done.4 = bf16[4,128,768]{1,2,0:T(8,128)(2,1)S(1)} async-done(((bf16[4,128,768]{1,2,0:T(8,128)(2,1)}), bf16[4,128,768]{1,2,0:T(8,128)(2,1)S(1)}, u32[]{:S(2)}, u32[]{:S(2)}) %all-to-all-start.4) | async-done | bytes 786464 | tf_op jit(solution)/shard_map/all_to_all | solution.py:30
  265.1 1.2 copy.241
  (276 shorter events, 39.0 us)
Async XLA Ops:
  0.6 19.3 %copy-start.35 = (bf16[1,128,3072]{2,1,0:T(8,128)(2,1)S(1)}, bf16[1,128,3072]{2,1,0:T(8,128)(2,1)}, u32[]{:S(2)}) copy-start(bf16[1,128,3072]{2,1,0:T(8,128)(2,1)} %param.16) | copy-start | bytes 2359300
  2.0 19.1 %all-to-all-start.1 = ((bf16[4,128,12]{1,2,0:T(8,128)(2,1)}), bf16[4,128,12]{1,2,0:T(8,128)(2,1)S(1)}, u32[]{:S(2)}, u32[]{:S(2)}) async-start(bf16[4,128,12]{1,2,0:T(8,128)(2,1)} %bitcast.2), calls=%async_computation.1 | async-start | bytes 32768 | tf_op jit(solution)/shard_map/all_to_all | solution.py:23
  8.1 13.1 %copy-start.66 = (f32[3,12]{1,0:T(4,128)}, f32[3,12]{1,0:T(4,128)S(1)}, u32[]{:S(2)}) copy-start(f32[3,12]{1,0:T(4,128)S(1)} %constant_dynamic-slice_fusion.4) | copy-start | bytes 436
  8.1 16.6 %copy-start.62 = (f32[12]{0:T(128)}, f32[12]{0:T(128)S(1)}, u32[]{:S(2)}) copy-start(f32[12]{0:T(128)S(1)} %get-tuple-element.513) | copy-start | bytes 148
  8.1 16.6 %copy-start.63 = (f32[12]{0:T(128)}, f32[12]{0:T(128)S(1)}, u32[]{:S(2)}) copy-start(f32[12]{0:T(128)S(1)} %get-tuple-element.514) | copy-start | bytes 148
  8.1 44.2 %copy-start.60 = (f32[12]{0:T(128)}, f32[12]{0:T(128)S(1)}, u32[]{:S(2)}) copy-start(f32[12]{0:T(128)S(1)} %get-tuple-element.512) | copy-start | bytes 148
  19.8 11.5 %copy-start.23 = (f32[2,256,256]{2,1,0:T(8,128)}, f32[2,256,256]{2,1,0:T(8,128)S(1)}, u32[]{:S(2)}) copy-start(f32[2,256,256]{2,1,0:T(8,128)S(1)} %fusion.82) | copy-start | bytes 1572868
  19.9 11.5 %copy-start.36 = (pred[256,256]{1,0:T(8,128)(4,1)}, pred[256,256]{1,0:T(8,128)(4,1)S(1)}, u32[]{:S(2)}) copy-start(pred[256,256]{1,0:T(8,128)(4,1)S(1)} %iota_compare_fusion) | copy-start | bytes 196612
  19.9 7.7 %copy-start.25 = (f32[2,256,128]{2,1,0:T(8,128)}, f32[2,256,128]{2,1,0:T(8,128)S(1)}, u32[]{:S(2)}) copy-start(f32[2,256,128]{2,1,0:T(8,128)S(1)} %convert_element_type.192) | copy-start | bytes 786436
  20.0 9.5 %copy-start.27 = (f32[2,256,128]{2,1,0:T(8,128)}, f32[2,256,128]{2,1,0:T(8,128)S(1)}, u32[]{:S(2)}) copy-start(f32[2,256,128]{2,1,0:T(8,128)S(1)} %convert_element_type.195) | copy-start | bytes 786436
  21.2 13.0 %all-to-all-start = ((bf16[4,128,768]{1,2,0:T(8,128)(2,1)}), bf16[4,128,768]{1,2,0:T(8,128)(2,1)S(1)}, u32[]{:S(2)}, u32[]{:S(2)}) async-start(bf16[4,128,768]{1,2,0:T(8,128)(2,1)} %bitcast.1), calls=%async_computation | async-start | bytes 1572864 | tf_op jit(solution)/shard_map/all_to_all | solution.py:23
  24.9 14.7 %copy-start.40 = (f32[2,256,12]{1,2,0:T(8,128)}, f32[2,256,12]{1,2,0:T(8,128)S(1)}, u32[]{:S(2)}) copy-start(f32[2,256,12]{1,2,0:T(8,128)S(1)} %get-tuple-element.505) | copy-start | bytes 73732
  26.5 4.9 %copy-start.38 = (f32[2,12,2,128]{3,1,2,0:T(8,128)}, f32[2,12,2,128]{3,1,2,0:T(8,128)S(1)}, u32[]{:S(2)}) copy-start(f32[2,12,2,128]{3,1,2,0:T(8,128)S(1)} %reduce-window.24) | copy-start | bytes 73732
  27.3 4.0 %copy-start.39 = (f32[2,12,256]{2,0,1:T(2,128)}, f32[2,12,256]{2,0,1:T(2,128)S(1)}, u32[]{:S(2)}) copy-start(f32[2,12,256]{2,0,1:T(2,128)S(1)} %reduce_window_sum.56) | copy-start | bytes 73732
  27.6 3.8 %copy-start.42 = (f32[2,12,256]{2,1,0:T(8,128)}, f32[2,12,256]{2,1,0:T(8,128)S(1)}, u32[]{:S(2)}) copy-start(f32[2,12,256]{2,1,0:T(8,128)S(1)} %get-tuple-element.508) | copy-start | bytes 73732
  27.6 3.8 %copy-start.44 = (f32[2,12,256]{2,1,0:T(8,128)}, f32[2,12,256]{2,1,0:T(8,128)S(1)}, u32[]{:S(2)}) copy-start(f32[2,12,256]{2,1,0:T(8,128)S(1)} %get-tuple-element.509) | copy-start | bytes 73732
  27.6 3.8 %copy-start.33 = (f32[2,12,256]{2,1,0:T(8,128)}, f32[2,12,256]{2,1,0:T(8,128)S(1)}, u32[]{:S(2)}) copy-start(f32[2,12,256]{2,1,0:T(8,128)S(1)} %get-tuple-element.507) | copy-start | bytes 73732
  39.5 2.0 copy-start.12
  49.6 2.7 %copy-start.53 = (f32[2,12]{1,0:T(2,128)}, f32[2,12]{1,0:T(2,128)S(1)}, u32[]{:S(2)}) copy-start(f32[2,12]{1,0:T(2,128)S(1)} %get-tuple-element.719) | copy-start | bytes 292
  49.6 2.7 %copy-start.5 = (f32[2,256,12,64]{1,0,3,2:T(2,128)S(1)}, f32[2,256,12,64]{1,0,3,2:T(2,128)}, u32[]{:S(2)}) copy-start(f32[2,256,12,64]{1,0,3,2:T(2,128)} %copy-done.4) | copy-start | bytes 4718596
  49.8 2.5 copy-start.18
  49.8 3.0 %copy-start.2 = (bf16[2,12,256,256]{3,2,1,0:T(8,128)(2,1)S(1)}, bf16[2,12,256,256]{3,2,1,0:T(8,128)(2,1)}, u32[]{:S(2)}) copy-start(bf16[2,12,256,256]{3,2,1,0:T(8,128)(2,1)} %multiply_convert_fusion) | copy-start | bytes 9437188
  49.8 3.1 %copy-start.8 = (bf16[2,256,12,64]{1,3,2,0:T(8,128)(2,1)S(1)}, bf16[2,256,12,64]{1,3,2,0:T(8,128)(2,1)}, u32[]{:S(2)}) copy-start(bf16[2,256,12,64]{1,3,2,0:T(8,128)(2,1)} %copy-done.7) | copy-start | bytes 2359300
  55.3 5.4 %copy-start.50 = (f32[3216]{0:T(1024)S(1)}, f32[3216]{0:T(1024)}, u32[]{:S(2)}) copy-start(f32[3216]{0:T(1024)} %param.23) | copy-start | bytes 38596
  55.3 5.5 %copy-start.54 = (s32[8]{0:T(128)S(1)}, s32[8]{0:T(128)}, u32[]{:S(2)}) copy-start(s32[8]{0:T(128)} %param.27) | copy-start | bytes 100
  56.3 20.8 %all-to-all-start.2 = ((bf16[4,128,768]{1,2,0:T(8,128)(2,1)}), bf16[4,128,768]{1,2,0:T(8,128)(2,1)}, u32[]{:S(2)}, u32[]{:S(2)}) async-start(bf16[4,128,768]{1,2,0:T(8,128)(2,1)} %copy.214), calls=%async_computation.2 | async-start | bytes 1572864 | tf_op jit(solution)/shard_map/all_to_all | solution.py:30
  71.1 3.8 %copy-start.70 = (s32[8]{0:T(128)S(1)}, s32[8]{0:T(128)}, u32[]{:S(2)}) copy-start(s32[8]{0:T(128)} %param.26) | copy-start | bytes 100
  83.7 26.6 %copy-start.58 = (f32[1,804]{1,0:T(1,128)S(1)}, f32[1,804]{1,0:T(1,128)}, u32[]{:S(2)}) copy-start(f32[1,804]{1,0:T(1,128)} %param.25) | copy-start | bytes 9652
  83.7 26.6 %copy-start.59 = (f32[1,804]{1,0:T(1,128)S(1)}, f32[1,804]{1,0:T(1,128)}, u32[]{:S(2)}) copy-start(f32[1,804]{1,0:T(1,128)} %param.24) | copy-start | bytes 9652
  83.7 50.0 %all-to-all-start.3 = ((bf16[4,128,768]{1,2,0:T(8,128)(2,1)}), bf16[4,128,768]{1,2,0:T(8,128)(2,1)S(1)}, u32[]{:S(2)}, u32[]{:S(2)}) async-start(bf16[4,128,768]{1,2,0:T(8,128)(2,1)} %bitcast.186), calls=%async_computation.3 | async-start | bytes 1572864 | tf_op jit(solution)/shard_map/all_to_all | solution.py:23
  138.4 4.9 %copy-start = (bf16[2,256,12,64]{1,0,3,2:T(2,128)(2,1)}, bf16[2,256,12,64]{1,0,3,2:T(2,128)(2,1)S(1)}, u32[]{:S(2)}) copy-start(bf16[2,256,12,64]{1,0,3,2:T(2,128)(2,1)S(1)} %squeeze_broadcast_in_dim_reshape.2) | copy-start | bytes 2359300
  138.4 2.1 copy-start.9
  140.5 2.7 %copy-start.19 = (bf16[2,12,128,64]{3,2,1,0:T(8,128)(2,1)S(1)}, bf16[2,12,128,64]{3,2,1,0:T(8,128)(2,1)}, u32[]{:S(2)}) copy-start(bf16[2,12,128,64]{3,2,1,0:T(8,128)(2,1)} %copy-done.18) | copy-start | bytes 1179652
  148.0 2.8 %copy-start.64 = (f32[2,12]{1,0:T(2,128)}, f32[2,12]{1,0:T(2,128)S(1)}, u32[]{:S(2)}) copy-start(f32[2,12]{1,0:T(2,128)S(1)} %get-tuple-element.708) | copy-start | bytes 292 | tf_op jit(solution)/shard_map/transpose(jvp())/while
  148.0 2.8 %copy-start.72 = (f32[2]{0:T(128)}, f32[2]{0:T(128)S(1)}, u32[]{:S(2)}) copy-start(f32[2]{0:T(128)S(1)} %get-tuple-element.706) | copy-start | bytes 28 | tf_op jit(solution)/shard_map/transpose(jvp())/while
  152.1 2.2 copy-start.73
  154.3 2.8 %copy-start.64 = (f32[2,12]{1,0:T(2,128)}, f32[2,12]{1,0:T(2,128)S(1)}, u32[]{:S(2)}) copy-start(f32[2,12]{1,0:T(2,128)S(1)} %get-tuple-element.708) | copy-start | bytes 292 | tf_op jit(solution)/shard_map/transpose(jvp())/while
  154.3 2.8 %copy-start.72 = (f32[2]{0:T(128)}, f32[2]{0:T(128)S(1)}, u32[]{:S(2)}) copy-start(f32[2]{0:T(128)S(1)} %get-tuple-element.706) | copy-start | bytes 28 | tf_op jit(solution)/shard_map/transpose(jvp())/while
  158.4 2.2 copy-start.73
  160.6 3.8 %copy-start.10 = (bf16[2,256,12,64]{1,3,2,0:T(8,128)(2,1)S(1)}, bf16[2,256,12,64]{1,3,2,0:T(8,128)(2,1)}, u32[]{:S(2)}) copy-start(bf16[2,256,12,64]{1,3,2,0:T(8,128)(2,1)} %copy-done.7) | copy-start | bytes 2359300
  160.6 3.8 %copy-start.13 = (f32[2,12,128,64]{3,2,1,0:T(8,128)S(1)}, f32[2,12,128,64]{3,2,1,0:T(8,128)}, u32[]{:S(2)}) copy-start(f32[2,12,128,64]{3,2,1,0:T(8,128)} %get-tuple-element.236) | copy-start | bytes 2359300
  164.5 2.1 copy-start.3
  168.0 2.7 copy-start.34
  168.0 2.7 copy-start.37
  170.7 6.7 %copy-start.21 = (bf16[2,12,256,128]{3,2,1,0:T(8,128)(2,1)S(1)}, bf16[2,12,256,128]{3,2,1,0:T(8,128)(2,1)}, u32[]{:S(2)}) copy-start(bf16[2,12,256,128]{3,2,1,0:T(8,128)(2,1)} %convolution_convert_fusion.2) | copy-start | bytes 4718596
  170.7 6.7 %copy-start.26 = (f32[2,256,128]{2,1,0:T(8,128)S(1)}, f32[2,256,128]{2,1,0:T(8,128)}, u32[]{:S(2)}) copy-start(f32[2,256,128]{2,1,0:T(8,128)} %copy-done.25) | copy-start | bytes 786436
  170.7 6.7 %copy-start.28 = (f32[2,256,128]{2,1,0:T(8,128)S(1)}, f32[2,256,128]{2,1,0:T(8,128)}, u32[]{:S(2)}) copy-start(f32[2,256,128]{2,1,0:T(8,128)} %copy-done.27) | copy-start | bytes 786436
  170.7 6.7 %copy-start.43 = (f32[2,12,256]{2,1,0:T(8,128)S(1)}, f32[2,12,256]{2,1,0:T(8,128)}, u32[]{:S(2)}) copy-start(f32[2,12,256]{2,1,0:T(8,128)} %copy-done.42) | copy-start | bytes 73732
  170.7 6.7 %copy-start.45 = (f32[2,12,256]{2,1,0:T(8,128)S(1)}, f32[2,12,256]{2,1,0:T(8,128)}, u32[]{:S(2)}) copy-start(f32[2,12,256]{2,1,0:T(8,128)} %copy-done.44) | copy-start | bytes 73732
  177.4 20.7 %copy-start.32 = (bf16[1,512,128]{2,1,0:T(8,128)(2,1)S(1)}, bf16[1,512,128]{2,1,0:T(8,128)(2,1)}, u32[]{:S(2)}) copy-start(bf16[1,512,128]{2,1,0:T(8,128)(2,1)} %copy-done.31) | copy-start | bytes 393220
  181.9 17.7 %copy-start.22 = (f32[2,256,256]{2,1,0:T(8,128)S(1)}, f32[2,256,256]{2,1,0:T(8,128)}, u32[]{:S(2)}) copy-start(f32[2,256,256]{2,1,0:T(8,128)} %get-tuple-element.435) | copy-start | bytes 1572868
  181.9 17.7 %copy-start.30 = (bf16[1,512,128]{2,1,0:T(8,128)(2,1)S(1)}, bf16[1,512,128]{2,1,0:T(8,128)(2,1)}, u32[]{:S(2)}) copy-start(bf16[1,512,128]{2,1,0:T(8,128)(2,1)} %copy-done.29) | copy-start | bytes 393220
  182.8 17.6 %copy-start.15 = (bf16[4,128,768]{1,2,0:T(8,128)(2,1)S(1)}, bf16[4,128,768]{1,2,0:T(8,128)(2,1)}, u32[]{:S(2)}) copy-start(bf16[4,128,768]{1,2,0:T(8,128)(2,1)} %copy-done.14) | copy-start | bytes 2359300
  182.8 17.6 %copy-start.17 = (bf16[4,128,768]{1,2,0:T(8,128)(2,1)S(1)}, bf16[4,128,768]{1,2,0:T(8,128)(2,1)}, u32[]{:S(2)}) copy-start(bf16[4,128,768]{1,2,0:T(8,128)(2,1)} %copy-done.16) | copy-start | bytes 2359300
  194.0 10.9 %all-to-all-start.5 = ((bf16[4,128,12]{1,2,0:T(8,128)(2,1)}), bf16[4,128,12]{1,2,0:T(8,128)(2,1)S(1)}, u32[]{:S(2)}, u32[]{:S(2)}) async-start(bf16[4,128,12]{1,2,0:T(8,128)(2,1)} %fusion.47), calls=%async_computation.5 | async-start | bytes 32768 | tf_op jit(solution)/shard_map/all_to_all | solution.py:30
  199.7 2.6 copy-start.24
  203.1 6.0 %copy-start.52 = (f32[3072]{0:T(1024)S(1)}, f32[3072]{0:T(1024)}, u32[]{:S(2)}) copy-start(f32[3072]{0:T(1024)} %get-tuple-element.436) | copy-start | bytes 36868
  203.7 51.2 %copy-start.56 = (f32[804]{0:T(1024)S(1)}, f32[804]{0:T(1024)}, u32[]{:S(2)}) copy-start(f32[804]{0:T(1024)} %get-tuple-element.534) | copy-start | bytes 9652
  203.7 51.2 %copy-start.57 = (f32[804]{0:T(1024)S(1)}, f32[804]{0:T(1024)}, u32[]{:S(2)}) copy-start(f32[804]{0:T(1024)} %get-tuple-element.535) | copy-start | bytes 9652
  203.7 53.1 %copy-start.48 = (f32[3216]{0:T(1024)S(1)}, f32[3216]{0:T(1024)}, u32[]{:S(2)}) copy-start(f32[3216]{0:T(1024)} %get-tuple-element.444) | copy-start | bytes 38596
  203.7 53.0 %copy-start.49 = (f32[3216]{0:T(1024)S(1)}, f32[3216]{0:T(1024)}, u32[]{:S(2)}) copy-start(f32[3216]{0:T(1024)} %get-tuple-element.445) | copy-start | bytes 38596
  203.7 53.0 %copy-start.51 = (f32[3216]{0:T(1024)S(1)}, f32[3216]{0:T(1024)}, u32[]{:S(2)}) copy-start(f32[3216]{0:T(1024)} %param.23) | copy-start | bytes 38596
  204.9 46.4 %all-to-all-start.6 = ((bf16[4,128,256]{2,1,0:T(8,128)(2,1)}), bf16[4,128,256]{2,1,0:T(8,128)(2,1)S(1)}, u32[]{:S(2)}, u32[]{:S(2)}) async-start(bf16[4,128,256]{2,1,0:T(8,128)(2,1)} %pad_maximum_fusion), calls=%async_computation.6 | async-start | bytes 524288 | tf_op jit(solution)/shard_map/all_to_all | solution.py:30
  251.3 13.8 %all-to-all-start.4 = ((bf16[4,128,768]{1,2,0:T(8,128)(2,1)}), bf16[4,128,768]{1,2,0:T(8,128)(2,1)S(1)}, u32[]{:S(2)}, u32[]{:S(2)}) async-start(bf16[4,128,768]{1,2,0:T(8,128)(2,1)} %copy.223), calls=%async_computation.4 | async-start | bytes 1572864 | tf_op jit(solution)/shard_map/all_to_all | solution.py:30
  (24 other events, 29.9 us)

commit v3 on v2

--- a/solution.py
+++ b/solution.py
@@ -34,6 +34,17 @@
     parts = from_heads(x, groups)
     _, t, w = parts.shape
     return parts.transpose(1, 0, 2).reshape(1, t, groups * w)
+
+
+def tree_sum(x, axis):
+    size = lax.axis_size(axis)
+    if size & (size - 1):
+        return lax.psum(x, axis)
+    step = 1
+    while step < size:
+        x = x + lax.ppermute(x, axis, [(i, i ^ step) for i in range(size)])
+        step *= 2
+    return x
 
 
 def rounded(value):
@@ -131,16 +142,6 @@
     b_all = bc_all[..., :state_size]
     c_all = bc_all[..., state_size:]
     seq_resets = resets[0]
-    owners_n = lax.axis_size("dp")
-    cap_n = adam_mean.shape[1]
-    len_n = parameters.shape[0]
-    state_all = lax.all_gather(jnp.stack([adam_mean[0], adam_square[0]]), "dp", axis=0)
-    starts = jnp.cumsum(bucket_size) - bucket_size
-    laid = jnp.zeros((2, len_n + cap_n), jnp.float32)
-    for k in range(owners_n):
-        laid = lax.dynamic_update_slice(laid, state_all[bucket_owner[k]], (0, starts[k]))
-    mean_flat = laid[0, :len_n]
-    square_flat = laid[1, :len_n]
 
     def local_fn(x_arg, dt_arg, b_arg, c_arg, a_arg, bias_arg, skip_arg):
         return ssd_group(x_arg, dt_arg, b_arg, c_arg, seq_resets, a_arg, bias_arg, skip_arg)
@@ -182,9 +183,6 @@
         jnp.zeros((3, heads_all), jnp.float32), head_grads, (0, first)
     )
     grad_part = jnp.concatenate([full_heads.reshape(-1), d_gain])
-    gradient = lax.psum(grad_part, ("dp", "ctx"))
-    grad_norm = jnp.sqrt(jnp.sum(gradient * gradient))
-    shrink = jnp.minimum(1.0, clip_norm / (grad_norm + 1e-06))
     owners = lax.axis_size("dp")
     slot_cap = adam_mean.shape[1]
     total_len = parameters.shape[0]
@@ -198,6 +196,17 @@
     slots = jnp.arange(slot_cap, dtype=jnp.int32)
     valid = slots < row_size
     padding = jnp.zeros((slot_cap,), jnp.float32)
+    sender = (lax.axis_index("ctx") == 0) & valid
+    own_state = jnp.where(sender, jnp.stack([adam_mean[0], adam_square[0]]), 0.0)
+    laid = lax.dynamic_update_slice(
+        jnp.zeros((2, total_len + slot_cap), jnp.float32), own_state, (0, row_begin)
+    )[:, :total_len]
+    summed = tree_sum(tree_sum(jnp.concatenate([grad_part[None], laid]), "ctx"), "dp")
+    gradient = summed[0]
+    mean_flat = summed[1]
+    square_flat = summed[2]
+    grad_norm = jnp.sqrt(jnp.sum(gradient * gradient))
+    shrink = jnp.minimum(1.0, clip_norm / (grad_norm + 1e-06))
     grad_row = (
         jnp.where(
             valid,

time: 269 us -> 188 us (0.70)
  blocking collectives: 64.4 us -> 9.49 us
  between operations: 33.8 us -> 4.39 us
  waiting for transfers between devices: 6.4 us -> 21.8 us
  local copies, waits for them, and re-layouts: 56 us -> 47.1 us
  other arithmetic: 55.5 us -> 49.9 us
  starting transfers between devices: 29.5 us -> 34.4 us
    psum x1 -> x0, blocking collectives: 40.7 us -> none  [on_device(): gradient = lax.psum(grad_part, ('dp', 'ctx'))]
    all_gather x1 -> x0, blocking collectives: 14.3 us -> none  [on_device(): lax.all_gather(jnp.stack([adam_mean[0], adam_square[0]]), 'dp', axis=0)]
    all_to_all x4, waiting for transfers between devices: 6.4 us -> 15.7 us  [from_heads(): return lax.all_to_all(x, 'ctx', 0, 0, tiled=True)]
    ppermute x0 -> x5, starting transfers between devices: none -> 6.51 us  [tree_sum(): x = x + lax.ppermute(x, axis, [(i, i ^ step) for i in range(size)])]
    all_to_all x3, waiting for transfers between devices: 0.01 us -> 3.33 us  [to_heads(): x = lax.all_to_all(x, 'ctx', 0, 0, tiled=True)]
    unnamed x140 -> x148, local copies, waits for them, and re-layouts: 18.8 us -> 15.9 us
    dynamic_update_slice x8 -> x1, local copies, waits for them, and re-layouts: 3.13 us -> 0.28 us  [on_device(): lax.dynamic_update_slice(jnp.zeros((2, total_len + slot_cap), jnp.float32...]
    ppermute x0 -> x5, waiting for transfers between devices: none -> 2.74 us  [tree_sum(): x = x + lax.ppermute(x, axis, [(i, i ^ step) for i in range(size)])]
  transfers between devices with their start and end apart: 7 -> 12, of which waited for: 1 -> 6; matrix products, arithmetic and copies ran while one was open for 15% -> 16% of each run, Pallas kernels for 0% -> 0%
where the time goes in v3:
time: 188 us; the launch traced here: 187 us
  other arithmetic  49.9 us (27%)
  local copies, waits for them, and re-layouts  47.1 us (25%)
  starting transfers between devices  34.4 us (18%)
  waiting for transfers between devices  21.8 us (12%)
  matrix products  19.3 us (10%)
  blocking collectives  9.49 us (5%)
  between operations  4.39 us (2%)
    unnamed x148, local copies, waits for them, and re-layouts  15.9 us
    all_to_all x4, waiting for transfers between devices, from_heads(): return lax.all_to_all(x, 'ctx', 0, 0, tiled=True)  15.7 us
    all_to_all x4, starting transfers between devices, from_heads(): return lax.all_to_all(x, 'ctx', 0, 0, tiled=True)  15.5 us
    all_to_all x3, starting transfers between devices, to_heads(): x = lax.all_to_all(x, 'ctx', 0, 0, tiled=True)  12.3 us
    all_gather x1, blocking collectives, on_device(): lax.all_gather(jnp.concatenate([b_input, c_input], axis=2), 'ctx', axis=1...  9.49 us
    convert_element_type x6, other arithmetic, rounded(): value.astype(jnp.bfloat16)  7.71 us
    dot_general x3, matrix products, ssd_group(): jnp.einsum('chsn,cshp->chnp', b_decayed, scaled, precision=highest)  7.29 us
    another operation x9, other arithmetic  7.28 us
  transfers between devices with their start and end apart: 12, of which 6 were waited for; matrix products, arithmetic and copies ran while one was open for 16% of the time, Pallas kernels for 0%

profile of v3, /device:TPU:0, one launch (start us, length us, event | category | flops | bytes accessed | tf_op | source)
XLA Modules:
  0.0 186.5 jit_solution(17351764636696480327)
XLA Ops:
  0.7 1.4 reshape.401
  2.0 5.2 %all-to-all-start.1 = ((bf16[4,128,12]{1,2,0:T(8,128)(2,1)}), bf16[4,128,12]{1,2,0:T(8,128)(2,1)S(1)}, u32[]{:S(2)}, u32[]{:S(2)}) async-start(bf16[4,128,12]{1,2,0:T(8,128)(2,1)} %bitcast.2), calls=%async_computation.1 | async-start | bytes 32768 | tf_op jit(solution)/shard_map/all_to_all | solution.py:23
  9.6 9.5 %all_gather.3 = bf16[1,512,256]{2,1,0:T(8,128)(2,1)S(1)} all-gather(bf16[1,128,256]{2,1,0:T(8,128)(2,1)S(1)} %pad_maximum_fusion.1), channel_id=1, replica_groups=mesh['dp'=8,'ctx'=4] {'ctx'}, dimensions={1}, use_global_device_ids=true | all-gather | bytes 327680 | tf_op jit(solution)/shard_map/all_gather | solution.py:141
  19.5 1.2 copy.197
  20.7 3.5 %all-to-all-start = ((bf16[4,128,768]{1,2,0:T(8,128)(2,1)}), bf16[4,128,768]{1,2,0:T(8,128)(2,1)S(1)}, u32[]{:S(2)}, u32[]{:S(2)}) async-start(bf16[4,128,768]{1,2,0:T(8,128)(2,1)} %bitcast.1), calls=%async_computation | async-start | bytes 1572864 | tf_op jit(solution)/shard_map/all_to_all | solution.py:23
  24.8 1.1 reduce-window.24
  27.1 1.9 multiply_convert_fusion.2
  29.0 1.8 multiply_convert_fusion.1
  30.9 2.7 %multiply_convert_fusion = bf16[2,12,256,256]{3,2,1,0:T(8,128)(2,1)} fusion(f32[2,12,256]{2,1,0:T(8,128)S(1)} %get-tuple-element.500, f32[2,256,256]{2,1,0:T(8,128)S(1)} %fusion.82, pred[256,256]{1,0:T(8,128)(4,1)S(1)} %iota_compare_fusion), kind=kLoop, calls=%fused_computation.22 | loop fusion | flops 7864320 | bytes 3760128 | tf_op jit(solution)/shard_map/jvp()/convert_element_type | solution.py:51
  33.6 0.9 copy-done.17
  34.5 1.8 copy.198
  36.3 2.6 %reshape.419 = f32[2,256,12,64]{1,0,3,2:T(2,128)S(1)} reshape(f32[4,128,768]{1,0,2:T(4,128)} %copy.198) | data formatting | bytes 3145728 | tf_op jit(solution)/shard_map/jvp()/convert_element_type | solution.py:62
  39.2 1.0 copy-done.4
  41.0 1.8 fusion.83
  42.9 5.7 %while.36 = (s32[]{:T(128)}, f32[12,128,64]{2,1,0:T(8,128)S(1)}, f32[2,12,128,64]{3,2,1,0:T(8,128)S(1)}, f32[2,12]{1,0:T(2,128)S(1)}, f32[2,12,1,1]{1,3,2,0:T(1,...) while((s32[]{:T(128)}, f32[12,128,64]{2,1,0:T(8,128)S(1)}, ...), condition=%wide.region_3.4_spmd.clone, body=%wide.region_2.3_spmd.clone.sunk | while | flops 589827 | bytes 5900104 | solution.py:83
  48.8 2.5 %fusion.84 = f32[2,12,64,256]{3,2,1,0:T(8,128)S(1)} fusion(bf16[2,12,128,64]{3,2,1,0:T(8,128)(2,1)S(1)} %convert_element_type.194, bf16[2,12,256,128]{3,2,1,0:T(8,128)(2,1)} %multiply_convert_fusion.1), kind=kOutput, calls=%fused_computation.176 | convolution fusion | flops 100663296 | bytes 3538944 | tf_op jit(solution)/shard_map/jvp(chtn,chnp->cthp)/dot_general | solution.py:85
  52.0 1.1 fusion.32
  54.4 1.0 copy.214
  55.3 4.5 %all-to-all-start.2 = ((bf16[4,128,768]{1,2,0:T(8,128)(2,1)}), bf16[4,128,768]{1,2,0:T(8,128)(2,1)}, u32[]{:S(2)}, u32[]{:S(2)}) async-start(bf16[4,128,768]{1,2,0:T(8,128)(2,1)} %copy.214), calls=%async_computation.2 | async-start | bytes 1572864 | tf_op jit(solution)/shard_map/all_to_all | solution.py:30
  60.3 1.5 copy.216
  61.8 7.0 %all-to-all-done.2 = bf16[4,128,768]{1,2,0:T(8,128)(2,1)} async-done(((bf16[4,128,768]{1,2,0:T(8,128)(2,1)}), bf16[4,128,768]{1,2,0:T(8,128)(2,1)}, u32[]{:S(2)}, u32[]{:S(2)}) %all-to-all-start.2) | async-done | bytes 786464 | tf_op jit(solution)/shard_map/all_to_all | solution.py:30
  68.9 1.2 convert_element_type.233
  70.7 1.5 fusion.21
  72.2 2.6 %fusion.30 = (bf16[1,128,3072]{1,2,0:T(8,128)(2,1)}, bf16[1,128,3072]{1,2,0:T(8,128)(2,1)}, bf16[1,128,3072]{1,2,0:T(8,128)(2,1)}) fusion(bf16[1,128,3072]{1,2,0:T(8,128)(2,1)S(1)} %copy.215, f32[1,128,3072]{1,2,0:T(8,128)S(1)} %get-tuple-element.486, bf16[1,128,3072]{1,2,0:T(8,128)(2,1)S(1)} %copy.216, f32[128]{0:T(128)S(1)} %fusion.76, ...), kind=kLoop, calls=%fused_computation.61 | loop fusion | flops 8650752 | bytes 7091200 | tf_op jit(solution)/shard_map/convert_element_type | solution.py:111
  74.9 3.6 %all-to-all-start.3 = ((bf16[4,128,768]{1,2,0:T(8,128)(2,1)}), bf16[4,128,768]{1,2,0:T(8,128)(2,1)S(1)}, u32[]{:S(2)}, u32[]{:S(2)}) async-start(bf16[4,128,768]{1,2,0:T(8,128)(2,1)} %bitcast.153), calls=%async_computation.3 | async-start | bytes 1572864 | tf_op jit(solution)/shard_map/all_to_all | solution.py:23
  79.4 1.3 fusion.74
  84.2 3.3 %all-to-all-done.3 = bf16[4,128,768]{1,2,0:T(8,128)(2,1)S(1)} async-done(((bf16[4,128,768]{1,2,0:T(8,128)(2,1)}), bf16[4,128,768]{1,2,0:T(8,128)(2,1)S(1)}, u32[]{:S(2)}, u32[]{:S(2)}) %all-to-all-start.3) | async-done | bytes 786464 | tf_op jit(solution)/shard_map/all_to_all | solution.py:23
  88.4 1.5 copy.217
  89.9 2.3 %squeeze_broadcast_in_dim_reshape.2 = bf16[2,256,12,64]{1,0,3,2:T(2,128)(2,1)S(1)} reshape(bf16[4,128,768]{1,0,2:T(4,128)(2,1)} %copy.217) | data formatting | bytes 1572864 | tf_op jit(solution)/shard_map/squeeze;broadcast_in_dim;reshape | solution.py:171
  92.2 2.1 %convolution_convert_fusion.3 = bf16[2,12,128,64]{2,3,1,0:T(8,128)(2,1)S(1)} fusion(bf16[2,12,256,128]{3,2,1,0:T(8,128)(2,1)} %multiply_convert_fusion.1, bf16[2,256,12,64]{1,0,3,2:T(2,128)(2,1)S(1)} %squeeze_broadcast_in_dim_reshape.2), kind=kOutput, calls=%fused_computation.74 | convolution fusion | flops 100859904 | bytes 2752512 | tf_op jit(solution)/shard_map/transpose(jvp(chtn,chnp->cthp))/dot_general | solution.py:85
  94.3 2.7 %convolution_convert_fusion = bf16[2,12,256,256]{3,2,1,0:T(8,128)(2,1)} fusion(bf16[2,256,12,64]{1,3,2,0:T(8,128)(2,1)S(1)} %copy-done.9, bf16[2,256,12,64]{1,0,3,2:T(2,128)(2,1)S(1)} %squeeze_broadcast_in_dim_reshape.2), kind=kOutput, calls=%fused_computation.40 | convolution fusion | flops 202899456 | bytes 4718592 | tf_op jit(solution)/shard_map/transpose(jvp(chts,cshp->cthp))/dot_general | solution.py:71
  97.0 1.8 convolution_convert_fusion.2
  98.8 1.0 convert_element_type.208
  99.8 1.4 broadcast.150
  101.2 7.8 %while.37 = (s32[]{:T(128)}, f32[12,128,64]{2,1,0:T(8,128)S(1)}, f32[2,12]{1,0:T(2,128)S(1)}, f32[2,12,128,64]{3,2,1,0:T(8,128)}, f32[2,12,128,64]{2,3,1,0:T(8,1...) while((s32[]{:T(128)}, f32[12,128,64]{2,1,0:T(8,128)S(1)}, ...), condition=%wide.region_8.9_spmd.clone, body=%wide.region_6.8_spmd.clone.sunk | while | flops 688132 | bytes 4326932 | solution.py:83
  101.2 1.0 bitcast_dynamic-update-slice_fusion.5
  102.7 1.0 constant_dynamic-slice_fusion.6
  104.1 0.9 fusion.110
  105.1 0.9 bitcast_dynamic-update-slice_fusion.5
  106.6 1.0 constant_dynamic-slice_fusion.6
  107.9 0.9 fusion.110
  109.0 3.8 %fusion.85 = f32[2,12,64,256]{3,2,1,0:T(8,128)S(1)} fusion(f32[2,12,128,64]{3,2,1,0:T(8,128)} %get-tuple-element.236, bf16[2,12,256,128]{3,2,1,0:T(8,128)(2,1)} %multiply_convert_fusion.2), kind=kOutput, calls=%fused_computation.177 | convolution fusion | flops 603979776 | bytes 3932160 | tf_op jit(solution)/shard_map/transpose(jvp(chsn,cshp->chnp))/dot_general | solution.py:74
  112.8 1.7 convolution_convert_fusion.1
  117.0 1.3 copy-done.14
  118.4 4.6 %fusion.11 = (f32[2,12,256]{2,1,0:T(8,128)}, f32[2,12,256]{2,1,0:T(8,128)}, f32[2,256,256]{2,1,0:T(8,128)S(1)}) fusion(bf16[2,12,256,256]{3,2,1,0:T(8,128)(2,1)S(1)} %copy-done.14, f32[2,12,256]{2,1,0:T(8,128)S(1)} %copy-done.34, f32[2,256,256]{2,1,0:T(8,128)S(1)} %copy-done.23, pred[256,256]{1,0:T(8,128)(4,1)S(1)} %copy-done.38), kind=kLoop, calls=%fused_computation.26 | loop fusion | flops 18731008 | bytes 4333568 | tf_op jit(solution)/shard_map/transpose(jvp())/reduce_sum | solution.py:68
  123.0 4.4 %fusion.13 = (f32[2,256,128]{2,1,0:T(8,128)S(1)}, f32[2,12,256]{2,1,0:T(8,128)}, f32[2,12,256]{2,1,0:T(8,128)S(1)}, f32[2,256,128]{2,1,0:T(8,128)S(1)}) fusion(bf16[2,12,256,128]{3,2,1,0:T(8,128)(2,1)S(1)} %copy-done.21, f32[2,12,256]{2,1,0:T(8,128)S(1)} %copy-done.48, f32[2,256,128]{2,1,0:T(8,128)S(1)} %copy-done.28, f32[2,256,128]{2,1,0:T(8,128)S(1)} %copy-done.26, ...), kind=kLoop, calls=%fused_computation.32 | loop fusion | flops 7720960 | bytes 4292608 | tf_op jit(solution)/shard_map/transpose(jvp())/reduce_sum | solution.py:84
  128.0 1.5 fusion.52
  129.5 1.3 copy.231
  130.8 1.4 copy.227
  132.2 0.9 add_add_fusion
  133.7 5.7 %reduce-window.31 = f32[2,12,2,128]{3,1,2,0:T(8,128)S(1)} reduce-window(f32[2,12,2,128]{3,1,2,0:T(8,128)} %copy.233, f32[]{:T(128)} %constant.126.clone.1), window={size=1x1x1x128 pad=0_0x0_0x0_0x0_127}, to_apply=%region_15.16 | reduce-window | flops 780288 | bytes 49156 | tf_op jit(solution)/shard_map/reduce-window.2
  142.5 1.6 collective-permute-start
  144.1 2.3 %copy.240 = bf16[1,128,3072]{2,1,0:T(8,128)(2,1)} copy(bf16[1,128,3072]{1,2,0:T(8,128)(2,1)} %get-tuple-element.491) | data formatting | bytes 1572864
  146.4 1.2 copy.242
  149.1 3.3 %all-to-all-start.5 = ((bf16[4,128,12]{1,2,0:T(8,128)(2,1)}), bf16[4,128,12]{1,2,0:T(8,128)(2,1)S(1)}, u32[]{:S(2)}, u32[]{:S(2)}) async-start(bf16[4,128,12]{1,2,0:T(8,128)(2,1)} %fusion.47), calls=%async_computation.5 | async-start | bytes 32768 | tf_op jit(solution)/shard_map/all_to_all | solution.py:30
  153.7 1.6 collective-permute-start.3
  156.0 1.9 %collective-permute-done.3 = f32[3,3216]{1,0:T(4,128)S(1)} collective-permute-done((f32[3,3216]{1,0:T(4,128)S(1)}, f32[3,3216]{1,0:T(4,128)S(1)}, u32[]{:S(2)}, u32[]{:S(2)}) %collective-permute-start.3) | collective-permute-done | bytes 38624 | tf_op jit(solution)/shard_map/ppermute | solution.py:45
  157.9 2.6 %collective-permute-start.4 = (f32[3,3216]{1,0:T(4,128)S(1)}, f32[3,3216]{1,0:T(4,128)S(1)}, u32[]{:S(2)}, u32[]{:S(2)}) collective-permute-start(f32[3,3216]{1,0:T(4,128)S(1)} %add.160), channel_id=1, source_target_pairs={{0,16},{4,20},{8,24},{12,28},{16,0},{20,4},{24,8},{28,12},{1,17},{... | collective-permute-start | bytes 115784 | tf_op jit(solution)/shard_map/ppermute | solution.py:45
  162.6 1.0 copy.223
  163.6 4.3 %all-to-all-start.6 = ((bf16[4,128,256]{2,1,0:T(8,128)(2,1)}), bf16[4,128,256]{2,1,0:T(8,128)(2,1)S(1)}, u32[]{:S(2)}, u32[]{:S(2)}) async-start(bf16[4,128,256]{2,1,0:T(8,128)(2,1)} %pad_maximum_fusion), calls=%async_computation.6 | async-start | bytes 524288 | tf_op jit(solution)/shard_map/all_to_all | solution.py:30
  170.0 3.3 %all-to-all-done.6 = bf16[4,128,256]{2,1,0:T(8,128)(2,1)S(1)} async-done(((bf16[4,128,256]{2,1,0:T(8,128)(2,1)}), bf16[4,128,256]{2,1,0:T(8,128)(2,1)S(1)}, u32[]{:S(2)}, u32[]{:S(2)}) %all-to-all-start.6) | async-done | bytes 262176 | tf_op jit(solution)/shard_map/all_to_all | solution.py:30
  173.3 3.5 %all-to-all-start.4 = ((bf16[4,128,768]{1,2,0:T(8,128)(2,1)}), bf16[4,128,768]{1,2,0:T(8,128)(2,1)S(1)}, u32[]{:S(2)}, u32[]{:S(2)}) async-start(bf16[4,128,768]{1,2,0:T(8,128)(2,1)} %copy.223), calls=%async_computation.4 | async-start | bytes 1572864 | tf_op jit(solution)/shard_map/all_to_all | solution.py:30
  180.0 5.4 %all-to-all-done.4 = bf16[4,128,768]{1,2,0:T(8,128)(2,1)S(1)} async-done(((bf16[4,128,768]{1,2,0:T(8,128)(2,1)}), bf16[4,128,768]{1,2,0:T(8,128)(2,1)S(1)}, u32[]{:S(2)}, u32[]{:S(2)}) %all-to-all-start.4) | async-done | bytes 786464 | tf_op jit(solution)/shard_map/all_to_all | solution.py:30
  185.4 1.2 copy.241
  (283 shorter events, 36.3 us)
Async XLA Ops:
  0.6 18.8 %copy-start.35 = (bf16[1,128,3072]{2,1,0:T(8,128)(2,1)S(1)}, bf16[1,128,3072]{2,1,0:T(8,128)(2,1)}, u32[]{:S(2)}) copy-start(bf16[1,128,3072]{2,1,0:T(8,128)(2,1)} %param.16) | copy-start | bytes 2359300
  2.0 18.6 %all-to-all-start.1 = ((bf16[4,128,12]{1,2,0:T(8,128)(2,1)}), bf16[4,128,12]{1,2,0:T(8,128)(2,1)S(1)}, u32[]{:S(2)}, u32[]{:S(2)}) async-start(bf16[4,128,12]{1,2,0:T(8,128)(2,1)} %bitcast.2), calls=%async_computation.1 | async-start | bytes 32768 | tf_op jit(solution)/shard_map/all_to_all | solution.py:23
  8.1 12.6 %copy-start.68 = (f32[3,12]{1,0:T(4,128)}, f32[3,12]{1,0:T(4,128)S(1)}, u32[]{:S(2)}) copy-start(f32[3,12]{1,0:T(4,128)S(1)} %constant_dynamic-slice_fusion.4) | copy-start | bytes 436
  8.1 16.1 %copy-start.62 = (f32[12]{0:T(128)}, f32[12]{0:T(128)S(1)}, u32[]{:S(2)}) copy-start(f32[12]{0:T(128)S(1)} %get-tuple-element.506) | copy-start | bytes 148
  8.1 16.1 %copy-start.65 = (f32[12]{0:T(128)}, f32[12]{0:T(128)S(1)}, u32[]{:S(2)}) copy-start(f32[12]{0:T(128)S(1)} %get-tuple-element.507) | copy-start | bytes 148
  19.3 11.5 %copy-start.22 = (f32[2,256,256]{2,1,0:T(8,128)}, f32[2,256,256]{2,1,0:T(8,128)S(1)}, u32[]{:S(2)}) copy-start(f32[2,256,256]{2,1,0:T(8,128)S(1)} %fusion.82) | copy-start | bytes 1572868
  19.4 11.5 %copy-start.37 = (pred[256,256]{1,0:T(8,128)(4,1)}, pred[256,256]{1,0:T(8,128)(4,1)S(1)}, u32[]{:S(2)}) copy-start(pred[256,256]{1,0:T(8,128)(4,1)S(1)} %iota_compare_fusion) | copy-start | bytes 196612
  19.4 7.7 %copy-start.25 = (f32[2,256,128]{2,1,0:T(8,128)}, f32[2,256,128]{2,1,0:T(8,128)S(1)}, u32[]{:S(2)}) copy-start(f32[2,256,128]{2,1,0:T(8,128)S(1)} %convert_element_type.192) | copy-start | bytes 786436
  19.5 9.5 %copy-start.27 = (f32[2,256,128]{2,1,0:T(8,128)}, f32[2,256,128]{2,1,0:T(8,128)S(1)}, u32[]{:S(2)}) copy-start(f32[2,256,128]{2,1,0:T(8,128)S(1)} %convert_element_type.195) | copy-start | bytes 786436
  20.6 8.3 %copy-start.52 = (bf16[4,128,12]{1,2,0:T(8,128)(2,1)}, bf16[4,128,12]{1,2,0:T(8,128)(2,1)S(1)}, u32[]{:S(2)}) copy-start(bf16[4,128,12]{1,2,0:T(8,128)(2,1)S(1)} %all-to-all-done.1) | copy-start | bytes 36868
  20.7 12.9 %all-to-all-start = ((bf16[4,128,768]{1,2,0:T(8,128)(2,1)}), bf16[4,128,768]{1,2,0:T(8,128)(2,1)S(1)}, u32[]{:S(2)}, u32[]{:S(2)}) async-start(bf16[4,128,768]{1,2,0:T(8,128)(2,1)} %bitcast.1), calls=%async_computation | async-start | bytes 1572864 | tf_op jit(solution)/shard_map/all_to_all | solution.py:23
  24.3 14.6 %copy-start.43 = (f32[2,256,12]{1,2,0:T(8,128)}, f32[2,256,12]{1,2,0:T(8,128)S(1)}, u32[]{:S(2)}) copy-start(f32[2,256,12]{1,2,0:T(8,128)S(1)} %get-tuple-element.498) | copy-start | bytes 73732
  26.0 4.9 %copy-start.39 = (f32[2,12,2,128]{3,1,2,0:T(8,128)}, f32[2,12,2,128]{3,1,2,0:T(8,128)S(1)}, u32[]{:S(2)}) copy-start(f32[2,12,2,128]{3,1,2,0:T(8,128)S(1)} %reduce-window.24) | copy-start | bytes 73732
  26.8 4.0 %copy-start.41 = (f32[2,12,256]{2,0,1:T(2,128)}, f32[2,12,256]{2,0,1:T(2,128)S(1)}, u32[]{:S(2)}) copy-start(f32[2,12,256]{2,0,1:T(2,128)S(1)} %reduce_window_sum.55) | copy-start | bytes 73732
  27.1 3.7 %copy-start.45 = (f32[2,12,256]{2,1,0:T(8,128)}, f32[2,12,256]{2,1,0:T(8,128)S(1)}, u32[]{:S(2)}) copy-start(f32[2,12,256]{2,1,0:T(8,128)S(1)} %get-tuple-element.501) | copy-start | bytes 73732
  27.1 3.7 %copy-start.47 = (f32[2,12,256]{2,1,0:T(8,128)}, f32[2,12,256]{2,1,0:T(8,128)S(1)}, u32[]{:S(2)}) copy-start(f32[2,12,256]{2,1,0:T(8,128)S(1)} %get-tuple-element.502) | copy-start | bytes 73732
  27.1 3.8 %copy-start.33 = (f32[2,12,256]{2,1,0:T(8,128)}, f32[2,12,256]{2,1,0:T(8,128)S(1)}, u32[]{:S(2)}) copy-start(f32[2,12,256]{2,1,0:T(8,128)S(1)} %get-tuple-element.500) | copy-start | bytes 73732
  48.6 2.7 %copy-start.56 = (f32[2,12]{1,0:T(2,128)}, f32[2,12]{1,0:T(2,128)S(1)}, u32[]{:S(2)}) copy-start(f32[2,12]{1,0:T(2,128)S(1)} %get-tuple-element.705) | copy-start | bytes 292
  48.6 2.7 %copy-start.5 = (f32[2,256,12,64]{1,0,3,2:T(2,128)S(1)}, f32[2,256,12,64]{1,0,3,2:T(2,128)}, u32[]{:S(2)}) copy-start(f32[2,256,12,64]{1,0,3,2:T(2,128)} %copy-done.4) | copy-start | bytes 4718596
  48.8 2.5 %copy-start.19 = (bf16[2,12,128,64]{3,2,1,0:T(8,128)(2,1)}, bf16[2,12,128,64]{3,2,1,0:T(8,128)(2,1)S(1)}, u32[]{:S(2)}) copy-start(bf16[2,12,128,64]{3,2,1,0:T(8,128)(2,1)S(1)} %convert_element_type.194) | copy-start | bytes 1179652
  48.8 3.0 %copy-start.2 = (bf16[2,12,256,256]{3,2,1,0:T(8,128)(2,1)S(1)}, bf16[2,12,256,256]{3,2,1,0:T(8,128)(2,1)}, u32[]{:S(2)}) copy-start(bf16[2,12,256,256]{3,2,1,0:T(8,128)(2,1)} %multiply_convert_fusion) | copy-start | bytes 9437188
  48.8 3.1 %copy-start.8 = (bf16[2,256,12,64]{1,3,2,0:T(8,128)(2,1)S(1)}, bf16[2,256,12,64]{1,3,2,0:T(8,128)(2,1)}, u32[]{:S(2)}) copy-start(bf16[2,256,12,64]{1,3,2,0:T(8,128)(2,1)} %copy-done.7) | copy-start | bytes 2359300
  54.3 5.5 %copy-start.54 = (f32[3216]{0:T(1024)S(1)}, f32[3216]{0:T(1024)}, u32[]{:S(2)}) copy-start(f32[3216]{0:T(1024)} %param.23) | copy-start | bytes 38596
  55.3 4.6 %copy-start.36 = (bf16[1,128,3072]{2,1,0:T(8,128)(2,1)S(1)}, bf16[1,128,3072]{2,1,0:T(8,128)(2,1)}, u32[]{:S(2)}) copy-start(bf16[1,128,3072]{2,1,0:T(8,128)(2,1)} %param.17) | copy-start | bytes 2359300
  55.3 13.5 %all-to-all-start.2 = ((bf16[4,128,768]{1,2,0:T(8,128)(2,1)}), bf16[4,128,768]{1,2,0:T(8,128)(2,1)}, u32[]{:S(2)}, u32[]{:S(2)}) async-start(bf16[4,128,768]{1,2,0:T(8,128)(2,1)} %copy.214), calls=%async_computation.2 | async-start | bytes 1572864 | tf_op jit(solution)/shard_map/all_to_all | solution.py:30
  74.9 3.7 %copy-start.70 = (s32[8]{0:T(128)S(1)}, s32[8]{0:T(128)}, u32[]{:S(2)}) copy-start(s32[8]{0:T(128)} %param.26) | copy-start | bytes 100
  74.9 3.9 %copy-start.73 = (s32[8]{0:T(128)S(1)}, s32[8]{0:T(128)}, u32[]{:S(2)}) copy-start(s32[8]{0:T(128)} %param.27) | copy-start | bytes 100
  74.9 8.3 %copy-start.58 = (f32[1,804]{1,0:T(1,128)S(1)}, f32[1,804]{1,0:T(1,128)}, u32[]{:S(2)}) copy-start(f32[1,804]{1,0:T(1,128)} %param.25) | copy-start | bytes 9652
  74.9 8.4 %copy-start.60 = (f32[1,804]{1,0:T(1,128)S(1)}, f32[1,804]{1,0:T(1,128)}, u32[]{:S(2)}) copy-start(f32[1,804]{1,0:T(1,128)} %param.24) | copy-start | bytes 9652
  74.9 12.6 %all-to-all-start.3 = ((bf16[4,128,768]{1,2,0:T(8,128)(2,1)}), bf16[4,128,768]{1,2,0:T(8,128)(2,1)S(1)}, u32[]{:S(2)}, u32[]{:S(2)}) async-start(bf16[4,128,768]{1,2,0:T(8,128)(2,1)} %bitcast.153), calls=%async_computation.3 | async-start | bytes 1572864 | tf_op jit(solution)/shard_map/all_to_all | solution.py:23
  92.2 4.9 %copy-start = (bf16[2,256,12,64]{1,0,3,2:T(2,128)(2,1)}, bf16[2,256,12,64]{1,0,3,2:T(2,128)(2,1)S(1)}, u32[]{:S(2)}) copy-start(bf16[2,256,12,64]{1,0,3,2:T(2,128)(2,1)S(1)} %squeeze_broadcast_in_dim_reshape.2) | copy-start | bytes 2359300
  94.3 2.7 %copy-start.20 = (bf16[2,12,128,64]{3,2,1,0:T(8,128)(2,1)S(1)}, bf16[2,12,128,64]{3,2,1,0:T(8,128)(2,1)}, u32[]{:S(2)}) copy-start(bf16[2,12,128,64]{3,2,1,0:T(8,128)(2,1)} %copy-done.19) | copy-start | bytes 1179652
  108.9 3.8 %copy-start.69 = (f32[2,12]{1,0:T(2,128)}, f32[2,12]{1,0:T(2,128)S(1)}, u32[]{:S(2)}) copy-start(f32[2,12]{1,0:T(2,128)S(1)} %get-tuple-element.237) | copy-start | bytes 292
  108.9 3.8 %copy-start.10 = (bf16[2,256,12,64]{1,3,2,0:T(8,128)(2,1)S(1)}, bf16[2,256,12,64]{1,3,2,0:T(8,128)(2,1)}, u32[]{:S(2)}) copy-start(bf16[2,256,12,64]{1,3,2,0:T(8,128)(2,1)} %copy-done.7) | copy-start | bytes 2359300
  108.9 3.8 %copy-start.13 = (f32[2,12,128,64]{3,2,1,0:T(8,128)S(1)}, f32[2,12,128,64]{3,2,1,0:T(8,128)}, u32[]{:S(2)}) copy-start(f32[2,12,128,64]{3,2,1,0:T(8,128)} %get-tuple-element.236) | copy-start | bytes 2359300
  112.8 2.1 %copy-start.3 = (bf16[2,12,256,256]{3,2,1,0:T(8,128)(2,1)S(1)}, bf16[2,12,256,256]{3,2,1,0:T(8,128)(2,1)}, u32[]{:S(2)}) copy-start(bf16[2,12,256,256]{3,2,1,0:T(8,128)(2,1)} %multiply_convert_fusion) | copy-start | bytes 9437188
  118.3 4.6 %copy-start.21 = (bf16[2,12,256,128]{3,2,1,0:T(8,128)(2,1)S(1)}, bf16[2,12,256,128]{3,2,1,0:T(8,128)(2,1)}, u32[]{:S(2)}) copy-start(bf16[2,12,256,128]{3,2,1,0:T(8,128)(2,1)} %convolution_convert_fusion.2) | copy-start | bytes 4718596
  118.3 4.6 %copy-start.26 = (f32[2,256,128]{2,1,0:T(8,128)S(1)}, f32[2,256,128]{2,1,0:T(8,128)}, u32[]{:S(2)}) copy-start(f32[2,256,128]{2,1,0:T(8,128)} %copy-done.25) | copy-start | bytes 786436
  118.3 4.6 %copy-start.28 = (f32[2,256,128]{2,1,0:T(8,128)S(1)}, f32[2,256,128]{2,1,0:T(8,128)}, u32[]{:S(2)}) copy-start(f32[2,256,128]{2,1,0:T(8,128)} %copy-done.27) | copy-start | bytes 786436
  118.3 4.6 %copy-start.46 = (f32[2,12,256]{2,1,0:T(8,128)S(1)}, f32[2,12,256]{2,1,0:T(8,128)}, u32[]{:S(2)}) copy-start(f32[2,12,256]{2,1,0:T(8,128)} %copy-done.45) | copy-start | bytes 73732
  118.4 4.6 %copy-start.48 = (f32[2,12,256]{2,1,0:T(8,128)S(1)}, f32[2,12,256]{2,1,0:T(8,128)}, u32[]{:S(2)}) copy-start(f32[2,12,256]{2,1,0:T(8,128)} %copy-done.47) | copy-start | bytes 73732
  123.0 5.1 %copy-start.40 = (f32[2,12,2,128]{3,1,2,0:T(8,128)S(1)}, f32[2,12,2,128]{3,1,2,0:T(8,128)}, u32[]{:S(2)}) copy-start(f32[2,12,2,128]{3,1,2,0:T(8,128)} %copy-done.39) | copy-start | bytes 73732
  123.0 9.2 %copy-start.42 = (f32[2,12,256]{2,0,1:T(2,128)S(1)}, f32[2,12,256]{2,0,1:T(2,128)}, u32[]{:S(2)}) copy-start(f32[2,12,256]{2,0,1:T(2,128)} %copy-done.41) | copy-start | bytes 73732
  123.0 16.7 %copy-start.16 = (bf16[4,128,768]{1,2,0:T(8,128)(2,1)S(1)}, bf16[4,128,768]{1,2,0:T(8,128)(2,1)}, u32[]{:S(2)}) copy-start(bf16[4,128,768]{1,2,0:T(8,128)(2,1)} %copy-done.15) | copy-start | bytes 2359300
  123.0 16.7 %copy-start.18 = (bf16[4,128,768]{1,2,0:T(8,128)(2,1)S(1)}, bf16[4,128,768]{1,2,0:T(8,128)(2,1)}, u32[]{:S(2)}) copy-start(bf16[4,128,768]{1,2,0:T(8,128)(2,1)} %copy-done.17) | copy-start | bytes 2359300
  127.4 12.7 %copy-start.51 = (f32[2,256,12]{1,0,2:T(2,128)S(1)}, f32[2,256,12]{1,0,2:T(2,128)}, u32[]{:S(2)}) copy-start(f32[2,256,12]{1,0,2:T(2,128)} %copy-done.50) | copy-start | bytes 73732
  133.1 9.4 %copy-start.49 = (f32[2,3216]{1,0:T(2,128)S(1)}, f32[2,3216]{1,0:T(2,128)}, u32[]{:S(2)}) copy-start(f32[2,3216]{1,0:T(2,128)} %slice.90) | copy-start | bytes 77188
  139.7 4.3 %copy-start.59 = (f32[1,804]{1,0:T(1,128)S(1)}, f32[1,804]{1,0:T(1,128)}, u32[]{:S(2)}) copy-start(f32[1,804]{1,0:T(1,128)} %param.25) | copy-start | bytes 9652
  139.7 4.3 %copy-start.61 = (f32[1,804]{1,0:T(1,128)S(1)}, f32[1,804]{1,0:T(1,128)}, u32[]{:S(2)}) copy-start(f32[1,804]{1,0:T(1,128)} %param.24) | copy-start | bytes 9652
  140.0 6.4 %copy-start.24 = (bf16[1,128,3072]{1,2,0:T(8,128)(2,1)S(1)}, bf16[1,128,3072]{1,2,0:T(8,128)(2,1)}, u32[]{:S(2)}) copy-start(bf16[1,128,3072]{1,2,0:T(8,128)(2,1)} %get-tuple-element.489) | copy-start | bytes 2359300
  142.5 5.2 %collective-permute-start = (f32[3,3216]{1,0:T(4,128)S(1)}, f32[3,3216]{1,0:T(4,128)S(1)}, u32[]{:S(2)}, u32[]{:S(2)}) collective-permute-start(f32[3,3216]{1,0:T(4,128)S(1)} %pad_maximum_fusion.2), channel_id=1, source_target_pairs={{0,1},{1,0},{2,3},{3,2},{4,5},{5,4},{6,7},{7,6},{8,9},{9,8},{10,11... | collective-permute-start | bytes 115784 | tf_op jit(solution)/shard_map/ppermute | solution.py:45
  144.1 4.3 %copy-start.53 = (bf16[4,128,12]{1,2,0:T(8,128)(2,1)S(1)}, bf16[4,128,12]{1,2,0:T(8,128)(2,1)}, u32[]{:S(2)}) copy-start(bf16[4,128,12]{1,2,0:T(8,128)(2,1)} %copy-done.52) | copy-start | bytes 36868
  144.1 4.3 %copy-start.64 = (f32[12]{0:T(128)S(1)}, f32[12]{0:T(128)}, u32[]{:S(2)}) copy-start(f32[12]{0:T(128)} %copy-done.62) | copy-start | bytes 148
  144.1 4.3 %copy-start.67 = (f32[12]{0:T(128)S(1)}, f32[12]{0:T(128)}, u32[]{:S(2)}) copy-start(f32[12]{0:T(128)} %copy-done.65) | copy-start | bytes 148
  144.1 8.4 %copy-start.32 = (bf16[1,512,128]{2,1,0:T(8,128)(2,1)S(1)}, bf16[1,512,128]{2,1,0:T(8,128)(2,1)}, u32[]{:S(2)}) copy-start(bf16[1,512,128]{2,1,0:T(8,128)(2,1)} %copy-done.31) | copy-start | bytes 393220
  146.4 8.9 %copy-start.30 = (bf16[1,512,128]{2,1,0:T(8,128)(2,1)S(1)}, bf16[1,512,128]{2,1,0:T(8,128)(2,1)}, u32[]{:S(2)}) copy-start(bf16[1,512,128]{2,1,0:T(8,128)(2,1)} %copy-done.29) | copy-start | bytes 393220
  147.8 4.6 %collective-permute-start.1 = (f32[3,3216]{1,0:T(4,128)S(1)}, f32[3,3216]{1,0:T(4,128)S(1)}, u32[]{:S(2)}, u32[]{:S(2)}) collective-permute-start(f32[3,3216]{1,0:T(4,128)S(1)} %fusion.77), channel_id=1, source_target_pairs={{0,2},{1,3},{2,0},{3,1},{4,6},{5,7},{6,4},{7,5},{8,10},{9,11},{10,... | collective-permute-start | bytes 115784 | tf_op jit(solution)/shard_map/ppermute | solution.py:45
  149.1 14.5 %all-to-all-start.5 = ((bf16[4,128,12]{1,2,0:T(8,128)(2,1)}), bf16[4,128,12]{1,2,0:T(8,128)(2,1)S(1)}, u32[]{:S(2)}, u32[]{:S(2)}) async-start(bf16[4,128,12]{1,2,0:T(8,128)(2,1)} %fusion.47), calls=%async_computation.5 | async-start | bytes 32768 | tf_op jit(solution)/shard_map/all_to_all | solution.py:30
  152.4 1.3 collective-permute-start.2
  153.7 4.2 %collective-permute-start.3 = (f32[3,3216]{1,0:T(4,128)S(1)}, f32[3,3216]{1,0:T(4,128)S(1)}, u32[]{:S(2)}, u32[]{:S(2)}) collective-permute-start(f32[3,3216]{1,0:T(4,128)S(1)} %add.159), channel_id=1, source_target_pairs={{0,8},{4,12},{8,0},{12,4},{16,24},{20,28},{24,16},{28,20},{1,9},{5... | collective-permute-start | bytes 115784 | tf_op jit(solution)/shard_map/ppermute | solution.py:45
  157.9 10.6 %collective-permute-start.4 = (f32[3,3216]{1,0:T(4,128)S(1)}, f32[3,3216]{1,0:T(4,128)S(1)}, u32[]{:S(2)}, u32[]{:S(2)}) collective-permute-start(f32[3,3216]{1,0:T(4,128)S(1)} %add.160), channel_id=1, source_target_pairs={{0,16},{4,20},{8,24},{12,28},{16,0},{20,4},{24,8},{28,12},{1,17},{... | collective-permute-start | bytes 115784 | tf_op jit(solution)/shard_map/ppermute | solution.py:45
  163.6 15.0 %copy-start.55 = (f32[3216]{0:T(1024)S(1)}, f32[3216]{0:T(1024)}, u32[]{:S(2)}) copy-start(f32[3216]{0:T(1024)} %param.23) | copy-start | bytes 38596
  163.6 9.7 %all-to-all-start.6 = ((bf16[4,128,256]{2,1,0:T(8,128)(2,1)}), bf16[4,128,256]{2,1,0:T(8,128)(2,1)S(1)}, u32[]{:S(2)}, u32[]{:S(2)}) async-start(bf16[4,128,256]{2,1,0:T(8,128)(2,1)} %pad_maximum_fusion), calls=%async_computation.6 | async-start | bytes 524288 | tf_op jit(solution)/shard_map/all_to_all | solution.py:30
  173.3 12.1 %all-to-all-start.4 = ((bf16[4,128,768]{1,2,0:T(8,128)(2,1)}), bf16[4,128,768]{1,2,0:T(8,128)(2,1)S(1)}, u32[]{:S(2)}, u32[]{:S(2)}) async-start(bf16[4,128,768]{1,2,0:T(8,128)(2,1)} %copy.223), calls=%async_computation.4 | async-start | bytes 1572864 | tf_op jit(solution)/shard_map/all_to_all | solution.py:30
  (29 other events, 40.1 us)

commit v4 on v3

--- a/solution.py
+++ b/solution.py
@@ -138,18 +138,26 @@
     head_params = parameters[: 3 * heads_all].reshape(3, heads_all)
     gain = parameters[3 * heads_all :]
     local_params = lax.dynamic_slice_in_dim(head_params, first, group, 1)
-    bc_all = lax.all_gather(jnp.concatenate([b_input, c_input], axis=2), "ctx", axis=1, tiled=True)
-    b_all = bc_all[..., :state_size]
-    c_all = bc_all[..., state_size:]
+    width = hidden.shape[2] // groups
+    shared = jnp.concatenate([b_input[0], c_input[0]], axis=1)
+    packed = jnp.concatenate(
+        [
+            hidden[0].reshape(tokens, groups, width).transpose(1, 0, 2),
+            jnp.broadcast_to(shared[None], (groups,) + shared.shape),
+            dt_raw[0].reshape(tokens, groups, group).transpose(1, 0, 2),
+        ],
+        axis=2,
+    )
+    arrived = lax.all_to_all(packed, "ctx", 0, 0, tiled=True).reshape(groups * tokens, -1)
+    b_all = arrived[None, :, width : width + state_size]
+    c_all = arrived[None, :, width + state_size : width + 2 * state_size]
     seq_resets = resets[0]
 
     def local_fn(x_arg, dt_arg, b_arg, c_arg, a_arg, bias_arg, skip_arg):
         return ssd_group(x_arg, dt_arg, b_arg, c_arg, seq_resets, a_arg, bias_arg, skip_arg)
 
-    x_heads, dt_heads = (
-        to_heads(hidden, groups)[None],
-        to_heads(dt_raw, groups)[None],
-    )
+    x_heads = arrived[None, :, :width]
+    dt_heads = arrived[None, :, width + 2 * state_size :]
     y_heads, pullback = jax.vjp(
         local_fn,
         x_heads[0],
@@ -169,13 +177,12 @@
     )
     d_y_heads = to_heads(d_y, groups)[None]
     d_x, d_dt, d_b, d_c, d_alog, d_bias, d_skip = pullback(d_y_heads[0])
-    d_pair = jnp.concatenate([d_b, d_c], axis=-1)
-    grad_hidden, grad_dt, pair_parts = (
-        to_positions(d_x, groups),
-        to_positions(d_dt, groups),
-        from_heads(d_pair, groups),
-    )
-    pair_sum = jnp.sum(pair_parts.astype(jnp.float32), axis=0)[None].astype(jnp.bfloat16)
+    back = from_heads(jnp.concatenate([d_x, d_b, d_c, d_dt], axis=-1), groups)
+    grad_hidden = back[..., :width].transpose(1, 0, 2).reshape(1, tokens, groups * width)
+    grad_dt = back[..., width + 2 * state_size :].transpose(1, 0, 2).reshape(1, tokens, heads_all)
+    pair_sum = jnp.sum(
+        back[..., width : width + 2 * state_size].astype(jnp.float32), axis=0
+    )[None].astype(jnp.bfloat16)
     grad_b = pair_sum[..., :state_size]
     grad_c = pair_sum[..., state_size:]
     head_grads = jnp.stack([d_alog, d_bias, d_skip])

time: 188 us -> 182 us (0.968)
  waiting for transfers between devices: 21.8 us -> 35.7 us
  starting transfers between devices: 34.4 us -> 24.8 us
  blocking collectives: 9.49 us -> 0 us
  local copies, waits for them, and re-layouts: 47.1 us -> 51.1 us
  other arithmetic: 49.9 us -> 47.5 us
  matrix products: 19.3 us -> 17.3 us
    all_to_all x0 -> x1, waiting for transfers between devices: none -> 13.5 us  [on_device(): lax.all_to_all(packed, 'ctx', 0, 0, tiled=True).reshape(groups * tokens, -1)]
    all_gather x1 -> x0, blocking collectives: 9.49 us -> none  [on_device(): lax.all_gather(jnp.concatenate([b_input, c_input], axis=2), 'ctx', axis=1...]
    all_to_all x3 -> x1, starting transfers between devices: 12.3 us -> 3.64 us  [to_heads(): x = lax.all_to_all(x, 'ctx', 0, 0, tiled=True)]
    all_to_all x4 -> x2, starting transfers between devices: 15.5 us -> 8.16 us  [from_heads(): return lax.all_to_all(x, 'ctx', 0, 0, tiled=True)]
    convert_element_type x5 -> x1, local copies, waits for them, and re-layouts: 6.71 us -> 0.81 us  [ssd_group(): inputs = hidden.astype(jnp.float32).reshape(blocks, SPAN, heads, width)]
    all_to_all x0 -> x1, starting transfers between devices: none -> 5.32 us  [on_device(): lax.all_to_all(packed, 'ctx', 0, 0, tiled=True).reshape(groups * tokens, -1)]
    all_to_all x0 -> x1, local copies, waits for them, and re-layouts: none -> 3.84 us  [on_device(): lax.all_to_all(packed, 'ctx', 0, 0, tiled=True).reshape(groups * tokens, -1)]
    unnamed x148 -> x143, local copies, waits for them, and re-layouts: 15.9 us -> 19 us
  transfers between devices with their start and end apart: 12 -> 9, of which waited for: 6 -> 7; matrix products, arithmetic and copies ran while one was open for 16% -> 9% of each run, Pallas kernels for 0% -> 0%
where the time goes in v4:
time: 182 us; the launch traced here: 181 us
  local copies, waits for them, and re-layouts  51.1 us (28%)
  other arithmetic  47.5 us (26%)
  waiting for transfers between devices  35.7 us (20%)
  starting transfers between devices  24.8 us (14%)
  matrix products  17.3 us (10%)
  between operations  4.48 us (2%)
    unnamed x143, local copies, waits for them, and re-layouts  19 us
    all_to_all x1, waiting for transfers between devices, on_device(): lax.all_to_all(packed, 'ctx', 0, 0, tiled=True).reshape(groups * tokens, -1)  13.5 us
    all_to_all x2, waiting for transfers between devices, from_heads(): return lax.all_to_all(x, 'ctx', 0, 0, tiled=True)  12.8 us
    all_to_all x2, starting transfers between devices, from_heads(): return lax.all_to_all(x, 'ctx', 0, 0, tiled=True)  8.16 us
    ppermute x5, starting transfers between devices, tree_sum(): x = x + lax.ppermute(x, axis, [(i, i ^ step) for i in range(size)])  7.63 us
    dot_general x3, matrix products, ssd_group(): jnp.einsum('chsn,cshp->chnp', b_decayed, scaled, precision=highest)  7.26 us
    another operation x9, other arithmetic  6.86 us
    convert_element_type x6, other arithmetic, rounded(): value.astype(jnp.bfloat16)  5.86 us
  transfers between devices with their start and end apart: 9, of which 7 were waited for; matrix products, arithmetic and copies ran while one was open for 9% of the time, Pallas kernels for 0%

profile of v4, /device:TPU:0, one launch (start us, length us, event | category | flops | bytes accessed | tf_op | source)
XLA Modules:
  0.0 181.0 jit_solution(1360655912477165652)
XLA Ops:
  2.3 1.5 copy.215
  3.8 1.1 pad_maximum_fusion
  4.9 5.3 %all-to-all-start = ((bf16[4,128,1036]{1,2,0:T(8,128)(2,1)}), bf16[4,128,1036]{1,2,0:T(8,128)(2,1)S(1)}, u32[]{:S(2)}, u32[]{:S(2)}) async-start(bf16[4,128,1036]{1,2,0:T(8,128)(2,1)} %pad_maximum_fusion), calls=%async_computation | async-start | bytes 2129920 | tf_op jit(solution)/shard_map/all_to_all | solution.py:151
  10.5 13.5 %all-to-all-done = bf16[4,128,1036]{1,2,0:T(8,128)(2,1)S(1)} async-done(((bf16[4,128,1036]{1,2,0:T(8,128)(2,1)}), bf16[4,128,1036]{1,2,0:T(8,128)(2,1)S(1)}, u32[]{:S(2)}, u32[]{:S(2)}) %all-to-all-start) | async-done | bytes 1060896 | tf_op jit(solution)/shard_map/all_to_all | solution.py:151
  24.0 3.8 %copy.314 = bf16[4,128,1036]{1,0,2:T(4,128)(2,1)S(1)} copy(bf16[4,128,1036]{1,2,0:T(8,128)(2,1)S(1)} %all-to-all-done) | data formatting | bytes 2121728 | tf_op jit(solution)/shard_map/all_to_all | solution.py:151
  28.6 1.5 slice_convert_fusion
  30.3 1.2 reduce-window.24
  33.8 1.9 %multiply_convert_fusion.2 = bf16[2,12,256,128]{3,2,1,0:T(8,128)(2,1)} fusion(f32[2,12,256]{2,1,0:T(8,128)S(1)} %get-tuple-element.502, f32[2,256,128]{2,1,0:T(8,128)S(1)} %bitcast_convert_fusion), kind=kLoop, calls=%fused_computation.36 | loop fusion | flops 1572864 | bytes 1859584 | tf_op jit(solution)/shard_map/jvp()/convert_element_type | solution.py:51
  35.7 2.3 %reshape.326 = f32[2,256,12,64]{1,0,3,2:T(2,128)S(1)} reshape(f32[512,768]{0,1:T(8,128)} %slice_convert_fusion) | data formatting | bytes 3145728 | tf_op jit(solution)/shard_map/jvp()/reshape | solution.py:62
  39.1 0.9 copy-done.12
  40.0 1.8 fusion.75
  42.0 5.7 %while.36 = (s32[]{:T(128)}, f32[12,128,64]{2,1,0:T(8,128)S(1)}, f32[2,12,128,64]{3,2,1,0:T(8,128)S(1)}, f32[2,12]{1,0:T(2,128)S(1)}, f32[2,12,1,1]{1,3,2,0:T(1,...) while((s32[]{:T(128)}, f32[12,128,64]{2,1,0:T(8,128)S(1)}, ...), condition=%wide.region_3.4_spmd.clone, body=%wide.region_2.3_spmd.clone.sunk | while | flops 589827 | bytes 5900104 | solution.py:83
  48.0 1.0 multiply_convert_fusion.1
  49.3 1.7 multiply_convert_fusion
  51.7 0.9 copy-done.2
  52.6 0.9 copy-done.5
  53.8 1.1 fusion.33
  56.2 1.0 copy.233
  57.1 4.5 %all-to-all-start.1 = ((bf16[4,128,768]{1,2,0:T(8,128)(2,1)}), bf16[4,128,768]{1,2,0:T(8,128)(2,1)}, u32[]{:S(2)}, u32[]{:S(2)}) async-start(bf16[4,128,768]{1,2,0:T(8,128)(2,1)} %copy.233), calls=%async_computation.1 | async-start | bytes 1572864 | tf_op jit(solution)/shard_map/all_to_all | solution.py:30
  62.1 1.5 copy.235
  63.6 8.2 %all-to-all-done.1 = bf16[4,128,768]{1,2,0:T(8,128)(2,1)} async-done(((bf16[4,128,768]{1,2,0:T(8,128)(2,1)}), bf16[4,128,768]{1,2,0:T(8,128)(2,1)}, u32[]{:S(2)}, u32[]{:S(2)}) %all-to-all-start.1) | async-done | bytes 786464 | tf_op jit(solution)/shard_map/all_to_all | solution.py:30
  71.9 1.2 convert_element_type.194
  73.7 1.5 fusion.21
  75.2 2.6 %fusion.30 = (bf16[1,128,3072]{1,2,0:T(8,128)(2,1)}, bf16[1,128,3072]{1,2,0:T(8,128)(2,1)}, bf16[1,128,3072]{1,2,0:T(8,128)(2,1)}) fusion(bf16[1,128,3072]{1,2,0:T(8,128)(2,1)S(1)} %copy.234, f32[1,128,3072]{1,2,0:T(8,128)S(1)} %get-tuple-element.486, bf16[1,128,3072]{1,2,0:T(8,128)(2,1)S(1)} %copy.235, f32[128]{0:T(128)S(1)} %fusion.66, ...), kind=kLoop, calls=%fused_computation.61 | loop fusion | flops 8650752 | bytes 7091200 | tf_op jit(solution)/shard_map/convert_element_type | solution.py:111
  77.9 3.6 %all-to-all-start.2 = ((bf16[4,128,768]{1,2,0:T(8,128)(2,1)}), bf16[4,128,768]{1,2,0:T(8,128)(2,1)S(1)}, u32[]{:S(2)}, u32[]{:S(2)}) async-start(bf16[4,128,768]{1,2,0:T(8,128)(2,1)} %bitcast.198), calls=%async_computation.2 | async-start | bytes 1572864 | tf_op jit(solution)/shard_map/all_to_all | solution.py:23
  82.4 1.3 fusion.64
  87.2 4.6 %all-to-all-done.2 = bf16[4,128,768]{1,2,0:T(8,128)(2,1)S(1)} async-done(((bf16[4,128,768]{1,2,0:T(8,128)(2,1)}), bf16[4,128,768]{1,2,0:T(8,128)(2,1)S(1)}, u32[]{:S(2)}, u32[]{:S(2)}) %all-to-all-start.2) | async-done | bytes 786464 | tf_op jit(solution)/shard_map/all_to_all | solution.py:23
  91.8 0.9 copy-done.18
  92.7 1.5 copy.236
  94.2 2.3 %squeeze_broadcast_in_dim_reshape.3 = bf16[2,256,12,64]{1,0,3,2:T(2,128)(2,1)S(1)} reshape(bf16[4,128,768]{1,0,2:T(4,128)(2,1)} %copy.236) | data formatting | bytes 1572864 | tf_op jit(solution)/shard_map/squeeze;broadcast_in_dim;reshape | solution.py:179
  96.5 2.1 %convolution_convert_fusion.3 = bf16[2,12,128,64]{2,3,1,0:T(8,128)(2,1)S(1)} fusion(bf16[2,12,256,128]{3,2,1,0:T(8,128)(2,1)} %copy-done.13, bf16[2,256,12,64]{1,0,3,2:T(2,128)(2,1)S(1)} %squeeze_broadcast_in_dim_reshape.3), kind=kOutput, calls=%fused_computation.76 | convolution fusion | flops 100859904 | bytes 2752512 | tf_op jit(solution)/shard_map/transpose(jvp(chtn,chnp->cthp))/dot_general | solution.py:85
  98.7 2.7 %convolution_convert_fusion = bf16[2,12,256,256]{3,2,1,0:T(8,128)(2,1)} fusion(bf16[2,256,12,64]{1,3,2,0:T(8,128)(2,1)S(1)} %copy-done.9, bf16[2,256,12,64]{1,0,3,2:T(2,128)(2,1)S(1)} %squeeze_broadcast_in_dim_reshape.3), kind=kOutput, calls=%fused_computation.40 | convolution fusion | flops 202899456 | bytes 4718592 | tf_op jit(solution)/shard_map/transpose(jvp(chts,cshp->cthp))/dot_general | solution.py:71
  101.4 1.0 convert_element_type.171
  102.9 1.3 broadcast.99
  104.2 8.9 %while.37 = (s32[]{:T(128)}, f32[12,128,64]{2,1,0:T(8,128)S(1)}, f32[2,12]{1,0:T(2,128)}, f32[2,12,128,64]{3,2,1,0:T(8,128)}, f32[2,12,128,64]{2,3,1,0:T(8,128)}...) while((s32[]{:T(128)}, f32[12,128,64]{2,1,0:T(8,128)S(1)}, ...), condition=%wide.region_8.9_spmd.clone, body=%wide.region_6.8_spmd.clone.sunk | while | flops 688132 | bytes 4327756 | solution.py:83
  104.3 1.0 bitcast_dynamic-update-slice_fusion.5
  105.8 1.0 constant_dynamic-slice_fusion.6
  107.1 0.9 fusion.102
  108.7 0.9 bitcast_dynamic-update-slice_fusion.5
  110.2 1.0 constant_dynamic-slice_fusion.6
  111.6 0.9 fusion.102
  113.1 3.8 %fusion.77 = f32[2,12,64,256]{3,2,1,0:T(8,128)S(1)} fusion(f32[2,12,128,64]{3,2,1,0:T(8,128)} %get-tuple-element.236, bf16[2,12,256,128]{3,2,1,0:T(8,128)(2,1)} %multiply_convert_fusion.2), kind=kOutput, calls=%fused_computation.172 | convolution fusion | flops 603979776 | bytes 3932160 | tf_op jit(solution)/shard_map/transpose(jvp(chsn,cshp->chnp))/dot_general | solution.py:74
  116.9 1.7 convolution_convert_fusion.2
  119.3 1.2 copy-done.3
  122.7 1.2 copy-done.15
  124.0 3.9 %fusion.11 = (f32[2,12,256]{2,1,0:T(8,128)S(1)}, f32[2,12,256]{2,1,0:T(8,128)S(1)}, f32[2,256,256]{2,1,0:T(8,128)S(1)}) fusion(bf16[2,12,256,256]{3,2,1,0:T(8,128)(2,1)S(1)} %copy-done.15, f32[2,12,256]{2,1,0:T(8,128)S(1)} %copy-done.36, f32[2,256,256]{2,1,0:T(8,128)S(1)} %copy-done.23, pred[256,256]{1,0:T(8,128)(4,1)S(1)} %copy-done.39), kind=kLoop, calls=%fused_computation.26 | loop fusion | flops 18731008 | bytes 4333568 | tf_op jit(solution)/shard_map/transpose(jvp())/reduce_sum | solution.py:68
  128.0 4.6 %fusion.12 = (f32[2,256,128]{2,1,0:T(8,128)}, f32[2,12,256]{2,1,0:T(8,128)S(1)}, f32[2,12,256]{2,1,0:T(8,128)S(1)}, f32[2,256,128]{2,1,0:T(8,128)}) fusion(bf16[2,12,256,128]{3,2,1,0:T(8,128)(2,1)S(1)} %convolution_convert_fusion.2, f32[2,12,256]{2,1,0:T(8,128)S(1)} %copy-done.47, f32[2,256,128]{2,1,0:T(8,128)S(1)} %copy-done.27, ...), kind=kLoop, calls=%fused_computation.31 | loop fusion | flops 7720960 | bytes 4292608 | tf_op jit(solution)/shard_map/transpose(jvp())/reduce_sum | solution.py:73
  133.2 0.9 fusion.48
  134.8 1.3 copy.247
  137.1 5.2 %reduce-window.31 = f32[2,12,2,128]{3,1,2,0:T(8,128)S(1)} reduce-window(f32[2,12,2,128]{3,1,2,0:T(8,128)S(1)} %copy.252, f32[]{:T(128)} %constant.126.clone.1), window={size=1x1x1x128 pad=0_0x0_0x0_0x0_127}, to_apply=%region_18.19 | reduce-window | flops 780288 | bytes 49156 | tf_op jit(solution)/shard_map/reduce-window.2
  143.0 0.9 fusion.69
  145.8 1.6 collective-permute-start
  147.4 2.6 %collective-permute-done = f32[3,3216]{1,0:T(4,128)S(1)} collective-permute-done((f32[3,3216]{1,0:T(4,128)S(1)}, f32[3,3216]{1,0:T(4,128)S(1)}, u32[]{:S(2)}, u32[]{:S(2)}) %collective-permute-start) | collective-permute-done | bytes 38624 | tf_op jit(solution)/shard_map/ppermute | solution.py:45
  150.0 1.6 collective-permute-start.1
  151.6 1.3 fusion.36
  153.0 1.2 collective-permute-done.1
  156.3 1.7 collective-permute-start.3
  158.4 1.1 copy.256
  159.6 3.7 %all-to-all-start.3 = ((bf16[4,128,1036]{1,2,0:T(8,128)(2,1)}), bf16[4,128,1036]{1,2,0:T(8,128)(2,1)S(1)}, u32[]{:S(2)}, u32[]{:S(2)}) async-start(bf16[4,128,1036]{1,2,0:T(8,128)(2,1)} %copy.256), calls=%async_computation.3 | async-start | bytes 2129920 | tf_op jit(solution)/shard_map/all_to_all | solution.py:30
  163.3 2.6 %collective-permute-start.4 = (f32[3,3216]{1,0:T(4,128)S(1)}, f32[3,3216]{1,0:T(4,128)S(1)}, u32[]{:S(2)}, u32[]{:S(2)}) collective-permute-start(f32[3,3216]{1,0:T(4,128)S(1)} %add.135), channel_id=1, source_target_pairs={{0,16},{4,20},{8,24},{12,28},{16,0},{20,4},{24,8},{28,12},{1,17},{... | collective-permute-start | bytes 115784 | tf_op jit(solution)/shard_map/ppermute | solution.py:45
  166.0 1.2 copy.259
  167.1 1.2 copy.261
  173.1 4.6 %all-to-all-done.3 = bf16[4,128,1036]{1,2,0:T(8,128)(2,1)S(1)} async-done(((bf16[4,128,1036]{1,2,0:T(8,128)(2,1)}), bf16[4,128,1036]{1,2,0:T(8,128)(2,1)S(1)}, u32[]{:S(2)}, u32[]{:S(2)}) %all-to-all-start.3) | async-done | bytes 1060896 | tf_op jit(solution)/shard_map/all_to_all | solution.py:30
  177.7 1.2 copy.260
  (287 shorter events, 38.0 us)
Async XLA Ops:
  4.9 5.3 %slice-start = ((f32[3216]{0:T(1024)}), f32[144]{0:T(256)S(1)}, s32[]{:S(2)}) async-start(f32[3216]{0:T(1024)} %param.23), calls=%async_computation.4 | async-start | bytes 2048 | tf_op jit(solution)/shard_map/slice | solution.py:138
  4.9 5.5 %copy-start.67 = (s32[1,2]{1,0:T(1,128)S(1)}, s32[1,2]{1,0:T(1,128)}, u32[]{:S(2)}) copy-start(s32[1,2]{1,0:T(1,128)} %param.21) | copy-start | bytes 28
  4.9 19.1 %all-to-all-start = ((bf16[4,128,1036]{1,2,0:T(8,128)(2,1)}), bf16[4,128,1036]{1,2,0:T(8,128)(2,1)S(1)}, u32[]{:S(2)}, u32[]{:S(2)}) async-start(bf16[4,128,1036]{1,2,0:T(8,128)(2,1)} %pad_maximum_fusion), calls=%async_computation | async-start | bytes 2129920 | tf_op jit(solution)/shard_map/all_to_all | solution.py:151
  10.4 18.0 %copy-start.59 = (f32[3,12]{1,0:T(4,128)}, f32[3,12]{1,0:T(4,128)S(1)}, u32[]{:S(2)}) copy-start(f32[3,12]{1,0:T(4,128)S(1)} %constant_dynamic-slice_fusion.4) | copy-start | bytes 436
  10.4 38.9 %copy-start.38 = (pred[256,256]{1,0:T(8,128)(4,1)}, pred[256,256]{1,0:T(8,128)(4,1)S(1)}, u32[]{:S(2)}) copy-start(pred[256,256]{1,0:T(8,128)(4,1)S(1)} %iota_compare_fusion) | copy-start | bytes 196612
  10.4 19.6 %copy-start.60 = (f32[12]{0:T(128)}, f32[12]{0:T(128)S(1)}, u32[]{:S(2)}) copy-start(f32[12]{0:T(128)S(1)} %get-tuple-element.507) | copy-start | bytes 148
  10.5 19.6 %copy-start.61 = (f32[12]{0:T(128)}, f32[12]{0:T(128)S(1)}, u32[]{:S(2)}) copy-start(f32[12]{0:T(128)S(1)} %get-tuple-element.508) | copy-start | bytes 148
  32.9 15.1 %copy-start.48 = (f32[2,12,256]{2,1,0:T(8,128)}, f32[2,12,256]{2,1,0:T(8,128)S(1)}, u32[]{:S(2)}) copy-start(f32[2,12,256]{2,1,0:T(8,128)S(1)} %get-tuple-element.503) | copy-start | bytes 73732
  32.9 16.3 %copy-start.35 = (f32[2,12,256]{2,1,0:T(8,128)}, f32[2,12,256]{2,1,0:T(8,128)S(1)}, u32[]{:S(2)}) copy-start(f32[2,12,256]{2,1,0:T(8,128)S(1)} %get-tuple-element.501) | copy-start | bytes 73732
  33.1 15.9 %copy-start.30 = (bf16[512,128]{1,0:T(8,128)(2,1)}, bf16[512,128]{1,0:T(8,128)(2,1)S(1)}, u32[]{:S(2)}) copy-start(bf16[512,128]{1,0:T(8,128)(2,1)S(1)} %copy.221) | copy-start | bytes 393220
  38.0 2.0 %copy-start.12 = (bf16[2,12,256,128]{3,2,1,0:T(8,128)(2,1)S(1)}, bf16[2,12,256,128]{3,2,1,0:T(8,128)(2,1)}, u32[]{:S(2)}) copy-start(bf16[2,12,256,128]{3,2,1,0:T(8,128)(2,1)} %multiply_convert_fusion.2) | copy-start | bytes 4718596
  38.1 3.7 %copy-start.44 = (f32[2,256,12]{1,2,0:T(8,128)}, f32[2,256,12]{1,2,0:T(8,128)S(1)}, u32[]{:S(2)}) copy-start(f32[2,256,12]{1,2,0:T(8,128)S(1)} %copy.218) | copy-start | bytes 73732
  40.0 1.8 copy-start.7
  47.8 3.1 %copy-start.20 = (bf16[2,12,128,64]{3,2,1,0:T(8,128)(2,1)}, bf16[2,12,128,64]{3,2,1,0:T(8,128)(2,1)S(1)}, u32[]{:S(2)}) copy-start(bf16[2,12,128,64]{3,2,1,0:T(8,128)(2,1)S(1)} %convert_element_type.158) | copy-start | bytes 1179652
  48.0 3.0 %copy-start.32 = (bf16[512,128]{1,0:T(8,128)(2,1)}, bf16[512,128]{1,0:T(8,128)(2,1)S(1)}, u32[]{:S(2)}) copy-start(bf16[512,128]{1,0:T(8,128)(2,1)S(1)} %copy.220) | copy-start | bytes 393220
  49.0 2.0 %copy-start.13 = (bf16[2,12,256,128]{3,2,1,0:T(8,128)(2,1)}, bf16[2,12,256,128]{3,2,1,0:T(8,128)(2,1)S(1)}, u32[]{:S(2)}) copy-start(bf16[2,12,256,128]{3,2,1,0:T(8,128)(2,1)S(1)} %multiply_convert_fusion.1) | copy-start | bytes 4718596
  49.3 1.7 copy-start.22
  51.0 1.6 copy-start.2
  51.0 2.5 %copy-start.5 = (f32[2,256,12,64]{1,0,3,2:T(2,128)S(1)}, f32[2,256,12,64]{1,0,3,2:T(2,128)}, u32[]{:S(2)}) copy-start(f32[2,256,12,64]{1,0,3,2:T(2,128)} %copy-done.4) | copy-start | bytes 4718596
  51.0 2.7 %copy-start.8 = (bf16[2,256,12,64]{1,3,2,0:T(8,128)(2,1)S(1)}, bf16[2,256,12,64]{1,3,2,0:T(8,128)(2,1)}, u32[]{:S(2)}) copy-start(bf16[2,256,12,64]{1,3,2,0:T(8,128)(2,1)} %copy-done.7) | copy-start | bytes 2359300
  56.1 5.5 %copy-start.51 = (f32[3216]{0:T(1024)S(1)}, f32[3216]{0:T(1024)}, u32[]{:S(2)}) copy-start(f32[3216]{0:T(1024)} %param.23) | copy-start | bytes 38596
  57.1 4.6 %copy-start.37 = (bf16[1,128,3072]{2,1,0:T(8,128)(2,1)S(1)}, bf16[1,128,3072]{2,1,0:T(8,128)(2,1)}, u32[]{:S(2)}) copy-start(bf16[1,128,3072]{2,1,0:T(8,128)(2,1)} %param.17) | copy-start | bytes 2359300
  57.1 14.7 %all-to-all-start.1 = ((bf16[4,128,768]{1,2,0:T(8,128)(2,1)}), bf16[4,128,768]{1,2,0:T(8,128)(2,1)}, u32[]{:S(2)}, u32[]{:S(2)}) async-start(bf16[4,128,768]{1,2,0:T(8,128)(2,1)} %copy.233), calls=%async_computation.1 | async-start | bytes 1572864 | tf_op jit(solution)/shard_map/all_to_all | solution.py:30
  77.9 3.7 %copy-start.64 = (s32[8]{0:T(128)S(1)}, s32[8]{0:T(128)}, u32[]{:S(2)}) copy-start(s32[8]{0:T(128)} %param.26) | copy-start | bytes 100
  77.9 3.9 %copy-start.68 = (s32[8]{0:T(128)S(1)}, s32[8]{0:T(128)}, u32[]{:S(2)}) copy-start(s32[8]{0:T(128)} %param.27) | copy-start | bytes 100
  77.9 8.2 %copy-start.55 = (f32[1,804]{1,0:T(1,128)S(1)}, f32[1,804]{1,0:T(1,128)}, u32[]{:S(2)}) copy-start(f32[1,804]{1,0:T(1,128)} %param.25) | copy-start | bytes 9652
  77.9 8.2 %copy-start.57 = (f32[1,804]{1,0:T(1,128)S(1)}, f32[1,804]{1,0:T(1,128)}, u32[]{:S(2)}) copy-start(f32[1,804]{1,0:T(1,128)} %param.24) | copy-start | bytes 9652
  77.9 14.0 %all-to-all-start.2 = ((bf16[4,128,768]{1,2,0:T(8,128)(2,1)}), bf16[4,128,768]{1,2,0:T(8,128)(2,1)S(1)}, u32[]{:S(2)}, u32[]{:S(2)}) async-start(bf16[4,128,768]{1,2,0:T(8,128)(2,1)} %bitcast.198), calls=%async_computation.2 | async-start | bytes 1572864 | tf_op jit(solution)/shard_map/all_to_all | solution.py:23
  96.5 4.9 %copy-start = (bf16[2,256,12,64]{1,0,3,2:T(2,128)(2,1)}, bf16[2,256,12,64]{1,0,3,2:T(2,128)(2,1)S(1)}, u32[]{:S(2)}) copy-start(bf16[2,256,12,64]{1,0,3,2:T(2,128)(2,1)S(1)} %squeeze_broadcast_in_dim_reshape.3) | copy-start | bytes 2359300
  96.5 2.1 %copy-start.9 = (bf16[2,256,12,64]{1,3,2,0:T(8,128)(2,1)S(1)}, bf16[2,256,12,64]{1,3,2,0:T(8,128)(2,1)}, u32[]{:S(2)}) copy-start(bf16[2,256,12,64]{1,3,2,0:T(8,128)(2,1)} %copy-done.7) | copy-start | bytes 2359300
  104.3 1.6 copy-start.69
  113.1 3.8 %copy-start.10 = (bf16[2,256,12,64]{1,3,2,0:T(8,128)(2,1)S(1)}, bf16[2,256,12,64]{1,3,2,0:T(8,128)(2,1)}, u32[]{:S(2)}) copy-start(bf16[2,256,12,64]{1,3,2,0:T(8,128)(2,1)} %copy-done.7) | copy-start | bytes 2359300
  113.1 3.8 %copy-start.14 = (f32[2,12,128,64]{3,2,1,0:T(8,128)S(1)}, f32[2,12,128,64]{3,2,1,0:T(8,128)}, u32[]{:S(2)}) copy-start(f32[2,12,128,64]{3,2,1,0:T(8,128)} %get-tuple-element.236) | copy-start | bytes 2359300
  116.9 1.7 copy-start.1
  116.9 1.7 copy-start.21
  118.7 1.9 %copy-start.3 = (bf16[2,12,256,256]{3,2,1,0:T(8,128)(2,1)S(1)}, bf16[2,12,256,256]{3,2,1,0:T(8,128)(2,1)}, u32[]{:S(2)}) copy-start(bf16[2,12,256,256]{3,2,1,0:T(8,128)(2,1)} %copy-done.2) | copy-start | bytes 9437188
  122.0 1.9 %copy-start.15 = (bf16[2,12,256,256]{3,2,1,0:T(8,128)(2,1)S(1)}, bf16[2,12,256,256]{3,2,1,0:T(8,128)(2,1)}, u32[]{:S(2)}) copy-start(bf16[2,12,256,256]{3,2,1,0:T(8,128)(2,1)} %convolution_convert_fusion) | copy-start | bytes 9437188
  122.0 2.0 %copy-start.23 = (f32[2,256,256]{2,1,0:T(8,128)S(1)}, f32[2,256,256]{2,1,0:T(8,128)}, u32[]{:S(2)}) copy-start(f32[2,256,256]{2,1,0:T(8,128)} %copy-done.22) | copy-start | bytes 1572868
  122.0 2.0 %copy-start.36 = (f32[2,12,256]{2,1,0:T(8,128)S(1)}, f32[2,12,256]{2,1,0:T(8,128)}, u32[]{:S(2)}) copy-start(f32[2,12,256]{2,1,0:T(8,128)} %copy-done.35) | copy-start | bytes 73732
  122.0 2.0 %copy-start.39 = (pred[256,256]{1,0:T(8,128)(4,1)S(1)}, pred[256,256]{1,0:T(8,128)(4,1)}, u32[]{:S(2)}) copy-start(pred[256,256]{1,0:T(8,128)(4,1)} %copy-done.38) | copy-start | bytes 196612
  124.0 4.0 %copy-start.27 = (f32[2,256,128]{2,1,0:T(8,128)S(1)}, f32[2,256,128]{2,1,0:T(8,128)}, u32[]{:S(2)}) copy-start(f32[2,256,128]{2,1,0:T(8,128)} %copy-done.26) | copy-start | bytes 786436
  124.0 4.0 %copy-start.29 = (f32[2,256,128]{2,1,0:T(8,128)S(1)}, f32[2,256,128]{2,1,0:T(8,128)}, u32[]{:S(2)}) copy-start(f32[2,256,128]{2,1,0:T(8,128)} %copy-done.28) | copy-start | bytes 786436
  124.0 4.0 %copy-start.47 = (f32[2,12,256]{2,1,0:T(8,128)S(1)}, f32[2,12,256]{2,1,0:T(8,128)}, u32[]{:S(2)}) copy-start(f32[2,12,256]{2,1,0:T(8,128)} %copy-done.46) | copy-start | bytes 73732
  124.0 4.0 %copy-start.49 = (f32[2,12,256]{2,1,0:T(8,128)S(1)}, f32[2,12,256]{2,1,0:T(8,128)}, u32[]{:S(2)}) copy-start(f32[2,12,256]{2,1,0:T(8,128)} %copy-done.48) | copy-start | bytes 73732
  128.0 5.2 %copy-start.41 = (f32[2,12,2,128]{3,1,2,0:T(8,128)S(1)}, f32[2,12,2,128]{3,1,2,0:T(8,128)}, u32[]{:S(2)}) copy-start(f32[2,12,2,128]{3,1,2,0:T(8,128)} %copy-done.40) | copy-start | bytes 73732
  128.0 5.2 %copy-start.54 = (f32[2,12,2]{1,2,0:T(2,128)S(1)}, f32[2,12,2]{1,2,0:T(2,128)}, u32[]{:S(2)}) copy-start(f32[2,12,2]{1,2,0:T(2,128)} %copy-done.53) | copy-start | bytes 580
  128.0 8.2 %copy-start.43 = (f32[2,12,256]{2,0,1:T(2,128)S(1)}, f32[2,12,256]{2,0,1:T(2,128)}, u32[]{:S(2)}) copy-start(f32[2,12,256]{2,0,1:T(2,128)} %copy-done.42) | copy-start | bytes 73732
  128.0 14.6 %copy-start.17 = (bf16[130,8,4,128]{3,1,2,0:T(8,128)(2,1)S(1)}, bf16[130,8,4,128]{3,1,2,0:T(8,128)(2,1)}, u32[]{:S(2)}) copy-start(bf16[130,8,4,128]{3,1,2,0:T(8,128)(2,1)} %copy-done.16) | copy-start | bytes 3194884
  128.0 14.6 %copy-start.19 = (bf16[4,128,768]{1,2,0:T(8,128)(2,1)S(1)}, bf16[4,128,768]{1,2,0:T(8,128)(2,1)}, u32[]{:S(2)}) copy-start(bf16[4,128,768]{1,2,0:T(8,128)(2,1)} %copy-done.18) | copy-start | bytes 2359300
  132.6 13.1 %copy-start.50 = (f32[2,3216]{1,0:T(2,128)S(1)}, f32[2,3216]{1,0:T(2,128)}, u32[]{:S(2)}) copy-start(f32[2,3216]{1,0:T(2,128)} %slice.115) | copy-start | bytes 77188
  132.6 19.0 %copy-start.31 = (bf16[512,128]{1,0:T(8,128)(2,1)S(1)}, bf16[512,128]{1,0:T(8,128)(2,1)}, u32[]{:S(2)}) copy-start(bf16[512,128]{1,0:T(8,128)(2,1)} %copy-done.30) | copy-start | bytes 393220
  142.6 11.7 %copy-start.33 = (bf16[512,128]{1,0:T(8,128)(2,1)S(1)}, bf16[512,128]{1,0:T(8,128)(2,1)}, u32[]{:S(2)}) copy-start(bf16[512,128]{1,0:T(8,128)(2,1)} %copy-done.32) | copy-start | bytes 393220
  142.9 11.4 %copy-start.34 = (f32[2,256,128]{2,1,0:T(8,128)S(1)}, f32[2,256,128]{2,1,0:T(8,128)}, u32[]{:S(2)}) copy-start(f32[2,256,128]{2,1,0:T(8,128)} %get-tuple-element.438) | copy-start | bytes 786436
  145.8 4.2 %collective-permute-start = (f32[3,3216]{1,0:T(4,128)S(1)}, f32[3,3216]{1,0:T(4,128)S(1)}, u32[]{:S(2)}, u32[]{:S(2)}) collective-permute-start(f32[3,3216]{1,0:T(4,128)S(1)} %pad_maximum_fusion.3), channel_id=1, source_target_pairs={{0,1},{1,0},{2,3},{3,2},{4,5},{5,4},{6,7},{7,6},{8,9},{9,8},{10,11... | collective-permute-start | bytes 115784 | tf_op jit(solution)/shard_map/ppermute | solution.py:45
  150.0 4.2 %collective-permute-start.1 = (f32[3,3216]{1,0:T(4,128)S(1)}, f32[3,3216]{1,0:T(4,128)S(1)}, u32[]{:S(2)}, u32[]{:S(2)}) collective-permute-start(f32[3,3216]{1,0:T(4,128)S(1)} %fusion.67), channel_id=1, source_target_pairs={{0,2},{1,3},{2,0},{3,1},{4,6},{5,7},{6,4},{7,5},{8,10},{9,11},{10,... | collective-permute-start | bytes 115784 | tf_op jit(solution)/shard_map/ppermute | solution.py:45
  154.2 2.0 %collective-permute-start.2 = (f32[3,3216]{1,0:T(4,128)S(1)}, f32[3,3216]{1,0:T(4,128)S(1)}, u32[]{:S(2)}, u32[]{:S(2)}) collective-permute-start(f32[3,3216]{1,0:T(4,128)S(1)} %add.133), channel_id=1, source_target_pairs={{0,4},{4,0},{8,12},{12,8},{16,20},{20,16},{24,28},{28,24},{1,5},{5... | collective-permute-start | bytes 115784 | tf_op jit(solution)/shard_map/ppermute | solution.py:45
  156.3 6.9 %collective-permute-start.3 = (f32[3,3216]{1,0:T(4,128)S(1)}, f32[3,3216]{1,0:T(4,128)S(1)}, u32[]{:S(2)}, u32[]{:S(2)}) collective-permute-start(f32[3,3216]{1,0:T(4,128)S(1)} %add.134), channel_id=1, source_target_pairs={{0,8},{4,12},{8,0},{12,4},{16,24},{20,28},{24,16},{28,20},{1,9},{5... | collective-permute-start | bytes 115784 | tf_op jit(solution)/shard_map/ppermute | solution.py:45
  159.5 6.4 %copy-start.56 = (f32[1,804]{1,0:T(1,128)S(1)}, f32[1,804]{1,0:T(1,128)}, u32[]{:S(2)}) copy-start(f32[1,804]{1,0:T(1,128)} %param.25) | copy-start | bytes 9652
  159.5 6.4 %copy-start.58 = (f32[1,804]{1,0:T(1,128)S(1)}, f32[1,804]{1,0:T(1,128)}, u32[]{:S(2)}) copy-start(f32[1,804]{1,0:T(1,128)} %param.24) | copy-start | bytes 9652
  159.5 6.4 %copy-start.25 = (bf16[1,128,3072]{1,2,0:T(8,128)(2,1)S(1)}, bf16[1,128,3072]{1,2,0:T(8,128)(2,1)}, u32[]{:S(2)}) copy-start(bf16[1,128,3072]{1,2,0:T(8,128)(2,1)} %get-tuple-element.491) | copy-start | bytes 2359300
  159.5 7.6 %copy-start.24 = (bf16[1,128,3072]{1,2,0:T(8,128)(2,1)S(1)}, bf16[1,128,3072]{1,2,0:T(8,128)(2,1)}, u32[]{:S(2)}) copy-start(bf16[1,128,3072]{1,2,0:T(8,128)(2,1)} %get-tuple-element.489) | copy-start | bytes 2359300
  159.6 18.1 %all-to-all-start.3 = ((bf16[4,128,1036]{1,2,0:T(8,128)(2,1)}), bf16[4,128,1036]{1,2,0:T(8,128)(2,1)S(1)}, u32[]{:S(2)}, u32[]{:S(2)}) async-start(bf16[4,128,1036]{1,2,0:T(8,128)(2,1)} %copy.256), calls=%async_computation.3 | async-start | bytes 2129920 | tf_op jit(solution)/shard_map/all_to_all | solution.py:30
  163.3 5.9 %collective-permute-start.4 = (f32[3,3216]{1,0:T(4,128)S(1)}, f32[3,3216]{1,0:T(4,128)S(1)}, u32[]{:S(2)}, u32[]{:S(2)}) collective-permute-start(f32[3,3216]{1,0:T(4,128)S(1)} %add.135), channel_id=1, source_target_pairs={{0,16},{4,20},{8,24},{12,28},{16,0},{20,4},{24,8},{28,12},{1,17},{... | collective-permute-start | bytes 115784 | tf_op jit(solution)/shard_map/ppermute | solution.py:45
  165.9 6.5 %copy-start.52 = (f32[3216]{0:T(1024)S(1)}, f32[3216]{0:T(1024)}, u32[]{:S(2)}) copy-start(f32[3216]{0:T(1024)} %param.23) | copy-start | bytes 38596
  (24 other events, 28.1 us)

commit v5 on v4

--- a/solution.py
+++ b/solution.py
@@ -58,7 +58,8 @@
     blocks = length // SPAN
     step_sizes = jax.nn.softplus(dt_raw.astype(jnp.float32) + dt_bias)
     log_decay = (step_sizes * -jnp.exp(a_log)).reshape(blocks, SPAN, heads).transpose(0, 2, 1)
-    cumul = jnp.cumsum(log_decay, axis=2)
+    lower = (jnp.arange(SPAN)[:, None] >= jnp.arange(SPAN)[None, :]).astype(jnp.float32)
+    cumul = jnp.einsum("chs,ts->cht", log_decay, lower, precision=highest)
     inputs = hidden.astype(jnp.float32).reshape(blocks, SPAN, heads, width)
     scaled = rounded(inputs * step_sizes.reshape(blocks, SPAN, heads, 1))
     b_rows = b_input.astype(jnp.float32).reshape(blocks, SPAN, -1)
@@ -80,7 +81,9 @@
         return (jnp.exp(total)[:, None, None] * entering + added, entering)
 
     start_state = jnp.zeros(block_state.shape[1:], jnp.float32)
-    last_state, entering = lax.scan(advance, start_state, (keep, cumul[:, :, -1], block_state))
+    last_state, entering = lax.scan(
+        advance, start_state, (keep, cumul[:, :, -1], block_state), unroll=True
+    )
     c_decayed = rounded(c_rows[:, None] * jnp.exp(cumul)[..., None])
     inter = jnp.einsum("chtn,chnp->cthp", c_decayed, rounded(entering), precision=highest)
     output = intra + inter + skip[:, None] * inputs

time: 182 us -> 166 us (0.912)
  other arithmetic: 47.5 us -> 38.2 us
  waiting for transfers between devices: 35.7 us -> 28 us
  local copies, waits for them, and re-layouts: 51.1 us -> 48.9 us
    another operation x9 -> x1, other arithmetic: 6.86 us -> 0.18 us
    dynamic_slice x8 -> x0, local copies, waits for them, and re-layouts: 4.94 us -> none  [ssd_group(): lax.scan(advance, start_state, (keep, cumul[:, :, -1], block_state))]
    convert_element_type x3, local copies, waits for them, and re-layouts: 2.29 us -> 7.14 us  [ssd_group(): return output.reshape(length, heads * width).astype(jnp.bfloat16)]
    dynamic_update_slice x4 -> x0, other arithmetic: 3.55 us -> none  [ssd_group(): lax.scan(advance, start_state, (keep, cumul[:, :, -1], block_state))]
    all_to_all x2, waiting for transfers between devices: 12.8 us -> 9.42 us  [from_heads(): return lax.all_to_all(x, 'ctx', 0, 0, tiled=True)]
    dot_general x3 -> x2, matrix products: 7.26 us -> 3.98 us  [ssd_group(): jnp.einsum('chsn,cshp->chnp', b_decayed, scaled, precision=highest)]
    all_to_all x1, waiting for transfers between devices: 4.63 us -> 1.39 us  [to_heads(): x = lax.all_to_all(x, 'ctx', 0, 0, tiled=True)]
    while x28 -> x0, local copies, waits for them, and re-layouts: 2.31 us -> none
  transfers between devices with their start and end apart: 9 -> 9, of which waited for: 7 -> 7; matrix products, arithmetic and copies ran while one was open for 9% -> 14% of each run, Pallas kernels for 0% -> 0%
where the time goes in v5:
time: 166 us; the launch traced here: 164 us
  local copies, waits for them, and re-layouts  48.9 us (29%)
  other arithmetic  38.2 us (23%)
  waiting for transfers between devices  28 us (17%)
  starting transfers between devices  25.2 us (15%)
  matrix products  18.7 us (11%)
  between operations  5.28 us (3%)
    unnamed x155, local copies, waits for them, and re-layouts  17.1 us
    all_to_all x1, waiting for transfers between devices, on_device(): lax.all_to_all(packed, 'ctx', 0, 0, tiled=True).reshape(groups * tokens, -1)  11.7 us
    all_to_all x2, waiting for transfers between devices, from_heads(): return lax.all_to_all(x, 'ctx', 0, 0, tiled=True)  9.42 us
    all_to_all x2, starting transfers between devices, from_heads(): return lax.all_to_all(x, 'ctx', 0, 0, tiled=True)  8.03 us
    ppermute x5, starting transfers between devices, tree_sum(): x = x + lax.ppermute(x, axis, [(i, i ^ step) for i in range(size)])  7.55 us
    convert_element_type x3, local copies, waits for them, and re-layouts, ssd_group(): return output.reshape(length, heads * width).astype(jnp.bfloat16)  7.14 us
    reduce_sum x1, other arithmetic, ssd_group(): b_decayed = rounded(b_rows[:, None] * jnp.exp(tail)[..., None])  5.97 us
    reduce_sum x1, other arithmetic, ssd_group(): spread = cumul[:, :, :, None] - cumul[:, :, None, :]  5.72 us
  transfers between devices with their start and end apart: 9, of which 7 were waited for; matrix products, arithmetic and copies ran while one was open for 14% of the time, Pallas kernels for 0%

profile of v5, /device:TPU:0, one launch (start us, length us, event | category | flops | bytes accessed | tf_op | source)
XLA Modules:
  0.0 164.3 jit_solution(12034560526574491434)
XLA Ops:
  0.7 1.5 copy.145
  2.4 1.0 pad_maximum_fusion
  3.5 5.3 %all-to-all-start = ((bf16[4,128,1036]{1,2,0:T(8,128)(2,1)}), bf16[4,128,1036]{1,2,0:T(8,128)(2,1)S(1)}, u32[]{:S(2)}, u32[]{:S(2)}) async-start(bf16[4,128,1036]{1,2,0:T(8,128)(2,1)} %pad_maximum_fusion), calls=%async_computation | async-start | bytes 2129920 | tf_op jit(solution)/shard_map/all_to_all | solution.py:154
  10.9 11.7 %all-to-all-done = bf16[4,128,1036]{1,2,0:T(8,128)(2,1)S(1)} async-done(((bf16[4,128,1036]{1,2,0:T(8,128)(2,1)}), bf16[4,128,1036]{1,2,0:T(8,128)(2,1)S(1)}, u32[]{:S(2)}, u32[]{:S(2)}) %all-to-all-start) | async-done | bytes 1060896 | tf_op jit(solution)/shard_map/all_to_all | solution.py:154
  22.6 3.8 %copy.211 = bf16[4,128,1036]{1,0,2:T(4,128)(2,1)S(1)} copy(bf16[4,128,1036]{1,2,0:T(8,128)(2,1)S(1)} %all-to-all-done) | data formatting | bytes 2121728 | tf_op jit(solution)/shard_map/all_to_all | solution.py:154
  27.1 0.7 fusion.95
  28.4 0.8 fusion.77
  29.2 1.4 slice_convert_fusion
  32.7 1.0 multiply_convert_fusion.2
  33.8 2.8 %reshape.306 = f32[2,256,12,64]{1,0,3,2:T(2,128)S(1)} reshape(f32[512,768]{0,1:T(8,128)} %slice_convert_fusion) | data formatting | bytes 3145728 | tf_op jit(solution)/shard_map/jvp()/reshape | solution.py:63
  36.8 1.9 %multiply_convert_fusion.6 = (bf16[1,12,128,64]{2,3,1,0:T(8,128)(2,1)S(1)}, f32[1,12,128,64]{2,3,1,0:T(8,128)}) fusion(f32[]{:T(128)} %bitcast.12, f32[12]{0:T(128)S(1)} %get-tuple-element.60, bf16[2,256,12,64]{1,3,2,0:T(8,128)(2,1)S(1)} %multiply_convert_fusion.5, bf16[2,12,256,128]{3,2,1,0:T(8,128)(2,1)S(1)} %multiply_convert_fusion.2), kind=kOutput, calls=%fused_computation.91 | convolution fusion | flops 50626560 | bytes 2949172 | tf_op jit(solution)/shard_map/jvp()/slice | solution.py:84
  38.8 1.0 copy.150
  40.5 1.1 fusion.99
  41.6 0.8 copy-done.19
  42.4 2.9 %multiply_convert_fusion = bf16[2,12,256,256]{3,2,1,0:T(8,128)(2,1)S(1)} fusion(f32[2,12,256]{2,1,0:T(8,128)} %copy-done.31, f32[2,256,256]{2,1,0:T(8,128)S(1)} %fusion.99, pred[256,256]{1,0:T(8,128)(4,1)} %iota_compare_fusion), kind=kLoop, calls=%fused_computation.6 | loop fusion | flops 7864320 | bytes 3760128 | tf_op jit(solution)/shard_map/jvp()/convert_element_type | solution.py:51
  45.3 1.1 fusion.100
  46.4 1.0 multiply_convert_fusion.1
  48.6 1.7 %copy.154 = bf16[2,256,12,64]{1,0,3,2:T(2,128)(2,1)} copy(bf16[2,256,12,64]{1,3,2,0:T(8,128)(2,1)S(1)} %fusion.28) | data formatting | bytes 1572864 | tf_op jit(solution)/shard_map/jvp()/convert_element_type | solution.py:90
  50.3 3.3 %convert_element_type.157 = bf16[4,128,768]{1,0,2:T(4,128)(2,1)} reshape(bf16[2,256,12,64]{1,0,3,2:T(2,128)(2,1)} %copy.154) | data formatting | bytes 1572864 | tf_op jit(solution)/shard_map/jvp()/convert_element_type | solution.py:90
  53.6 2.1 %copy.155 = bf16[4,128,768]{1,2,0:T(8,128)(2,1)} copy(bf16[4,128,768]{1,0,2:T(4,128)(2,1)} %convert_element_type.157) | data formatting | bytes 1572864 | tf_op jit(solution)/shard_map/jvp()/convert_element_type | solution.py:90
  55.7 4.4 %all-to-all-start.1 = ((bf16[4,128,768]{1,2,0:T(8,128)(2,1)}), bf16[4,128,768]{1,2,0:T(8,128)(2,1)}, u32[]{:S(2)}, u32[]{:S(2)}) async-start(bf16[4,128,768]{1,2,0:T(8,128)(2,1)} %copy.155), calls=%async_computation.1 | async-start | bytes 1572864 | tf_op jit(solution)/shard_map/all_to_all | solution.py:30
  60.1 0.8 slice.107
  60.9 2.3 %copy.156 = bf16[1,128,3072]{1,2,0:T(8,128)(2,1)} copy(bf16[1,128,3072]{2,1,0:T(8,128)(2,1)} %param.13) | data formatting | bytes 1572864 | tf_op args[1]
  63.2 2.3 %copy.157 = bf16[1,128,3072]{1,2,0:T(8,128)(2,1)} copy(bf16[1,128,3072]{2,1,0:T(8,128)(2,1)} %param.18) | data formatting | bytes 1572864 | tf_op args[6]
  65.5 4.8 %all-to-all-done.1 = bf16[4,128,768]{1,2,0:T(8,128)(2,1)} async-done(((bf16[4,128,768]{1,2,0:T(8,128)(2,1)}), bf16[4,128,768]{1,2,0:T(8,128)(2,1)}, u32[]{:S(2)}, u32[]{:S(2)}) %all-to-all-start.1) | async-done | bytes 786464 | tf_op jit(solution)/shard_map/all_to_all | solution.py:30
  70.3 1.3 convert_element_type.189
  72.8 1.5 fusion.16
  74.3 2.6 %fusion.25 = (bf16[1,128,3072]{1,2,0:T(8,128)(2,1)}, bf16[1,128,3072]{1,2,0:T(8,128)(2,1)}, bf16[1,128,3072]{1,2,0:T(8,128)(2,1)}) fusion(bf16[1,128,3072]{1,2,0:T(8,128)(2,1)S(1)} %copy-done.15, f32[1,128,3072]{1,2,0:T(8,128)S(1)} %get-tuple-element.66, bf16[1,128,3072]{1,2,0:T(8,128)(2,1)S(1)} %copy-done.16, f32[128]{0:T(128)S(1)} %fusion.87, ...), kind=kLoop, calls=%fused_computation.45 | loop fusion | flops 8650752 | bytes 7091200 | tf_op jit(solution)/shard_map/convert_element_type | solution.py:114
  77.0 4.3 %all-to-all-start.2 = ((bf16[4,128,768]{1,2,0:T(8,128)(2,1)}), bf16[4,128,768]{1,2,0:T(8,128)(2,1)}, u32[]{:S(2)}, u32[]{:S(2)}) async-start(bf16[4,128,768]{1,2,0:T(8,128)(2,1)} %bitcast.181), calls=%async_computation.2 | async-start | bytes 1572864 | tf_op jit(solution)/shard_map/all_to_all | solution.py:23
  81.5 1.4 fusion.86
  82.9 1.3 fusion.85
  87.5 1.5 dynamic_update_slice.7
  89.0 1.3 slice.133
  90.3 1.4 all-to-all-done.2
  91.7 2.6 %copy.158 = bf16[4,128,768]{1,0,2:T(4,128)(2,1)} copy(bf16[4,128,768]{1,2,0:T(8,128)(2,1)} %all-to-all-done.2) | data formatting | bytes 1572864 | tf_op jit(solution)/shard_map/all_to_all | solution.py:23
  94.3 3.0 %squeeze_broadcast_in_dim_reshape.3 = bf16[2,256,12,64]{1,0,3,2:T(2,128)(2,1)} reshape(bf16[4,128,768]{1,0,2:T(4,128)(2,1)} %copy.158) | data formatting | bytes 1572864 | tf_op jit(solution)/shard_map/squeeze;broadcast_in_dim;reshape | solution.py:182
  97.3 2.1 %convolution_convert_fusion.3 = bf16[2,12,128,64]{2,3,1,0:T(8,128)(2,1)S(1)} fusion(bf16[2,12,256,128]{3,2,1,0:T(8,128)(2,1)} %copy-done.11, bf16[2,256,12,64]{1,0,3,2:T(2,128)(2,1)} %squeeze_broadcast_in_dim_reshape.3), kind=kOutput, calls=%fused_computation.60 | convolution fusion | flops 100859904 | bytes 2752512 | tf_op jit(solution)/shard_map/transpose(jvp(chtn,chnp->cthp))/dot_general | solution.py:88
  99.5 1.9 %convolution_convert_fusion.2 = bf16[2,12,256,128]{3,2,1,0:T(8,128)(2,1)} fusion(bf16[2,12,128,64]{2,3,1,0:T(8,128)(2,1)S(1)} %concatenate.29, bf16[2,256,12,64]{1,0,3,2:T(2,128)(2,1)S(1)} %copy-done), kind=kOutput, calls=%fused_computation.32 | convolution fusion | flops 101449728 | bytes 2752512 | tf_op jit(solution)/shard_map/transpose(jvp(chtn,chnp->cthp))/dot_general | solution.py:88
  101.3 2.7 %convolution_convert_fusion = bf16[2,12,256,256]{3,2,1,0:T(8,128)(2,1)} fusion(bf16[2,256,12,64]{1,3,2,0:T(8,128)(2,1)S(1)} %copy-done.7, bf16[2,256,12,64]{1,0,3,2:T(2,128)(2,1)S(1)} %copy-done), kind=kOutput, calls=%fused_computation.24 | convolution fusion | flops 202899456 | bytes 4718592 | tf_op jit(solution)/shard_map/transpose(jvp(chts,cshp->cthp))/dot_general | solution.py:72
  104.0 1.8 %fusion.34 = f32[2,12,64,256]{3,2,1,0:T(8,128)} fusion(bf16[2,12,256,256]{3,2,1,0:T(8,128)(2,1)S(1)} %multiply_convert_fusion, bf16[2,256,12,64]{1,0,3,2:T(2,128)(2,1)S(1)} %copy-done), kind=kOutput, calls=%fused_computation.72 | convolution fusion | flops 201326592 | bytes 5505024 | tf_op jit(solution)/shard_map/transpose(jvp(chts,cshp->cthp))/dot_general | solution.py:72
  105.8 0.8 fusion.42
  106.7 1.0 fusion.46
  107.8 1.5 convolution_convert_fusion.1
  109.4 6.0 %fusion.7 = (f32[2,256,128]{2,1,0:T(8,128)}, f32[2,12,256]{2,1,0:T(8,128)S(1)}, f32[2,12,256]{2,1,0:T(8,128)}, f32[2,256,128]{2,1,0:T(8,128)}) fusion(bf16[2,12,256,128]{3,2,1,0:T(8,128)(2,1)S(1)} %convolution_convert_fusion.1, f32[2,12,256]{2,1,0:T(8,128)S(1)} %copy-done.37, f32[2,256,128]{2,1,0:T(8,128)S(1)} %copy-done.25, f32[2,256,128]{2,1,0:T(8,128)} %copy-done.26, ...), kind=kLoop, calls=%fused_computation.15 | loop fusion | flops 7720960 | bytes 4292608 | tf_op jit(solution)/shard_map/transpose(jvp())/reduce_sum | solution.py:74
  116.2 5.7 %fusion.6 = (f32[2,12,256]{2,1,0:T(8,128)S(1)}, f32[2,12,256]{2,1,0:T(8,128)S(1)}, f32[2,256,256]{2,1,0:T(8,128)}) fusion(bf16[2,12,256,256]{3,2,1,0:T(8,128)(2,1)S(1)} %copy-done.12, f32[2,12,256]{2,1,0:T(8,128)S(1)} %copy-done.32, f32[2,256,256]{2,1,0:T(8,128)} %copy-done.19, pred[256,256]{1,0:T(8,128)(4,1)S(1)} %copy-done.38), kind=kLoop, calls=%fused_computation.10 | loop fusion | flops 18731008 | bytes 4333568 | tf_op jit(solution)/shard_map/transpose(jvp())/reduce_sum | solution.py:69
  122.3 2.5 %fusion.29 = bf16[2,256,12,64]{1,3,2,0:T(8,128)(2,1)S(1)} fusion(f32[2,12,64,256]{3,2,1,0:T(8,128)S(1)} %copy-done.17, bf16[2,12,256,128]{3,2,1,0:T(8,128)(2,1)S(1)} %copy-done.10, f32[12]{0:T(128)S(1)} %copy-done.56, f32[]{:T(128)} %bitcast.12, bf16[2,12,128,64]{2,3,1,0:T(8,128)(2,1)S(1)} %copy-done.23), kind=kOutput, calls=%fused_computation.59 | convolution fusion | flops 303071232 | bytes 4129284 | tf_op jit(solution)/shard_map/transpose(jvp(chsn,cshp->chnp))/dot_general | solution.py:75
  126.4 0.7 bitcast_multiply_fusion.5
  127.1 1.4 fusion.26
  129.4 1.5 collective-permute-start
  130.9 2.7 %collective-permute-done = f32[3,3216]{1,0:T(4,128)S(1)} collective-permute-done((f32[3,3216]{1,0:T(4,128)S(1)}, f32[3,3216]{1,0:T(4,128)S(1)}, u32[]{:S(2)}, u32[]{:S(2)}) %collective-permute-start) | collective-permute-done | bytes 38624 | tf_op jit(solution)/shard_map/ppermute | solution.py:45
  133.6 1.6 collective-permute-start.1
  135.9 1.9 %collective-permute-done.1 = f32[3,3216]{1,0:T(4,128)S(1)} collective-permute-done((f32[3,3216]{1,0:T(4,128)S(1)}, f32[3,3216]{1,0:T(4,128)S(1)}, u32[]{:S(2)}, u32[]{:S(2)}) %collective-permute-start.1) | collective-permute-done | bytes 38624 | tf_op jit(solution)/shard_map/ppermute | solution.py:45
  138.5 0.8 copy.161
  139.6 1.7 %collective-permute-start.3 = (f32[3,3216]{1,0:T(4,128)S(1)}, f32[3,3216]{1,0:T(4,128)S(1)}, u32[]{:S(2)}, u32[]{:S(2)}) collective-permute-start(f32[3,3216]{1,0:T(4,128)S(1)} %add.124), channel_id=1, source_target_pairs={{0,8},{4,12},{8,0},{12,4},{16,24},{20,28},{24,16},{28,20},{1,9},{5... | collective-permute-start | bytes 115784 | tf_op jit(solution)/shard_map/ppermute | solution.py:45
  141.7 1.1 copy.170
  142.8 3.7 %all-to-all-start.3 = ((bf16[4,128,1036]{1,2,0:T(8,128)(2,1)}), bf16[4,128,1036]{1,2,0:T(8,128)(2,1)S(1)}, u32[]{:S(2)}, u32[]{:S(2)}) async-start(bf16[4,128,1036]{1,2,0:T(8,128)(2,1)} %copy.170), calls=%async_computation.3 | async-start | bytes 2129920 | tf_op jit(solution)/shard_map/all_to_all | solution.py:30
  146.5 2.6 %collective-permute-start.4 = (f32[3,3216]{1,0:T(4,128)S(1)}, f32[3,3216]{1,0:T(4,128)S(1)}, u32[]{:S(2)}, u32[]{:S(2)}) collective-permute-start(f32[3,3216]{1,0:T(4,128)S(1)} %add.125), channel_id=1, source_target_pairs={{0,16},{4,20},{8,24},{12,28},{16,0},{20,4},{24,8},{28,12},{1,17},{... | collective-permute-start | bytes 115784 | tf_op jit(solution)/shard_map/ppermute | solution.py:45
  149.2 1.2 copy.173
  150.4 1.2 copy.175
  151.6 0.8 collective-permute-done.4
  156.3 4.6 %all-to-all-done.3 = bf16[4,128,1036]{1,2,0:T(8,128)(2,1)S(1)} async-done(((bf16[4,128,1036]{1,2,0:T(8,128)(2,1)}), bf16[4,128,1036]{1,2,0:T(8,128)(2,1)S(1)}, u32[]{:S(2)}, u32[]{:S(2)}) %all-to-all-start.3) | async-done | bytes 1060896 | tf_op jit(solution)/shard_map/all_to_all | solution.py:30
  161.0 1.2 copy.174
  162.2 0.7 copy.176
  162.9 0.7 copy.177
  (224 shorter events, 19.0 us)
Async XLA Ops:
  0.7 1.7 %copy-start.54 = (bf16[1,128,48]{1,2,0:T(8,128)(2,1)S(1)}, bf16[1,128,48]{1,2,0:T(8,128)(2,1)}, u32[]{:S(2)}) copy-start(bf16[1,128,48]{1,2,0:T(8,128)(2,1)} %param.14) | copy-start | bytes 36868
  3.5 5.3 %slice-start = ((f32[3216]{0:T(1024)}), f32[144]{0:T(256)S(1)}, s32[]{:S(2)}) async-start(f32[3216]{0:T(1024)} %param.19), calls=%async_computation.4 | async-start | bytes 2048 | tf_op jit(solution)/shard_map/slice | solution.py:141
  3.5 5.4 %copy-start.69 = (s32[1,2]{1,0:T(1,128)S(1)}, s32[1,2]{1,0:T(1,128)}, u32[]{:S(2)}) copy-start(s32[1,2]{1,0:T(1,128)} %param.17) | copy-start | bytes 28
  3.5 19.1 %all-to-all-start = ((bf16[4,128,1036]{1,2,0:T(8,128)(2,1)}), bf16[4,128,1036]{1,2,0:T(8,128)(2,1)S(1)}, u32[]{:S(2)}, u32[]{:S(2)}) async-start(bf16[4,128,1036]{1,2,0:T(8,128)(2,1)} %pad_maximum_fusion), calls=%async_computation | async-start | bytes 2129920 | tf_op jit(solution)/shard_map/all_to_all | solution.py:154
  10.9 17.0 %copy-start.60 = (f32[12]{0:T(128)}, f32[12]{0:T(128)S(1)}, u32[]{:S(2)}) copy-start(f32[12]{0:T(128)S(1)} %get-tuple-element.84) | copy-start | bytes 148
  10.9 17.0 %copy-start.62 = (f32[12]{0:T(128)}, f32[12]{0:T(128)S(1)}, u32[]{:S(2)}) copy-start(f32[12]{0:T(128)S(1)} %get-tuple-element.85) | copy-start | bytes 148
  10.9 36.5 %copy-start.58 = (f32[12]{0:T(128)}, f32[12]{0:T(128)S(1)}, u32[]{:S(2)}) copy-start(f32[12]{0:T(128)S(1)} %get-tuple-element.83) | copy-start | bytes 148
  27.1 3.5 %copy-start.13 = (bf16[130,8,4,128]{3,1,2,0:T(8,128)(2,1)}, bf16[130,8,4,128]{3,1,2,0:T(8,128)(2,1)S(1)}, u32[]{:S(2)}) copy-start(bf16[130,8,4,128]{3,1,2,0:T(8,128)(2,1)S(1)} %copy.181) | copy-start | bytes 3194884
  28.3 3.0 %copy-start.31 = (f32[2,12,256]{2,1,0:T(8,128)}, f32[2,12,256]{2,1,0:T(8,128)S(1)}, u32[]{:S(2)}) copy-start(f32[2,12,256]{2,1,0:T(8,128)S(1)} %fusion.51) | copy-start | bytes 73732
  29.2 7.6 %copy-start.64 = (f32[12]{0:T(128)}, f32[12]{0:T(128)S(1)}, u32[]{:S(2)}) copy-start(f32[12]{0:T(128)S(1)} %get-tuple-element.60) | copy-start | bytes 148
  31.3 2.5 %copy-start.36 = (f32[2,12,256]{2,1,0:T(8,128)}, f32[2,12,256]{2,1,0:T(8,128)S(1)}, u32[]{:S(2)}) copy-start(f32[2,12,256]{2,1,0:T(8,128)S(1)} %get-tuple-element.80) | copy-start | bytes 73732
  33.7 3.1 %copy-start.9 = (bf16[2,12,256,128]{3,2,1,0:T(8,128)(2,1)}, bf16[2,12,256,128]{3,2,1,0:T(8,128)(2,1)S(1)}, u32[]{:S(2)}) copy-start(bf16[2,12,256,128]{3,2,1,0:T(8,128)(2,1)S(1)} %multiply_convert_fusion.2) | copy-start | bytes 4718596
  33.8 3.0 %copy-start.39 = (f32[2,256,12]{1,2,0:T(8,128)}, f32[2,256,12]{1,2,0:T(8,128)S(1)}, u32[]{:S(2)}) copy-start(f32[2,256,12]{1,2,0:T(8,128)S(1)} %copy.148) | copy-start | bytes 73732
  36.6 2.1 %copy-start.2 = (f32[2,256,12,64]{1,0,3,2:T(2,128)}, f32[2,256,12,64]{1,0,3,2:T(2,128)S(1)}, u32[]{:S(2)}) copy-start(f32[2,256,12,64]{1,0,3,2:T(2,128)S(1)} %reshape.306) | copy-start | bytes 4718596
  36.8 2.0 %copy-start.5 = (bf16[2,256,12,64]{1,3,2,0:T(8,128)(2,1)}, bf16[2,256,12,64]{1,3,2,0:T(8,128)(2,1)S(1)}, u32[]{:S(2)}) copy-start(bf16[2,256,12,64]{1,3,2,0:T(8,128)(2,1)S(1)} %multiply_convert_fusion.5) | copy-start | bytes 2359300
  39.8 6.6 %copy-start.26 = (f32[2,256,128]{2,1,0:T(8,128)}, f32[2,256,128]{2,1,0:T(8,128)S(1)}, u32[]{:S(2)}) copy-start(f32[2,256,128]{2,1,0:T(8,128)S(1)} %bitcast_convert_fusion.1) | copy-start | bytes 786436
  42.4 2.9 %copy-start.6 = (bf16[2,256,12,64]{1,3,2,0:T(8,128)(2,1)S(1)}, bf16[2,256,12,64]{1,3,2,0:T(8,128)(2,1)}, u32[]{:S(2)}) copy-start(bf16[2,256,12,64]{1,3,2,0:T(8,128)(2,1)} %copy-done.5) | copy-start | bytes 2359300
  55.7 14.6 %all-to-all-start.1 = ((bf16[4,128,768]{1,2,0:T(8,128)(2,1)}), bf16[4,128,768]{1,2,0:T(8,128)(2,1)}, u32[]{:S(2)}, u32[]{:S(2)}) async-start(bf16[4,128,768]{1,2,0:T(8,128)(2,1)} %copy.155), calls=%async_computation.1 | async-start | bytes 1572864 | tf_op jit(solution)/shard_map/all_to_all | solution.py:30
  77.0 4.4 %copy-start.66 = (s32[8]{0:T(128)S(1)}, s32[8]{0:T(128)}, u32[]{:S(2)}) copy-start(s32[8]{0:T(128)} %param.22) | copy-start | bytes 100
  77.0 9.8 %copy-start.50 = (f32[1,804]{1,0:T(1,128)S(1)}, f32[1,804]{1,0:T(1,128)}, u32[]{:S(2)}) copy-start(f32[1,804]{1,0:T(1,128)} %param.21) | copy-start | bytes 9652
  77.0 9.8 %copy-start.52 = (f32[1,804]{1,0:T(1,128)S(1)}, f32[1,804]{1,0:T(1,128)}, u32[]{:S(2)}) copy-start(f32[1,804]{1,0:T(1,128)} %param.20) | copy-start | bytes 9652
  77.0 14.7 %all-to-all-start.2 = ((bf16[4,128,768]{1,2,0:T(8,128)(2,1)}), bf16[4,128,768]{1,2,0:T(8,128)(2,1)}, u32[]{:S(2)}, u32[]{:S(2)}) async-start(bf16[4,128,768]{1,2,0:T(8,128)(2,1)} %bitcast.181), calls=%async_computation.2 | async-start | bytes 1572864 | tf_op jit(solution)/shard_map/all_to_all | solution.py:23
  97.3 2.1 %copy-start = (bf16[2,256,12,64]{1,0,3,2:T(2,128)(2,1)S(1)}, bf16[2,256,12,64]{1,0,3,2:T(2,128)(2,1)}, u32[]{:S(2)}) copy-start(bf16[2,256,12,64]{1,0,3,2:T(2,128)(2,1)} %squeeze_broadcast_in_dim_reshape.3) | copy-start | bytes 2359300
  99.5 7.2 %copy-start.22 = (bf16[2,12,128,64]{2,3,1,0:T(8,128)(2,1)}, bf16[2,12,128,64]{2,3,1,0:T(8,128)(2,1)S(1)}, u32[]{:S(2)}) copy-start(bf16[2,12,128,64]{2,3,1,0:T(8,128)(2,1)S(1)} %convolution_convert_fusion.3) | copy-start | bytes 1179652
  99.5 1.9 %copy-start.7 = (bf16[2,256,12,64]{1,3,2,0:T(8,128)(2,1)S(1)}, bf16[2,256,12,64]{1,3,2,0:T(8,128)(2,1)}, u32[]{:S(2)}) copy-start(bf16[2,256,12,64]{1,3,2,0:T(8,128)(2,1)} %copy-done.5) | copy-start | bytes 2359300
  104.0 1.8 %copy-start.55 = (f32[12]{0:T(128)S(1)}, f32[12]{0:T(128)}, u32[]{:S(2)}) copy-start(f32[12]{0:T(128)} %get-tuple-element.59) | copy-start | bytes 148
  104.0 2.6 %copy-start.33 = (f32[1,12,128,64]{2,3,1,0:T(8,128)S(1)}, f32[1,12,128,64]{2,3,1,0:T(8,128)}, u32[]{:S(2)}) copy-start(f32[1,12,128,64]{2,3,1,0:T(8,128)} %get-tuple-element.89) | copy-start | bytes 1179652
  104.0 2.6 %copy-start.65 = (f32[12]{0:T(128)S(1)}, f32[12]{0:T(128)}, u32[]{:S(2)}) copy-start(f32[12]{0:T(128)} %copy-done.64) | copy-start | bytes 148
  104.0 3.7 %copy-start.68 = (f32[12]{0:T(128)S(1)}, f32[12]{0:T(128)}, u32[]{:S(2)}) copy-start(f32[12]{0:T(128)} %get-tuple-element.57) | copy-start | bytes 148
  104.0 3.7 %copy-start.67 = (f32[12]{0:T(128)S(1)}, f32[12]{0:T(128)}, u32[]{:S(2)}) copy-start(f32[12]{0:T(128)} %get-tuple-element.58) | copy-start | bytes 148
  105.8 2.0 %copy-start.8 = (bf16[2,256,12,64]{1,3,2,0:T(8,128)(2,1)S(1)}, bf16[2,256,12,64]{1,3,2,0:T(8,128)(2,1)}, u32[]{:S(2)}) copy-start(bf16[2,256,12,64]{1,3,2,0:T(8,128)(2,1)} %copy-done.5) | copy-start | bytes 2359300
  106.7 2.6 %copy-start.25 = (f32[2,256,128]{2,1,0:T(8,128)S(1)}, f32[2,256,128]{2,1,0:T(8,128)}, u32[]{:S(2)}) copy-start(f32[2,256,128]{2,1,0:T(8,128)} %copy-done.24) | copy-start | bytes 786436
  106.7 2.6 %copy-start.37 = (f32[2,12,256]{2,1,0:T(8,128)S(1)}, f32[2,12,256]{2,1,0:T(8,128)}, u32[]{:S(2)}) copy-start(f32[2,12,256]{2,1,0:T(8,128)} %copy-done.36) | copy-start | bytes 73732
  109.3 6.8 %copy-start.12 = (bf16[2,12,256,256]{3,2,1,0:T(8,128)(2,1)S(1)}, bf16[2,12,256,256]{3,2,1,0:T(8,128)(2,1)}, u32[]{:S(2)}) copy-start(bf16[2,12,256,256]{3,2,1,0:T(8,128)(2,1)} %convolution_convert_fusion) | copy-start | bytes 9437188
  109.3 6.8 %copy-start.32 = (f32[2,12,256]{2,1,0:T(8,128)S(1)}, f32[2,12,256]{2,1,0:T(8,128)}, u32[]{:S(2)}) copy-start(f32[2,12,256]{2,1,0:T(8,128)} %copy-done.31) | copy-start | bytes 73732
  109.4 6.8 %copy-start.38 = (pred[256,256]{1,0:T(8,128)(4,1)S(1)}, pred[256,256]{1,0:T(8,128)(4,1)}, u32[]{:S(2)}) copy-start(pred[256,256]{1,0:T(8,128)(4,1)} %iota_compare_fusion) | copy-start | bytes 196612
  116.2 5.8 %copy-start.43 = (f32[2,12,256]{2,1,0:T(8,128)S(1)}, f32[2,12,256]{2,1,0:T(8,128)}, u32[]{:S(2)}) copy-start(f32[2,12,256]{2,1,0:T(8,128)} %copy-done.42) | copy-start | bytes 73732
  116.2 5.8 %copy-start.45 = (f32[2,12,256]{2,1,0:T(8,128)S(1)}, f32[2,12,256]{2,1,0:T(8,128)}, u32[]{:S(2)}) copy-start(f32[2,12,256]{2,1,0:T(8,128)} %get-tuple-element.92) | copy-start | bytes 73732
  116.2 6.1 %copy-start.10 = (bf16[2,12,256,128]{3,2,1,0:T(8,128)(2,1)S(1)}, bf16[2,12,256,128]{3,2,1,0:T(8,128)(2,1)}, u32[]{:S(2)}) copy-start(bf16[2,12,256,128]{3,2,1,0:T(8,128)(2,1)} %copy-done.9) | copy-start | bytes 4718596
  116.2 6.1 %copy-start.17 = (f32[2,12,64,256]{3,2,1,0:T(8,128)S(1)}, f32[2,12,64,256]{3,2,1,0:T(8,128)}, u32[]{:S(2)}) copy-start(f32[2,12,64,256]{3,2,1,0:T(8,128)} %fusion.34) | copy-start | bytes 4718596
  116.2 6.1 %copy-start.23 = (bf16[2,12,128,64]{2,3,1,0:T(8,128)(2,1)S(1)}, bf16[2,12,128,64]{2,3,1,0:T(8,128)(2,1)}, u32[]{:S(2)}) copy-start(bf16[2,12,128,64]{2,3,1,0:T(8,128)(2,1)} %copy-done.22) | copy-start | bytes 1179652
  116.2 6.1 %copy-start.56 = (f32[12]{0:T(128)S(1)}, f32[12]{0:T(128)}, u32[]{:S(2)}) copy-start(f32[12]{0:T(128)} %get-tuple-element.59) | copy-start | bytes 148
  122.3 2.6 %copy-start.1 = (bf16[2,256,12,64]{1,0,3,2:T(2,128)(2,1)S(1)}, bf16[2,256,12,64]{1,0,3,2:T(2,128)(2,1)}, u32[]{:S(2)}) copy-start(bf16[2,256,12,64]{1,0,3,2:T(2,128)(2,1)} %squeeze_broadcast_in_dim_reshape.3) | copy-start | bytes 2359300
  122.3 2.6 %copy-start.4 = (f32[2,256,12,64]{1,0,3,2:T(2,128)S(1)}, f32[2,256,12,64]{1,0,3,2:T(2,128)}, u32[]{:S(2)}) copy-start(f32[2,256,12,64]{1,0,3,2:T(2,128)} %copy-done.2) | copy-start | bytes 4718596
  122.3 2.6 %copy-start.40 = (f32[2,256,12]{1,2,0:T(8,128)S(1)}, f32[2,256,12]{1,2,0:T(8,128)}, u32[]{:S(2)}) copy-start(f32[2,256,12]{1,2,0:T(8,128)} %copy-done.39) | copy-start | bytes 73732
  122.3 2.6 %copy-start.59 = (f32[12]{0:T(128)S(1)}, f32[12]{0:T(128)}, u32[]{:S(2)}) copy-start(f32[12]{0:T(128)} %copy-done.58) | copy-start | bytes 148
  125.5 3.7 %copy-start.47 = (f32[3072]{0:T(1024)S(1)}, f32[3072]{0:T(1024)}, u32[]{:S(2)}) copy-start(f32[3072]{0:T(1024)} %get-tuple-element.48) | copy-start | bytes 36868
  125.5 3.8 %copy-start.44 = (f32[2,3216]{1,0:T(2,128)S(1)}, f32[2,3216]{1,0:T(2,128)}, u32[]{:S(2)}) copy-start(f32[2,3216]{1,0:T(2,128)} %slice.133) | copy-start | bytes 77188
  125.6 9.6 %copy-start.18 = (f32[2,256,256]{2,1,0:T(8,128)S(1)}, f32[2,256,256]{2,1,0:T(8,128)}, u32[]{:S(2)}) copy-start(f32[2,256,256]{2,1,0:T(8,128)} %get-tuple-element.47) | copy-start | bytes 1572868
  125.6 9.6 %copy-start.30 = (bf16[512,128]{1,0:T(8,128)(2,1)S(1)}, bf16[512,128]{1,0:T(8,128)(2,1)}, u32[]{:S(2)}) copy-start(bf16[512,128]{1,0:T(8,128)(2,1)} %copy-done.29) | copy-start | bytes 393220
  125.6 9.6 %copy-start.35 = (f32[2,256,128]{2,1,0:T(8,128)S(1)}, f32[2,256,128]{2,1,0:T(8,128)}, u32[]{:S(2)}) copy-start(f32[2,256,128]{2,1,0:T(8,128)} %get-tuple-element.50) | copy-start | bytes 786436
  126.4 11.5 %copy-start.28 = (bf16[512,128]{1,0:T(8,128)(2,1)S(1)}, bf16[512,128]{1,0:T(8,128)(2,1)}, u32[]{:S(2)}) copy-start(bf16[512,128]{1,0:T(8,128)(2,1)} %copy-done.27) | copy-start | bytes 393220
  126.4 11.5 %copy-start.34 = (f32[2,256,128]{2,1,0:T(8,128)S(1)}, f32[2,256,128]{2,1,0:T(8,128)}, u32[]{:S(2)}) copy-start(f32[2,256,128]{2,1,0:T(8,128)} %get-tuple-element.93) | copy-start | bytes 786436
  129.4 4.2 %collective-permute-start = (f32[3,3216]{1,0:T(4,128)S(1)}, f32[3,3216]{1,0:T(4,128)S(1)}, u32[]{:S(2)}, u32[]{:S(2)}) collective-permute-start(f32[3,3216]{1,0:T(4,128)S(1)} %pad_maximum_fusion.3), channel_id=1, source_target_pairs={{0,1},{1,0},{2,3},{3,2},{4,5},{5,4},{6,7},{7,6},{8,9},{9,8},{10,11... | collective-permute-start | bytes 115784 | tf_op jit(solution)/shard_map/ppermute | solution.py:45
  133.6 4.2 %collective-permute-start.1 = (f32[3,3216]{1,0:T(4,128)S(1)}, f32[3,3216]{1,0:T(4,128)S(1)}, u32[]{:S(2)}, u32[]{:S(2)}) collective-permute-start(f32[3,3216]{1,0:T(4,128)S(1)} %fusion.91), channel_id=1, source_target_pairs={{0,2},{1,3},{2,0},{3,1},{4,6},{5,7},{6,4},{7,5},{8,10},{9,11},{10,... | collective-permute-start | bytes 115784 | tf_op jit(solution)/shard_map/ppermute | solution.py:45
  137.8 1.7 %collective-permute-start.2 = (f32[3,3216]{1,0:T(4,128)S(1)}, f32[3,3216]{1,0:T(4,128)S(1)}, u32[]{:S(2)}, u32[]{:S(2)}) collective-permute-start(f32[3,3216]{1,0:T(4,128)S(1)} %add.123), channel_id=1, source_target_pairs={{0,4},{4,0},{8,12},{12,8},{16,20},{20,16},{24,28},{28,24},{1,5},{5... | collective-permute-start | bytes 115784 | tf_op jit(solution)/shard_map/ppermute | solution.py:45
  139.6 6.9 %collective-permute-start.3 = (f32[3,3216]{1,0:T(4,128)S(1)}, f32[3,3216]{1,0:T(4,128)S(1)}, u32[]{:S(2)}, u32[]{:S(2)}) collective-permute-start(f32[3,3216]{1,0:T(4,128)S(1)} %add.124), channel_id=1, source_target_pairs={{0,8},{4,12},{8,0},{12,4},{16,24},{20,28},{24,16},{28,20},{1,9},{5... | collective-permute-start | bytes 115784 | tf_op jit(solution)/shard_map/ppermute | solution.py:45
  142.8 6.4 %copy-start.51 = (f32[1,804]{1,0:T(1,128)S(1)}, f32[1,804]{1,0:T(1,128)}, u32[]{:S(2)}) copy-start(f32[1,804]{1,0:T(1,128)} %param.21) | copy-start | bytes 9652
  142.8 6.4 %copy-start.53 = (f32[1,804]{1,0:T(1,128)S(1)}, f32[1,804]{1,0:T(1,128)}, u32[]{:S(2)}) copy-start(f32[1,804]{1,0:T(1,128)} %param.20) | copy-start | bytes 9652
  142.8 6.4 %copy-start.21 = (bf16[1,128,3072]{1,2,0:T(8,128)(2,1)S(1)}, bf16[1,128,3072]{1,2,0:T(8,128)(2,1)}, u32[]{:S(2)}) copy-start(bf16[1,128,3072]{1,2,0:T(8,128)(2,1)} %get-tuple-element.69) | copy-start | bytes 2359300
  142.8 7.6 %copy-start.20 = (bf16[1,128,3072]{1,2,0:T(8,128)(2,1)S(1)}, bf16[1,128,3072]{1,2,0:T(8,128)(2,1)}, u32[]{:S(2)}) copy-start(bf16[1,128,3072]{1,2,0:T(8,128)(2,1)} %get-tuple-element.67) | copy-start | bytes 2359300
  142.8 18.1 %all-to-all-start.3 = ((bf16[4,128,1036]{1,2,0:T(8,128)(2,1)}), bf16[4,128,1036]{1,2,0:T(8,128)(2,1)S(1)}, u32[]{:S(2)}, u32[]{:S(2)}) async-start(bf16[4,128,1036]{1,2,0:T(8,128)(2,1)} %copy.170), calls=%async_computation.3 | async-start | bytes 2129920 | tf_op jit(solution)/shard_map/all_to_all | solution.py:30
  146.5 5.9 %collective-permute-start.4 = (f32[3,3216]{1,0:T(4,128)S(1)}, f32[3,3216]{1,0:T(4,128)S(1)}, u32[]{:S(2)}, u32[]{:S(2)}) collective-permute-start(f32[3,3216]{1,0:T(4,128)S(1)} %add.125), channel_id=1, source_target_pairs={{0,16},{4,20},{8,24},{12,28},{16,0},{20,4},{24,8},{28,12},{1,17},{... | collective-permute-start | bytes 115784 | tf_op jit(solution)/shard_map/ppermute | solution.py:45
  149.2 6.5 %copy-start.46 = (f32[3216]{0:T(1024)S(1)}, f32[3216]{0:T(1024)}, u32[]{:S(2)}) copy-start(f32[3216]{0:T(1024)} %param.19) | copy-start | bytes 38596
  (16 other events, 17.1 us)

commit v6 on v5

--- a/solution.py
+++ b/solution.py
@@ -81,9 +81,7 @@
         return (jnp.exp(total)[:, None, None] * entering + added, entering)
 
     start_state = jnp.zeros(block_state.shape[1:], jnp.float32)
-    last_state, entering = lax.scan(
-        advance, start_state, (keep, cumul[:, :, -1], block_state), unroll=True
-    )
+    _, entering = lax.scan(advance, start_state, (keep, cumul[:, :, -1], block_state), unroll=True)
     c_decayed = rounded(c_rows[:, None] * jnp.exp(cumul)[..., None])
     inter = jnp.einsum("chtn,chnp->cthp", c_decayed, rounded(entering), precision=highest)
     output = intra + inter + skip[:, None] * inputs
@@ -211,7 +209,7 @@
     laid = lax.dynamic_update_slice(
         jnp.zeros((2, total_len + slot_cap), jnp.float32), own_state, (0, row_begin)
     )[:, :total_len]
-    summed = tree_sum(tree_sum(jnp.concatenate([grad_part[None], laid]), "ctx"), "dp")
+    summed = tree_sum(tree_sum(jnp.concatenate([grad_part[None], laid]), "dp"), "ctx")
     gradient = summed[0]
     mean_flat = summed[1]
     square_flat = summed[2]

time: 166 us -> 168 us (1.012)
  waiting for transfers between devices: 28 us -> 30.3 us
    ppermute x5, waiting for transfers between devices: 5.45 us -> 12.4 us  [tree_sum(): x = x + lax.ppermute(x, axis, [(i, i ^ step) for i in range(size)])]
    all_to_all x2, waiting for transfers between devices: 9.42 us -> 4.85 us  [from_heads(): return lax.all_to_all(x, 'ctx', 0, 0, tiled=True)]
where the time goes in v6:
time: 168 us; the launch traced here: 167 us
  local copies, waits for them, and re-layouts  48.9 us (29%)
  other arithmetic  38.2 us (23%)
  waiting for transfers between devices  30.3 us (18%)
  starting transfers between devices  25.7 us (15%)
  matrix products  18.7 us (11%)
  between operations  5.25 us (3%)
    unnamed x155, local copies, waits for them, and re-layouts  17.1 us
    ppermute x5, waiting for transfers between devices, tree_sum(): x = x + lax.ppermute(x, axis, [(i, i ^ step) for i in range(size)])  12.4 us
    all_to_all x1, waiting for transfers between devices, on_device(): lax.all_to_all(packed, 'ctx', 0, 0, tiled=True).reshape(groups * tokens, -1)  11.7 us
    ppermute x5, starting transfers between devices, tree_sum(): x = x + lax.ppermute(x, axis, [(i, i ^ step) for i in range(size)])  8.07 us
    all_to_all x2, starting transfers between devices, from_heads(): return lax.all_to_all(x, 'ctx', 0, 0, tiled=True)  8.03 us
    convert_element_type x3, local copies, waits for them, and re-layouts, ssd_group(): return output.reshape(length, heads * width).astype(jnp.bfloat16)  7.14 us
    reduce_sum x1, other arithmetic, ssd_group(): b_decayed = rounded(b_rows[:, None] * jnp.exp(tail)[..., None])  5.97 us
    reduce_sum x1, other arithmetic, ssd_group(): spread = cumul[:, :, :, None] - cumul[:, :, None, :]  5.72 us
  transfers between devices with their start and end apart: 9, of which 7 were waited for; matrix products, arithmetic and copies ran while one was open for 14% of the time, Pallas kernels for 0%

profile of v6, /device:TPU:0, one launch (start us, length us, event | category | flops | bytes accessed | tf_op | source)
XLA Modules:
  0.0 167.1 jit_solution(1962803043244012982)
XLA Ops:
  0.7 1.5 copy.145
  2.4 1.0 pad_maximum_fusion
  3.5 5.3 %all-to-all-start = ((bf16[4,128,1036]{1,2,0:T(8,128)(2,1)}), bf16[4,128,1036]{1,2,0:T(8,128)(2,1)S(1)}, u32[]{:S(2)}, u32[]{:S(2)}) async-start(bf16[4,128,1036]{1,2,0:T(8,128)(2,1)} %pad_maximum_fusion), calls=%async_computation | async-start | bytes 2129920 | tf_op jit(solution)/shard_map/all_to_all | solution.py:152
  10.9 11.7 %all-to-all-done = bf16[4,128,1036]{1,2,0:T(8,128)(2,1)S(1)} async-done(((bf16[4,128,1036]{1,2,0:T(8,128)(2,1)}), bf16[4,128,1036]{1,2,0:T(8,128)(2,1)S(1)}, u32[]{:S(2)}, u32[]{:S(2)}) %all-to-all-start) | async-done | bytes 1060896 | tf_op jit(solution)/shard_map/all_to_all | solution.py:152
  22.6 3.8 %copy.211 = bf16[4,128,1036]{1,0,2:T(4,128)(2,1)S(1)} copy(bf16[4,128,1036]{1,2,0:T(8,128)(2,1)S(1)} %all-to-all-done) | data formatting | bytes 2121728 | tf_op jit(solution)/shard_map/all_to_all | solution.py:152
  27.1 0.7 fusion.95
  28.4 0.8 fusion.77
  29.2 1.4 slice_convert_fusion
  32.7 1.0 multiply_convert_fusion.2
  33.8 2.8 %reshape.306 = f32[2,256,12,64]{1,0,3,2:T(2,128)S(1)} reshape(f32[512,768]{0,1:T(8,128)} %slice_convert_fusion) | data formatting | bytes 3145728 | tf_op jit(solution)/shard_map/jvp()/reshape | solution.py:63
  36.8 1.9 %multiply_convert_fusion.6 = (bf16[1,12,128,64]{2,3,1,0:T(8,128)(2,1)S(1)}, f32[1,12,128,64]{2,3,1,0:T(8,128)}) fusion(f32[]{:T(128)} %bitcast.12, f32[12]{0:T(128)S(1)} %get-tuple-element.60, bf16[2,256,12,64]{1,3,2,0:T(8,128)(2,1)S(1)} %multiply_convert_fusion.5, bf16[2,12,256,128]{3,2,1,0:T(8,128)(2,1)S(1)} %multiply_convert_fusion.2), kind=kOutput, calls=%fused_computation.91 | convolution fusion | flops 50626560 | bytes 2949172 | tf_op jit(solution)/shard_map/jvp()/slice | solution.py:84
  38.8 1.0 copy.150
  40.5 1.1 fusion.99
  41.6 0.8 copy-done.19
  42.4 2.9 %multiply_convert_fusion = bf16[2,12,256,256]{3,2,1,0:T(8,128)(2,1)S(1)} fusion(f32[2,12,256]{2,1,0:T(8,128)} %copy-done.31, f32[2,256,256]{2,1,0:T(8,128)S(1)} %fusion.99, pred[256,256]{1,0:T(8,128)(4,1)} %iota_compare_fusion), kind=kLoop, calls=%fused_computation.6 | loop fusion | flops 7864320 | bytes 3760128 | tf_op jit(solution)/shard_map/jvp()/convert_element_type | solution.py:51
  45.3 1.1 fusion.100
  46.4 1.0 multiply_convert_fusion.1
  48.6 1.7 %copy.154 = bf16[2,256,12,64]{1,0,3,2:T(2,128)(2,1)} copy(bf16[2,256,12,64]{1,3,2,0:T(8,128)(2,1)S(1)} %fusion.28) | data formatting | bytes 1572864 | tf_op jit(solution)/shard_map/jvp()/convert_element_type | solution.py:88
  50.3 3.3 %convert_element_type.157 = bf16[4,128,768]{1,0,2:T(4,128)(2,1)} reshape(bf16[2,256,12,64]{1,0,3,2:T(2,128)(2,1)} %copy.154) | data formatting | bytes 1572864 | tf_op jit(solution)/shard_map/jvp()/convert_element_type | solution.py:88
  53.6 2.1 %copy.155 = bf16[4,128,768]{1,2,0:T(8,128)(2,1)} copy(bf16[4,128,768]{1,0,2:T(4,128)(2,1)} %convert_element_type.157) | data formatting | bytes 1572864 | tf_op jit(solution)/shard_map/jvp()/convert_element_type | solution.py:88
  55.7 4.4 %all-to-all-start.1 = ((bf16[4,128,768]{1,2,0:T(8,128)(2,1)}), bf16[4,128,768]{1,2,0:T(8,128)(2,1)}, u32[]{:S(2)}, u32[]{:S(2)}) async-start(bf16[4,128,768]{1,2,0:T(8,128)(2,1)} %copy.155), calls=%async_computation.1 | async-start | bytes 1572864 | tf_op jit(solution)/shard_map/all_to_all | solution.py:30
  60.1 0.8 slice.107
  60.9 2.3 %copy.156 = bf16[1,128,3072]{1,2,0:T(8,128)(2,1)} copy(bf16[1,128,3072]{2,1,0:T(8,128)(2,1)} %param.13) | data formatting | bytes 1572864 | tf_op args[1]
  63.2 2.3 %copy.157 = bf16[1,128,3072]{1,2,0:T(8,128)(2,1)} copy(bf16[1,128,3072]{2,1,0:T(8,128)(2,1)} %param.18) | data formatting | bytes 1572864 | tf_op args[6]
  65.5 4.8 %all-to-all-done.1 = bf16[4,128,768]{1,2,0:T(8,128)(2,1)} async-done(((bf16[4,128,768]{1,2,0:T(8,128)(2,1)}), bf16[4,128,768]{1,2,0:T(8,128)(2,1)}, u32[]{:S(2)}, u32[]{:S(2)}) %all-to-all-start.1) | async-done | bytes 786464 | tf_op jit(solution)/shard_map/all_to_all | solution.py:30
  70.3 1.3 convert_element_type.189
  72.8 1.5 fusion.16
  74.3 2.6 %fusion.25 = (bf16[1,128,3072]{1,2,0:T(8,128)(2,1)}, bf16[1,128,3072]{1,2,0:T(8,128)(2,1)}, bf16[1,128,3072]{1,2,0:T(8,128)(2,1)}) fusion(bf16[1,128,3072]{1,2,0:T(8,128)(2,1)S(1)} %copy-done.15, f32[1,128,3072]{1,2,0:T(8,128)S(1)} %get-tuple-element.66, bf16[1,128,3072]{1,2,0:T(8,128)(2,1)S(1)} %copy-done.16, f32[128]{0:T(128)S(1)} %fusion.87, ...), kind=kLoop, calls=%fused_computation.45 | loop fusion | flops 8650752 | bytes 7091200 | tf_op jit(solution)/shard_map/convert_element_type | solution.py:112
  77.0 4.3 %all-to-all-start.2 = ((bf16[4,128,768]{1,2,0:T(8,128)(2,1)}), bf16[4,128,768]{1,2,0:T(8,128)(2,1)}, u32[]{:S(2)}, u32[]{:S(2)}) async-start(bf16[4,128,768]{1,2,0:T(8,128)(2,1)} %bitcast.181), calls=%async_computation.2 | async-start | bytes 1572864 | tf_op jit(solution)/shard_map/all_to_all | solution.py:23
  81.5 1.4 fusion.86
  82.9 1.3 fusion.85
  87.5 1.5 dynamic_update_slice.7
  89.0 1.3 slice.133
  90.3 1.4 all-to-all-done.2
  91.7 2.6 %copy.158 = bf16[4,128,768]{1,0,2:T(4,128)(2,1)} copy(bf16[4,128,768]{1,2,0:T(8,128)(2,1)} %all-to-all-done.2) | data formatting | bytes 1572864 | tf_op jit(solution)/shard_map/all_to_all | solution.py:23
  94.3 3.0 %squeeze_broadcast_in_dim_reshape.3 = bf16[2,256,12,64]{1,0,3,2:T(2,128)(2,1)} reshape(bf16[4,128,768]{1,0,2:T(4,128)(2,1)} %copy.158) | data formatting | bytes 1572864 | tf_op jit(solution)/shard_map/squeeze;broadcast_in_dim;reshape | solution.py:180
  97.3 2.1 %convolution_convert_fusion.3 = bf16[2,12,128,64]{2,3,1,0:T(8,128)(2,1)S(1)} fusion(bf16[2,12,256,128]{3,2,1,0:T(8,128)(2,1)} %copy-done.11, bf16[2,256,12,64]{1,0,3,2:T(2,128)(2,1)} %squeeze_broadcast_in_dim_reshape.3), kind=kOutput, calls=%fused_computation.60 | convolution fusion | flops 100859904 | bytes 2752512 | tf_op jit(solution)/shard_map/transpose(jvp(chtn,chnp->cthp))/dot_general | solution.py:86
  99.5 1.9 %convolution_convert_fusion.2 = bf16[2,12,256,128]{3,2,1,0:T(8,128)(2,1)} fusion(bf16[2,12,128,64]{2,3,1,0:T(8,128)(2,1)S(1)} %concatenate.29, bf16[2,256,12,64]{1,0,3,2:T(2,128)(2,1)S(1)} %copy-done), kind=kOutput, calls=%fused_computation.32 | convolution fusion | flops 101449728 | bytes 2752512 | tf_op jit(solution)/shard_map/transpose(jvp(chtn,chnp->cthp))/dot_general | solution.py:86
  101.3 2.7 %convolution_convert_fusion = bf16[2,12,256,256]{3,2,1,0:T(8,128)(2,1)} fusion(bf16[2,256,12,64]{1,3,2,0:T(8,128)(2,1)S(1)} %copy-done.7, bf16[2,256,12,64]{1,0,3,2:T(2,128)(2,1)S(1)} %copy-done), kind=kOutput, calls=%fused_computation.24 | convolution fusion | flops 202899456 | bytes 4718592 | tf_op jit(solution)/shard_map/transpose(jvp(chts,cshp->cthp))/dot_general | solution.py:72
  104.0 1.8 %fusion.34 = f32[2,12,64,256]{3,2,1,0:T(8,128)} fusion(bf16[2,12,256,256]{3,2,1,0:T(8,128)(2,1)S(1)} %multiply_convert_fusion, bf16[2,256,12,64]{1,0,3,2:T(2,128)(2,1)S(1)} %copy-done), kind=kOutput, calls=%fused_computation.72 | convolution fusion | flops 201326592 | bytes 5505024 | tf_op jit(solution)/shard_map/transpose(jvp(chts,cshp->cthp))/dot_general | solution.py:72
  105.8 0.8 fusion.42
  106.7 1.0 fusion.46
  107.8 1.5 convolution_convert_fusion.1
  109.4 6.0 %fusion.7 = (f32[2,256,128]{2,1,0:T(8,128)}, f32[2,12,256]{2,1,0:T(8,128)S(1)}, f32[2,12,256]{2,1,0:T(8,128)}, f32[2,256,128]{2,1,0:T(8,128)}) fusion(bf16[2,12,256,128]{3,2,1,0:T(8,128)(2,1)S(1)} %convolution_convert_fusion.1, f32[2,12,256]{2,1,0:T(8,128)S(1)} %copy-done.37, f32[2,256,128]{2,1,0:T(8,128)S(1)} %copy-done.25, f32[2,256,128]{2,1,0:T(8,128)} %copy-done.26, ...), kind=kLoop, calls=%fused_computation.15 | loop fusion | flops 7720960 | bytes 4292608 | tf_op jit(solution)/shard_map/transpose(jvp())/reduce_sum | solution.py:74
  116.2 5.7 %fusion.6 = (f32[2,12,256]{2,1,0:T(8,128)S(1)}, f32[2,12,256]{2,1,0:T(8,128)S(1)}, f32[2,256,256]{2,1,0:T(8,128)}) fusion(bf16[2,12,256,256]{3,2,1,0:T(8,128)(2,1)S(1)} %copy-done.12, f32[2,12,256]{2,1,0:T(8,128)S(1)} %copy-done.32, f32[2,256,256]{2,1,0:T(8,128)} %copy-done.19, pred[256,256]{1,0:T(8,128)(4,1)S(1)} %copy-done.38), kind=kLoop, calls=%fused_computation.10 | loop fusion | flops 18731008 | bytes 4333568 | tf_op jit(solution)/shard_map/transpose(jvp())/reduce_sum | solution.py:69
  122.3 2.5 %fusion.29 = bf16[2,256,12,64]{1,3,2,0:T(8,128)(2,1)S(1)} fusion(f32[2,12,64,256]{3,2,1,0:T(8,128)S(1)} %copy-done.17, bf16[2,12,256,128]{3,2,1,0:T(8,128)(2,1)S(1)} %copy-done.10, f32[12]{0:T(128)S(1)} %copy-done.56, f32[]{:T(128)} %bitcast.12, bf16[2,12,128,64]{2,3,1,0:T(8,128)(2,1)S(1)} %copy-done.23), kind=kOutput, calls=%fused_computation.59 | convolution fusion | flops 303071232 | bytes 4129284 | tf_op jit(solution)/shard_map/transpose(jvp(chsn,cshp->chnp))/dot_general | solution.py:75
  126.4 0.7 bitcast_multiply_fusion.5
  127.1 1.4 fusion.26
  129.4 1.2 collective-permute-done
  130.7 1.7 %collective-permute-start.1 = (f32[3,3216]{1,0:T(4,128)S(1)}, f32[3,3216]{1,0:T(4,128)S(1)}, u32[]{:S(2)}, u32[]{:S(2)}) collective-permute-start(f32[3,3216]{1,0:T(4,128)S(1)} %fusion.91), channel_id=1, source_target_pairs={{0,8},{4,12},{8,0},{12,4},{16,24},{20,28},{24,16},{28,20},{1,9},{5... | collective-permute-start | bytes 115784 | tf_op jit(solution)/shard_map/ppermute | solution.py:45
  133.1 1.8 %collective-permute-done.1 = f32[3,3216]{1,0:T(4,128)S(1)} collective-permute-done((f32[3,3216]{1,0:T(4,128)S(1)}, f32[3,3216]{1,0:T(4,128)S(1)}, u32[]{:S(2)}, u32[]{:S(2)}) %collective-permute-start.1) | collective-permute-done | bytes 38624 | tf_op jit(solution)/shard_map/ppermute | solution.py:45
  134.9 2.7 %collective-permute-start.2 = (f32[3,3216]{1,0:T(4,128)S(1)}, f32[3,3216]{1,0:T(4,128)S(1)}, u32[]{:S(2)}, u32[]{:S(2)}) collective-permute-start(f32[3,3216]{1,0:T(4,128)S(1)} %add.123), channel_id=1, source_target_pairs={{0,16},{4,20},{8,24},{12,28},{16,0},{20,4},{24,8},{28,12},{1,17},{... | collective-permute-start | bytes 115784 | tf_op jit(solution)/shard_map/ppermute | solution.py:45
  138.3 0.8 copy.161
  139.3 0.8 collective-permute-done.2
  140.0 1.5 collective-permute-start.3
  142.0 1.1 copy.170
  143.1 3.7 %all-to-all-start.3 = ((bf16[4,128,1036]{1,2,0:T(8,128)(2,1)}), bf16[4,128,1036]{1,2,0:T(8,128)(2,1)S(1)}, u32[]{:S(2)}, u32[]{:S(2)}) async-start(bf16[4,128,1036]{1,2,0:T(8,128)(2,1)} %copy.170), calls=%async_computation.3 | async-start | bytes 2129920 | tf_op jit(solution)/shard_map/all_to_all | solution.py:30
  146.8 2.0 %collective-permute-start.4 = (f32[3,3216]{1,0:T(4,128)S(1)}, f32[3,3216]{1,0:T(4,128)S(1)}, u32[]{:S(2)}, u32[]{:S(2)}) collective-permute-start(f32[3,3216]{1,0:T(4,128)S(1)} %add.125), channel_id=1, source_target_pairs={{0,2},{1,3},{2,0},{3,1},{4,6},{5,7},{6,4},{7,5},{8,10},{9,11},{10,... | collective-permute-start | bytes 115784 | tf_op jit(solution)/shard_map/ppermute | solution.py:45
  148.9 1.2 copy.173
  150.1 1.2 copy.175
  151.3 8.6 %collective-permute-done.4 = f32[3,3216]{1,0:T(4,128)S(1)} collective-permute-done((f32[3,3216]{1,0:T(4,128)S(1)}, f32[3,3216]{1,0:T(4,128)S(1)}, u32[]{:S(2)}, u32[]{:S(2)}) %collective-permute-start.4) | collective-permute-done | bytes 38624 | tf_op jit(solution)/shard_map/ppermute | solution.py:45
  163.8 1.2 copy.174
  165.0 0.7 copy.176
  165.8 0.7 copy.177
  (224 shorter events, 19.0 us)
Async XLA Ops:
  0.7 1.7 %copy-start.54 = (bf16[1,128,48]{1,2,0:T(8,128)(2,1)S(1)}, bf16[1,128,48]{1,2,0:T(8,128)(2,1)}, u32[]{:S(2)}) copy-start(bf16[1,128,48]{1,2,0:T(8,128)(2,1)} %param.14) | copy-start | bytes 36868
  3.5 5.3 %slice-start = ((f32[3216]{0:T(1024)}), f32[144]{0:T(256)S(1)}, s32[]{:S(2)}) async-start(f32[3216]{0:T(1024)} %param.19), calls=%async_computation.4 | async-start | bytes 2048 | tf_op jit(solution)/shard_map/slice | solution.py:139
  3.5 5.4 %copy-start.69 = (s32[1,2]{1,0:T(1,128)S(1)}, s32[1,2]{1,0:T(1,128)}, u32[]{:S(2)}) copy-start(s32[1,2]{1,0:T(1,128)} %param.17) | copy-start | bytes 28
  3.5 19.1 %all-to-all-start = ((bf16[4,128,1036]{1,2,0:T(8,128)(2,1)}), bf16[4,128,1036]{1,2,0:T(8,128)(2,1)S(1)}, u32[]{:S(2)}, u32[]{:S(2)}) async-start(bf16[4,128,1036]{1,2,0:T(8,128)(2,1)} %pad_maximum_fusion), calls=%async_computation | async-start | bytes 2129920 | tf_op jit(solution)/shard_map/all_to_all | solution.py:152
  10.9 17.0 %copy-start.60 = (f32[12]{0:T(128)}, f32[12]{0:T(128)S(1)}, u32[]{:S(2)}) copy-start(f32[12]{0:T(128)S(1)} %get-tuple-element.84) | copy-start | bytes 148
  10.9 17.0 %copy-start.62 = (f32[12]{0:T(128)}, f32[12]{0:T(128)S(1)}, u32[]{:S(2)}) copy-start(f32[12]{0:T(128)S(1)} %get-tuple-element.85) | copy-start | bytes 148
  10.9 36.5 %copy-start.58 = (f32[12]{0:T(128)}, f32[12]{0:T(128)S(1)}, u32[]{:S(2)}) copy-start(f32[12]{0:T(128)S(1)} %get-tuple-element.83) | copy-start | bytes 148
  27.1 3.5 %copy-start.13 = (bf16[130,8,4,128]{3,1,2,0:T(8,128)(2,1)}, bf16[130,8,4,128]{3,1,2,0:T(8,128)(2,1)S(1)}, u32[]{:S(2)}) copy-start(bf16[130,8,4,128]{3,1,2,0:T(8,128)(2,1)S(1)} %copy.181) | copy-start | bytes 3194884
  28.3 3.0 %copy-start.31 = (f32[2,12,256]{2,1,0:T(8,128)}, f32[2,12,256]{2,1,0:T(8,128)S(1)}, u32[]{:S(2)}) copy-start(f32[2,12,256]{2,1,0:T(8,128)S(1)} %fusion.51) | copy-start | bytes 73732
  29.2 7.6 %copy-start.64 = (f32[12]{0:T(128)}, f32[12]{0:T(128)S(1)}, u32[]{:S(2)}) copy-start(f32[12]{0:T(128)S(1)} %get-tuple-element.60) | copy-start | bytes 148
  31.3 2.5 %copy-start.36 = (f32[2,12,256]{2,1,0:T(8,128)}, f32[2,12,256]{2,1,0:T(8,128)S(1)}, u32[]{:S(2)}) copy-start(f32[2,12,256]{2,1,0:T(8,128)S(1)} %get-tuple-element.80) | copy-start | bytes 73732
  33.7 3.1 %copy-start.9 = (bf16[2,12,256,128]{3,2,1,0:T(8,128)(2,1)}, bf16[2,12,256,128]{3,2,1,0:T(8,128)(2,1)S(1)}, u32[]{:S(2)}) copy-start(bf16[2,12,256,128]{3,2,1,0:T(8,128)(2,1)S(1)} %multiply_convert_fusion.2) | copy-start | bytes 4718596
  33.8 3.0 %copy-start.39 = (f32[2,256,12]{1,2,0:T(8,128)}, f32[2,256,12]{1,2,0:T(8,128)S(1)}, u32[]{:S(2)}) copy-start(f32[2,256,12]{1,2,0:T(8,128)S(1)} %copy.148) | copy-start | bytes 73732
  36.6 2.1 %copy-start.2 = (f32[2,256,12,64]{1,0,3,2:T(2,128)}, f32[2,256,12,64]{1,0,3,2:T(2,128)S(1)}, u32[]{:S(2)}) copy-start(f32[2,256,12,64]{1,0,3,2:T(2,128)S(1)} %reshape.306) | copy-start | bytes 4718596
  36.8 2.0 %copy-start.5 = (bf16[2,256,12,64]{1,3,2,0:T(8,128)(2,1)}, bf16[2,256,12,64]{1,3,2,0:T(8,128)(2,1)S(1)}, u32[]{:S(2)}) copy-start(bf16[2,256,12,64]{1,3,2,0:T(8,128)(2,1)S(1)} %multiply_convert_fusion.5) | copy-start | bytes 2359300
  39.8 6.6 %copy-start.26 = (f32[2,256,128]{2,1,0:T(8,128)}, f32[2,256,128]{2,1,0:T(8,128)S(1)}, u32[]{:S(2)}) copy-start(f32[2,256,128]{2,1,0:T(8,128)S(1)} %bitcast_convert_fusion.1) | copy-start | bytes 786436
  42.4 2.9 %copy-start.6 = (bf16[2,256,12,64]{1,3,2,0:T(8,128)(2,1)S(1)}, bf16[2,256,12,64]{1,3,2,0:T(8,128)(2,1)}, u32[]{:S(2)}) copy-start(bf16[2,256,12,64]{1,3,2,0:T(8,128)(2,1)} %copy-done.5) | copy-start | bytes 2359300
  55.7 14.6 %all-to-all-start.1 = ((bf16[4,128,768]{1,2,0:T(8,128)(2,1)}), bf16[4,128,768]{1,2,0:T(8,128)(2,1)}, u32[]{:S(2)}, u32[]{:S(2)}) async-start(bf16[4,128,768]{1,2,0:T(8,128)(2,1)} %copy.155), calls=%async_computation.1 | async-start | bytes 1572864 | tf_op jit(solution)/shard_map/all_to_all | solution.py:30
  77.0 4.4 %copy-start.66 = (s32[8]{0:T(128)S(1)}, s32[8]{0:T(128)}, u32[]{:S(2)}) copy-start(s32[8]{0:T(128)} %param.22) | copy-start | bytes 100
  77.0 9.8 %copy-start.50 = (f32[1,804]{1,0:T(1,128)S(1)}, f32[1,804]{1,0:T(1,128)}, u32[]{:S(2)}) copy-start(f32[1,804]{1,0:T(1,128)} %param.21) | copy-start | bytes 9652
  77.0 9.8 %copy-start.52 = (f32[1,804]{1,0:T(1,128)S(1)}, f32[1,804]{1,0:T(1,128)}, u32[]{:S(2)}) copy-start(f32[1,804]{1,0:T(1,128)} %param.20) | copy-start | bytes 9652
  77.0 14.7 %all-to-all-start.2 = ((bf16[4,128,768]{1,2,0:T(8,128)(2,1)}), bf16[4,128,768]{1,2,0:T(8,128)(2,1)}, u32[]{:S(2)}, u32[]{:S(2)}) async-start(bf16[4,128,768]{1,2,0:T(8,128)(2,1)} %bitcast.181), calls=%async_computation.2 | async-start | bytes 1572864 | tf_op jit(solution)/shard_map/all_to_all | solution.py:23
  97.3 2.1 %copy-start = (bf16[2,256,12,64]{1,0,3,2:T(2,128)(2,1)S(1)}, bf16[2,256,12,64]{1,0,3,2:T(2,128)(2,1)}, u32[]{:S(2)}) copy-start(bf16[2,256,12,64]{1,0,3,2:T(2,128)(2,1)} %squeeze_broadcast_in_dim_reshape.3) | copy-start | bytes 2359300
  99.5 7.2 %copy-start.22 = (bf16[2,12,128,64]{2,3,1,0:T(8,128)(2,1)}, bf16[2,12,128,64]{2,3,1,0:T(8,128)(2,1)S(1)}, u32[]{:S(2)}) copy-start(bf16[2,12,128,64]{2,3,1,0:T(8,128)(2,1)S(1)} %convolution_convert_fusion.3) | copy-start | bytes 1179652
  99.5 1.9 %copy-start.7 = (bf16[2,256,12,64]{1,3,2,0:T(8,128)(2,1)S(1)}, bf16[2,256,12,64]{1,3,2,0:T(8,128)(2,1)}, u32[]{:S(2)}) copy-start(bf16[2,256,12,64]{1,3,2,0:T(8,128)(2,1)} %copy-done.5) | copy-start | bytes 2359300
  104.0 1.8 %copy-start.55 = (f32[12]{0:T(128)S(1)}, f32[12]{0:T(128)}, u32[]{:S(2)}) copy-start(f32[12]{0:T(128)} %get-tuple-element.59) | copy-start | bytes 148
  104.0 2.6 %copy-start.33 = (f32[1,12,128,64]{2,3,1,0:T(8,128)S(1)}, f32[1,12,128,64]{2,3,1,0:T(8,128)}, u32[]{:S(2)}) copy-start(f32[1,12,128,64]{2,3,1,0:T(8,128)} %get-tuple-element.89) | copy-start | bytes 1179652
  104.0 2.6 %copy-start.65 = (f32[12]{0:T(128)S(1)}, f32[12]{0:T(128)}, u32[]{:S(2)}) copy-start(f32[12]{0:T(128)} %copy-done.64) | copy-start | bytes 148
  104.0 3.7 %copy-start.68 = (f32[12]{0:T(128)S(1)}, f32[12]{0:T(128)}, u32[]{:S(2)}) copy-start(f32[12]{0:T(128)} %get-tuple-element.57) | copy-start | bytes 148
  104.0 3.7 %copy-start.67 = (f32[12]{0:T(128)S(1)}, f32[12]{0:T(128)}, u32[]{:S(2)}) copy-start(f32[12]{0:T(128)} %get-tuple-element.58) | copy-start | bytes 148
  105.8 2.0 %copy-start.8 = (bf16[2,256,12,64]{1,3,2,0:T(8,128)(2,1)S(1)}, bf16[2,256,12,64]{1,3,2,0:T(8,128)(2,1)}, u32[]{:S(2)}) copy-start(bf16[2,256,12,64]{1,3,2,0:T(8,128)(2,1)} %copy-done.5) | copy-start | bytes 2359300
  106.7 2.6 %copy-start.25 = (f32[2,256,128]{2,1,0:T(8,128)S(1)}, f32[2,256,128]{2,1,0:T(8,128)}, u32[]{:S(2)}) copy-start(f32[2,256,128]{2,1,0:T(8,128)} %copy-done.24) | copy-start | bytes 786436
  106.7 2.6 %copy-start.37 = (f32[2,12,256]{2,1,0:T(8,128)S(1)}, f32[2,12,256]{2,1,0:T(8,128)}, u32[]{:S(2)}) copy-start(f32[2,12,256]{2,1,0:T(8,128)} %copy-done.36) | copy-start | bytes 73732
  109.3 6.8 %copy-start.12 = (bf16[2,12,256,256]{3,2,1,0:T(8,128)(2,1)S(1)}, bf16[2,12,256,256]{3,2,1,0:T(8,128)(2,1)}, u32[]{:S(2)}) copy-start(bf16[2,12,256,256]{3,2,1,0:T(8,128)(2,1)} %convolution_convert_fusion) | copy-start | bytes 9437188
  109.3 6.8 %copy-start.32 = (f32[2,12,256]{2,1,0:T(8,128)S(1)}, f32[2,12,256]{2,1,0:T(8,128)}, u32[]{:S(2)}) copy-start(f32[2,12,256]{2,1,0:T(8,128)} %copy-done.31) | copy-start | bytes 73732
  109.4 6.8 %copy-start.38 = (pred[256,256]{1,0:T(8,128)(4,1)S(1)}, pred[256,256]{1,0:T(8,128)(4,1)}, u32[]{:S(2)}) copy-start(pred[256,256]{1,0:T(8,128)(4,1)} %iota_compare_fusion) | copy-start | bytes 196612
  116.2 5.8 %copy-start.43 = (f32[2,12,256]{2,1,0:T(8,128)S(1)}, f32[2,12,256]{2,1,0:T(8,128)}, u32[]{:S(2)}) copy-start(f32[2,12,256]{2,1,0:T(8,128)} %copy-done.42) | copy-start | bytes 73732
  116.2 5.8 %copy-start.45 = (f32[2,12,256]{2,1,0:T(8,128)S(1)}, f32[2,12,256]{2,1,0:T(8,128)}, u32[]{:S(2)}) copy-start(f32[2,12,256]{2,1,0:T(8,128)} %get-tuple-element.92) | copy-start | bytes 73732
  116.2 6.1 %copy-start.10 = (bf16[2,12,256,128]{3,2,1,0:T(8,128)(2,1)S(1)}, bf16[2,12,256,128]{3,2,1,0:T(8,128)(2,1)}, u32[]{:S(2)}) copy-start(bf16[2,12,256,128]{3,2,1,0:T(8,128)(2,1)} %copy-done.9) | copy-start | bytes 4718596
  116.2 6.1 %copy-start.17 = (f32[2,12,64,256]{3,2,1,0:T(8,128)S(1)}, f32[2,12,64,256]{3,2,1,0:T(8,128)}, u32[]{:S(2)}) copy-start(f32[2,12,64,256]{3,2,1,0:T(8,128)} %fusion.34) | copy-start | bytes 4718596
  116.2 6.1 %copy-start.23 = (bf16[2,12,128,64]{2,3,1,0:T(8,128)(2,1)S(1)}, bf16[2,12,128,64]{2,3,1,0:T(8,128)(2,1)}, u32[]{:S(2)}) copy-start(bf16[2,12,128,64]{2,3,1,0:T(8,128)(2,1)} %copy-done.22) | copy-start | bytes 1179652
  116.2 6.1 %copy-start.56 = (f32[12]{0:T(128)S(1)}, f32[12]{0:T(128)}, u32[]{:S(2)}) copy-start(f32[12]{0:T(128)} %get-tuple-element.59) | copy-start | bytes 148
  122.3 2.6 %copy-start.1 = (bf16[2,256,12,64]{1,0,3,2:T(2,128)(2,1)S(1)}, bf16[2,256,12,64]{1,0,3,2:T(2,128)(2,1)}, u32[]{:S(2)}) copy-start(bf16[2,256,12,64]{1,0,3,2:T(2,128)(2,1)} %squeeze_broadcast_in_dim_reshape.3) | copy-start | bytes 2359300
  122.3 2.6 %copy-start.4 = (f32[2,256,12,64]{1,0,3,2:T(2,128)S(1)}, f32[2,256,12,64]{1,0,3,2:T(2,128)}, u32[]{:S(2)}) copy-start(f32[2,256,12,64]{1,0,3,2:T(2,128)} %copy-done.2) | copy-start | bytes 4718596
  122.3 2.6 %copy-start.40 = (f32[2,256,12]{1,2,0:T(8,128)S(1)}, f32[2,256,12]{1,2,0:T(8,128)}, u32[]{:S(2)}) copy-start(f32[2,256,12]{1,2,0:T(8,128)} %copy-done.39) | copy-start | bytes 73732
  122.3 2.6 %copy-start.59 = (f32[12]{0:T(128)S(1)}, f32[12]{0:T(128)}, u32[]{:S(2)}) copy-start(f32[12]{0:T(128)} %copy-done.58) | copy-start | bytes 148
  125.5 3.7 %copy-start.47 = (f32[3072]{0:T(1024)S(1)}, f32[3072]{0:T(1024)}, u32[]{:S(2)}) copy-start(f32[3072]{0:T(1024)} %get-tuple-element.48) | copy-start | bytes 36868
  125.5 3.8 %copy-start.44 = (f32[2,3216]{1,0:T(2,128)S(1)}, f32[2,3216]{1,0:T(2,128)}, u32[]{:S(2)}) copy-start(f32[2,3216]{1,0:T(2,128)} %slice.133) | copy-start | bytes 77188
  125.6 6.8 %copy-start.18 = (f32[2,256,256]{2,1,0:T(8,128)S(1)}, f32[2,256,256]{2,1,0:T(8,128)}, u32[]{:S(2)}) copy-start(f32[2,256,256]{2,1,0:T(8,128)} %get-tuple-element.47) | copy-start | bytes 1572868
  125.6 6.8 %copy-start.30 = (bf16[512,128]{1,0:T(8,128)(2,1)S(1)}, bf16[512,128]{1,0:T(8,128)(2,1)}, u32[]{:S(2)}) copy-start(bf16[512,128]{1,0:T(8,128)(2,1)} %copy-done.29) | copy-start | bytes 393220
  125.6 6.8 %copy-start.35 = (f32[2,256,128]{2,1,0:T(8,128)S(1)}, f32[2,256,128]{2,1,0:T(8,128)}, u32[]{:S(2)}) copy-start(f32[2,256,128]{2,1,0:T(8,128)} %get-tuple-element.50) | copy-start | bytes 786436
  126.4 11.3 %copy-start.28 = (bf16[512,128]{1,0:T(8,128)(2,1)S(1)}, bf16[512,128]{1,0:T(8,128)(2,1)}, u32[]{:S(2)}) copy-start(bf16[512,128]{1,0:T(8,128)(2,1)} %copy-done.27) | copy-start | bytes 393220
  126.4 11.3 %copy-start.34 = (f32[2,256,128]{2,1,0:T(8,128)S(1)}, f32[2,256,128]{2,1,0:T(8,128)}, u32[]{:S(2)}) copy-start(f32[2,256,128]{2,1,0:T(8,128)} %get-tuple-element.93) | copy-start | bytes 786436
  129.4 1.3 collective-permute-start
  130.7 4.2 %collective-permute-start.1 = (f32[3,3216]{1,0:T(4,128)S(1)}, f32[3,3216]{1,0:T(4,128)S(1)}, u32[]{:S(2)}, u32[]{:S(2)}) collective-permute-start(f32[3,3216]{1,0:T(4,128)S(1)} %fusion.91), channel_id=1, source_target_pairs={{0,8},{4,12},{8,0},{12,4},{16,24},{20,28},{24,16},{28,20},{1,9},{5... | collective-permute-start | bytes 115784 | tf_op jit(solution)/shard_map/ppermute | solution.py:45
  134.9 5.1 %collective-permute-start.2 = (f32[3,3216]{1,0:T(4,128)S(1)}, f32[3,3216]{1,0:T(4,128)S(1)}, u32[]{:S(2)}, u32[]{:S(2)}) collective-permute-start(f32[3,3216]{1,0:T(4,128)S(1)} %add.123), channel_id=1, source_target_pairs={{0,16},{4,20},{8,24},{12,28},{16,0},{20,4},{24,8},{28,12},{1,17},{... | collective-permute-start | bytes 115784 | tf_op jit(solution)/shard_map/ppermute | solution.py:45
  140.0 6.8 %collective-permute-start.3 = (f32[3,3216]{1,0:T(4,128)S(1)}, f32[3,3216]{1,0:T(4,128)S(1)}, u32[]{:S(2)}, u32[]{:S(2)}) collective-permute-start(f32[3,3216]{1,0:T(4,128)S(1)} %add.124), channel_id=1, source_target_pairs={{0,1},{1,0},{2,3},{3,2},{4,5},{5,4},{6,7},{7,6},{8,9},{9,8},{10,11... | collective-permute-start | bytes 115784 | tf_op jit(solution)/shard_map/ppermute | solution.py:45
  143.1 5.8 %copy-start.51 = (f32[1,804]{1,0:T(1,128)S(1)}, f32[1,804]{1,0:T(1,128)}, u32[]{:S(2)}) copy-start(f32[1,804]{1,0:T(1,128)} %param.21) | copy-start | bytes 9652
  143.1 5.8 %copy-start.53 = (f32[1,804]{1,0:T(1,128)S(1)}, f32[1,804]{1,0:T(1,128)}, u32[]{:S(2)}) copy-start(f32[1,804]{1,0:T(1,128)} %param.20) | copy-start | bytes 9652
  143.1 5.8 %copy-start.21 = (bf16[1,128,3072]{1,2,0:T(8,128)(2,1)S(1)}, bf16[1,128,3072]{1,2,0:T(8,128)(2,1)}, u32[]{:S(2)}) copy-start(bf16[1,128,3072]{1,2,0:T(8,128)(2,1)} %get-tuple-element.69) | copy-start | bytes 2359300
  143.1 7.0 %copy-start.20 = (bf16[1,128,3072]{1,2,0:T(8,128)(2,1)S(1)}, bf16[1,128,3072]{1,2,0:T(8,128)(2,1)}, u32[]{:S(2)}) copy-start(bf16[1,128,3072]{1,2,0:T(8,128)(2,1)} %get-tuple-element.67) | copy-start | bytes 2359300
  143.1 20.6 %all-to-all-start.3 = ((bf16[4,128,1036]{1,2,0:T(8,128)(2,1)}), bf16[4,128,1036]{1,2,0:T(8,128)(2,1)S(1)}, u32[]{:S(2)}, u32[]{:S(2)}) async-start(bf16[4,128,1036]{1,2,0:T(8,128)(2,1)} %copy.170), calls=%async_computation.3 | async-start | bytes 2129920 | tf_op jit(solution)/shard_map/all_to_all | solution.py:30
  146.8 13.0 %collective-permute-start.4 = (f32[3,3216]{1,0:T(4,128)S(1)}, f32[3,3216]{1,0:T(4,128)S(1)}, u32[]{:S(2)}, u32[]{:S(2)}) collective-permute-start(f32[3,3216]{1,0:T(4,128)S(1)} %add.125), channel_id=1, source_target_pairs={{0,2},{1,3},{2,0},{3,1},{4,6},{5,7},{6,4},{7,5},{8,10},{9,11},{10,... | collective-permute-start | bytes 115784 | tf_op jit(solution)/shard_map/ppermute | solution.py:45
  148.9 14.2 %copy-start.46 = (f32[3216]{0:T(1024)S(1)}, f32[3216]{0:T(1024)}, u32[]{:S(2)}) copy-start(f32[3216]{0:T(1024)} %param.19) | copy-start | bytes 38596
  (16 other events, 17.1 us)

commit v7 on v6

--- a/solution.py
+++ b/solution.py
@@ -40,7 +40,17 @@
     size = lax.axis_size(axis)
     if size & (size - 1):
         return lax.psum(x, axis)
+    idx = lax.axis_index(axis)
     step = 1
+    while step * 4 <= size:
+        got = [x] + [
+            lax.ppermute(x, axis, [(i, i ^ (k * step)) for i in range(size)]) for k in (1, 2, 3)
+        ]
+        held = jnp.stack(got)
+        place = (idx // step) % 4
+        parts = [lax.dynamic_index_in_dim(held, place ^ m, 0, keepdims=False) for m in range(4)]
+        x = (parts[0] + parts[1]) + (parts[2] + parts[3])
+        step *= 4
     while step < size:
         x = x + lax.ppermute(x, axis, [(i, i ^ step) for i in range(size)])
         step *= 2
@@ -141,24 +151,24 @@
     local_params = lax.dynamic_slice_in_dim(head_params, first, group, 1)
     width = hidden.shape[2] // groups
     shared = jnp.concatenate([b_input[0], c_input[0]], axis=1)
-    packed = jnp.concatenate(
+    small = jnp.concatenate(
         [
-            hidden[0].reshape(tokens, groups, width).transpose(1, 0, 2),
             jnp.broadcast_to(shared[None], (groups,) + shared.shape),
             dt_raw[0].reshape(tokens, groups, group).transpose(1, 0, 2),
         ],
         axis=2,
     )
-    arrived = lax.all_to_all(packed, "ctx", 0, 0, tiled=True).reshape(groups * tokens, -1)
-    b_all = arrived[None, :, width : width + state_size]
-    c_all = arrived[None, :, width + state_size : width + 2 * state_size]
+    small_in = lax.all_to_all(small, "ctx", 0, 0, tiled=True).reshape(groups * tokens, -1)
+    x_in = to_heads(hidden, groups)
+    b_all = small_in[None, :, :state_size]
+    c_all = small_in[None, :, state_size : 2 * state_size]
     seq_resets = resets[0]
 
     def local_fn(x_arg, dt_arg, b_arg, c_arg, a_arg, bias_arg, skip_arg):
         return ssd_group(x_arg, dt_arg, b_arg, c_arg, seq_resets, a_arg, bias_arg, skip_arg)
 
-    x_heads = arrived[None, :, :width]
-    dt_heads = arrived[None, :, width + 2 * state_size :]
+    x_heads = x_in[None]
+    dt_heads = small_in[None, :, 2 * state_size :]
     y_heads, pullback = jax.vjp(
         local_fn,
         x_heads[0],

time: 168 us -> 162 us (0.964)
  waiting for transfers between devices: 30.3 us -> 19.6 us
  starting transfers between devices: 25.7 us -> 30.6 us
    ppermute x5 -> x1, waiting for transfers between devices: 12.4 us -> 1.76 us  [tree_sum(): x = x + lax.ppermute(x, axis, [(i, i ^ step) for i in range(size)])]
    all_to_all x1, waiting for transfers between devices: 11.7 us -> 2.84 us  [on_device(): lax.all_to_all(small, 'ctx', 0, 0, tiled=True).reshape(groups * tokens, -1)]
    all_to_all x2, waiting for transfers between devices: 4.85 us -> 12.1 us  [from_heads(): return lax.all_to_all(x, 'ctx', 0, 0, tiled=True)]
    convert_element_type x1 -> x3, local copies, waits for them, and re-layouts: 0.81 us -> 7.12 us  [ssd_group(): inputs = hidden.astype(jnp.float32).reshape(blocks, SPAN, heads, width)]
    ppermute x0 -> x6, starting transfers between devices: none -> 5.59 us  [tree_sum(): lax.ppermute(x, axis, [(i, i ^ k * step) for i in range(size)])]
    ppermute x5 -> x1, starting transfers between devices: 8.07 us -> 2.65 us  [tree_sum(): x = x + lax.ppermute(x, axis, [(i, i ^ step) for i in range(size)])]
    all_to_all x1 -> x2, starting transfers between devices: 4.32 us -> 8.54 us  [to_heads(): x = lax.all_to_all(x, 'ctx', 0, 0, tiled=True)]
    all_to_all x1, local copies, waits for them, and re-layouts: 3.84 us -> 0.11 us  [on_device(): lax.all_to_all(small, 'ctx', 0, 0, tiled=True).reshape(groups * tokens, -1)]
  transfers between devices with their start and end apart: 9 -> 12, of which waited for: 7 -> 6; matrix products, arithmetic and copies ran while one was open for 14% -> 21% of each run, Pallas kernels for 0% -> 0%
where the time goes in v7:
time: 162 us; the launch traced here: 161 us
  local copies, waits for them, and re-layouts  48.4 us (30%)
  other arithmetic  39.2 us (24%)
  starting transfers between devices  30.6 us (19%)
  waiting for transfers between devices  19.6 us (12%)
  matrix products  17.7 us (11%)
  between operations  5.15 us (3%)
    unnamed x145, local copies, waits for them, and re-layouts  17.7 us
    all_to_all x2, waiting for transfers between devices, from_heads(): return lax.all_to_all(x, 'ctx', 0, 0, tiled=True)  12.1 us
    all_to_all x2, starting transfers between devices, from_heads(): return lax.all_to_all(x, 'ctx', 0, 0, tiled=True)  8.63 us
    all_to_all x2, starting transfers between devices, to_heads(): x = lax.all_to_all(x, 'ctx', 0, 0, tiled=True)  8.54 us
    convert_element_type x3, local copies, waits for them, and re-layouts, ssd_group(): return output.reshape(length, heads * width).astype(jnp.bfloat16)  7.13 us
    convert_element_type x3, local copies, waits for them, and re-layouts, ssd_group(): inputs = hidden.astype(jnp.float32).reshape(blocks, SPAN, heads, width)  7.12 us
    convert_element_type x4, other arithmetic, rounded(): value.astype(jnp.bfloat16)  7.04 us
    reduce_sum x1, other arithmetic, ssd_group(): b_decayed = rounded(b_rows[:, None] * jnp.exp(tail)[..., None])  5.97 us
  transfers between devices with their start and end apart: 12, of which 6 were waited for; matrix products, arithmetic and copies ran while one was open for 21% of the time, Pallas kernels for 0%

profile of v7, /device:TPU:0, one launch (start us, length us, event | category | flops | bytes accessed | tf_op | source)
XLA Modules:
  0.0 160.6 jit_solution(7960504983975466907)
XLA Ops:
  0.7 0.9 pad_maximum_fusion.4
  1.7 0.7 reshape_squeeze.3
  2.4 0.7 pad_maximum_fusion.1
  3.1 5.2 %all-to-all-start.1 = ((bf16[4,128,268]{1,2,0:T(8,128)(2,1)}), bf16[4,128,268]{1,2,0:T(8,128)(2,1)S(1)}, u32[]{:S(2)}, u32[]{:S(2)}) async-start(bf16[4,128,268]{1,2,0:T(8,128)(2,1)} %pad_maximum_fusion.1), calls=%async_computation.1 | async-start | bytes 557056 | tf_op jit(solution)/shard_map/all_to_all | solution.py:161
  9.1 1.2 copy.143
  11.0 2.8 %all-to-all-done.1 = bf16[4,128,268]{1,2,0:T(8,128)(2,1)S(1)} async-done(((bf16[4,128,268]{1,2,0:T(8,128)(2,1)}), bf16[4,128,268]{1,2,0:T(8,128)(2,1)S(1)}, u32[]{:S(2)}, u32[]{:S(2)}) %all-to-all-start.1) | async-done | bytes 274464 | tf_op jit(solution)/shard_map/all_to_all | solution.py:161
  13.8 4.2 %all-to-all-start = ((bf16[4,128,768]{1,2,0:T(8,128)(2,1)}), bf16[4,128,768]{1,2,0:T(8,128)(2,1)}, u32[]{:S(2)}, u32[]{:S(2)}) async-start(bf16[4,128,768]{1,2,0:T(8,128)(2,1)} %bitcast.1), calls=%async_computation | async-start | bytes 1572864 | tf_op jit(solution)/shard_map/all_to_all | solution.py:23
  19.9 0.7 copy-done.18
  20.6 1.8 %multiply_convert_fusion.2 = bf16[2,12,256,128]{3,2,1,0:T(8,128)(2,1)} fusion(f32[2,12,256]{2,1,0:T(8,128)S(1)} %get-tuple-element.82, f32[2,256,128]{2,1,0:T(8,128)S(1)} %bitcast_convert_fusion), kind=kLoop, calls=%fused_computation.20 | loop fusion | flops 1572864 | bytes 1859584 | tf_op jit(solution)/shard_map/jvp()/convert_element_type | solution.py:61
  22.9 1.7 %multiply_convert_fusion = bf16[2,12,256,256]{3,2,1,0:T(8,128)(2,1)S(1)} fusion(f32[2,12,256]{2,1,0:T(8,128)S(1)} %fusion.50, f32[2,256,256]{2,1,0:T(8,128)S(1)} %fusion.98, pred[256,256]{1,0:T(8,128)(4,1)S(1)} %iota_compare_fusion), kind=kLoop, calls=%fused_computation.6 | loop fusion | flops 7864320 | bytes 3760128 | tf_op jit(solution)/shard_map/jvp()/convert_element_type | solution.py:61
  24.6 0.7 copy-done.20
  25.3 1.8 %multiply_convert_fusion.1 = bf16[2,12,256,128]{3,2,1,0:T(8,128)(2,1)} fusion(f32[2,12,256]{2,1,0:T(8,128)S(1)} %get-tuple-element.81, f32[2,256,128]{2,1,0:T(8,128)S(1)} %bitcast_convert_fusion.1), kind=kLoop, calls=%fused_computation.19 | loop fusion | flops 1572864 | bytes 1859584 | tf_op jit(solution)/shard_map/jvp()/convert_element_type | solution.py:61
  27.1 0.8 fusion.76
  27.9 2.9 %copy.144 = f32[4,128,768]{1,0,2:T(4,128)} copy(bf16[4,128,768]{1,2,0:T(8,128)(2,1)} %all-to-all-done) | data formatting | bytes 2359296 | tf_op jit(solution)/shard_map/jvp()/convert_element_type | solution.py:73
  30.8 3.4 %reshape.339 = f32[2,256,12,64]{1,0,3,2:T(2,128)} reshape(f32[4,128,768]{1,0,2:T(4,128)} %copy.144) | data formatting | bytes 3145728 | tf_op jit(solution)/shard_map/jvp()/convert_element_type | solution.py:73
  34.2 1.7 %multiply_convert_fusion.5 = bf16[2,256,12,64]{1,3,2,0:T(8,128)(2,1)S(1)} fusion(f32[2,256,12,64]{1,0,3,2:T(2,128)} %reshape.339, f32[2,256,12]{1,2,0:T(8,128)S(1)} %copy.147), kind=kLoop, calls=%fused_computation.56 | loop fusion | flops 786432 | bytes 2383872 | tf_op jit(solution)/shard_map/jvp()/convert_element_type | solution.py:61
  36.1 1.8 %multiply_convert_fusion.6 = (bf16[1,12,128,64]{2,3,1,0:T(8,128)(2,1)S(1)}, f32[1,12,128,64]{2,3,1,0:T(8,128)}) fusion(f32[]{:T(128)} %bitcast.12, f32[12]{0:T(128)S(1)} %get-tuple-element.60, bf16[2,256,12,64]{1,3,2,0:T(8,128)(2,1)S(1)} %multiply_convert_fusion.5, bf16[2,12,256,128]{3,2,1,0:T(8,128)(2,1)S(1)} %copy-done.7), kind=kOutput, calls=%fused_computation.86 | convolution fusion | flops 50626560 | bytes 2949172 | tf_op jit(solution)/shard_map/jvp()/slice | solution.py:94
  38.0 1.1 fusion.99
  40.6 1.7 %copy.153 = bf16[2,256,12,64]{1,0,3,2:T(2,128)(2,1)} copy(bf16[2,256,12,64]{1,3,2,0:T(8,128)(2,1)S(1)} %fusion.27) | data formatting | bytes 1572864 | tf_op jit(solution)/shard_map/jvp()/convert_element_type | solution.py:98
  42.3 3.3 %convert_element_type.162 = bf16[4,128,768]{1,0,2:T(4,128)(2,1)} reshape(bf16[2,256,12,64]{1,0,3,2:T(2,128)(2,1)} %copy.153) | data formatting | bytes 1572864 | tf_op jit(solution)/shard_map/jvp()/convert_element_type | solution.py:98
  45.6 2.1 %copy.154 = bf16[4,128,768]{1,2,0:T(8,128)(2,1)} copy(bf16[4,128,768]{1,0,2:T(4,128)(2,1)} %convert_element_type.162) | data formatting | bytes 1572864 | tf_op jit(solution)/shard_map/jvp()/convert_element_type | solution.py:98
  47.7 4.4 %all-to-all-start.2 = ((bf16[4,128,768]{1,2,0:T(8,128)(2,1)}), bf16[4,128,768]{1,2,0:T(8,128)(2,1)}, u32[]{:S(2)}, u32[]{:S(2)}) async-start(bf16[4,128,768]{1,2,0:T(8,128)(2,1)} %copy.154), calls=%async_computation.2 | async-start | bytes 1572864 | tf_op jit(solution)/shard_map/all_to_all | solution.py:30
  52.1 0.8 slice.106
  52.9 2.3 %copy.155 = bf16[1,128,3072]{1,2,0:T(8,128)(2,1)} copy(bf16[1,128,3072]{2,1,0:T(8,128)(2,1)} %param.13) | data formatting | bytes 1572864 | tf_op args[1]
  55.2 2.3 %copy.156 = bf16[1,128,3072]{1,2,0:T(8,128)(2,1)} copy(bf16[1,128,3072]{2,1,0:T(8,128)(2,1)} %param.18) | data formatting | bytes 1572864 | tf_op args[6]
  57.5 4.8 %all-to-all-done.2 = bf16[4,128,768]{1,2,0:T(8,128)(2,1)} async-done(((bf16[4,128,768]{1,2,0:T(8,128)(2,1)}), bf16[4,128,768]{1,2,0:T(8,128)(2,1)}, u32[]{:S(2)}, u32[]{:S(2)}) %all-to-all-start.2) | async-done | bytes 786464 | tf_op jit(solution)/shard_map/all_to_all | solution.py:30
  62.3 1.3 convert_element_type.194
  64.8 1.5 fusion.16
  66.3 2.6 %fusion.25 = (bf16[1,128,3072]{1,2,0:T(8,128)(2,1)}, bf16[1,128,3072]{1,2,0:T(8,128)(2,1)}, bf16[1,128,3072]{1,2,0:T(8,128)(2,1)}) fusion(bf16[1,128,3072]{1,2,0:T(8,128)(2,1)S(1)} %copy-done.11, f32[1,128,3072]{1,2,0:T(8,128)S(1)} %get-tuple-element.66, bf16[1,128,3072]{1,2,0:T(8,128)(2,1)S(1)} %copy-done.12, f32[128]{0:T(128)S(1)} %fusion.86, ...), kind=kLoop, calls=%fused_computation.45 | loop fusion | flops 8650752 | bytes 7091200 | tf_op jit(solution)/shard_map/convert_element_type | solution.py:122
  69.0 4.3 %all-to-all-start.3 = ((bf16[4,128,768]{1,2,0:T(8,128)(2,1)}), bf16[4,128,768]{1,2,0:T(8,128)(2,1)}, u32[]{:S(2)}, u32[]{:S(2)}) async-start(bf16[4,128,768]{1,2,0:T(8,128)(2,1)} %bitcast.179), calls=%async_computation.3 | async-start | bytes 1572864 | tf_op jit(solution)/shard_map/all_to_all | solution.py:23
  74.1 1.3 fusion.84
  78.6 1.5 dynamic_update_slice.7
  80.1 1.3 slice.131
  82.1 2.3 %copy.171 = bf16[1,128,3072]{2,1,0:T(8,128)(2,1)} copy(bf16[1,128,3072]{1,2,0:T(8,128)(2,1)} %get-tuple-element.69) | data formatting | bytes 1572864
  84.4 2.3 %copy.173 = bf16[1,128,3072]{2,1,0:T(8,128)(2,1)} copy(bf16[1,128,3072]{1,2,0:T(8,128)(2,1)} %get-tuple-element.67) | data formatting | bytes 1572864
  86.7 2.6 %copy.157 = bf16[4,128,768]{1,0,2:T(4,128)(2,1)} copy(bf16[4,128,768]{1,2,0:T(8,128)(2,1)} %all-to-all-done.3) | data formatting | bytes 1572864 | tf_op jit(solution)/shard_map/all_to_all | solution.py:23
  89.3 3.0 %squeeze_broadcast_in_dim_reshape.4 = bf16[2,256,12,64]{1,0,3,2:T(2,128)(2,1)} reshape(bf16[4,128,768]{1,0,2:T(4,128)(2,1)} %copy.157) | data formatting | bytes 1572864 | tf_op jit(solution)/shard_map/squeeze;broadcast_in_dim;reshape | solution.py:190
  92.3 2.1 %convolution_convert_fusion.3 = bf16[2,12,128,64]{2,3,1,0:T(8,128)(2,1)S(1)} fusion(bf16[2,12,256,128]{3,2,1,0:T(8,128)(2,1)} %multiply_convert_fusion.1, bf16[2,256,12,64]{1,0,3,2:T(2,128)(2,1)} %squeeze_broadcast_in_dim_reshape.4), kind=kOutput, calls=%fused_computation.58 | convolution fusion | flops 100859904 | bytes 2752512 | tf_op jit(solution)/shard_map/transpose(jvp(chtn,chnp->cthp))/dot_general | solution.py:96
  94.4 1.9 %convolution_convert_fusion.2 = bf16[2,12,256,128]{3,2,1,0:T(8,128)(2,1)} fusion(bf16[2,12,128,64]{2,3,1,0:T(8,128)(2,1)S(1)} %concatenate.29, bf16[2,256,12,64]{1,0,3,2:T(2,128)(2,1)S(1)} %copy-done), kind=kOutput, calls=%fused_computation.32 | convolution fusion | flops 101449728 | bytes 2752512 | tf_op jit(solution)/shard_map/transpose(jvp(chtn,chnp->cthp))/dot_general | solution.py:96
  96.3 2.7 %convolution_convert_fusion = bf16[2,12,256,256]{3,2,1,0:T(8,128)(2,1)} fusion(bf16[2,256,12,64]{1,3,2,0:T(8,128)(2,1)S(1)} %copy-done.5, bf16[2,256,12,64]{1,0,3,2:T(2,128)(2,1)S(1)} %copy-done), kind=kOutput, calls=%fused_computation.24 | convolution fusion | flops 202899456 | bytes 4718592 | tf_op jit(solution)/shard_map/transpose(jvp(chts,cshp->cthp))/dot_general | solution.py:82
  99.0 1.8 %fusion.33 = f32[2,12,64,256]{3,2,1,0:T(8,128)} fusion(bf16[2,12,256,256]{3,2,1,0:T(8,128)(2,1)S(1)} %multiply_convert_fusion, bf16[2,256,12,64]{1,0,3,2:T(2,128)(2,1)S(1)} %copy-done), kind=kOutput, calls=%fused_computation.67 | convolution fusion | flops 201326592 | bytes 5505024 | tf_op jit(solution)/shard_map/transpose(jvp(chts,cshp->cthp))/dot_general | solution.py:82
  100.7 0.8 fusion.41
  101.6 1.0 fusion.45
  102.8 1.5 convolution_convert_fusion.1
  104.3 6.0 %fusion.7 = (f32[2,256,128]{2,1,0:T(8,128)}, f32[2,12,256]{2,1,0:T(8,128)S(1)}, f32[2,12,256]{2,1,0:T(8,128)}, f32[2,256,128]{2,1,0:T(8,128)}) fusion(bf16[2,12,256,128]{3,2,1,0:T(8,128)(2,1)S(1)} %convolution_convert_fusion.1, f32[2,12,256]{2,1,0:T(8,128)S(1)} %copy-done.32, f32[2,256,128]{2,1,0:T(8,128)S(1)} %copy-done.19, f32[2,256,128]{2,1,0:T(8,128)} %copy-done.20, ...), kind=kLoop, calls=%fused_computation.15 | loop fusion | flops 7720960 | bytes 4292608 | tf_op jit(solution)/shard_map/transpose(jvp())/reduce_sum | solution.py:84
  111.1 5.7 %fusion.6 = (f32[2,12,256]{2,1,0:T(8,128)S(1)}, f32[2,12,256]{2,1,0:T(8,128)S(1)}, f32[2,256,256]{2,1,0:T(8,128)}) fusion(bf16[2,12,256,256]{3,2,1,0:T(8,128)(2,1)S(1)} %copy-done.10, f32[2,12,256]{2,1,0:T(8,128)S(1)} %copy-done.26, f32[2,256,256]{2,1,0:T(8,128)} %copy-done.15, pred[256,256]{1,0:T(8,128)(4,1)S(1)} %copy-done.35), kind=kLoop, calls=%fused_computation.10 | loop fusion | flops 18731008 | bytes 4333568 | tf_op jit(solution)/shard_map/transpose(jvp())/reduce_sum | solution.py:79
  117.3 2.5 %fusion.28 = bf16[2,256,12,64]{1,3,2,0:T(8,128)(2,1)S(1)} fusion(f32[2,12,64,256]{3,2,1,0:T(8,128)S(1)} %copy-done.13, bf16[2,12,256,128]{3,2,1,0:T(8,128)(2,1)S(1)} %copy-done.8, f32[12]{0:T(128)S(1)} %copy-done.50, f32[]{:T(128)} %bitcast.12, bf16[2,12,128,64]{2,3,1,0:T(8,128)(2,1)S(1)} %copy-done.17), kind=kOutput, calls=%fused_computation.57 | convolution fusion | flops 303071232 | bytes 4129284 | tf_op jit(solution)/shard_map/transpose(jvp(chsn,cshp->chnp))/dot_general | solution.py:85
  120.6 1.0 fusion.92
  121.6 0.7 bitcast_multiply_fusion.4
  122.3 1.7 %multiply_reduce_fusion = f32[768]{0:T(1024)S(1)} fusion(bf16[4,128,768]{1,2,0:T(8,128)(2,1)} %all-to-all-done.3, bf16[4,128,768]{1,2,0:T(8,128)(2,1)} %all-to-all-done), kind=kLoop, calls=%fused_computation.51 | loop fusion | flops 1572096 | bytes 1575936 | tf_op jit(solution)/shard_map/transpose(jvp())/reduce_sum | solution.py:97
  124.9 1.7 %collective-permute-start.1 = (f32[3,3216]{1,0:T(4,128)S(1)}, f32[3,3216]{1,0:T(4,128)S(1)}, u32[]{:S(2)}, u32[]{:S(2)}) collective-permute-start(f32[3,3216]{1,0:T(4,128)S(1)} %get-tuple-element.80), channel_id=1, source_target_pairs={{0,8},{4,12},{8,0},{12,4},{16,24},{20,28},{24,16},{28,20},{1,9},{5... | collective-permute-start | bytes 115784 | tf_op jit(solution)/shard_map/ppermute | solution.py:47
  127.4 1.7 %collective-permute-done.1 = f32[3,3216]{1,0:T(4,128)S(1)} collective-permute-done((f32[3,3216]{1,0:T(4,128)S(1)}, f32[3,3216]{1,0:T(4,128)S(1)}, u32[]{:S(2)}, u32[]{:S(2)}) %collective-permute-start.1) | collective-permute-done | bytes 38624 | tf_op jit(solution)/shard_map/ppermute | solution.py:47
  129.1 1.2 collective-permute-done.2
  130.4 2.6 %collective-permute-start.3 = (f32[3,3216]{1,0:T(4,128)S(1)}, f32[3,3216]{1,0:T(4,128)S(1)}, u32[]{:S(2)}, u32[]{:S(2)}) collective-permute-start(f32[3,3216]{1,0:T(4,128)S(1)} %add_bitcast_fusion), channel_id=1, source_target_pairs={{0,16},{4,20},{8,24},{12,28},{16,0},{20,4},{24,8},{28,12},{1,17},{... | collective-permute-start | bytes 115784 | tf_op jit(solution)/shard_map/ppermute | solution.py:55
  133.7 0.8 copy.160
  134.7 1.8 %collective-permute-done.3 = f32[3,3216]{1,0:T(4,128)S(1)} collective-permute-done((f32[3,3216]{1,0:T(4,128)S(1)}, f32[3,3216]{1,0:T(4,128)S(1)}, u32[]{:S(2)}, u32[]{:S(2)}) %collective-permute-start.3) | collective-permute-done | bytes 38624 | tf_op jit(solution)/shard_map/ppermute | solution.py:55
  136.5 2.1 %collective-permute-start.4 = (f32[3,3216]{1,0:T(4,128)S(1)}, f32[3,3216]{1,0:T(4,128)S(1)}, u32[]{:S(2)}, u32[]{:S(2)}) collective-permute-start(f32[3,3216]{1,0:T(4,128)S(1)} %fusion.118), channel_id=1, source_target_pairs={{0,1},{1,0},{2,3},{3,2},{4,5},{5,4},{6,7},{7,6},{8,9},{9,8},{10,11... | collective-permute-start | bytes 115784 | tf_op jit(solution)/shard_map/ppermute | solution.py:47
  138.6 1.5 collective-permute-start.5
  140.6 1.1 copy.169
  141.7 4.3 %all-to-all-start.4 = ((bf16[4,128,1036]{1,2,0:T(8,128)(2,1)}), bf16[4,128,1036]{1,2,0:T(8,128)(2,1)S(1)}, u32[]{:S(2)}, u32[]{:S(2)}) async-start(bf16[4,128,1036]{1,2,0:T(8,128)(2,1)} %copy.169), calls=%async_computation.4 | async-start | bytes 2129920 | tf_op jit(solution)/shard_map/all_to_all | solution.py:30
  150.1 7.2 %all-to-all-done.4 = bf16[4,128,1036]{1,2,0:T(8,128)(2,1)S(1)} async-done(((bf16[4,128,1036]{1,2,0:T(8,128)(2,1)}), bf16[4,128,1036]{1,2,0:T(8,128)(2,1)S(1)}, u32[]{:S(2)}, u32[]{:S(2)}) %all-to-all-start.4) | async-done | bytes 1060896 | tf_op jit(solution)/shard_map/all_to_all | solution.py:30
  157.4 1.2 copy.172
  158.6 0.7 copy.174
  159.3 0.7 copy.175
  (220 shorter events, 17.7 us)
Async XLA Ops:
  0.6 7.7 %slice-start = ((f32[3216]{0:T(1024)}), f32[144]{0:T(256)S(1)}, s32[]{:S(2)}) async-start(f32[3216]{0:T(1024)} %param.19), calls=%async_computation.5 | async-start | bytes 2048 | tf_op jit(solution)/shard_map/slice | solution.py:149
  0.7 7.8 %copy-start.63 = (s32[1,2]{1,0:T(1,128)S(1)}, s32[1,2]{1,0:T(1,128)}, u32[]{:S(2)}) copy-start(s32[1,2]{1,0:T(1,128)} %param.17) | copy-start | bytes 28
  0.7 8.4 %copy-start.33 = (bf16[1,128,3072]{2,1,0:T(8,128)(2,1)S(1)}, bf16[1,128,3072]{2,1,0:T(8,128)(2,1)}, u32[]{:S(2)}) copy-start(bf16[1,128,3072]{2,1,0:T(8,128)(2,1)} %param.12) | copy-start | bytes 2359300
  3.1 10.7 %all-to-all-start.1 = ((bf16[4,128,268]{1,2,0:T(8,128)(2,1)}), bf16[4,128,268]{1,2,0:T(8,128)(2,1)S(1)}, u32[]{:S(2)}, u32[]{:S(2)}) async-start(bf16[4,128,268]{1,2,0:T(8,128)(2,1)} %pad_maximum_fusion.1), calls=%async_computation.1 | async-start | bytes 557056 | tf_op jit(solution)/shard_map/all_to_all | solution.py:161
  8.4 14.5 %copy-start.34 = (pred[256,256]{1,0:T(8,128)(4,1)}, pred[256,256]{1,0:T(8,128)(4,1)S(1)}, u32[]{:S(2)}) copy-start(pred[256,256]{1,0:T(8,128)(4,1)S(1)} %iota_compare_fusion) | copy-start | bytes 196612
  11.0 7.4 %copy-start.51 = (f32[3,12]{1,0:T(4,128)}, f32[3,12]{1,0:T(4,128)S(1)}, u32[]{:S(2)}) copy-start(f32[3,12]{1,0:T(4,128)S(1)} %constant_dynamic-slice_fusion) | copy-start | bytes 436
  11.0 7.4 %copy-start.54 = (f32[12]{0:T(128)}, f32[12]{0:T(128)S(1)}, u32[]{:S(2)}) copy-start(f32[12]{0:T(128)S(1)} %get-tuple-element.86) | copy-start | bytes 148
  11.0 7.4 %copy-start.56 = (f32[12]{0:T(128)}, f32[12]{0:T(128)S(1)}, u32[]{:S(2)}) copy-start(f32[12]{0:T(128)S(1)} %get-tuple-element.87) | copy-start | bytes 148
  11.0 28.1 %copy-start.52 = (f32[12]{0:T(128)}, f32[12]{0:T(128)S(1)}, u32[]{:S(2)}) copy-start(f32[12]{0:T(128)S(1)} %get-tuple-element.85) | copy-start | bytes 148
  13.8 14.1 %all-to-all-start = ((bf16[4,128,768]{1,2,0:T(8,128)(2,1)}), bf16[4,128,768]{1,2,0:T(8,128)(2,1)}, u32[]{:S(2)}, u32[]{:S(2)}) async-start(bf16[4,128,768]{1,2,0:T(8,128)(2,1)} %bitcast.1), calls=%async_computation | async-start | bytes 1572864 | tf_op jit(solution)/shard_map/all_to_all | solution.py:23
  19.4 7.7 %copy-start.25 = (f32[2,12,256]{2,1,0:T(8,128)}, f32[2,12,256]{2,1,0:T(8,128)S(1)}, u32[]{:S(2)}) copy-start(f32[2,12,256]{2,1,0:T(8,128)S(1)} %fusion.50) | copy-start | bytes 73732
  19.7 2.9 %copy-start.31 = (f32[2,12,256]{2,1,0:T(8,128)}, f32[2,12,256]{2,1,0:T(8,128)S(1)}, u32[]{:S(2)}) copy-start(f32[2,12,256]{2,1,0:T(8,128)S(1)} %get-tuple-element.82) | copy-start | bytes 73732
  19.7 4.9 %copy-start.38 = (f32[2,12,256]{2,1,0:T(8,128)}, f32[2,12,256]{2,1,0:T(8,128)S(1)}, u32[]{:S(2)}) copy-start(f32[2,12,256]{2,1,0:T(8,128)S(1)} %get-tuple-element.81) | copy-start | bytes 73732
  19.8 2.8 %copy-start.21 = (bf16[512,128]{1,0:T(8,128)(2,1)}, bf16[512,128]{1,0:T(8,128)(2,1)S(1)}, u32[]{:S(2)}) copy-start(bf16[512,128]{1,0:T(8,128)(2,1)S(1)} %copy.150) | copy-start | bytes 393220
  22.4 11.8 %copy-start.36 = (f32[2,256,12]{1,2,0:T(8,128)}, f32[2,256,12]{1,2,0:T(8,128)S(1)}, u32[]{:S(2)}) copy-start(f32[2,256,12]{1,2,0:T(8,128)S(1)} %copy.147) | copy-start | bytes 73732
  22.6 2.0 %copy-start.23 = (bf16[512,128]{1,0:T(8,128)(2,1)}, bf16[512,128]{1,0:T(8,128)(2,1)S(1)}, u32[]{:S(2)}) copy-start(bf16[512,128]{1,0:T(8,128)(2,1)S(1)} %copy.149) | copy-start | bytes 393220
  27.9 8.0 %copy-start.58 = (f32[12]{0:T(128)}, f32[12]{0:T(128)S(1)}, u32[]{:S(2)}) copy-start(f32[12]{0:T(128)S(1)} %get-tuple-element.60) | copy-start | bytes 148
  35.9 2.1 %copy-start.4 = (bf16[2,256,12,64]{1,3,2,0:T(8,128)(2,1)}, bf16[2,256,12,64]{1,3,2,0:T(8,128)(2,1)S(1)}, u32[]{:S(2)}) copy-start(bf16[2,256,12,64]{1,3,2,0:T(8,128)(2,1)S(1)} %multiply_convert_fusion.5) | copy-start | bytes 2359300
  47.7 14.6 %all-to-all-start.2 = ((bf16[4,128,768]{1,2,0:T(8,128)(2,1)}), bf16[4,128,768]{1,2,0:T(8,128)(2,1)}, u32[]{:S(2)}, u32[]{:S(2)}) async-start(bf16[4,128,768]{1,2,0:T(8,128)(2,1)} %copy.154), calls=%async_computation.2 | async-start | bytes 1572864 | tf_op jit(solution)/shard_map/all_to_all | solution.py:30
  68.9 4.4 %copy-start.64 = (s32[8]{0:T(128)S(1)}, s32[8]{0:T(128)}, u32[]{:S(2)}) copy-start(s32[8]{0:T(128)} %param.23) | copy-start | bytes 100
  68.9 5.0 %copy-start.60 = (s32[8]{0:T(128)S(1)}, s32[8]{0:T(128)}, u32[]{:S(2)}) copy-start(s32[8]{0:T(128)} %param.22) | copy-start | bytes 100
  68.9 9.0 %copy-start.47 = (f32[1,804]{1,0:T(1,128)S(1)}, f32[1,804]{1,0:T(1,128)}, u32[]{:S(2)}) copy-start(f32[1,804]{1,0:T(1,128)} %param.21) | copy-start | bytes 9652
  69.0 9.0 %copy-start.48 = (f32[1,804]{1,0:T(1,128)S(1)}, f32[1,804]{1,0:T(1,128)}, u32[]{:S(2)}) copy-start(f32[1,804]{1,0:T(1,128)} %param.20) | copy-start | bytes 9652
  69.0 17.7 %all-to-all-start.3 = ((bf16[4,128,768]{1,2,0:T(8,128)(2,1)}), bf16[4,128,768]{1,2,0:T(8,128)(2,1)}, u32[]{:S(2)}, u32[]{:S(2)}) async-start(bf16[4,128,768]{1,2,0:T(8,128)(2,1)} %bitcast.179), calls=%async_computation.3 | async-start | bytes 1572864 | tf_op jit(solution)/shard_map/all_to_all | solution.py:23
  92.3 2.1 %copy-start = (bf16[2,256,12,64]{1,0,3,2:T(2,128)(2,1)S(1)}, bf16[2,256,12,64]{1,0,3,2:T(2,128)(2,1)}, u32[]{:S(2)}) copy-start(bf16[2,256,12,64]{1,0,3,2:T(2,128)(2,1)} %squeeze_broadcast_in_dim_reshape.4) | copy-start | bytes 2359300
  94.4 7.2 %copy-start.16 = (bf16[2,12,128,64]{2,3,1,0:T(8,128)(2,1)}, bf16[2,12,128,64]{2,3,1,0:T(8,128)(2,1)S(1)}, u32[]{:S(2)}) copy-start(bf16[2,12,128,64]{2,3,1,0:T(8,128)(2,1)S(1)} %convolution_convert_fusion.3) | copy-start | bytes 1179652
  99.0 2.6 %copy-start.27 = (f32[1,12,128,64]{2,3,1,0:T(8,128)S(1)}, f32[1,12,128,64]{2,3,1,0:T(8,128)}, u32[]{:S(2)}) copy-start(f32[1,12,128,64]{2,3,1,0:T(8,128)} %get-tuple-element.91) | copy-start | bytes 1179652
  99.0 2.6 %copy-start.59 = (f32[12]{0:T(128)S(1)}, f32[12]{0:T(128)}, u32[]{:S(2)}) copy-start(f32[12]{0:T(128)} %copy-done.58) | copy-start | bytes 148
  99.0 3.7 %copy-start.62 = (f32[12]{0:T(128)S(1)}, f32[12]{0:T(128)}, u32[]{:S(2)}) copy-start(f32[12]{0:T(128)} %get-tuple-element.57) | copy-start | bytes 148
  99.0 3.7 %copy-start.61 = (f32[12]{0:T(128)S(1)}, f32[12]{0:T(128)}, u32[]{:S(2)}) copy-start(f32[12]{0:T(128)} %get-tuple-element.58) | copy-start | bytes 148
  100.7 2.0 %copy-start.6 = (bf16[2,256,12,64]{1,3,2,0:T(8,128)(2,1)S(1)}, bf16[2,256,12,64]{1,3,2,0:T(8,128)(2,1)}, u32[]{:S(2)}) copy-start(bf16[2,256,12,64]{1,3,2,0:T(8,128)(2,1)} %copy-done.4) | copy-start | bytes 2359300
  101.6 2.6 %copy-start.19 = (f32[2,256,128]{2,1,0:T(8,128)S(1)}, f32[2,256,128]{2,1,0:T(8,128)}, u32[]{:S(2)}) copy-start(f32[2,256,128]{2,1,0:T(8,128)} %copy-done.18) | copy-start | bytes 786436
  101.6 2.6 %copy-start.32 = (f32[2,12,256]{2,1,0:T(8,128)S(1)}, f32[2,12,256]{2,1,0:T(8,128)}, u32[]{:S(2)}) copy-start(f32[2,12,256]{2,1,0:T(8,128)} %copy-done.31) | copy-start | bytes 73732
  104.3 6.8 %copy-start.10 = (bf16[2,12,256,256]{3,2,1,0:T(8,128)(2,1)S(1)}, bf16[2,12,256,256]{3,2,1,0:T(8,128)(2,1)}, u32[]{:S(2)}) copy-start(bf16[2,12,256,256]{3,2,1,0:T(8,128)(2,1)} %convolution_convert_fusion) | copy-start | bytes 9437188
  104.3 6.8 %copy-start.26 = (f32[2,12,256]{2,1,0:T(8,128)S(1)}, f32[2,12,256]{2,1,0:T(8,128)}, u32[]{:S(2)}) copy-start(f32[2,12,256]{2,1,0:T(8,128)} %copy-done.25) | copy-start | bytes 73732
  104.3 6.8 %copy-start.35 = (pred[256,256]{1,0:T(8,128)(4,1)S(1)}, pred[256,256]{1,0:T(8,128)(4,1)}, u32[]{:S(2)}) copy-start(pred[256,256]{1,0:T(8,128)(4,1)} %copy-done.34) | copy-start | bytes 196612
  111.1 5.8 %copy-start.40 = (f32[2,12,256]{2,1,0:T(8,128)S(1)}, f32[2,12,256]{2,1,0:T(8,128)}, u32[]{:S(2)}) copy-start(f32[2,12,256]{2,1,0:T(8,128)} %copy-done.39) | copy-start | bytes 73732
  111.1 5.8 %copy-start.41 = (f32[2,12,256]{2,1,0:T(8,128)S(1)}, f32[2,12,256]{2,1,0:T(8,128)}, u32[]{:S(2)}) copy-start(f32[2,12,256]{2,1,0:T(8,128)} %get-tuple-element.94) | copy-start | bytes 73732
  111.1 6.1 %copy-start.8 = (bf16[2,12,256,128]{3,2,1,0:T(8,128)(2,1)S(1)}, bf16[2,12,256,128]{3,2,1,0:T(8,128)(2,1)}, u32[]{:S(2)}) copy-start(bf16[2,12,256,128]{3,2,1,0:T(8,128)(2,1)} %multiply_convert_fusion.2) | copy-start | bytes 4718596
  111.1 6.1 %copy-start.13 = (f32[2,12,64,256]{3,2,1,0:T(8,128)S(1)}, f32[2,12,64,256]{3,2,1,0:T(8,128)}, u32[]{:S(2)}) copy-start(f32[2,12,64,256]{3,2,1,0:T(8,128)} %fusion.33) | copy-start | bytes 4718596
  111.1 6.1 %copy-start.17 = (bf16[2,12,128,64]{2,3,1,0:T(8,128)(2,1)S(1)}, bf16[2,12,128,64]{2,3,1,0:T(8,128)(2,1)}, u32[]{:S(2)}) copy-start(bf16[2,12,128,64]{2,3,1,0:T(8,128)(2,1)} %copy-done.16) | copy-start | bytes 1179652
  111.1 6.1 %copy-start.50 = (f32[12]{0:T(128)S(1)}, f32[12]{0:T(128)}, u32[]{:S(2)}) copy-start(f32[12]{0:T(128)} %get-tuple-element.59) | copy-start | bytes 148
  117.2 2.6 %copy-start.1 = (bf16[2,256,12,64]{1,0,3,2:T(2,128)(2,1)S(1)}, bf16[2,256,12,64]{1,0,3,2:T(2,128)(2,1)}, u32[]{:S(2)}) copy-start(bf16[2,256,12,64]{1,0,3,2:T(2,128)(2,1)} %squeeze_broadcast_in_dim_reshape.4) | copy-start | bytes 2359300
  117.2 2.6 %copy-start.3 = (f32[2,256,12,64]{1,0,3,2:T(2,128)S(1)}, f32[2,256,12,64]{1,0,3,2:T(2,128)}, u32[]{:S(2)}) copy-start(f32[2,256,12,64]{1,0,3,2:T(2,128)} %reshape.339) | copy-start | bytes 4718596
  117.2 2.6 %copy-start.37 = (f32[2,256,12]{1,2,0:T(8,128)S(1)}, f32[2,256,12]{1,2,0:T(8,128)}, u32[]{:S(2)}) copy-start(f32[2,256,12]{1,2,0:T(8,128)} %copy-done.36) | copy-start | bytes 73732
  117.3 2.6 %copy-start.53 = (f32[12]{0:T(128)S(1)}, f32[12]{0:T(128)}, u32[]{:S(2)}) copy-start(f32[12]{0:T(128)} %copy-done.52) | copy-start | bytes 148
  120.4 4.2 %copy-start.44 = (f32[3072]{0:T(1024)S(1)}, f32[3072]{0:T(1024)}, u32[]{:S(2)}) copy-start(f32[3072]{0:T(1024)} %get-tuple-element.48) | copy-start | bytes 36868
  120.5 4.3 %copy-start.42 = (f32[2,3216]{1,0:T(2,128)S(1)}, f32[2,3216]{1,0:T(2,128)}, u32[]{:S(2)}) copy-start(f32[2,3216]{1,0:T(2,128)} %slice.131) | copy-start | bytes 77188
  120.5 6.3 %copy-start.14 = (f32[2,256,256]{2,1,0:T(8,128)S(1)}, f32[2,256,256]{2,1,0:T(8,128)}, u32[]{:S(2)}) copy-start(f32[2,256,256]{2,1,0:T(8,128)} %get-tuple-element.47) | copy-start | bytes 1572868
  120.5 6.2 %copy-start.24 = (bf16[512,128]{1,0:T(8,128)(2,1)S(1)}, bf16[512,128]{1,0:T(8,128)(2,1)}, u32[]{:S(2)}) copy-start(bf16[512,128]{1,0:T(8,128)(2,1)} %copy-done.23) | copy-start | bytes 393220
  120.5 6.2 %copy-start.30 = (f32[2,256,128]{2,1,0:T(8,128)S(1)}, f32[2,256,128]{2,1,0:T(8,128)}, u32[]{:S(2)}) copy-start(f32[2,256,128]{2,1,0:T(8,128)} %get-tuple-element.50) | copy-start | bytes 786436
  122.3 10.8 %copy-start.22 = (bf16[512,128]{1,0:T(8,128)(2,1)S(1)}, bf16[512,128]{1,0:T(8,128)(2,1)}, u32[]{:S(2)}) copy-start(bf16[512,128]{1,0:T(8,128)(2,1)} %copy-done.21) | copy-start | bytes 393220
  122.3 10.8 %copy-start.29 = (f32[2,256,128]{2,1,0:T(8,128)S(1)}, f32[2,256,128]{2,1,0:T(8,128)}, u32[]{:S(2)}) copy-start(f32[2,256,128]{2,1,0:T(8,128)} %get-tuple-element.95) | copy-start | bytes 786436
  124.8 2.6 %collective-permute-start = (f32[3,3216]{1,0:T(4,128)S(1)}, f32[3,3216]{1,0:T(4,128)S(1)}, u32[]{:S(2)}, u32[]{:S(2)}) collective-permute-start(f32[3,3216]{1,0:T(4,128)S(1)} %get-tuple-element.80), channel_id=1, source_target_pairs={{0,4},{4,0},{8,12},{12,8},{16,20},{20,16},{24,28},{28,24},{1,5},{5... | collective-permute-start | bytes 115784 | tf_op jit(solution)/shard_map/ppermute | solution.py:47
  124.9 4.2 %collective-permute-start.1 = (f32[3,3216]{1,0:T(4,128)S(1)}, f32[3,3216]{1,0:T(4,128)S(1)}, u32[]{:S(2)}, u32[]{:S(2)}) collective-permute-start(f32[3,3216]{1,0:T(4,128)S(1)} %get-tuple-element.80), channel_id=1, source_target_pairs={{0,8},{4,12},{8,0},{12,4},{16,24},{20,28},{24,16},{28,20},{1,9},{5... | collective-permute-start | bytes 115784 | tf_op jit(solution)/shard_map/ppermute | solution.py:47
  126.5 3.8 %collective-permute-start.2 = (f32[3,3216]{1,0:T(4,128)S(1)}, f32[3,3216]{1,0:T(4,128)S(1)}, u32[]{:S(2)}, u32[]{:S(2)}) collective-permute-start(f32[3,3216]{1,0:T(4,128)S(1)} %get-tuple-element.80), channel_id=1, source_target_pairs={{0,12},{4,8},{8,4},{12,0},{16,28},{20,24},{24,20},{28,16},{1,13},{... | collective-permute-start | bytes 115784 | tf_op jit(solution)/shard_map/ppermute | solution.py:47
  130.4 6.0 %collective-permute-start.3 = (f32[3,3216]{1,0:T(4,128)S(1)}, f32[3,3216]{1,0:T(4,128)S(1)}, u32[]{:S(2)}, u32[]{:S(2)}) collective-permute-start(f32[3,3216]{1,0:T(4,128)S(1)} %add_bitcast_fusion), channel_id=1, source_target_pairs={{0,16},{4,20},{8,24},{12,28},{16,0},{20,4},{24,8},{28,12},{1,17},{... | collective-permute-start | bytes 115784 | tf_op jit(solution)/shard_map/ppermute | solution.py:55
  136.5 9.5 %collective-permute-start.4 = (f32[3,3216]{1,0:T(4,128)S(1)}, f32[3,3216]{1,0:T(4,128)S(1)}, u32[]{:S(2)}, u32[]{:S(2)}) collective-permute-start(f32[3,3216]{1,0:T(4,128)S(1)} %fusion.118), channel_id=1, source_target_pairs={{0,1},{1,0},{2,3},{3,2},{4,5},{5,4},{6,7},{7,6},{8,9},{9,8},{10,11... | collective-permute-start | bytes 115784 | tf_op jit(solution)/shard_map/ppermute | solution.py:47
  138.6 7.4 %collective-permute-start.5 = (f32[3,3216]{1,0:T(4,128)S(1)}, f32[3,3216]{1,0:T(4,128)S(1)}, u32[]{:S(2)}, u32[]{:S(2)}) collective-permute-start(f32[3,3216]{1,0:T(4,128)S(1)} %fusion.118), channel_id=1, source_target_pairs={{0,2},{1,3},{2,0},{3,1},{4,6},{5,7},{6,4},{7,5},{8,10},{9,11},{10,... | collective-permute-start | bytes 115784 | tf_op jit(solution)/shard_map/ppermute | solution.py:47
  140.1 5.9 %collective-permute-start.6 = (f32[3,3216]{1,0:T(4,128)S(1)}, f32[3,3216]{1,0:T(4,128)S(1)}, u32[]{:S(2)}, u32[]{:S(2)}) collective-permute-start(f32[3,3216]{1,0:T(4,128)S(1)} %fusion.118), channel_id=1, source_target_pairs={{0,3},{1,2},{2,1},{3,0},{4,7},{5,6},{6,5},{7,4},{8,11},{9,10},{10,... | collective-permute-start | bytes 115784 | tf_op jit(solution)/shard_map/ppermute | solution.py:47
  141.7 5.8 %copy-start.45 = (f32[804]{0:T(1024)S(1)}, f32[804]{0:T(1024)}, u32[]{:S(2)}) copy-start(f32[804]{0:T(1024)} %get-tuple-element.96) | copy-start | bytes 9652
  141.7 5.9 %copy-start.46 = (f32[804]{0:T(1024)S(1)}, f32[804]{0:T(1024)}, u32[]{:S(2)}) copy-start(f32[804]{0:T(1024)} %get-tuple-element.97) | copy-start | bytes 9652
  141.7 7.7 %copy-start.43 = (f32[3216]{0:T(1024)S(1)}, f32[3216]{0:T(1024)}, u32[]{:S(2)}) copy-start(f32[3216]{0:T(1024)} %param.19) | copy-start | bytes 38596
  141.7 15.6 %all-to-all-start.4 = ((bf16[4,128,1036]{1,2,0:T(8,128)(2,1)}), bf16[4,128,1036]{1,2,0:T(8,128)(2,1)S(1)}, u32[]{:S(2)}, u32[]{:S(2)}) async-start(bf16[4,128,1036]{1,2,0:T(8,128)(2,1)} %copy.169), calls=%async_computation.4 | async-start | bytes 2129920 | tf_op jit(solution)/shard_map/all_to_all | solution.py:30
  (14 other events, 17.2 us)

commit v8 on v7

--- a/solution.py
+++ b/solution.py
@@ -40,17 +40,7 @@
     size = lax.axis_size(axis)
     if size & (size - 1):
         return lax.psum(x, axis)
-    idx = lax.axis_index(axis)
     step = 1
-    while step * 4 <= size:
-        got = [x] + [
-            lax.ppermute(x, axis, [(i, i ^ (k * step)) for i in range(size)]) for k in (1, 2, 3)
-        ]
-        held = jnp.stack(got)
-        place = (idx // step) % 4
-        parts = [lax.dynamic_index_in_dim(held, place ^ m, 0, keepdims=False) for m in range(4)]
-        x = (parts[0] + parts[1]) + (parts[2] + parts[3])
-        step *= 4
     while step < size:
         x = x + lax.ppermute(x, axis, [(i, i ^ step) for i in range(size)])
         step *= 2

time: 162 us -> 161 us (level)
  local copies, waits for them, and re-layouts: 48.4 us -> 46.2 us
  waiting for transfers between devices: 19.6 us -> 21.4 us
    ppermute x1 -> x5, waiting for transfers between devices: 1.76 us -> 12.4 us  [tree_sum(): x = x + lax.ppermute(x, axis, [(i, i ^ step) for i in range(size)])]
    all_to_all x2, waiting for transfers between devices: 12.1 us -> 4.81 us  [from_heads(): return lax.all_to_all(x, 'ctx', 0, 0, tiled=True)]
    ppermute x6 -> x0, starting transfers between devices: 5.59 us -> none  [tree_sum(): lax.ppermute(x, axis, [(i, i ^ k * step) for i in range(size)])]
    ppermute x1 -> x5, starting transfers between devices: 2.65 us -> 7.96 us  [tree_sum(): x = x + lax.ppermute(x, axis, [(i, i ^ step) for i in range(size)])]
    ppermute x6 -> x0, waiting for transfers between devices: 2.92 us -> none  [tree_sum(): lax.ppermute(x, axis, [(i, i ^ k * step) for i in range(size)])]
    unnamed x145 -> x147, local copies, waits for them, and re-layouts: 17.7 us -> 15.5 us
  transfers between devices with their start and end apart: 12 -> 10, of which waited for: 6 -> 7; matrix products, arithmetic and copies ran while one was open for 21% -> 20% of each run, Pallas kernels for 0% -> 0%
where the time goes in v8:
time: 161 us; the launch traced here: 160 us
  local copies, waits for them, and re-layouts  46.2 us (29%)
  other arithmetic  39.3 us (24%)
  starting transfers between devices  29.7 us (18%)
  waiting for transfers between devices  21.4 us (13%)
  matrix products  17.8 us (11%)
  between operations  5.28 us (3%)
    unnamed x147, local copies, waits for them, and re-layouts  15.5 us
    ppermute x5, waiting for transfers between devices, tree_sum(): x = x + lax.ppermute(x, axis, [(i, i ^ step) for i in range(size)])  12.4 us
    all_to_all x2, starting transfers between devices, to_heads(): x = lax.all_to_all(x, 'ctx', 0, 0, tiled=True)  8.55 us
    all_to_all x2, starting transfers between devices, from_heads(): return lax.all_to_all(x, 'ctx', 0, 0, tiled=True)  8.03 us
    ppermute x5, starting transfers between devices, tree_sum(): x = x + lax.ppermute(x, axis, [(i, i ^ step) for i in range(size)])  7.96 us
    convert_element_type x3, local copies, waits for them, and re-layouts, ssd_group(): return output.reshape(length, heads * width).astype(jnp.bfloat16)  7.13 us
    convert_element_type x3, local copies, waits for them, and re-layouts, ssd_group(): inputs = hidden.astype(jnp.float32).reshape(blocks, SPAN, heads, width)  7.13 us
    convert_element_type x4, other arithmetic, rounded(): value.astype(jnp.bfloat16)  7.04 us
  transfers between devices with their start and end apart: 10, of which 7 were waited for; matrix products, arithmetic and copies ran while one was open for 20% of the time, Pallas kernels for 0%

profile of v8, /device:TPU:0, one launch (start us, length us, event | category | flops | bytes accessed | tf_op | source)
XLA Modules:
  0.0 159.6 jit_solution(16295449456059202846)
XLA Ops:
  0.7 0.9 pad_maximum_fusion.2
  1.7 0.7 reshape_squeeze.3
  2.4 0.7 pad_maximum_fusion.1
  3.1 5.2 %all-to-all-start.1 = ((bf16[4,128,268]{1,2,0:T(8,128)(2,1)}), bf16[4,128,268]{1,2,0:T(8,128)(2,1)S(1)}, u32[]{:S(2)}, u32[]{:S(2)}) async-start(bf16[4,128,268]{1,2,0:T(8,128)(2,1)} %pad_maximum_fusion.1), calls=%async_computation.1 | async-start | bytes 557056 | tf_op jit(solution)/shard_map/all_to_all | solution.py:151
  9.1 1.2 copy.143
  11.0 2.8 %all-to-all-done.1 = bf16[4,128,268]{1,2,0:T(8,128)(2,1)S(1)} async-done(((bf16[4,128,268]{1,2,0:T(8,128)(2,1)}), bf16[4,128,268]{1,2,0:T(8,128)(2,1)S(1)}, u32[]{:S(2)}, u32[]{:S(2)}) %all-to-all-start.1) | async-done | bytes 274464 | tf_op jit(solution)/shard_map/all_to_all | solution.py:151
  13.8 4.2 %all-to-all-start = ((bf16[4,128,768]{1,2,0:T(8,128)(2,1)}), bf16[4,128,768]{1,2,0:T(8,128)(2,1)}, u32[]{:S(2)}, u32[]{:S(2)}) async-start(bf16[4,128,768]{1,2,0:T(8,128)(2,1)} %bitcast.1), calls=%async_computation | async-start | bytes 1572864 | tf_op jit(solution)/shard_map/all_to_all | solution.py:23
  20.6 1.8 %multiply_convert_fusion.2 = bf16[2,12,256,128]{3,2,1,0:T(8,128)(2,1)} fusion(f32[2,12,256]{2,1,0:T(8,128)S(1)} %get-tuple-element.80, f32[2,256,128]{2,1,0:T(8,128)S(1)} %bitcast_convert_fusion), kind=kLoop, calls=%fused_computation.20 | loop fusion | flops 1572864 | bytes 1859584 | tf_op jit(solution)/shard_map/jvp()/convert_element_type | solution.py:51
  22.9 1.7 %multiply_convert_fusion = bf16[2,12,256,256]{3,2,1,0:T(8,128)(2,1)S(1)} fusion(f32[2,12,256]{2,1,0:T(8,128)S(1)} %fusion.50, f32[2,256,256]{2,1,0:T(8,128)S(1)} %fusion.98, pred[256,256]{1,0:T(8,128)(4,1)S(1)} %iota_compare_fusion), kind=kLoop, calls=%fused_computation.6 | loop fusion | flops 7864320 | bytes 3760128 | tf_op jit(solution)/shard_map/jvp()/convert_element_type | solution.py:51
  25.3 1.8 %multiply_convert_fusion.1 = bf16[2,12,256,128]{3,2,1,0:T(8,128)(2,1)} fusion(f32[2,12,256]{2,1,0:T(8,128)S(1)} %get-tuple-element.79, f32[2,256,128]{2,1,0:T(8,128)S(1)} %bitcast_convert_fusion.1), kind=kLoop, calls=%fused_computation.19 | loop fusion | flops 1572864 | bytes 1859584 | tf_op jit(solution)/shard_map/jvp()/convert_element_type | solution.py:51
  27.1 0.8 fusion.76
  28.0 2.9 %copy.144 = f32[4,128,768]{1,0,2:T(4,128)} copy(bf16[4,128,768]{1,2,0:T(8,128)(2,1)} %all-to-all-done) | data formatting | bytes 2359296 | tf_op jit(solution)/shard_map/jvp()/convert_element_type | solution.py:63
  30.9 3.4 %reshape.323 = f32[2,256,12,64]{1,0,3,2:T(2,128)} reshape(f32[4,128,768]{1,0,2:T(4,128)} %copy.144) | data formatting | bytes 3145728 | tf_op jit(solution)/shard_map/jvp()/convert_element_type | solution.py:63
  34.3 1.7 %multiply_convert_fusion.5 = bf16[2,256,12,64]{1,3,2,0:T(8,128)(2,1)S(1)} fusion(f32[2,256,12,64]{1,0,3,2:T(2,128)} %reshape.323, f32[2,256,12]{1,2,0:T(8,128)S(1)} %copy.147), kind=kLoop, calls=%fused_computation.56 | loop fusion | flops 786432 | bytes 2383872 | tf_op jit(solution)/shard_map/jvp()/convert_element_type | solution.py:51
  36.2 1.8 %multiply_convert_fusion.6 = (bf16[1,12,128,64]{2,3,1,0:T(8,128)(2,1)S(1)}, f32[1,12,128,64]{2,3,1,0:T(8,128)}) fusion(f32[]{:T(128)} %bitcast.12, f32[12]{0:T(128)S(1)} %get-tuple-element.60, bf16[2,256,12,64]{1,3,2,0:T(8,128)(2,1)S(1)} %multiply_convert_fusion.5, bf16[2,12,256,128]{3,2,1,0:T(8,128)(2,1)S(1)} %copy-done.7), kind=kOutput, calls=%fused_computation.86 | convolution fusion | flops 50626560 | bytes 2949172 | tf_op jit(solution)/shard_map/jvp()/slice | solution.py:84
  38.1 1.1 fusion.99
  40.6 1.7 %copy.153 = bf16[2,256,12,64]{1,0,3,2:T(2,128)(2,1)} copy(bf16[2,256,12,64]{1,3,2,0:T(8,128)(2,1)S(1)} %fusion.27) | data formatting | bytes 1572864 | tf_op jit(solution)/shard_map/jvp()/convert_element_type | solution.py:88
  42.3 3.3 %convert_element_type.162 = bf16[4,128,768]{1,0,2:T(4,128)(2,1)} reshape(bf16[2,256,12,64]{1,0,3,2:T(2,128)(2,1)} %copy.153) | data formatting | bytes 1572864 | tf_op jit(solution)/shard_map/jvp()/convert_element_type | solution.py:88
  45.7 2.1 %copy.154 = bf16[4,128,768]{1,2,0:T(8,128)(2,1)} copy(bf16[4,128,768]{1,0,2:T(4,128)(2,1)} %convert_element_type.162) | data formatting | bytes 1572864 | tf_op jit(solution)/shard_map/jvp()/convert_element_type | solution.py:88
  47.8 4.4 %all-to-all-start.2 = ((bf16[4,128,768]{1,2,0:T(8,128)(2,1)}), bf16[4,128,768]{1,2,0:T(8,128)(2,1)}, u32[]{:S(2)}, u32[]{:S(2)}) async-start(bf16[4,128,768]{1,2,0:T(8,128)(2,1)} %copy.154), calls=%async_computation.2 | async-start | bytes 1572864 | tf_op jit(solution)/shard_map/all_to_all | solution.py:30
  52.1 0.8 slice.103
  52.9 2.3 %copy.155 = bf16[1,128,3072]{1,2,0:T(8,128)(2,1)} copy(bf16[1,128,3072]{2,1,0:T(8,128)(2,1)} %param.13) | data formatting | bytes 1572864 | tf_op args[1]
  55.2 2.3 %copy.156 = bf16[1,128,3072]{1,2,0:T(8,128)(2,1)} copy(bf16[1,128,3072]{2,1,0:T(8,128)(2,1)} %param.18) | data formatting | bytes 1572864 | tf_op args[6]
  57.5 4.8 %all-to-all-done.2 = bf16[4,128,768]{1,2,0:T(8,128)(2,1)} async-done(((bf16[4,128,768]{1,2,0:T(8,128)(2,1)}), bf16[4,128,768]{1,2,0:T(8,128)(2,1)}, u32[]{:S(2)}, u32[]{:S(2)}) %all-to-all-start.2) | async-done | bytes 786464 | tf_op jit(solution)/shard_map/all_to_all | solution.py:30
  62.3 1.3 convert_element_type.194
  64.8 1.5 fusion.16
  66.3 2.6 %fusion.25 = (bf16[1,128,3072]{1,2,0:T(8,128)(2,1)}, bf16[1,128,3072]{1,2,0:T(8,128)(2,1)}, bf16[1,128,3072]{1,2,0:T(8,128)(2,1)}) fusion(bf16[1,128,3072]{1,2,0:T(8,128)(2,1)S(1)} %copy-done.11, f32[1,128,3072]{1,2,0:T(8,128)S(1)} %get-tuple-element.66, bf16[1,128,3072]{1,2,0:T(8,128)(2,1)S(1)} %copy-done.12, f32[128]{0:T(128)S(1)} %fusion.86, ...), kind=kLoop, calls=%fused_computation.45 | loop fusion | flops 8650752 | bytes 7091200 | tf_op jit(solution)/shard_map/convert_element_type | solution.py:112
  69.0 4.3 %all-to-all-start.3 = ((bf16[4,128,768]{1,2,0:T(8,128)(2,1)}), bf16[4,128,768]{1,2,0:T(8,128)(2,1)}, u32[]{:S(2)}, u32[]{:S(2)}) async-start(bf16[4,128,768]{1,2,0:T(8,128)(2,1)} %bitcast.166), calls=%async_computation.3 | async-start | bytes 1572864 | tf_op jit(solution)/shard_map/all_to_all | solution.py:23
  73.5 1.3 fusion.85
  74.9 1.3 fusion.84
  79.6 1.5 dynamic_update_slice.7
  81.1 1.4 slice.128
  82.4 1.3 all-to-all-done.3
  83.7 2.6 %copy.157 = bf16[4,128,768]{1,0,2:T(4,128)(2,1)} copy(bf16[4,128,768]{1,2,0:T(8,128)(2,1)} %all-to-all-done.3) | data formatting | bytes 1572864 | tf_op jit(solution)/shard_map/all_to_all | solution.py:23
  86.4 3.0 %squeeze_broadcast_in_dim_reshape.4 = bf16[2,256,12,64]{1,0,3,2:T(2,128)(2,1)} reshape(bf16[4,128,768]{1,0,2:T(4,128)(2,1)} %copy.157) | data formatting | bytes 1572864 | tf_op jit(solution)/shard_map/squeeze;broadcast_in_dim;reshape | solution.py:180
  89.3 2.1 %convolution_convert_fusion.3 = bf16[2,12,128,64]{2,3,1,0:T(8,128)(2,1)S(1)} fusion(bf16[2,12,256,128]{3,2,1,0:T(8,128)(2,1)} %multiply_convert_fusion.1, bf16[2,256,12,64]{1,0,3,2:T(2,128)(2,1)} %squeeze_broadcast_in_dim_reshape.4), kind=kOutput, calls=%fused_computation.58 | convolution fusion | flops 100859904 | bytes 2752512 | tf_op jit(solution)/shard_map/transpose(jvp(chtn,chnp->cthp))/dot_general | solution.py:86
  91.5 1.9 %convolution_convert_fusion.2 = bf16[2,12,256,128]{3,2,1,0:T(8,128)(2,1)} fusion(bf16[2,12,128,64]{2,3,1,0:T(8,128)(2,1)S(1)} %concatenate.29, bf16[2,256,12,64]{1,0,3,2:T(2,128)(2,1)S(1)} %copy-done), kind=kOutput, calls=%fused_computation.32 | convolution fusion | flops 101449728 | bytes 2752512 | tf_op jit(solution)/shard_map/transpose(jvp(chtn,chnp->cthp))/dot_general | solution.py:86
  93.3 2.7 %convolution_convert_fusion = bf16[2,12,256,256]{3,2,1,0:T(8,128)(2,1)} fusion(bf16[2,256,12,64]{1,3,2,0:T(8,128)(2,1)S(1)} %copy-done.5, bf16[2,256,12,64]{1,0,3,2:T(2,128)(2,1)S(1)} %copy-done), kind=kOutput, calls=%fused_computation.24 | convolution fusion | flops 202899456 | bytes 4718592 | tf_op jit(solution)/shard_map/transpose(jvp(chts,cshp->cthp))/dot_general | solution.py:72
  96.1 1.8 %fusion.33 = f32[2,12,64,256]{3,2,1,0:T(8,128)} fusion(bf16[2,12,256,256]{3,2,1,0:T(8,128)(2,1)S(1)} %multiply_convert_fusion, bf16[2,256,12,64]{1,0,3,2:T(2,128)(2,1)S(1)} %copy-done), kind=kOutput, calls=%fused_computation.67 | convolution fusion | flops 201326592 | bytes 5505024 | tf_op jit(solution)/shard_map/transpose(jvp(chts,cshp->cthp))/dot_general | solution.py:72
  97.8 0.8 fusion.41
  98.7 1.0 fusion.45
  99.9 1.5 convolution_convert_fusion.1
  101.4 6.0 %fusion.7 = (f32[2,256,128]{2,1,0:T(8,128)}, f32[2,12,256]{2,1,0:T(8,128)S(1)}, f32[2,12,256]{2,1,0:T(8,128)}, f32[2,256,128]{2,1,0:T(8,128)}) fusion(bf16[2,12,256,128]{3,2,1,0:T(8,128)(2,1)S(1)} %convolution_convert_fusion.1, f32[2,12,256]{2,1,0:T(8,128)S(1)} %copy-done.34, f32[2,256,128]{2,1,0:T(8,128)S(1)} %copy-done.21, f32[2,256,128]{2,1,0:T(8,128)} %copy-done.22, ...), kind=kLoop, calls=%fused_computation.15 | loop fusion | flops 7720960 | bytes 4292608 | tf_op jit(solution)/shard_map/transpose(jvp())/reduce_sum | solution.py:74
  108.2 5.7 %fusion.6 = (f32[2,12,256]{2,1,0:T(8,128)S(1)}, f32[2,12,256]{2,1,0:T(8,128)S(1)}, f32[2,256,256]{2,1,0:T(8,128)}) fusion(bf16[2,12,256,256]{3,2,1,0:T(8,128)(2,1)S(1)} %copy-done.10, f32[2,12,256]{2,1,0:T(8,128)S(1)} %copy-done.28, f32[2,256,256]{2,1,0:T(8,128)} %copy-done.15, pred[256,256]{1,0:T(8,128)(4,1)S(1)} %copy-done.37), kind=kLoop, calls=%fused_computation.10 | loop fusion | flops 18731008 | bytes 4333568 | tf_op jit(solution)/shard_map/transpose(jvp())/reduce_sum | solution.py:69
  114.3 2.5 %fusion.28 = bf16[2,256,12,64]{1,3,2,0:T(8,128)(2,1)S(1)} fusion(f32[2,12,64,256]{3,2,1,0:T(8,128)S(1)} %copy-done.13, bf16[2,12,256,128]{3,2,1,0:T(8,128)(2,1)S(1)} %copy-done.8, f32[12]{0:T(128)S(1)} %copy-done.52, f32[]{:T(128)} %bitcast.12, bf16[2,12,128,64]{2,3,1,0:T(8,128)(2,1)S(1)} %copy-done.19), kind=kOutput, calls=%fused_computation.57 | convolution fusion | flops 303071232 | bytes 4129284 | tf_op jit(solution)/shard_map/transpose(jvp(chsn,cshp->chnp))/dot_general | solution.py:75
  117.6 1.0 fusion.92
  118.7 0.7 bitcast_multiply_fusion.4
  119.4 1.6 %multiply_reduce_fusion = f32[768]{0:T(1024)S(1)} fusion(bf16[4,128,768]{1,2,0:T(8,128)(2,1)} %all-to-all-done.3, bf16[4,128,768]{1,2,0:T(8,128)(2,1)} %all-to-all-done), kind=kLoop, calls=%fused_computation.51 | loop fusion | flops 1572096 | bytes 1575936 | tf_op jit(solution)/shard_map/transpose(jvp())/reduce_sum | solution.py:87
  121.9 1.2 collective-permute-done
  123.2 1.6 %collective-permute-start.1 = (f32[3,3216]{1,0:T(4,128)S(1)}, f32[3,3216]{1,0:T(4,128)S(1)}, u32[]{:S(2)}, u32[]{:S(2)}) collective-permute-start(f32[3,3216]{1,0:T(4,128)S(1)} %fusion.90), channel_id=1, source_target_pairs={{0,8},{4,12},{8,0},{12,4},{16,24},{20,28},{24,16},{28,20},{1,9},{5... | collective-permute-start | bytes 115784 | tf_op jit(solution)/shard_map/ppermute | solution.py:45
  125.5 1.9 %collective-permute-done.1 = f32[3,3216]{1,0:T(4,128)S(1)} collective-permute-done((f32[3,3216]{1,0:T(4,128)S(1)}, f32[3,3216]{1,0:T(4,128)S(1)}, u32[]{:S(2)}, u32[]{:S(2)}) %collective-permute-start.1) | collective-permute-done | bytes 38624 | tf_op jit(solution)/shard_map/ppermute | solution.py:45
  127.4 2.7 %collective-permute-start.2 = (f32[3,3216]{1,0:T(4,128)S(1)}, f32[3,3216]{1,0:T(4,128)S(1)}, u32[]{:S(2)}, u32[]{:S(2)}) collective-permute-start(f32[3,3216]{1,0:T(4,128)S(1)} %add.123), channel_id=1, source_target_pairs={{0,16},{4,20},{8,24},{12,28},{16,0},{20,4},{24,8},{28,12},{1,17},{... | collective-permute-start | bytes 115784 | tf_op jit(solution)/shard_map/ppermute | solution.py:45
  130.7 0.8 copy.160
  131.7 0.8 collective-permute-done.2
  132.5 1.5 collective-permute-start.3
  134.5 1.1 copy.169
  135.7 3.7 %all-to-all-start.4 = ((bf16[4,128,1036]{1,2,0:T(8,128)(2,1)}), bf16[4,128,1036]{1,2,0:T(8,128)(2,1)S(1)}, u32[]{:S(2)}, u32[]{:S(2)}) async-start(bf16[4,128,1036]{1,2,0:T(8,128)(2,1)} %copy.169), calls=%async_computation.4 | async-start | bytes 2129920 | tf_op jit(solution)/shard_map/all_to_all | solution.py:30
  139.4 2.0 %collective-permute-start.4 = (f32[3,3216]{1,0:T(4,128)S(1)}, f32[3,3216]{1,0:T(4,128)S(1)}, u32[]{:S(2)}, u32[]{:S(2)}) collective-permute-start(f32[3,3216]{1,0:T(4,128)S(1)} %add.125), channel_id=1, source_target_pairs={{0,2},{1,3},{2,0},{3,1},{4,6},{5,7},{6,4},{7,5},{8,10},{9,11},{10,... | collective-permute-start | bytes 115784 | tf_op jit(solution)/shard_map/ppermute | solution.py:45
  141.5 1.2 copy.171
  142.6 1.2 copy.173
  143.8 8.5 %collective-permute-done.4 = f32[3,3216]{1,0:T(4,128)S(1)} collective-permute-done((f32[3,3216]{1,0:T(4,128)S(1)}, f32[3,3216]{1,0:T(4,128)S(1)}, u32[]{:S(2)}, u32[]{:S(2)}) %collective-permute-start.4) | collective-permute-done | bytes 38624 | tf_op jit(solution)/shard_map/ppermute | solution.py:45
  156.3 1.2 copy.172
  157.6 0.7 copy.174
  158.3 0.7 copy.175
  (218 shorter events, 17.6 us)
Async XLA Ops:
  0.6 7.7 %slice-start = ((f32[3216]{0:T(1024)}), f32[144]{0:T(256)S(1)}, s32[]{:S(2)}) async-start(f32[3216]{0:T(1024)} %param.19), calls=%async_computation.5 | async-start | bytes 2048 | tf_op jit(solution)/shard_map/slice | solution.py:139
  0.7 7.8 %copy-start.65 = (s32[1,2]{1,0:T(1,128)S(1)}, s32[1,2]{1,0:T(1,128)}, u32[]{:S(2)}) copy-start(s32[1,2]{1,0:T(1,128)} %param.17) | copy-start | bytes 28
  0.7 8.4 %copy-start.35 = (bf16[1,128,3072]{2,1,0:T(8,128)(2,1)S(1)}, bf16[1,128,3072]{2,1,0:T(8,128)(2,1)}, u32[]{:S(2)}) copy-start(bf16[1,128,3072]{2,1,0:T(8,128)(2,1)} %param.12) | copy-start | bytes 2359300
  3.1 10.7 %all-to-all-start.1 = ((bf16[4,128,268]{1,2,0:T(8,128)(2,1)}), bf16[4,128,268]{1,2,0:T(8,128)(2,1)S(1)}, u32[]{:S(2)}, u32[]{:S(2)}) async-start(bf16[4,128,268]{1,2,0:T(8,128)(2,1)} %pad_maximum_fusion.1), calls=%async_computation.1 | async-start | bytes 557056 | tf_op jit(solution)/shard_map/all_to_all | solution.py:151
  8.4 14.5 %copy-start.36 = (pred[256,256]{1,0:T(8,128)(4,1)}, pred[256,256]{1,0:T(8,128)(4,1)S(1)}, u32[]{:S(2)}) copy-start(pred[256,256]{1,0:T(8,128)(4,1)S(1)} %iota_compare_fusion) | copy-start | bytes 196612
  11.0 7.4 %copy-start.53 = (f32[3,12]{1,0:T(4,128)}, f32[3,12]{1,0:T(4,128)S(1)}, u32[]{:S(2)}) copy-start(f32[3,12]{1,0:T(4,128)S(1)} %constant_dynamic-slice_fusion) | copy-start | bytes 436
  11.0 7.4 %copy-start.56 = (f32[12]{0:T(128)}, f32[12]{0:T(128)S(1)}, u32[]{:S(2)}) copy-start(f32[12]{0:T(128)S(1)} %get-tuple-element.84) | copy-start | bytes 148
  11.0 7.4 %copy-start.58 = (f32[12]{0:T(128)}, f32[12]{0:T(128)S(1)}, u32[]{:S(2)}) copy-start(f32[12]{0:T(128)S(1)} %get-tuple-element.85) | copy-start | bytes 148
  11.0 28.2 %copy-start.54 = (f32[12]{0:T(128)}, f32[12]{0:T(128)S(1)}, u32[]{:S(2)}) copy-start(f32[12]{0:T(128)S(1)} %get-tuple-element.83) | copy-start | bytes 148
  13.8 14.1 %all-to-all-start = ((bf16[4,128,768]{1,2,0:T(8,128)(2,1)}), bf16[4,128,768]{1,2,0:T(8,128)(2,1)}, u32[]{:S(2)}, u32[]{:S(2)}) async-start(bf16[4,128,768]{1,2,0:T(8,128)(2,1)} %bitcast.1), calls=%async_computation | async-start | bytes 1572864 | tf_op jit(solution)/shard_map/all_to_all | solution.py:23
  19.4 7.7 %copy-start.27 = (f32[2,12,256]{2,1,0:T(8,128)}, f32[2,12,256]{2,1,0:T(8,128)S(1)}, u32[]{:S(2)}) copy-start(f32[2,12,256]{2,1,0:T(8,128)S(1)} %fusion.50) | copy-start | bytes 73732
  19.7 2.9 %copy-start.33 = (f32[2,12,256]{2,1,0:T(8,128)}, f32[2,12,256]{2,1,0:T(8,128)S(1)}, u32[]{:S(2)}) copy-start(f32[2,12,256]{2,1,0:T(8,128)S(1)} %get-tuple-element.80) | copy-start | bytes 73732
  19.7 4.9 %copy-start.40 = (f32[2,12,256]{2,1,0:T(8,128)}, f32[2,12,256]{2,1,0:T(8,128)S(1)}, u32[]{:S(2)}) copy-start(f32[2,12,256]{2,1,0:T(8,128)S(1)} %get-tuple-element.79) | copy-start | bytes 73732
  19.8 2.8 %copy-start.23 = (bf16[512,128]{1,0:T(8,128)(2,1)}, bf16[512,128]{1,0:T(8,128)(2,1)S(1)}, u32[]{:S(2)}) copy-start(bf16[512,128]{1,0:T(8,128)(2,1)S(1)} %copy.150) | copy-start | bytes 393220
  22.5 11.8 %copy-start.38 = (f32[2,256,12]{1,2,0:T(8,128)}, f32[2,256,12]{1,2,0:T(8,128)S(1)}, u32[]{:S(2)}) copy-start(f32[2,256,12]{1,2,0:T(8,128)S(1)} %copy.147) | copy-start | bytes 73732
  22.6 2.0 %copy-start.25 = (bf16[512,128]{1,0:T(8,128)(2,1)}, bf16[512,128]{1,0:T(8,128)(2,1)S(1)}, u32[]{:S(2)}) copy-start(bf16[512,128]{1,0:T(8,128)(2,1)S(1)} %copy.149) | copy-start | bytes 393220
  28.0 8.0 %copy-start.60 = (f32[12]{0:T(128)}, f32[12]{0:T(128)S(1)}, u32[]{:S(2)}) copy-start(f32[12]{0:T(128)S(1)} %get-tuple-element.60) | copy-start | bytes 148
  34.3 1.9 %copy-start.7 = (bf16[2,12,256,128]{3,2,1,0:T(8,128)(2,1)S(1)}, bf16[2,12,256,128]{3,2,1,0:T(8,128)(2,1)}, u32[]{:S(2)}) copy-start(bf16[2,12,256,128]{3,2,1,0:T(8,128)(2,1)} %multiply_convert_fusion.2) | copy-start | bytes 4718596
  36.0 2.1 %copy-start.4 = (bf16[2,256,12,64]{1,3,2,0:T(8,128)(2,1)}, bf16[2,256,12,64]{1,3,2,0:T(8,128)(2,1)S(1)}, u32[]{:S(2)}) copy-start(bf16[2,256,12,64]{1,3,2,0:T(8,128)(2,1)S(1)} %multiply_convert_fusion.5) | copy-start | bytes 2359300
  47.8 14.6 %all-to-all-start.2 = ((bf16[4,128,768]{1,2,0:T(8,128)(2,1)}), bf16[4,128,768]{1,2,0:T(8,128)(2,1)}, u32[]{:S(2)}, u32[]{:S(2)}) async-start(bf16[4,128,768]{1,2,0:T(8,128)(2,1)} %copy.154), calls=%async_computation.2 | async-start | bytes 1572864 | tf_op jit(solution)/shard_map/all_to_all | solution.py:30
  69.0 4.4 %copy-start.62 = (s32[8]{0:T(128)S(1)}, s32[8]{0:T(128)}, u32[]{:S(2)}) copy-start(s32[8]{0:T(128)} %param.22) | copy-start | bytes 100
  69.0 9.9 %copy-start.47 = (f32[1,804]{1,0:T(1,128)S(1)}, f32[1,804]{1,0:T(1,128)}, u32[]{:S(2)}) copy-start(f32[1,804]{1,0:T(1,128)} %param.21) | copy-start | bytes 9652
  69.0 9.9 %copy-start.49 = (f32[1,804]{1,0:T(1,128)S(1)}, f32[1,804]{1,0:T(1,128)}, u32[]{:S(2)}) copy-start(f32[1,804]{1,0:T(1,128)} %param.20) | copy-start | bytes 9652
  69.0 14.8 %all-to-all-start.3 = ((bf16[4,128,768]{1,2,0:T(8,128)(2,1)}), bf16[4,128,768]{1,2,0:T(8,128)(2,1)}, u32[]{:S(2)}, u32[]{:S(2)}) async-start(bf16[4,128,768]{1,2,0:T(8,128)(2,1)} %bitcast.166), calls=%async_computation.3 | async-start | bytes 1572864 | tf_op jit(solution)/shard_map/all_to_all | solution.py:23
  89.3 2.1 %copy-start = (bf16[2,256,12,64]{1,0,3,2:T(2,128)(2,1)S(1)}, bf16[2,256,12,64]{1,0,3,2:T(2,128)(2,1)}, u32[]{:S(2)}) copy-start(bf16[2,256,12,64]{1,0,3,2:T(2,128)(2,1)} %squeeze_broadcast_in_dim_reshape.4) | copy-start | bytes 2359300
  91.5 7.2 %copy-start.18 = (bf16[2,12,128,64]{2,3,1,0:T(8,128)(2,1)}, bf16[2,12,128,64]{2,3,1,0:T(8,128)(2,1)S(1)}, u32[]{:S(2)}) copy-start(bf16[2,12,128,64]{2,3,1,0:T(8,128)(2,1)S(1)} %convolution_convert_fusion.3) | copy-start | bytes 1179652
  96.0 2.6 %copy-start.29 = (f32[1,12,128,64]{2,3,1,0:T(8,128)S(1)}, f32[1,12,128,64]{2,3,1,0:T(8,128)}, u32[]{:S(2)}) copy-start(f32[1,12,128,64]{2,3,1,0:T(8,128)} %get-tuple-element.89) | copy-start | bytes 1179652
  96.0 2.7 %copy-start.61 = (f32[12]{0:T(128)S(1)}, f32[12]{0:T(128)}, u32[]{:S(2)}) copy-start(f32[12]{0:T(128)} %copy-done.60) | copy-start | bytes 148
  96.0 3.7 %copy-start.64 = (f32[12]{0:T(128)S(1)}, f32[12]{0:T(128)}, u32[]{:S(2)}) copy-start(f32[12]{0:T(128)} %get-tuple-element.57) | copy-start | bytes 148
  96.0 3.7 %copy-start.63 = (f32[12]{0:T(128)S(1)}, f32[12]{0:T(128)}, u32[]{:S(2)}) copy-start(f32[12]{0:T(128)} %get-tuple-element.58) | copy-start | bytes 148
  97.8 2.0 %copy-start.6 = (bf16[2,256,12,64]{1,3,2,0:T(8,128)(2,1)S(1)}, bf16[2,256,12,64]{1,3,2,0:T(8,128)(2,1)}, u32[]{:S(2)}) copy-start(bf16[2,256,12,64]{1,3,2,0:T(8,128)(2,1)} %copy-done.4) | copy-start | bytes 2359300
  98.7 2.6 %copy-start.21 = (f32[2,256,128]{2,1,0:T(8,128)S(1)}, f32[2,256,128]{2,1,0:T(8,128)}, u32[]{:S(2)}) copy-start(f32[2,256,128]{2,1,0:T(8,128)} %copy-done.20) | copy-start | bytes 786436
  98.7 2.6 %copy-start.34 = (f32[2,12,256]{2,1,0:T(8,128)S(1)}, f32[2,12,256]{2,1,0:T(8,128)}, u32[]{:S(2)}) copy-start(f32[2,12,256]{2,1,0:T(8,128)} %copy-done.33) | copy-start | bytes 73732
  101.4 6.8 %copy-start.10 = (bf16[2,12,256,256]{3,2,1,0:T(8,128)(2,1)S(1)}, bf16[2,12,256,256]{3,2,1,0:T(8,128)(2,1)}, u32[]{:S(2)}) copy-start(bf16[2,12,256,256]{3,2,1,0:T(8,128)(2,1)} %convolution_convert_fusion) | copy-start | bytes 9437188
  101.4 6.8 %copy-start.28 = (f32[2,12,256]{2,1,0:T(8,128)S(1)}, f32[2,12,256]{2,1,0:T(8,128)}, u32[]{:S(2)}) copy-start(f32[2,12,256]{2,1,0:T(8,128)} %copy-done.27) | copy-start | bytes 73732
  101.4 6.8 %copy-start.37 = (pred[256,256]{1,0:T(8,128)(4,1)S(1)}, pred[256,256]{1,0:T(8,128)(4,1)}, u32[]{:S(2)}) copy-start(pred[256,256]{1,0:T(8,128)(4,1)} %copy-done.36) | copy-start | bytes 196612
  108.1 5.8 %copy-start.42 = (f32[2,12,256]{2,1,0:T(8,128)S(1)}, f32[2,12,256]{2,1,0:T(8,128)}, u32[]{:S(2)}) copy-start(f32[2,12,256]{2,1,0:T(8,128)} %copy-done.41) | copy-start | bytes 73732
  108.2 5.8 %copy-start.44 = (f32[2,12,256]{2,1,0:T(8,128)S(1)}, f32[2,12,256]{2,1,0:T(8,128)}, u32[]{:S(2)}) copy-start(f32[2,12,256]{2,1,0:T(8,128)} %get-tuple-element.92) | copy-start | bytes 73732
  108.2 6.1 %copy-start.8 = (bf16[2,12,256,128]{3,2,1,0:T(8,128)(2,1)S(1)}, bf16[2,12,256,128]{3,2,1,0:T(8,128)(2,1)}, u32[]{:S(2)}) copy-start(bf16[2,12,256,128]{3,2,1,0:T(8,128)(2,1)} %multiply_convert_fusion.2) | copy-start | bytes 4718596
  108.2 6.1 %copy-start.13 = (f32[2,12,64,256]{3,2,1,0:T(8,128)S(1)}, f32[2,12,64,256]{3,2,1,0:T(8,128)}, u32[]{:S(2)}) copy-start(f32[2,12,64,256]{3,2,1,0:T(8,128)} %fusion.33) | copy-start | bytes 4718596
  108.2 6.1 %copy-start.19 = (bf16[2,12,128,64]{2,3,1,0:T(8,128)(2,1)S(1)}, bf16[2,12,128,64]{2,3,1,0:T(8,128)(2,1)}, u32[]{:S(2)}) copy-start(bf16[2,12,128,64]{2,3,1,0:T(8,128)(2,1)} %copy-done.18) | copy-start | bytes 1179652
  108.2 6.1 %copy-start.52 = (f32[12]{0:T(128)S(1)}, f32[12]{0:T(128)}, u32[]{:S(2)}) copy-start(f32[12]{0:T(128)} %get-tuple-element.59) | copy-start | bytes 148
  114.3 2.6 %copy-start.1 = (bf16[2,256,12,64]{1,0,3,2:T(2,128)(2,1)S(1)}, bf16[2,256,12,64]{1,0,3,2:T(2,128)(2,1)}, u32[]{:S(2)}) copy-start(bf16[2,256,12,64]{1,0,3,2:T(2,128)(2,1)} %squeeze_broadcast_in_dim_reshape.4) | copy-start | bytes 2359300
  114.3 2.6 %copy-start.3 = (f32[2,256,12,64]{1,0,3,2:T(2,128)S(1)}, f32[2,256,12,64]{1,0,3,2:T(2,128)}, u32[]{:S(2)}) copy-start(f32[2,256,12,64]{1,0,3,2:T(2,128)} %reshape.323) | copy-start | bytes 4718596
  114.3 2.6 %copy-start.39 = (f32[2,256,12]{1,2,0:T(8,128)S(1)}, f32[2,256,12]{1,2,0:T(8,128)}, u32[]{:S(2)}) copy-start(f32[2,256,12]{1,2,0:T(8,128)} %copy-done.38) | copy-start | bytes 73732
  114.3 2.6 %copy-start.55 = (f32[12]{0:T(128)S(1)}, f32[12]{0:T(128)}, u32[]{:S(2)}) copy-start(f32[12]{0:T(128)} %copy-done.54) | copy-start | bytes 148
  117.5 4.2 %copy-start.46 = (f32[3072]{0:T(1024)S(1)}, f32[3072]{0:T(1024)}, u32[]{:S(2)}) copy-start(f32[3072]{0:T(1024)} %get-tuple-element.48) | copy-start | bytes 36868
  117.5 4.3 %copy-start.43 = (f32[2,3216]{1,0:T(2,128)S(1)}, f32[2,3216]{1,0:T(2,128)}, u32[]{:S(2)}) copy-start(f32[2,3216]{1,0:T(2,128)} %slice.128) | copy-start | bytes 77188
  117.5 7.3 %copy-start.14 = (f32[2,256,256]{2,1,0:T(8,128)S(1)}, f32[2,256,256]{2,1,0:T(8,128)}, u32[]{:S(2)}) copy-start(f32[2,256,256]{2,1,0:T(8,128)} %get-tuple-element.47) | copy-start | bytes 1572868
  117.5 7.3 %copy-start.26 = (bf16[512,128]{1,0:T(8,128)(2,1)S(1)}, bf16[512,128]{1,0:T(8,128)(2,1)}, u32[]{:S(2)}) copy-start(bf16[512,128]{1,0:T(8,128)(2,1)} %copy-done.25) | copy-start | bytes 393220
  117.5 7.3 %copy-start.32 = (f32[2,256,128]{2,1,0:T(8,128)S(1)}, f32[2,256,128]{2,1,0:T(8,128)}, u32[]{:S(2)}) copy-start(f32[2,256,128]{2,1,0:T(8,128)} %get-tuple-element.50) | copy-start | bytes 786436
  118.6 11.4 %copy-start.24 = (bf16[512,128]{1,0:T(8,128)(2,1)S(1)}, bf16[512,128]{1,0:T(8,128)(2,1)}, u32[]{:S(2)}) copy-start(bf16[512,128]{1,0:T(8,128)(2,1)} %copy-done.23) | copy-start | bytes 393220
  118.6 11.4 %copy-start.31 = (f32[2,256,128]{2,1,0:T(8,128)S(1)}, f32[2,256,128]{2,1,0:T(8,128)}, u32[]{:S(2)}) copy-start(f32[2,256,128]{2,1,0:T(8,128)} %get-tuple-element.93) | copy-start | bytes 786436
  121.9 1.3 collective-permute-start
  123.2 4.2 %collective-permute-start.1 = (f32[3,3216]{1,0:T(4,128)S(1)}, f32[3,3216]{1,0:T(4,128)S(1)}, u32[]{:S(2)}, u32[]{:S(2)}) collective-permute-start(f32[3,3216]{1,0:T(4,128)S(1)} %fusion.90), channel_id=1, source_target_pairs={{0,8},{4,12},{8,0},{12,4},{16,24},{20,28},{24,16},{28,20},{1,9},{5... | collective-permute-start | bytes 115784 | tf_op jit(solution)/shard_map/ppermute | solution.py:45
  127.4 5.1 %collective-permute-start.2 = (f32[3,3216]{1,0:T(4,128)S(1)}, f32[3,3216]{1,0:T(4,128)S(1)}, u32[]{:S(2)}, u32[]{:S(2)}) collective-permute-start(f32[3,3216]{1,0:T(4,128)S(1)} %add.123), channel_id=1, source_target_pairs={{0,16},{4,20},{8,24},{12,28},{16,0},{20,4},{24,8},{28,12},{1,17},{... | collective-permute-start | bytes 115784 | tf_op jit(solution)/shard_map/ppermute | solution.py:45
  132.5 6.8 %collective-permute-start.3 = (f32[3,3216]{1,0:T(4,128)S(1)}, f32[3,3216]{1,0:T(4,128)S(1)}, u32[]{:S(2)}, u32[]{:S(2)}) collective-permute-start(f32[3,3216]{1,0:T(4,128)S(1)} %add.124), channel_id=1, source_target_pairs={{0,1},{1,0},{2,3},{3,2},{4,5},{5,4},{6,7},{7,6},{8,9},{9,8},{10,11... | collective-permute-start | bytes 115784 | tf_op jit(solution)/shard_map/ppermute | solution.py:45
  135.6 5.8 %copy-start.48 = (f32[1,804]{1,0:T(1,128)S(1)}, f32[1,804]{1,0:T(1,128)}, u32[]{:S(2)}) copy-start(f32[1,804]{1,0:T(1,128)} %param.21) | copy-start | bytes 9652
  135.6 5.8 %copy-start.50 = (f32[1,804]{1,0:T(1,128)S(1)}, f32[1,804]{1,0:T(1,128)}, u32[]{:S(2)}) copy-start(f32[1,804]{1,0:T(1,128)} %param.20) | copy-start | bytes 9652
  135.7 5.8 %copy-start.17 = (bf16[1,128,3072]{1,2,0:T(8,128)(2,1)S(1)}, bf16[1,128,3072]{1,2,0:T(8,128)(2,1)}, u32[]{:S(2)}) copy-start(bf16[1,128,3072]{1,2,0:T(8,128)(2,1)} %get-tuple-element.69) | copy-start | bytes 2359300
  135.7 7.0 %copy-start.16 = (bf16[1,128,3072]{1,2,0:T(8,128)(2,1)S(1)}, bf16[1,128,3072]{1,2,0:T(8,128)(2,1)}, u32[]{:S(2)}) copy-start(bf16[1,128,3072]{1,2,0:T(8,128)(2,1)} %get-tuple-element.67) | copy-start | bytes 2359300
  135.7 20.6 %all-to-all-start.4 = ((bf16[4,128,1036]{1,2,0:T(8,128)(2,1)}), bf16[4,128,1036]{1,2,0:T(8,128)(2,1)S(1)}, u32[]{:S(2)}, u32[]{:S(2)}) async-start(bf16[4,128,1036]{1,2,0:T(8,128)(2,1)} %copy.169), calls=%async_computation.4 | async-start | bytes 2129920 | tf_op jit(solution)/shard_map/all_to_all | solution.py:30
  139.4 12.9 %collective-permute-start.4 = (f32[3,3216]{1,0:T(4,128)S(1)}, f32[3,3216]{1,0:T(4,128)S(1)}, u32[]{:S(2)}, u32[]{:S(2)}) collective-permute-start(f32[3,3216]{1,0:T(4,128)S(1)} %add.125), channel_id=1, source_target_pairs={{0,2},{1,3},{2,0},{3,1},{4,6},{5,7},{6,4},{7,5},{8,10},{9,11},{10,... | collective-permute-start | bytes 115784 | tf_op jit(solution)/shard_map/ppermute | solution.py:45
  141.4 14.2 %copy-start.45 = (f32[3216]{0:T(1024)S(1)}, f32[3216]{0:T(1024)}, u32[]{:S(2)}) copy-start(f32[3216]{0:T(1024)} %param.19) | copy-start | bytes 38596
  (13 other events, 15.4 us)

commit v9 on v8

--- a/solution.py
+++ b/solution.py
@@ -204,13 +204,12 @@
     slots = jnp.arange(slot_cap, dtype=jnp.int32)
     valid = slots < row_size
     padding = jnp.zeros((slot_cap,), jnp.float32)
-    sender = (lax.axis_index("ctx") == 0) & valid
-    own_state = jnp.where(sender, jnp.stack([adam_mean[0], adam_square[0]]), 0.0)
+    own_state = jnp.where(valid, jnp.stack([adam_mean[0], adam_square[0]]), 0.0)
     laid = lax.dynamic_update_slice(
         jnp.zeros((2, total_len + slot_cap), jnp.float32), own_state, (0, row_begin)
     )[:, :total_len]
-    summed = tree_sum(tree_sum(jnp.concatenate([grad_part[None], laid]), "dp"), "ctx")
-    gradient = summed[0]
+    summed = tree_sum(jnp.concatenate([grad_part[None], laid]), "dp")
+    gradient = tree_sum(summed[0], "ctx")
     mean_flat = summed[1]
     square_flat = summed[2]
     grad_norm = jnp.sqrt(jnp.sum(gradient * gradient))

time: 161 us -> 160 us (level)
  no operation moved by 1% of the time
where the time goes in v9:
time: 160 us; the launch traced here: 159 us
  local copies, waits for them, and re-layouts  46.1 us (29%)
  other arithmetic  39.5 us (25%)
  starting transfers between devices  29.7 us (19%)
  waiting for transfers between devices  20.7 us (13%)
  matrix products  17.8 us (11%)
  between operations  5.12 us (3%)
    unnamed x147, local copies, waits for them, and re-layouts  15.5 us
    ppermute x5, waiting for transfers between devices, tree_sum(): x = x + lax.ppermute(x, axis, [(i, i ^ step) for i in range(size)])  11.6 us
    all_to_all x2, starting transfers between devices, to_heads(): x = lax.all_to_all(x, 'ctx', 0, 0, tiled=True)  8.55 us
    all_to_all x2, starting transfers between devices, from_heads(): return lax.all_to_all(x, 'ctx', 0, 0, tiled=True)  8.05 us
    ppermute x5, starting transfers between devices, tree_sum(): x = x + lax.ppermute(x, axis, [(i, i ^ step) for i in range(size)])  7.96 us
    convert_element_type x3, local copies, waits for them, and re-layouts, ssd_group(): inputs = hidden.astype(jnp.float32).reshape(blocks, SPAN, heads, width)  7.15 us
    convert_element_type x3, local copies, waits for them, and re-layouts, ssd_group(): return output.reshape(length, heads * width).astype(jnp.bfloat16)  7.13 us
    convert_element_type x4, other arithmetic, rounded(): value.astype(jnp.bfloat16)  7.06 us
  transfers between devices with their start and end apart: 10, of which 7 were waited for; matrix products, arithmetic and copies ran while one was open for 20% of the time, Pallas kernels for 0%

profile of v9, /device:TPU:0, one launch (start us, length us, event | category | flops | bytes accessed | tf_op | source)
XLA Modules:
  0.0 158.9 jit_solution(13001515911633090610)
XLA Ops:
  0.7 0.9 pad_maximum_fusion.2
  2.4 0.7 pad_maximum_fusion.1
  3.1 5.2 %all-to-all-start.1 = ((bf16[4,128,268]{1,2,0:T(8,128)(2,1)}), bf16[4,128,268]{1,2,0:T(8,128)(2,1)S(1)}, u32[]{:S(2)}, u32[]{:S(2)}) async-start(bf16[4,128,268]{1,2,0:T(8,128)(2,1)} %pad_maximum_fusion.1), calls=%async_computation.1 | async-start | bytes 557056 | tf_op jit(solution)/shard_map/all_to_all | solution.py:151
  9.1 1.2 copy.143
  11.0 2.8 %all-to-all-done.1 = bf16[4,128,268]{1,2,0:T(8,128)(2,1)S(1)} async-done(((bf16[4,128,268]{1,2,0:T(8,128)(2,1)}), bf16[4,128,268]{1,2,0:T(8,128)(2,1)S(1)}, u32[]{:S(2)}, u32[]{:S(2)}) %all-to-all-start.1) | async-done | bytes 274464 | tf_op jit(solution)/shard_map/all_to_all | solution.py:151
  13.8 4.2 %all-to-all-start = ((bf16[4,128,768]{1,2,0:T(8,128)(2,1)}), bf16[4,128,768]{1,2,0:T(8,128)(2,1)}, u32[]{:S(2)}, u32[]{:S(2)}) async-start(bf16[4,128,768]{1,2,0:T(8,128)(2,1)} %bitcast.1), calls=%async_computation | async-start | bytes 1572864 | tf_op jit(solution)/shard_map/all_to_all | solution.py:23
  20.6 1.8 %multiply_convert_fusion.2 = bf16[2,12,256,128]{3,2,1,0:T(8,128)(2,1)} fusion(f32[2,12,256]{2,1,0:T(8,128)S(1)} %get-tuple-element.82, f32[2,256,128]{2,1,0:T(8,128)S(1)} %bitcast_convert_fusion), kind=kLoop, calls=%fused_computation.20 | loop fusion | flops 1572864 | bytes 1859584 | tf_op jit(solution)/shard_map/jvp()/convert_element_type | solution.py:51
  22.9 1.7 %multiply_convert_fusion = bf16[2,12,256,256]{3,2,1,0:T(8,128)(2,1)S(1)} fusion(f32[2,12,256]{2,1,0:T(8,128)S(1)} %fusion.50, f32[2,256,256]{2,1,0:T(8,128)S(1)} %fusion.97, pred[256,256]{1,0:T(8,128)(4,1)S(1)} %iota_compare_fusion), kind=kLoop, calls=%fused_computation.6 | loop fusion | flops 7864320 | bytes 3760128 | tf_op jit(solution)/shard_map/jvp()/convert_element_type | solution.py:51
  25.3 1.9 %multiply_convert_fusion.1 = bf16[2,12,256,128]{3,2,1,0:T(8,128)(2,1)} fusion(f32[2,12,256]{2,1,0:T(8,128)S(1)} %get-tuple-element.81, f32[2,256,128]{2,1,0:T(8,128)S(1)} %bitcast_convert_fusion.1), kind=kLoop, calls=%fused_computation.19 | loop fusion | flops 1572864 | bytes 1859584 | tf_op jit(solution)/shard_map/jvp()/convert_element_type | solution.py:51
  27.1 0.8 fusion.76
  27.9 2.9 %copy.144 = f32[4,128,768]{1,0,2:T(4,128)} copy(bf16[4,128,768]{1,2,0:T(8,128)(2,1)} %all-to-all-done) | data formatting | bytes 2359296 | tf_op jit(solution)/shard_map/jvp()/convert_element_type | solution.py:63
  30.8 3.4 %reshape.323 = f32[2,256,12,64]{1,0,3,2:T(2,128)} reshape(f32[4,128,768]{1,0,2:T(4,128)} %copy.144) | data formatting | bytes 3145728 | tf_op jit(solution)/shard_map/jvp()/convert_element_type | solution.py:63
  34.3 1.7 %multiply_convert_fusion.5 = bf16[2,256,12,64]{1,3,2,0:T(8,128)(2,1)S(1)} fusion(f32[2,256,12,64]{1,0,3,2:T(2,128)} %reshape.323, f32[2,256,12]{1,2,0:T(8,128)S(1)} %copy.147), kind=kLoop, calls=%fused_computation.56 | loop fusion | flops 786432 | bytes 2383872 | tf_op jit(solution)/shard_map/jvp()/convert_element_type | solution.py:51
  36.1 1.8 %multiply_convert_fusion.6 = (bf16[1,12,128,64]{2,3,1,0:T(8,128)(2,1)S(1)}, f32[1,12,128,64]{2,3,1,0:T(8,128)}) fusion(f32[]{:T(128)} %bitcast.12, f32[12]{0:T(128)S(1)} %get-tuple-element.60, bf16[2,256,12,64]{1,3,2,0:T(8,128)(2,1)S(1)} %multiply_convert_fusion.5, bf16[2,12,256,128]{3,2,1,0:T(8,128)(2,1)S(1)} %copy-done.7), kind=kOutput, calls=%fused_computation.86 | convolution fusion | flops 50626560 | bytes 2949172 | tf_op jit(solution)/shard_map/jvp()/slice | solution.py:84
  38.1 1.1 fusion.98
  40.6 1.7 %copy.153 = bf16[2,256,12,64]{1,0,3,2:T(2,128)(2,1)} copy(bf16[2,256,12,64]{1,3,2,0:T(8,128)(2,1)S(1)} %fusion.27) | data formatting | bytes 1572864 | tf_op jit(solution)/shard_map/jvp()/convert_element_type | solution.py:88
  42.3 3.3 %convert_element_type.162 = bf16[4,128,768]{1,0,2:T(4,128)(2,1)} reshape(bf16[2,256,12,64]{1,0,3,2:T(2,128)(2,1)} %copy.153) | data formatting | bytes 1572864 | tf_op jit(solution)/shard_map/jvp()/convert_element_type | solution.py:88
  45.6 2.1 %copy.154 = bf16[4,128,768]{1,2,0:T(8,128)(2,1)} copy(bf16[4,128,768]{1,0,2:T(4,128)(2,1)} %convert_element_type.162) | data formatting | bytes 1572864 | tf_op jit(solution)/shard_map/jvp()/convert_element_type | solution.py:88
  47.7 4.4 %all-to-all-start.2 = ((bf16[4,128,768]{1,2,0:T(8,128)(2,1)}), bf16[4,128,768]{1,2,0:T(8,128)(2,1)}, u32[]{:S(2)}, u32[]{:S(2)}) async-start(bf16[4,128,768]{1,2,0:T(8,128)(2,1)} %copy.154), calls=%async_computation.2 | async-start | bytes 1572864 | tf_op jit(solution)/shard_map/all_to_all | solution.py:30
  52.1 0.8 slice.103
  52.9 2.3 %copy.155 = bf16[1,128,3072]{1,2,0:T(8,128)(2,1)} copy(bf16[1,128,3072]{2,1,0:T(8,128)(2,1)} %param.13) | data formatting | bytes 1572864 | tf_op args[1]
  55.2 2.3 %copy.156 = bf16[1,128,3072]{1,2,0:T(8,128)(2,1)} copy(bf16[1,128,3072]{2,1,0:T(8,128)(2,1)} %param.18) | data formatting | bytes 1572864 | tf_op args[6]
  57.5 4.9 %all-to-all-done.2 = bf16[4,128,768]{1,2,0:T(8,128)(2,1)} async-done(((bf16[4,128,768]{1,2,0:T(8,128)(2,1)}), bf16[4,128,768]{1,2,0:T(8,128)(2,1)}, u32[]{:S(2)}, u32[]{:S(2)}) %all-to-all-start.2) | async-done | bytes 786464 | tf_op jit(solution)/shard_map/all_to_all | solution.py:30
  62.3 1.3 convert_element_type.194
  64.9 1.5 fusion.16
  66.4 2.6 %fusion.25 = (bf16[1,128,3072]{1,2,0:T(8,128)(2,1)}, bf16[1,128,3072]{1,2,0:T(8,128)(2,1)}, bf16[1,128,3072]{1,2,0:T(8,128)(2,1)}) fusion(bf16[1,128,3072]{1,2,0:T(8,128)(2,1)S(1)} %copy-done.11, f32[1,128,3072]{1,2,0:T(8,128)S(1)} %get-tuple-element.68, bf16[1,128,3072]{1,2,0:T(8,128)(2,1)S(1)} %copy-done.12, f32[128]{0:T(128)S(1)} %fusion.85, ...), kind=kLoop, calls=%fused_computation.45 | loop fusion | flops 8650752 | bytes 7091200 | tf_op jit(solution)/shard_map/convert_element_type | solution.py:112
  69.0 4.4 %all-to-all-start.3 = ((bf16[4,128,768]{1,2,0:T(8,128)(2,1)}), bf16[4,128,768]{1,2,0:T(8,128)(2,1)}, u32[]{:S(2)}, u32[]{:S(2)}) async-start(bf16[4,128,768]{1,2,0:T(8,128)(2,1)} %bitcast.166), calls=%async_computation.3 | async-start | bytes 1572864 | tf_op jit(solution)/shard_map/all_to_all | solution.py:23
  73.6 1.4 fusion.84
  74.9 1.4 fusion.83
  79.6 1.5 dynamic_update_slice.7
  81.1 1.3 slice.128
  82.4 1.3 all-to-all-done.3
  83.8 2.6 %copy.157 = bf16[4,128,768]{1,0,2:T(4,128)(2,1)} copy(bf16[4,128,768]{1,2,0:T(8,128)(2,1)} %all-to-all-done.3) | data formatting | bytes 1572864 | tf_op jit(solution)/shard_map/all_to_all | solution.py:23
  86.4 3.0 %squeeze_broadcast_in_dim_reshape.4 = bf16[2,256,12,64]{1,0,3,2:T(2,128)(2,1)} reshape(bf16[4,128,768]{1,0,2:T(4,128)(2,1)} %copy.157) | data formatting | bytes 1572864 | tf_op jit(solution)/shard_map/squeeze;broadcast_in_dim;reshape | solution.py:180
  89.4 2.1 %convolution_convert_fusion.3 = bf16[2,12,128,64]{2,3,1,0:T(8,128)(2,1)S(1)} fusion(bf16[2,12,256,128]{3,2,1,0:T(8,128)(2,1)} %multiply_convert_fusion.1, bf16[2,256,12,64]{1,0,3,2:T(2,128)(2,1)} %squeeze_broadcast_in_dim_reshape.4), kind=kOutput, calls=%fused_computation.58 | convolution fusion | flops 100859904 | bytes 2752512 | tf_op jit(solution)/shard_map/transpose(jvp(chtn,chnp->cthp))/dot_general | solution.py:86
  91.5 1.9 %convolution_convert_fusion.2 = bf16[2,12,256,128]{3,2,1,0:T(8,128)(2,1)} fusion(bf16[2,12,128,64]{2,3,1,0:T(8,128)(2,1)S(1)} %concatenate.29, bf16[2,256,12,64]{1,0,3,2:T(2,128)(2,1)S(1)} %copy-done), kind=kOutput, calls=%fused_computation.32 | convolution fusion | flops 101449728 | bytes 2752512 | tf_op jit(solution)/shard_map/transpose(jvp(chtn,chnp->cthp))/dot_general | solution.py:86
  93.4 2.7 %convolution_convert_fusion = bf16[2,12,256,256]{3,2,1,0:T(8,128)(2,1)} fusion(bf16[2,256,12,64]{1,3,2,0:T(8,128)(2,1)S(1)} %copy-done.5, bf16[2,256,12,64]{1,0,3,2:T(2,128)(2,1)S(1)} %copy-done), kind=kOutput, calls=%fused_computation.24 | convolution fusion | flops 202899456 | bytes 4718592 | tf_op jit(solution)/shard_map/transpose(jvp(chts,cshp->cthp))/dot_general | solution.py:72
  96.1 1.8 %fusion.33 = f32[2,12,64,256]{3,2,1,0:T(8,128)} fusion(bf16[2,12,256,256]{3,2,1,0:T(8,128)(2,1)S(1)} %multiply_convert_fusion, bf16[2,256,12,64]{1,0,3,2:T(2,128)(2,1)S(1)} %copy-done), kind=kOutput, calls=%fused_computation.67 | convolution fusion | flops 201326592 | bytes 5505024 | tf_op jit(solution)/shard_map/transpose(jvp(chts,cshp->cthp))/dot_general | solution.py:72
  97.9 0.8 fusion.41
  98.7 1.0 fusion.45
  99.9 1.5 convolution_convert_fusion.1
  101.4 6.0 %fusion.7 = (f32[2,256,128]{2,1,0:T(8,128)}, f32[2,12,256]{2,1,0:T(8,128)S(1)}, f32[2,12,256]{2,1,0:T(8,128)}, f32[2,256,128]{2,1,0:T(8,128)}) fusion(bf16[2,12,256,128]{3,2,1,0:T(8,128)(2,1)S(1)} %convolution_convert_fusion.1, f32[2,12,256]{2,1,0:T(8,128)S(1)} %copy-done.34, f32[2,256,128]{2,1,0:T(8,128)S(1)} %copy-done.21, f32[2,256,128]{2,1,0:T(8,128)} %copy-done.22, ...), kind=kLoop, calls=%fused_computation.15 | loop fusion | flops 7720960 | bytes 4292608 | tf_op jit(solution)/shard_map/transpose(jvp())/reduce_sum | solution.py:74
  108.3 5.7 %fusion.6 = (f32[2,12,256]{2,1,0:T(8,128)S(1)}, f32[2,12,256]{2,1,0:T(8,128)S(1)}, f32[2,256,256]{2,1,0:T(8,128)}) fusion(bf16[2,12,256,256]{3,2,1,0:T(8,128)(2,1)S(1)} %copy-done.10, f32[2,12,256]{2,1,0:T(8,128)S(1)} %copy-done.28, f32[2,256,256]{2,1,0:T(8,128)} %copy-done.15, pred[256,256]{1,0:T(8,128)(4,1)S(1)} %copy-done.37), kind=kLoop, calls=%fused_computation.10 | loop fusion | flops 18731008 | bytes 4333568 | tf_op jit(solution)/shard_map/transpose(jvp())/reduce_sum | solution.py:69
  114.4 2.5 %fusion.28 = bf16[2,256,12,64]{1,3,2,0:T(8,128)(2,1)S(1)} fusion(f32[2,12,64,256]{3,2,1,0:T(8,128)S(1)} %copy-done.13, bf16[2,12,256,128]{3,2,1,0:T(8,128)(2,1)S(1)} %copy-done.8, f32[12]{0:T(128)S(1)} %copy-done.52, f32[]{:T(128)} %bitcast.12, bf16[2,12,128,64]{2,3,1,0:T(8,128)(2,1)S(1)} %copy-done.19), kind=kOutput, calls=%fused_computation.57 | convolution fusion | flops 303071232 | bytes 4129284 | tf_op jit(solution)/shard_map/transpose(jvp(chsn,cshp->chnp))/dot_general | solution.py:75
  117.7 1.0 fusion.91
  118.7 0.7 bitcast_multiply_fusion.4
  119.5 1.6 %multiply_reduce_fusion = f32[768]{0:T(1024)S(1)} fusion(bf16[4,128,768]{1,2,0:T(8,128)(2,1)} %all-to-all-done.3, bf16[4,128,768]{1,2,0:T(8,128)(2,1)} %all-to-all-done), kind=kLoop, calls=%fused_computation.51 | loop fusion | flops 1572096 | bytes 1575936 | tf_op jit(solution)/shard_map/transpose(jvp())/reduce_sum | solution.py:87
  122.0 1.2 collective-permute-done
  123.3 1.6 %collective-permute-start.1 = (f32[3,3216]{1,0:T(4,128)S(1)}, f32[3,3216]{1,0:T(4,128)S(1)}, u32[]{:S(2)}, u32[]{:S(2)}) collective-permute-start(f32[3,3216]{1,0:T(4,128)S(1)} %fusion.89), channel_id=1, source_target_pairs={{0,8},{4,12},{8,0},{12,4},{16,24},{20,28},{24,16},{28,20},{1,9},{5... | collective-permute-start | bytes 115784 | tf_op jit(solution)/shard_map/ppermute | solution.py:45
  125.6 1.9 %collective-permute-done.1 = f32[3,3216]{1,0:T(4,128)S(1)} collective-permute-done((f32[3,3216]{1,0:T(4,128)S(1)}, f32[3,3216]{1,0:T(4,128)S(1)}, u32[]{:S(2)}, u32[]{:S(2)}) %collective-permute-start.1) | collective-permute-done | bytes 38624 | tf_op jit(solution)/shard_map/ppermute | solution.py:45
  127.5 2.7 %collective-permute-start.2 = (f32[3,3216]{1,0:T(4,128)S(1)}, f32[3,3216]{1,0:T(4,128)S(1)}, u32[]{:S(2)}, u32[]{:S(2)}) collective-permute-start(f32[3,3216]{1,0:T(4,128)S(1)} %add.123), channel_id=1, source_target_pairs={{0,16},{4,20},{8,24},{12,28},{16,0},{20,4},{24,8},{28,12},{1,17},{... | collective-permute-start | bytes 115784 | tf_op jit(solution)/shard_map/ppermute | solution.py:45
  130.8 0.8 copy.160
  131.8 0.8 collective-permute-done.2
  132.7 1.5 collective-permute-start.3
  134.7 1.1 copy.169
  135.8 3.7 %all-to-all-start.4 = ((bf16[4,128,1036]{1,2,0:T(8,128)(2,1)}), bf16[4,128,1036]{1,2,0:T(8,128)(2,1)S(1)}, u32[]{:S(2)}, u32[]{:S(2)}) async-start(bf16[4,128,1036]{1,2,0:T(8,128)(2,1)} %copy.169), calls=%async_computation.4 | async-start | bytes 2129920 | tf_op jit(solution)/shard_map/all_to_all | solution.py:30
  139.5 2.0 %collective-permute-start.4 = (f32[3216]{0:T(1024)S(1)}, f32[3216]{0:T(1024)S(1)}, u32[]{:S(2)}, u32[]{:S(2)}) collective-permute-start(f32[3216]{0:T(1024)S(1)} %add.125), channel_id=1, source_target_pairs={{0,2},{1,3},{2,0},{3,1},{4,6},{5,7},{6,4},{7,5},{8,10},{9,11},{10,... | collective-permute-start | bytes 38600 | tf_op jit(solution)/shard_map/ppermute | solution.py:45
  141.6 1.2 copy.171
  142.8 1.2 copy.173
  144.0 7.7 %collective-permute-done.4 = f32[3216]{0:T(1024)S(1)} collective-permute-done((f32[3216]{0:T(1024)S(1)}, f32[3216]{0:T(1024)S(1)}, u32[]{:S(2)}, u32[]{:S(2)}) %collective-permute-start.4) | collective-permute-done | bytes 12896 | tf_op jit(solution)/shard_map/ppermute | solution.py:45
  153.0 0.8 fusion.78
  155.6 1.2 copy.172
  156.9 0.7 copy.174
  157.6 0.7 copy.175
  (217 shorter events, 17.6 us)
Async XLA Ops:
  0.6 7.7 %slice-start = ((f32[3216]{0:T(1024)}), f32[144]{0:T(256)S(1)}, s32[]{:S(2)}) async-start(f32[3216]{0:T(1024)} %param.19), calls=%async_computation.5 | async-start | bytes 2048 | tf_op jit(solution)/shard_map/slice | solution.py:139
  0.7 7.8 %copy-start.65 = (s32[1,2]{1,0:T(1,128)S(1)}, s32[1,2]{1,0:T(1,128)}, u32[]{:S(2)}) copy-start(s32[1,2]{1,0:T(1,128)} %param.17) | copy-start | bytes 28
  0.7 8.4 %copy-start.35 = (bf16[1,128,3072]{2,1,0:T(8,128)(2,1)S(1)}, bf16[1,128,3072]{2,1,0:T(8,128)(2,1)}, u32[]{:S(2)}) copy-start(bf16[1,128,3072]{2,1,0:T(8,128)(2,1)} %param.12) | copy-start | bytes 2359300
  3.1 10.7 %all-to-all-start.1 = ((bf16[4,128,268]{1,2,0:T(8,128)(2,1)}), bf16[4,128,268]{1,2,0:T(8,128)(2,1)S(1)}, u32[]{:S(2)}, u32[]{:S(2)}) async-start(bf16[4,128,268]{1,2,0:T(8,128)(2,1)} %pad_maximum_fusion.1), calls=%async_computation.1 | async-start | bytes 557056 | tf_op jit(solution)/shard_map/all_to_all | solution.py:151
  8.4 14.5 %copy-start.36 = (pred[256,256]{1,0:T(8,128)(4,1)}, pred[256,256]{1,0:T(8,128)(4,1)S(1)}, u32[]{:S(2)}) copy-start(pred[256,256]{1,0:T(8,128)(4,1)S(1)} %iota_compare_fusion) | copy-start | bytes 196612
  11.0 7.4 %copy-start.53 = (f32[3,12]{1,0:T(4,128)}, f32[3,12]{1,0:T(4,128)S(1)}, u32[]{:S(2)}) copy-start(f32[3,12]{1,0:T(4,128)S(1)} %constant_dynamic-slice_fusion) | copy-start | bytes 436
  11.0 7.4 %copy-start.56 = (f32[12]{0:T(128)}, f32[12]{0:T(128)S(1)}, u32[]{:S(2)}) copy-start(f32[12]{0:T(128)S(1)} %get-tuple-element.86) | copy-start | bytes 148
  11.0 7.4 %copy-start.58 = (f32[12]{0:T(128)}, f32[12]{0:T(128)S(1)}, u32[]{:S(2)}) copy-start(f32[12]{0:T(128)S(1)} %get-tuple-element.87) | copy-start | bytes 148
  11.0 28.1 %copy-start.54 = (f32[12]{0:T(128)}, f32[12]{0:T(128)S(1)}, u32[]{:S(2)}) copy-start(f32[12]{0:T(128)S(1)} %get-tuple-element.85) | copy-start | bytes 148
  13.8 14.1 %all-to-all-start = ((bf16[4,128,768]{1,2,0:T(8,128)(2,1)}), bf16[4,128,768]{1,2,0:T(8,128)(2,1)}, u32[]{:S(2)}, u32[]{:S(2)}) async-start(bf16[4,128,768]{1,2,0:T(8,128)(2,1)} %bitcast.1), calls=%async_computation | async-start | bytes 1572864 | tf_op jit(solution)/shard_map/all_to_all | solution.py:23
  19.4 7.7 %copy-start.27 = (f32[2,12,256]{2,1,0:T(8,128)}, f32[2,12,256]{2,1,0:T(8,128)S(1)}, u32[]{:S(2)}) copy-start(f32[2,12,256]{2,1,0:T(8,128)S(1)} %fusion.50) | copy-start | bytes 73732
  19.7 2.9 %copy-start.33 = (f32[2,12,256]{2,1,0:T(8,128)}, f32[2,12,256]{2,1,0:T(8,128)S(1)}, u32[]{:S(2)}) copy-start(f32[2,12,256]{2,1,0:T(8,128)S(1)} %get-tuple-element.82) | copy-start | bytes 73732
  19.7 4.9 %copy-start.40 = (f32[2,12,256]{2,1,0:T(8,128)}, f32[2,12,256]{2,1,0:T(8,128)S(1)}, u32[]{:S(2)}) copy-start(f32[2,12,256]{2,1,0:T(8,128)S(1)} %get-tuple-element.81) | copy-start | bytes 73732
  19.8 2.8 %copy-start.23 = (bf16[512,128]{1,0:T(8,128)(2,1)}, bf16[512,128]{1,0:T(8,128)(2,1)S(1)}, u32[]{:S(2)}) copy-start(bf16[512,128]{1,0:T(8,128)(2,1)S(1)} %copy.150) | copy-start | bytes 393220
  22.5 11.8 %copy-start.38 = (f32[2,256,12]{1,2,0:T(8,128)}, f32[2,256,12]{1,2,0:T(8,128)S(1)}, u32[]{:S(2)}) copy-start(f32[2,256,12]{1,2,0:T(8,128)S(1)} %copy.147) | copy-start | bytes 73732
  22.6 2.0 %copy-start.25 = (bf16[512,128]{1,0:T(8,128)(2,1)}, bf16[512,128]{1,0:T(8,128)(2,1)S(1)}, u32[]{:S(2)}) copy-start(bf16[512,128]{1,0:T(8,128)(2,1)S(1)} %copy.149) | copy-start | bytes 393220
  27.9 8.1 %copy-start.60 = (f32[12]{0:T(128)}, f32[12]{0:T(128)S(1)}, u32[]{:S(2)}) copy-start(f32[12]{0:T(128)S(1)} %get-tuple-element.60) | copy-start | bytes 148
  34.3 1.9 %copy-start.7 = (bf16[2,12,256,128]{3,2,1,0:T(8,128)(2,1)S(1)}, bf16[2,12,256,128]{3,2,1,0:T(8,128)(2,1)}, u32[]{:S(2)}) copy-start(bf16[2,12,256,128]{3,2,1,0:T(8,128)(2,1)} %multiply_convert_fusion.2) | copy-start | bytes 4718596
  36.0 2.1 %copy-start.4 = (bf16[2,256,12,64]{1,3,2,0:T(8,128)(2,1)}, bf16[2,256,12,64]{1,3,2,0:T(8,128)(2,1)S(1)}, u32[]{:S(2)}) copy-start(bf16[2,256,12,64]{1,3,2,0:T(8,128)(2,1)S(1)} %multiply_convert_fusion.5) | copy-start | bytes 2359300
  47.7 14.6 %all-to-all-start.2 = ((bf16[4,128,768]{1,2,0:T(8,128)(2,1)}), bf16[4,128,768]{1,2,0:T(8,128)(2,1)}, u32[]{:S(2)}, u32[]{:S(2)}) async-start(bf16[4,128,768]{1,2,0:T(8,128)(2,1)} %copy.154), calls=%async_computation.2 | async-start | bytes 1572864 | tf_op jit(solution)/shard_map/all_to_all | solution.py:30
  69.0 4.4 %copy-start.62 = (s32[8]{0:T(128)S(1)}, s32[8]{0:T(128)}, u32[]{:S(2)}) copy-start(s32[8]{0:T(128)} %param.22) | copy-start | bytes 100
  69.0 9.9 %copy-start.47 = (f32[1,804]{1,0:T(1,128)S(1)}, f32[1,804]{1,0:T(1,128)}, u32[]{:S(2)}) copy-start(f32[1,804]{1,0:T(1,128)} %param.21) | copy-start | bytes 9652
  69.0 9.9 %copy-start.49 = (f32[1,804]{1,0:T(1,128)S(1)}, f32[1,804]{1,0:T(1,128)}, u32[]{:S(2)}) copy-start(f32[1,804]{1,0:T(1,128)} %param.20) | copy-start | bytes 9652
  69.0 14.8 %all-to-all-start.3 = ((bf16[4,128,768]{1,2,0:T(8,128)(2,1)}), bf16[4,128,768]{1,2,0:T(8,128)(2,1)}, u32[]{:S(2)}, u32[]{:S(2)}) async-start(bf16[4,128,768]{1,2,0:T(8,128)(2,1)} %bitcast.166), calls=%async_computation.3 | async-start | bytes 1572864 | tf_op jit(solution)/shard_map/all_to_all | solution.py:23
  89.4 2.1 %copy-start = (bf16[2,256,12,64]{1,0,3,2:T(2,128)(2,1)S(1)}, bf16[2,256,12,64]{1,0,3,2:T(2,128)(2,1)}, u32[]{:S(2)}) copy-start(bf16[2,256,12,64]{1,0,3,2:T(2,128)(2,1)} %squeeze_broadcast_in_dim_reshape.4) | copy-start | bytes 2359300
  91.5 7.2 %copy-start.18 = (bf16[2,12,128,64]{2,3,1,0:T(8,128)(2,1)}, bf16[2,12,128,64]{2,3,1,0:T(8,128)(2,1)S(1)}, u32[]{:S(2)}) copy-start(bf16[2,12,128,64]{2,3,1,0:T(8,128)(2,1)S(1)} %convolution_convert_fusion.3) | copy-start | bytes 1179652
  96.1 2.6 %copy-start.29 = (f32[1,12,128,64]{2,3,1,0:T(8,128)S(1)}, f32[1,12,128,64]{2,3,1,0:T(8,128)}, u32[]{:S(2)}) copy-start(f32[1,12,128,64]{2,3,1,0:T(8,128)} %get-tuple-element.91) | copy-start | bytes 1179652
  96.1 2.6 %copy-start.61 = (f32[12]{0:T(128)S(1)}, f32[12]{0:T(128)}, u32[]{:S(2)}) copy-start(f32[12]{0:T(128)} %copy-done.60) | copy-start | bytes 148
  96.1 3.7 %copy-start.64 = (f32[12]{0:T(128)S(1)}, f32[12]{0:T(128)}, u32[]{:S(2)}) copy-start(f32[12]{0:T(128)} %get-tuple-element.57) | copy-start | bytes 148
  96.1 3.7 %copy-start.63 = (f32[12]{0:T(128)S(1)}, f32[12]{0:T(128)}, u32[]{:S(2)}) copy-start(f32[12]{0:T(128)} %get-tuple-element.58) | copy-start | bytes 148
  97.9 2.0 %copy-start.6 = (bf16[2,256,12,64]{1,3,2,0:T(8,128)(2,1)S(1)}, bf16[2,256,12,64]{1,3,2,0:T(8,128)(2,1)}, u32[]{:S(2)}) copy-start(bf16[2,256,12,64]{1,3,2,0:T(8,128)(2,1)} %copy-done.4) | copy-start | bytes 2359300
  98.7 2.6 %copy-start.21 = (f32[2,256,128]{2,1,0:T(8,128)S(1)}, f32[2,256,128]{2,1,0:T(8,128)}, u32[]{:S(2)}) copy-start(f32[2,256,128]{2,1,0:T(8,128)} %copy-done.20) | copy-start | bytes 786436
  98.7 2.6 %copy-start.34 = (f32[2,12,256]{2,1,0:T(8,128)S(1)}, f32[2,12,256]{2,1,0:T(8,128)}, u32[]{:S(2)}) copy-start(f32[2,12,256]{2,1,0:T(8,128)} %copy-done.33) | copy-start | bytes 73732
  101.4 6.8 %copy-start.10 = (bf16[2,12,256,256]{3,2,1,0:T(8,128)(2,1)S(1)}, bf16[2,12,256,256]{3,2,1,0:T(8,128)(2,1)}, u32[]{:S(2)}) copy-start(bf16[2,12,256,256]{3,2,1,0:T(8,128)(2,1)} %convolution_convert_fusion) | copy-start | bytes 9437188
  101.4 6.8 %copy-start.28 = (f32[2,12,256]{2,1,0:T(8,128)S(1)}, f32[2,12,256]{2,1,0:T(8,128)}, u32[]{:S(2)}) copy-start(f32[2,12,256]{2,1,0:T(8,128)} %copy-done.27) | copy-start | bytes 73732
  101.4 6.8 %copy-start.37 = (pred[256,256]{1,0:T(8,128)(4,1)S(1)}, pred[256,256]{1,0:T(8,128)(4,1)}, u32[]{:S(2)}) copy-start(pred[256,256]{1,0:T(8,128)(4,1)} %copy-done.36) | copy-start | bytes 196612
  108.2 5.8 %copy-start.42 = (f32[2,12,256]{2,1,0:T(8,128)S(1)}, f32[2,12,256]{2,1,0:T(8,128)}, u32[]{:S(2)}) copy-start(f32[2,12,256]{2,1,0:T(8,128)} %copy-done.41) | copy-start | bytes 73732
  108.2 5.8 %copy-start.44 = (f32[2,12,256]{2,1,0:T(8,128)S(1)}, f32[2,12,256]{2,1,0:T(8,128)}, u32[]{:S(2)}) copy-start(f32[2,12,256]{2,1,0:T(8,128)} %get-tuple-element.94) | copy-start | bytes 73732
  108.2 6.1 %copy-start.8 = (bf16[2,12,256,128]{3,2,1,0:T(8,128)(2,1)S(1)}, bf16[2,12,256,128]{3,2,1,0:T(8,128)(2,1)}, u32[]{:S(2)}) copy-start(bf16[2,12,256,128]{3,2,1,0:T(8,128)(2,1)} %multiply_convert_fusion.2) | copy-start | bytes 4718596
  108.2 6.1 %copy-start.13 = (f32[2,12,64,256]{3,2,1,0:T(8,128)S(1)}, f32[2,12,64,256]{3,2,1,0:T(8,128)}, u32[]{:S(2)}) copy-start(f32[2,12,64,256]{3,2,1,0:T(8,128)} %fusion.33) | copy-start | bytes 4718596
  108.3 6.1 %copy-start.19 = (bf16[2,12,128,64]{2,3,1,0:T(8,128)(2,1)S(1)}, bf16[2,12,128,64]{2,3,1,0:T(8,128)(2,1)}, u32[]{:S(2)}) copy-start(bf16[2,12,128,64]{2,3,1,0:T(8,128)(2,1)} %copy-done.18) | copy-start | bytes 1179652
  108.3 6.1 %copy-start.52 = (f32[12]{0:T(128)S(1)}, f32[12]{0:T(128)}, u32[]{:S(2)}) copy-start(f32[12]{0:T(128)} %get-tuple-element.59) | copy-start | bytes 148
  114.3 2.6 %copy-start.1 = (bf16[2,256,12,64]{1,0,3,2:T(2,128)(2,1)S(1)}, bf16[2,256,12,64]{1,0,3,2:T(2,128)(2,1)}, u32[]{:S(2)}) copy-start(bf16[2,256,12,64]{1,0,3,2:T(2,128)(2,1)} %squeeze_broadcast_in_dim_reshape.4) | copy-start | bytes 2359300
  114.4 2.6 %copy-start.3 = (f32[2,256,12,64]{1,0,3,2:T(2,128)S(1)}, f32[2,256,12,64]{1,0,3,2:T(2,128)}, u32[]{:S(2)}) copy-start(f32[2,256,12,64]{1,0,3,2:T(2,128)} %reshape.323) | copy-start | bytes 4718596
  114.4 2.6 %copy-start.39 = (f32[2,256,12]{1,2,0:T(8,128)S(1)}, f32[2,256,12]{1,2,0:T(8,128)}, u32[]{:S(2)}) copy-start(f32[2,256,12]{1,2,0:T(8,128)} %copy-done.38) | copy-start | bytes 73732
  114.4 2.6 %copy-start.55 = (f32[12]{0:T(128)S(1)}, f32[12]{0:T(128)}, u32[]{:S(2)}) copy-start(f32[12]{0:T(128)} %copy-done.54) | copy-start | bytes 148
  117.6 4.2 %copy-start.46 = (f32[3072]{0:T(1024)S(1)}, f32[3072]{0:T(1024)}, u32[]{:S(2)}) copy-start(f32[3072]{0:T(1024)} %get-tuple-element.48) | copy-start | bytes 36868
  117.6 4.3 %copy-start.43 = (f32[2,3216]{1,0:T(2,128)S(1)}, f32[2,3216]{1,0:T(2,128)}, u32[]{:S(2)}) copy-start(f32[2,3216]{1,0:T(2,128)} %slice.128) | copy-start | bytes 77188
  117.6 7.3 %copy-start.14 = (f32[2,256,256]{2,1,0:T(8,128)S(1)}, f32[2,256,256]{2,1,0:T(8,128)}, u32[]{:S(2)}) copy-start(f32[2,256,256]{2,1,0:T(8,128)} %get-tuple-element.47) | copy-start | bytes 1572868
  117.6 7.3 %copy-start.26 = (bf16[512,128]{1,0:T(8,128)(2,1)S(1)}, bf16[512,128]{1,0:T(8,128)(2,1)}, u32[]{:S(2)}) copy-start(bf16[512,128]{1,0:T(8,128)(2,1)} %copy-done.25) | copy-start | bytes 393220
  117.6 7.3 %copy-start.32 = (f32[2,256,128]{2,1,0:T(8,128)S(1)}, f32[2,256,128]{2,1,0:T(8,128)}, u32[]{:S(2)}) copy-start(f32[2,256,128]{2,1,0:T(8,128)} %get-tuple-element.50) | copy-start | bytes 786436
  118.7 11.4 %copy-start.24 = (bf16[512,128]{1,0:T(8,128)(2,1)S(1)}, bf16[512,128]{1,0:T(8,128)(2,1)}, u32[]{:S(2)}) copy-start(bf16[512,128]{1,0:T(8,128)(2,1)} %copy-done.23) | copy-start | bytes 393220
  118.7 11.4 %copy-start.31 = (f32[2,256,128]{2,1,0:T(8,128)S(1)}, f32[2,256,128]{2,1,0:T(8,128)}, u32[]{:S(2)}) copy-start(f32[2,256,128]{2,1,0:T(8,128)} %get-tuple-element.95) | copy-start | bytes 786436
  121.9 1.3 collective-permute-start
  123.3 4.2 %collective-permute-start.1 = (f32[3,3216]{1,0:T(4,128)S(1)}, f32[3,3216]{1,0:T(4,128)S(1)}, u32[]{:S(2)}, u32[]{:S(2)}) collective-permute-start(f32[3,3216]{1,0:T(4,128)S(1)} %fusion.89), channel_id=1, source_target_pairs={{0,8},{4,12},{8,0},{12,4},{16,24},{20,28},{24,16},{28,20},{1,9},{5... | collective-permute-start | bytes 115784 | tf_op jit(solution)/shard_map/ppermute | solution.py:45
  127.5 5.1 %collective-permute-start.2 = (f32[3,3216]{1,0:T(4,128)S(1)}, f32[3,3216]{1,0:T(4,128)S(1)}, u32[]{:S(2)}, u32[]{:S(2)}) collective-permute-start(f32[3,3216]{1,0:T(4,128)S(1)} %add.123), channel_id=1, source_target_pairs={{0,16},{4,20},{8,24},{12,28},{16,0},{20,4},{24,8},{28,12},{1,17},{... | collective-permute-start | bytes 115784 | tf_op jit(solution)/shard_map/ppermute | solution.py:45
  132.7 6.8 %collective-permute-start.3 = (f32[3216]{0:T(1024)S(1)}, f32[3216]{0:T(1024)S(1)}, u32[]{:S(2)}, u32[]{:S(2)}) collective-permute-start(f32[3216]{0:T(1024)S(1)} %get-tuple-element.54), channel_id=1, source_target_pairs={{0,1},{1,0},{2,3},{3,2},{4,5},{5,4},{6,7},{7,6},{8,9},{9,8},{10,11... | collective-permute-start | bytes 38600 | tf_op jit(solution)/shard_map/ppermute | solution.py:45
  135.8 5.7 %copy-start.48 = (f32[1,804]{1,0:T(1,128)S(1)}, f32[1,804]{1,0:T(1,128)}, u32[]{:S(2)}) copy-start(f32[1,804]{1,0:T(1,128)} %param.21) | copy-start | bytes 9652
  135.8 5.7 %copy-start.50 = (f32[1,804]{1,0:T(1,128)S(1)}, f32[1,804]{1,0:T(1,128)}, u32[]{:S(2)}) copy-start(f32[1,804]{1,0:T(1,128)} %param.20) | copy-start | bytes 9652
  135.8 5.8 %copy-start.17 = (bf16[1,128,3072]{1,2,0:T(8,128)(2,1)S(1)}, bf16[1,128,3072]{1,2,0:T(8,128)(2,1)}, u32[]{:S(2)}) copy-start(bf16[1,128,3072]{1,2,0:T(8,128)(2,1)} %get-tuple-element.71) | copy-start | bytes 2359300
  135.8 7.0 %copy-start.16 = (bf16[1,128,3072]{1,2,0:T(8,128)(2,1)S(1)}, bf16[1,128,3072]{1,2,0:T(8,128)(2,1)}, u32[]{:S(2)}) copy-start(bf16[1,128,3072]{1,2,0:T(8,128)(2,1)} %get-tuple-element.69) | copy-start | bytes 2359300
  135.8 19.7 %all-to-all-start.4 = ((bf16[4,128,1036]{1,2,0:T(8,128)(2,1)}), bf16[4,128,1036]{1,2,0:T(8,128)(2,1)S(1)}, u32[]{:S(2)}, u32[]{:S(2)}) async-start(bf16[4,128,1036]{1,2,0:T(8,128)(2,1)} %copy.169), calls=%async_computation.4 | async-start | bytes 2129920 | tf_op jit(solution)/shard_map/all_to_all | solution.py:30
  139.5 12.2 %collective-permute-start.4 = (f32[3216]{0:T(1024)S(1)}, f32[3216]{0:T(1024)S(1)}, u32[]{:S(2)}, u32[]{:S(2)}) collective-permute-start(f32[3216]{0:T(1024)S(1)} %add.125), channel_id=1, source_target_pairs={{0,2},{1,3},{2,0},{3,1},{4,6},{5,7},{6,4},{7,5},{8,10},{9,11},{10,... | collective-permute-start | bytes 38600 | tf_op jit(solution)/shard_map/ppermute | solution.py:45
  141.6 13.3 %copy-start.45 = (f32[3216]{0:T(1024)S(1)}, f32[3216]{0:T(1024)}, u32[]{:S(2)}) copy-start(f32[3216]{0:T(1024)} %param.19) | copy-start | bytes 38596
  (13 other events, 15.4 us)
